TPU v7x, 32 devices: a whole 2x2x4 slice. The times are simulated.
32 devices in a mesh: half: 2 (over x), row: 4 (over z), col: 4 (over y, core).
Axes of the slice: x: 2, y: 2, z: 4, core: 2. Of those that a mesh axis runs over, the one named last changes fastest.
Arguments:
- child_fronts: float32 [2, 6144, 6144], P('half', 'row', 'col'), may hold values from -1 to 40, as said below
- child_maps: int32 [2, 40], replicated, may hold values from 0 to 63, as said below
- parent_own: float32 [8192, 8192], P(('half', 'row'), 'col'), may hold values from -1 to 40, as said below
Outputs:
- child_factored: float32 [2, 6144, 6144], P('half', 'row', 'col')
- parent_factored: float32 [8192, 8192], P(('half', 'row'), 'col')
Inputs may be any that keep to these rules, and one draw needn't show every extreme that they name: child_fronts[h] is symmetric and positive definite. parent_own in logical order is symmetric and positive definite. child_maps[h, u] equals u + 1024 / 128 modulo 16; among the update tiles of one child with the same residue it increases with u.
All inputs are finite; a program needn't handle non-finite values.
Results may differ from a plain program's by a relative error of at most 0.0001.
Values sent between devices are 32-bit elements; how exact they have to be, the bound alone decides.
No kernel may reach another device: no remote copies, remote signals or barrier semaphores. Data moves between devices by JAX's collectives and lax.ppermute only.
A program may use at most 192 MiB of HBM per device.

v0:
```python
import jax
import jax.numpy as jnp
from jax import lax
from jax.sharding import PartitionSpec as P

TILE = 128
CHILD_PIVOTS = 1024
PARENT_PIVOTS = 128


def spread(shard, axis, root):
    mine = lax.axis_index(axis) == root
    return lax.psum(jnp.where(mine, shard, jnp.zeros_like(shard)), axis)


def from_partner(shard, axis, distance):
    return lax.ppermute(shard, axis, [(i, i ^ 1 << distance) for i in range(lax.axis_size(axis))])


def factor_front(
    front_work,
    pivot_count,
    row_groups,
    col_groups,
    my_row,
    my_col,
    fetch_panel,
    fetch_diag,
    fetch_across,
):
    row_count, col_count = front_work.shape
    row_tiles = jnp.arange(row_count, dtype=jnp.int32) // TILE * row_groups + my_row
    col_tiles = jnp.arange(col_count, dtype=jnp.int32) // TILE * col_groups + my_col

    def one_step(pivot_tile, current):
        row_slot = pivot_tile // row_groups
        col_slot = pivot_tile // col_groups
        column = lax.dynamic_slice_in_dim(current, col_slot * TILE, TILE, 1)
        col_panel = fetch_panel(column, pivot_tile)
        diag_block = fetch_diag(current, col_panel, pivot_tile, row_slot, col_slot)
        diag_factor = jnp.linalg.cholesky(diag_block)
        solved_panel = jax.scipy.linalg.solve_triangular(diag_factor, col_panel.T, lower=True).T
        across_panel = fetch_across(solved_panel)
        rows_after = (row_tiles > pivot_tile)[:, None]
        cols_after = (col_tiles > pivot_tile)[:, None]
        left_factor = jnp.where(rows_after, solved_panel, 0.0)
        right_factor = jnp.where(cols_after, across_panel, 0.0)
        current = current - jnp.dot(
            left_factor,
            right_factor.T,
            precision=lax.Precision.HIGHEST,
            preferred_element_type=jnp.float32,
        )
        pivot_rows = lax.dynamic_slice_in_dim(current, row_slot * TILE, TILE, 0)
        row_owner = my_row == pivot_tile % row_groups
        pivot_rows = jnp.where(row_owner & (col_tiles > pivot_tile)[None, :], 0.0, pivot_rows)
        current = lax.dynamic_update_slice_in_dim(current, pivot_rows, row_slot * TILE, 0)
        diag_rows = jnp.tile(jnp.tril(diag_factor), (row_count // TILE, 1))
        new_column = jnp.where(
            rows_after, solved_panel, jnp.where((row_tiles == pivot_tile)[:, None], diag_rows, 0.0)
        )
        old_column = lax.dynamic_slice_in_dim(current, col_slot * TILE, TILE, 1)
        new_column = jnp.where(my_col == pivot_tile % col_groups, new_column, old_column)
        return lax.dynamic_update_slice_in_dim(current, new_column, col_slot * TILE, 1)

    return lax.fori_loop(0, pivot_count // TILE, one_step, front_work)


def local(child_fronts, child_maps, parent_own):
    grid_size = lax.axis_size("row")
    half_index = lax.axis_index("half")
    my_row = lax.axis_index("row")
    my_col = lax.axis_index("col")

    def send_child_column(column, pivot_tile):
        return spread(column, "col", pivot_tile % grid_size)

    def send_child_block(current, col_panel, pivot_tile, row_slot, col_slot):
        own_block = lax.dynamic_slice_in_dim(col_panel, row_slot * TILE, TILE, 0)
        result_block = spread(own_block, "row", pivot_tile % grid_size)
        return result_block

    def send_child_rows(solved_panel):
        return spread(solved_panel, "row", my_col)

    child_done = factor_front(
        child_fronts[0],
        CHILD_PIVOTS,
        grid_size,
        grid_size,
        my_row,
        my_col,
        send_child_column,
        send_child_block,
        send_child_rows,
    )
    local_tiles = child_done.shape[0] // TILE
    pivot_tiles = CHILD_PIVOTS // TILE
    own_map = lax.dynamic_index_in_dim(child_maps, half_index, 0, keepdims=False)
    update_count = child_maps.shape[1]
    slot_ids = jnp.arange(local_tiles, dtype=jnp.int32)
    update_range = jnp.arange(update_count, dtype=jnp.int32)

    def parent_tile(offset):
        update_ids = slot_ids * grid_size + offset - pivot_tiles
        matches = update_ids[:, None] == update_range[None, :]
        return (jnp.sum(jnp.where(matches, own_map[None, :], 0), axis=1), update_ids >= 0)

    row_target, row_valid = parent_tile(my_row)
    col_target, col_valid = parent_tile(my_col)
    parent_row_tiles = parent_own.shape[0] // TILE
    parent_col_tiles = parent_own.shape[1] // TILE
    row_dest = (
        jnp.arange(parent_row_tiles, dtype=jnp.int32)[None, :] * (2 * grid_size)
        + jnp.arange(2, dtype=jnp.int32)[:, None] * grid_size
        + my_row
    )
    row_place = (
        (row_dest[:, :, None] == row_target[None, None, :]) & row_valid[None, None, :]
    ).astype(jnp.float32)
    col_dest = jnp.arange(parent_col_tiles, dtype=jnp.int32) * grid_size + my_col
    col_place = ((col_dest[:, None] == col_target[None, :]) & col_valid[None, :]).astype(
        jnp.float32
    )
    blocks = child_done.reshape(local_tiles, TILE, local_tiles, TILE)
    rows_moved = jnp.einsum("hak,kilj->hailj", row_place, blocks, precision=lax.Precision.HIGHEST)
    both_moved = jnp.einsum(
        "hailj,bl->haibj", rows_moved, col_place, precision=lax.Precision.HIGHEST
    )
    both_moved = both_moved.reshape(2, parent_own.shape[0], parent_own.shape[1])
    kept_part = lax.dynamic_index_in_dim(both_moved, half_index, 0, keepdims=False)
    sent_part = lax.dynamic_index_in_dim(both_moved, 1 - half_index, 0, keepdims=False)
    received = from_partner(sent_part, "half", 0)
    parent_start = parent_own + kept_part + received

    def send_parent_column(column, pivot_tile):
        return spread(column, "col", pivot_tile % grid_size)

    def send_parent_block(current, col_panel, pivot_tile, row_slot, col_slot):
        own_block = lax.dynamic_slice_in_dim(col_panel, row_slot * TILE, TILE, 0)
        result_block = spread(own_block, ("half", "row"), pivot_tile % (2 * grid_size))
        return result_block

    def send_parent_rows(solved_panel):
        pieces = [
            spread(solved_panel, ("half", "row"), which_half * grid_size + my_col)
            for which_half in range(2)
        ]
        even_tiles = pieces[0]
        odd_tiles = pieces[1]
        tile_count = solved_panel.shape[0] // TILE
        stacked = jnp.stack(
            [even_tiles.reshape(tile_count, TILE, TILE), odd_tiles.reshape(tile_count, TILE, TILE)],
            axis=1,
        )
        return stacked.reshape(2 * tile_count * TILE, TILE)

    parent_row = half_index * grid_size + my_row
    parent_done = factor_front(
        parent_start,
        PARENT_PIVOTS,
        2 * grid_size,
        grid_size,
        parent_row,
        my_col,
        send_parent_column,
        send_parent_block,
        send_parent_rows,
    )
    return (child_done[None], parent_done)


def solution(mesh):
    in_specs = (P("half", "row", "col"), P(), P(("half", "row"), "col"))
    out_specs = (P("half", "row", "col"), P(("half", "row"), "col"))
    return jax.shard_map(local, mesh=mesh, in_specs=in_specs, out_specs=out_specs, check_vma=False)
```

profile of v0, /device:TPU:4, one launch (start us, length us, event | category | flops | bytes accessed | tf_op | source)
XLA Modules:
  0.0 1818.0 jit_solution(15787087962608408631)
XLA Ops:
  16.3 1306.1 %while.22 = (s32[]{:T(128)}, f32[1536,1536]{1,0:T(8,128)}, s32[]{:T(128)}, s32[]{:T(128)}, s32[]{:T(128)}, /*index=5*/u32[]{:T(128)}, u32[]{:T(128)}, s32[]{:T(1...) while((s32[]{:T(128)}, f32[1536,1536]{1,0:T(8,128)}, ...), condition=%wide.region_6.8_spmd.clone.clone, body=%wide.region_0.7_spmd.clone.clone.sunk | while | flops 3930493696 | bytes 39205936 | solution.py:66
  18.6 36.5 %all-reduce.14.cloned.1.call-done = f32[1536,128]{1,0:T(8,128)} async-done(((f32[1536,128]{1,0:T(8,128)}), f32[1536,128]{1,0:T(8,128)}) %all-reduce.14.cloned.1.call-update) | async-done | bytes 786448 | tf_op jit(solution)/shard_map/while/body/eval_jaxpr/psum | solution.py:13
  56.7 36.6 %all-reduce.16.cloned.1.call-done = f32[128,128]{1,0:T(8,128)} async-done(((f32[128,128]{1,0:T(8,128)}), f32[128,128]{1,0:T(8,128)}) %all-reduce.16.cloned.1.call-update) | async-done | bytes 65552 | tf_op jit(solution)/shard_map/while/body/eval_jaxpr/psum | solution.py:13
  121.6 42.8 %all-reduce.18.cloned.1.call-done = f32[1536,128]{1,0:T(8,128)} async-done(((f32[1536,128]{1,0:T(8,128)}), f32[1536,128]{1,0:T(8,128)}) %all-reduce.18.cloned.1.call-update) | async-done | bytes 786448 | tf_op jit(solution)/shard_map/while/body/eval_jaxpr/psum | solution.py:13
  183.6 34.4 %all-reduce.14.cloned.1.call-done = f32[1536,128]{1,0:T(8,128)} async-done(((f32[1536,128]{1,0:T(8,128)}), f32[1536,128]{1,0:T(8,128)}) %all-reduce.14.cloned.1.call-update) | async-done | bytes 786448 | tf_op jit(solution)/shard_map/while/body/eval_jaxpr/psum | solution.py:13
  219.6 36.4 %all-reduce.16.cloned.1.call-done = f32[128,128]{1,0:T(8,128)} async-done(((f32[128,128]{1,0:T(8,128)}), f32[128,128]{1,0:T(8,128)}) %all-reduce.16.cloned.1.call-update) | async-done | bytes 65552 | tf_op jit(solution)/shard_map/while/body/eval_jaxpr/psum | solution.py:13
  284.3 42.8 %all-reduce.18.cloned.1.call-done = f32[1536,128]{1,0:T(8,128)} async-done(((f32[1536,128]{1,0:T(8,128)}), f32[1536,128]{1,0:T(8,128)}) %all-reduce.18.cloned.1.call-update) | async-done | bytes 786448 | tf_op jit(solution)/shard_map/while/body/eval_jaxpr/psum | solution.py:13
  346.4 34.7 %all-reduce.14.cloned.1.call-done = f32[1536,128]{1,0:T(8,128)} async-done(((f32[1536,128]{1,0:T(8,128)}), f32[1536,128]{1,0:T(8,128)}) %all-reduce.14.cloned.1.call-update) | async-done | bytes 786448 | tf_op jit(solution)/shard_map/while/body/eval_jaxpr/psum | solution.py:13
  382.6 36.6 %all-reduce.16.cloned.1.call-done = f32[128,128]{1,0:T(8,128)} async-done(((f32[128,128]{1,0:T(8,128)}), f32[128,128]{1,0:T(8,128)}) %all-reduce.16.cloned.1.call-update) | async-done | bytes 65552 | tf_op jit(solution)/shard_map/while/body/eval_jaxpr/psum | solution.py:13
  447.5 42.8 %all-reduce.18.cloned.1.call-done = f32[1536,128]{1,0:T(8,128)} async-done(((f32[1536,128]{1,0:T(8,128)}), f32[1536,128]{1,0:T(8,128)}) %all-reduce.18.cloned.1.call-update) | async-done | bytes 786448 | tf_op jit(solution)/shard_map/while/body/eval_jaxpr/psum | solution.py:13
  509.6 34.4 %all-reduce.14.cloned.1.call-done = f32[1536,128]{1,0:T(8,128)} async-done(((f32[1536,128]{1,0:T(8,128)}), f32[1536,128]{1,0:T(8,128)}) %all-reduce.14.cloned.1.call-update) | async-done | bytes 786448 | tf_op jit(solution)/shard_map/while/body/eval_jaxpr/psum | solution.py:13
  545.5 36.6 %all-reduce.16.cloned.1.call-done = f32[128,128]{1,0:T(8,128)} async-done(((f32[128,128]{1,0:T(8,128)}), f32[128,128]{1,0:T(8,128)}) %all-reduce.16.cloned.1.call-update) | async-done | bytes 65552 | tf_op jit(solution)/shard_map/while/body/eval_jaxpr/psum | solution.py:13
  610.4 42.8 %all-reduce.18.cloned.1.call-done = f32[1536,128]{1,0:T(8,128)} async-done(((f32[1536,128]{1,0:T(8,128)}), f32[1536,128]{1,0:T(8,128)}) %all-reduce.18.cloned.1.call-update) | async-done | bytes 786448 | tf_op jit(solution)/shard_map/while/body/eval_jaxpr/psum | solution.py:13
  672.5 34.7 %all-reduce.14.cloned.1.call-done = f32[1536,128]{1,0:T(8,128)} async-done(((f32[1536,128]{1,0:T(8,128)}), f32[1536,128]{1,0:T(8,128)}) %all-reduce.14.cloned.1.call-update) | async-done | bytes 786448 | tf_op jit(solution)/shard_map/while/body/eval_jaxpr/psum | solution.py:13
  708.7 36.4 %all-reduce.16.cloned.1.call-done = f32[128,128]{1,0:T(8,128)} async-done(((f32[128,128]{1,0:T(8,128)}), f32[128,128]{1,0:T(8,128)}) %all-reduce.16.cloned.1.call-update) | async-done | bytes 65552 | tf_op jit(solution)/shard_map/while/body/eval_jaxpr/psum | solution.py:13
  773.5 42.8 %all-reduce.18.cloned.1.call-done = f32[1536,128]{1,0:T(8,128)} async-done(((f32[1536,128]{1,0:T(8,128)}), f32[1536,128]{1,0:T(8,128)}) %all-reduce.18.cloned.1.call-update) | async-done | bytes 786448 | tf_op jit(solution)/shard_map/while/body/eval_jaxpr/psum | solution.py:13
  835.6 34.4 %all-reduce.14.cloned.1.call-done = f32[1536,128]{1,0:T(8,128)} async-done(((f32[1536,128]{1,0:T(8,128)}), f32[1536,128]{1,0:T(8,128)}) %all-reduce.14.cloned.1.call-update) | async-done | bytes 786448 | tf_op jit(solution)/shard_map/while/body/eval_jaxpr/psum | solution.py:13
  871.5 36.4 %all-reduce.16.cloned.1.call-done = f32[128,128]{1,0:T(8,128)} async-done(((f32[128,128]{1,0:T(8,128)}), f32[128,128]{1,0:T(8,128)}) %all-reduce.16.cloned.1.call-update) | async-done | bytes 65552 | tf_op jit(solution)/shard_map/while/body/eval_jaxpr/psum | solution.py:13
  936.2 42.8 %all-reduce.18.cloned.1.call-done = f32[1536,128]{1,0:T(8,128)} async-done(((f32[1536,128]{1,0:T(8,128)}), f32[1536,128]{1,0:T(8,128)}) %all-reduce.18.cloned.1.call-update) | async-done | bytes 786448 | tf_op jit(solution)/shard_map/while/body/eval_jaxpr/psum | solution.py:13
  998.3 34.7 %all-reduce.14.cloned.1.call-done = f32[1536,128]{1,0:T(8,128)} async-done(((f32[1536,128]{1,0:T(8,128)}), f32[1536,128]{1,0:T(8,128)}) %all-reduce.14.cloned.1.call-update) | async-done | bytes 786448 | tf_op jit(solution)/shard_map/while/body/eval_jaxpr/psum | solution.py:13
  1034.6 36.4 %all-reduce.16.cloned.1.call-done = f32[128,128]{1,0:T(8,128)} async-done(((f32[128,128]{1,0:T(8,128)}), f32[128,128]{1,0:T(8,128)}) %all-reduce.16.cloned.1.call-update) | async-done | bytes 65552 | tf_op jit(solution)/shard_map/while/body/eval_jaxpr/psum | solution.py:13
  1099.3 42.8 %all-reduce.18.cloned.1.call-done = f32[1536,128]{1,0:T(8,128)} async-done(((f32[1536,128]{1,0:T(8,128)}), f32[1536,128]{1,0:T(8,128)}) %all-reduce.18.cloned.1.call-update) | async-done | bytes 786448 | tf_op jit(solution)/shard_map/while/body/eval_jaxpr/psum | solution.py:13
  1161.4 34.7 %all-reduce.14.cloned.1.call-done = f32[1536,128]{1,0:T(8,128)} async-done(((f32[1536,128]{1,0:T(8,128)}), f32[1536,128]{1,0:T(8,128)}) %all-reduce.14.cloned.1.call-update) | async-done | bytes 786448 | tf_op jit(solution)/shard_map/while/body/eval_jaxpr/psum | solution.py:13
  1197.6 36.6 %all-reduce.16.cloned.1.call-done = f32[128,128]{1,0:T(8,128)} async-done(((f32[128,128]{1,0:T(8,128)}), f32[128,128]{1,0:T(8,128)}) %all-reduce.16.cloned.1.call-update) | async-done | bytes 65552 | tf_op jit(solution)/shard_map/while/body/eval_jaxpr/psum | solution.py:13
  1262.5 42.8 %all-reduce.18.cloned.1.call-done = f32[1536,128]{1,0:T(8,128)} async-done(((f32[1536,128]{1,0:T(8,128)}), f32[1536,128]{1,0:T(8,128)}) %all-reduce.18.cloned.1.call-update) | async-done | bytes 786448 | tf_op jit(solution)/shard_map/while/body/eval_jaxpr/psum | solution.py:13
  1334.3 16.0 fusion.26
  1350.3 12.6 fusion.30
  1362.9 18.0 reshape.205
  1390.3 181.0 %collective-permute-done = f32[1024,2048]{1,0:T(8,128)} collective-permute-done((f32[1024,2048]{1,0:T(8,128)}, f32[1024,2048]{1,0:T(8,128)}, u32[]{:S(2)}, u32[]{:S(2)}) %collective-permute-start) | collective-permute-done | bytes 8388640 | tf_op jit(solution)/shard_map/ppermute | solution.py:17
  1585.2 30.8 %all-reduce.8.cloned.1.call-done = f32[1024,128]{1,0:T(8,128)} async-done(((f32[1024,128]{1,0:T(8,128)}), f32[1024,128]{1,0:T(8,128)}) %all-reduce.8.cloned.1.call-update) | async-done | bytes 524304 | tf_op jit(solution)/shard_map/while/body/eval_jaxpr/psum | solution.py:13
  1617.6 71.4 %all-reduce.10.cloned.1.call-done = f32[128,128]{1,0:T(8,128)} async-done(((f32[128,128]{1,0:T(8,128)}), f32[128,128]{1,0:T(8,128)}) %all-reduce.10.cloned.1.call-update) | async-done | bytes 65552 | tf_op jit(solution)/shard_map/while/body/eval_jaxpr/psum | solution.py:13
  1717.3 78.3 %all-reduce.12.cloned.1.call-done = (f32[8,1,128,128]{3,2,1,0:T(8,128)}, f32[8,1,128,128]{3,2,1,0:T(8,128)}) async-done(((f32[8,1,128,128]{3,2,1,0:T(8,128)}, f32[8,1,128,128]{3,2,1,0:T(8,128)}), (f32[8,1,128,128]{3,2,1,0:T(8,128)}, f32[8,1,128,128]{3,2,1,0:T(8,128)})) %all-reduce.12.cloned.1.call-update) | async-done | bytes 1048592 | tf_op jit(solution)/shard_map/while/body/eval_jaxpr/psum | solution.py:13
  (240 shorter events, 480.5 us)
Async XLA Ops:
  8.0 1326.0 %copy-start = (s32[2,40]{1,0:T(2,128)S(1)}, s32[2,40]{1,0:T(2,128)}, u32[]{:S(2)}) copy-start(s32[2,40]{1,0:T(2,128)} %param.7) | copy-start | bytes 964
  16.4 38.8 %all-reduce.14.cloned.1.call-start = ((), (), s32[]{:S(2)}) async-start(), calls=%async_computation.3 | async-start | bytes 1572864 | tf_op jit(solution)/shard_map/while/body/eval_jaxpr/psum | solution.py:13
  18.5 74.7 %all-reduce.16.cloned.1.call-start = ((), (), s32[]{:S(2)}) async-start(), calls=%async_computation.4 | async-start | bytes 131072 | tf_op jit(solution)/shard_map/while/body/eval_jaxpr/psum | solution.py:13
  56.6 107.7 %all-reduce.18.cloned.1.call-start = ((), (), s32[]{:S(2)}) async-start(), calls=%async_computation.5 | async-start | bytes 1572864 | tf_op jit(solution)/shard_map/while/body/eval_jaxpr/psum | solution.py:13
  181.5 36.5 %all-reduce.14.cloned.1.call-start = ((), (), s32[]{:S(2)}) async-start(), calls=%async_computation.3 | async-start | bytes 1572864 | tf_op jit(solution)/shard_map/while/body/eval_jaxpr/psum | solution.py:13
  183.6 72.4 %all-reduce.16.cloned.1.call-start = ((), (), s32[]{:S(2)}) async-start(), calls=%async_computation.4 | async-start | bytes 131072 | tf_op jit(solution)/shard_map/while/body/eval_jaxpr/psum | solution.py:13
  219.5 107.6 %all-reduce.18.cloned.1.call-start = ((), (), s32[]{:S(2)}) async-start(), calls=%async_computation.5 | async-start | bytes 1572864 | tf_op jit(solution)/shard_map/while/body/eval_jaxpr/psum | solution.py:13
  344.2 36.8 %all-reduce.14.cloned.1.call-start = ((), (), s32[]{:S(2)}) async-start(), calls=%async_computation.3 | async-start | bytes 1572864 | tf_op jit(solution)/shard_map/while/body/eval_jaxpr/psum | solution.py:13
  346.3 72.9 %all-reduce.16.cloned.1.call-start = ((), (), s32[]{:S(2)}) async-start(), calls=%async_computation.4 | async-start | bytes 131072 | tf_op jit(solution)/shard_map/while/body/eval_jaxpr/psum | solution.py:13
  382.6 107.7 %all-reduce.18.cloned.1.call-start = ((), (), s32[]{:S(2)}) async-start(), calls=%async_computation.5 | async-start | bytes 1572864 | tf_op jit(solution)/shard_map/while/body/eval_jaxpr/psum | solution.py:13
  507.4 36.5 %all-reduce.14.cloned.1.call-start = ((), (), s32[]{:S(2)}) async-start(), calls=%async_computation.3 | async-start | bytes 1572864 | tf_op jit(solution)/shard_map/while/body/eval_jaxpr/psum | solution.py:13
  509.5 72.6 %all-reduce.16.cloned.1.call-start = ((), (), s32[]{:S(2)}) async-start(), calls=%async_computation.4 | async-start | bytes 131072 | tf_op jit(solution)/shard_map/while/body/eval_jaxpr/psum | solution.py:13
  545.5 107.7 %all-reduce.18.cloned.1.call-start = ((), (), s32[]{:S(2)}) async-start(), calls=%async_computation.5 | async-start | bytes 1572864 | tf_op jit(solution)/shard_map/while/body/eval_jaxpr/psum | solution.py:13
  670.3 36.8 %all-reduce.14.cloned.1.call-start = ((), (), s32[]{:S(2)}) async-start(), calls=%async_computation.3 | async-start | bytes 1572864 | tf_op jit(solution)/shard_map/while/body/eval_jaxpr/psum | solution.py:13
  672.4 72.7 %all-reduce.16.cloned.1.call-start = ((), (), s32[]{:S(2)}) async-start(), calls=%async_computation.4 | async-start | bytes 131072 | tf_op jit(solution)/shard_map/while/body/eval_jaxpr/psum | solution.py:13
  708.7 107.6 %all-reduce.18.cloned.1.call-start = ((), (), s32[]{:S(2)}) async-start(), calls=%async_computation.5 | async-start | bytes 1572864 | tf_op jit(solution)/shard_map/while/body/eval_jaxpr/psum | solution.py:13
  833.4 36.5 %all-reduce.14.cloned.1.call-start = ((), (), s32[]{:S(2)}) async-start(), calls=%async_computation.3 | async-start | bytes 1572864 | tf_op jit(solution)/shard_map/while/body/eval_jaxpr/psum | solution.py:13
  835.5 72.4 %all-reduce.16.cloned.1.call-start = ((), (), s32[]{:S(2)}) async-start(), calls=%async_computation.4 | async-start | bytes 131072 | tf_op jit(solution)/shard_map/while/body/eval_jaxpr/psum | solution.py:13
  871.4 107.6 %all-reduce.18.cloned.1.call-start = ((), (), s32[]{:S(2)}) async-start(), calls=%async_computation.5 | async-start | bytes 1572864 | tf_op jit(solution)/shard_map/while/body/eval_jaxpr/psum | solution.py:13
  996.2 36.8 %all-reduce.14.cloned.1.call-start = ((), (), s32[]{:S(2)}) async-start(), calls=%async_computation.3 | async-start | bytes 1572864 | tf_op jit(solution)/shard_map/while/body/eval_jaxpr/psum | solution.py:13
  998.2 72.7 %all-reduce.16.cloned.1.call-start = ((), (), s32[]{:S(2)}) async-start(), calls=%async_computation.4 | async-start | bytes 131072 | tf_op jit(solution)/shard_map/while/body/eval_jaxpr/psum | solution.py:13
  1034.5 107.6 %all-reduce.18.cloned.1.call-start = ((), (), s32[]{:S(2)}) async-start(), calls=%async_computation.5 | async-start | bytes 1572864 | tf_op jit(solution)/shard_map/while/body/eval_jaxpr/psum | solution.py:13
  1159.2 36.8 %all-reduce.14.cloned.1.call-start = ((), (), s32[]{:S(2)}) async-start(), calls=%async_computation.3 | async-start | bytes 1572864 | tf_op jit(solution)/shard_map/while/body/eval_jaxpr/psum | solution.py:13
  1161.3 72.9 %all-reduce.16.cloned.1.call-start = ((), (), s32[]{:S(2)}) async-start(), calls=%async_computation.4 | async-start | bytes 131072 | tf_op jit(solution)/shard_map/while/body/eval_jaxpr/psum | solution.py:13
  1197.6 107.7 %all-reduce.18.cloned.1.call-start = ((), (), s32[]{:S(2)}) async-start(), calls=%async_computation.5 | async-start | bytes 1572864 | tf_op jit(solution)/shard_map/while/body/eval_jaxpr/psum | solution.py:13
  1322.4 293.6 %all-reduce.8.cloned.1.call-start = ((), (), s32[]{:S(2)}) async-start(), calls=%async_computation | async-start | bytes 1048576 | tf_op jit(solution)/shard_map/while/body/eval_jaxpr/psum | solution.py:13
  1388.8 182.4 %collective-permute-start = (f32[1024,2048]{1,0:T(8,128)}, f32[1024,2048]{1,0:T(8,128)}, u32[]{:S(2)}, u32[]{:S(2)}) collective-permute-start(f32[1024,2048]{1,0:T(8,128)} %dynamic-slice_bitcast_fusion), channel_id=1, source_target_pairs={{0,16},{16,0},{1,17},{17,1},{2,18},{18,2},{3,19},{19,3},{4,20},{20... | collective-permute-start | bytes 25165832 | tf_op jit(solution)/shard_map/ppermute | solution.py:17
  1580.8 3.4 copy-start.2
  1585.1 103.9 %all-reduce.10.cloned.1.call-start = ((), (), s32[]{:S(2)}) async-start(), calls=%async_computation.1 | async-start | bytes 131072 | tf_op jit(solution)/shard_map/while/body/eval_jaxpr/psum | solution.py:13
  1617.5 178.0 %all-reduce.12.cloned.1.call-start = ((), (), s32[]{:S(2)}) async-start(), calls=%async_computation.2 | async-start | bytes 2097152 | tf_op jit(solution)/shard_map/while/body/eval_jaxpr/psum | solution.py:13
  1797.2 13.2 copy-start.1
  1807.0 3.4 copy-start.3
Sparse Core Ops, SparseCore 0:
  20.3 34.8 all-reduce.13
  58.1 35.0 all-reduce.15
  121.0 43.3 all-reduce.17
  185.1 32.9 all-reduce.13
  220.9 35.0 all-reduce.15
  283.7 43.3 all-reduce.17
  348.1 32.8 all-reduce.13
  384.1 35.0 all-reduce.15
  446.9 43.3 all-reduce.17
  511.0 32.9 all-reduce.13
  547.0 35.0 all-reduce.15
  609.8 43.3 all-reduce.17
  674.2 32.9 all-reduce.13
  710.0 35.0 all-reduce.15
  772.9 43.3 all-reduce.17
  837.0 32.9 all-reduce.13
  872.8 35.0 all-reduce.15
  935.6 43.3 all-reduce.17
  1000.1 32.8 all-reduce.13
  1035.8 35.0 all-reduce.15
  1098.7 43.3 all-reduce.17
  1163.1 32.9 all-reduce.13
  1199.1 35.0 all-reduce.15
  1261.9 43.3 all-reduce.17
Sparse Core Ops, SparseCore 1:
  1585.2 30.8 all-reduce.7
  1619.3 69.6 all-reduce.9
  1717.4 78.2 all-reduce.11
where the time goes:
time: 1820 us
  waiting for transfers between devices  1270 us (70%)
  other arithmetic  299 us (16%)
  matrix products  163 us (9%)
  local copies, waits for them, and re-layouts  61.7 us (3%)
    psum x27, waiting for transfers between devices, spread(): return lax.psum(jnp.where(mine, shard, jnp.zeros_like(shard)), axis)  1090 us
    ppermute x1, waiting for transfers between devices, from_partner(): lax.ppermute(shard, axis, [(i, i ^ 1 << distance) for i in range(lax.axis...  181 us
    another operation x27, other arithmetic, one_step(): diag_factor = jnp.linalg.cholesky(diag_block)  112 us
    dot_general x9, matrix products, one_step(): jnp.dot(left_factor, right_factor.T, precision=lax.Precision.HIGHEST, pre...  110 us
    another operation x27, other arithmetic, one_step(): jax.scipy.linalg.solve_triangular(diag_factor, col_panel.T, lower=True)  100 us
  transfers between devices with their start and end apart: 28, of which 28 were waited for; matrix products, arithmetic and copies ran while one was open for 0% of the time, Pallas kernels for 0%

commit v1 on v0

--- a/solution.py
+++ b/solution.py
@@ -66,34 +66,55 @@
     return lax.fori_loop(0, pivot_count // TILE, one_step, front_work)
 
 
+def pivot_order(pieces, slot_count, tile_count):
+    group_count, rest = pieces.shape[0], pieces.shape[2:]
+    shaped = pieces.reshape((group_count, slot_count, TILE) + rest)
+    shaped = jnp.moveaxis(shaped, 0, 1).reshape((slot_count * group_count * TILE,) + rest)
+    return shaped[: tile_count * TILE]
+
+
+def factor_child(front_work, pivot_count, grid_size, my_row, my_col):
+    local_count = front_work.shape[0]
+    tile_count = pivot_count // TILE
+    slot_count = -(-tile_count // grid_size)
+    width = slot_count * TILE
+    col_pieces = lax.all_gather(front_work[:, :width].T, "col", axis=0)
+    panel_rows = pivot_order(col_pieces, slot_count, tile_count)
+    row_pieces = lax.all_gather(front_work[:width, :], "row", axis=0)
+    panel_cols = pivot_order(row_pieces, slot_count, tile_count)
+    diag_pieces = lax.all_gather(panel_rows[:, :width].T, "row", axis=0)
+    diag_block = pivot_order(diag_pieces, slot_count, tile_count)
+    diag_factor = jnp.tril(jnp.linalg.cholesky(diag_block))
+    both = jnp.concatenate([panel_rows, panel_cols], axis=1)
+    solved = jax.scipy.linalg.solve_triangular(diag_factor, both, lower=True)
+    solved_rows = solved[:, :local_count].T
+    solved_cols = solved[:, local_count:].T
+    within = jnp.arange(local_count, dtype=jnp.int32)
+    row_index = within // TILE * grid_size * TILE + my_row * TILE + within % TILE
+    col_index = within // TILE * grid_size * TILE + my_col * TILE + within % TILE
+    rows_after = (row_index >= pivot_count)[:, None]
+    cols_after = (col_index >= pivot_count)[None, :]
+    update = jnp.dot(
+        jnp.where(rows_after, solved_rows, 0.0),
+        jnp.where(cols_after.T, solved_cols, 0.0).T,
+        precision=lax.Precision.HIGHEST,
+        preferred_element_type=jnp.float32,
+    )
+    diag_rows = jnp.take(diag_factor, jnp.minimum(row_index, pivot_count - 1), axis=0)
+    full_rows = jnp.where(rows_after, solved_rows, diag_rows)
+    pivot_cols = jnp.take(full_rows, jnp.minimum(col_index[:width], pivot_count - 1), axis=1)
+    trailing = jnp.where(rows_after & cols_after, front_work - update, 0.0)
+    head = jnp.where(cols_after[:, :width], trailing[:, :width], pivot_cols)
+    return jnp.concatenate([head, trailing[:, width:]], axis=1)
+
+
 def local(child_fronts, child_maps, parent_own):
     grid_size = lax.axis_size("row")
     half_index = lax.axis_index("half")
     my_row = lax.axis_index("row")
     my_col = lax.axis_index("col")
 
-    def send_child_column(column, pivot_tile):
-        return spread(column, "col", pivot_tile % grid_size)
-
-    def send_child_block(current, col_panel, pivot_tile, row_slot, col_slot):
-        own_block = lax.dynamic_slice_in_dim(col_panel, row_slot * TILE, TILE, 0)
-        result_block = spread(own_block, "row", pivot_tile % grid_size)
-        return result_block
-
-    def send_child_rows(solved_panel):
-        return spread(solved_panel, "row", my_col)
-
-    child_done = factor_front(
-        child_fronts[0],
-        CHILD_PIVOTS,
-        grid_size,
-        grid_size,
-        my_row,
-        my_col,
-        send_child_column,
-        send_child_block,
-        send_child_rows,
-    )
+    child_done = factor_child(child_fronts[0], CHILD_PIVOTS, grid_size, my_row, my_col)
     local_tiles = child_done.shape[0] // TILE
     pivot_tiles = CHILD_PIVOTS // TILE
     own_map = lax.dynamic_index_in_dim(child_maps, half_index, 0, keepdims=False)

time: 1820 us -> 1280 us (0.70)
  waiting for transfers between devices: 1270 us -> 580 us
  local copies, waits for them, and re-layouts: 61.7 us -> 181 us
  other arithmetic: 299 us -> 325 us
    psum x27 -> x3, waiting for transfers between devices: 1090 us -> 171 us  [spread(): return lax.psum(jnp.where(mine, shard, jnp.zeros_like(shard)), axis)]
    another operation x0 -> x33, other arithmetic: none -> 259 us  [the longest x30 172 us: factor_child(): diag_factor = jnp.tril(jnp.linalg.cholesky(diag_block))]
    all_gather x0 -> x3, waiting for transfers between devices: none -> 227 us  [the longest x1 108 us: factor_child(): row_pieces = lax.all_gather(front_work[:width, :], 'row', axis=0)]
    dot_general x9 -> x1, matrix products: 110 us -> 9.15 us  [one_step(): jnp.dot(left_factor, right_factor.T, precision=lax.Precision.HIGHEST, pre...]
    another operation x27 -> x3, other arithmetic: 112 us -> 12.4 us  [one_step(): diag_factor = jnp.linalg.cholesky(diag_block)]
    another operation x0 -> x29, matrix products: none -> 92.6 us  [the longest x15 69.6 us: factor_child(): solved = jax.scipy.linalg.solve_triangular(diag_factor, both, lower=True)]
    another operation x27 -> x3, other arithmetic: 100 us -> 11.1 us  [one_step(): jax.scipy.linalg.solve_triangular(diag_factor, col_panel.T, lower=True)]
    dot_general x0 -> x1, matrix products: none -> 40.1 us  [factor_child(): jnp.dot(jnp.where(rows_after, solved_rows, 0.0), jnp.where(cols_after.T,...]
  transfers between devices with their start and end apart: 28 -> 7, of which waited for: 28 -> 7; matrix products, arithmetic and copies ran while one was open for 0% -> 2% of each run, Pallas kernels for 0% -> 0%
where the time goes in v1:
time: 1280 us; the launch traced here: 1270 us
  waiting for transfers between devices  580 us (45%)
  other arithmetic  325 us (25%)
  local copies, waits for them, and re-layouts  181 us (14%)
  matrix products  167 us (13%)
  between operations  19.9 us (2%)
    ppermute x1, waiting for transfers between devices, from_partner(): lax.ppermute(shard, axis, [(i, i ^ 1 << distance) for i in range(lax.axis...  181 us
    another operation x30, other arithmetic, factor_child(): diag_factor = jnp.tril(jnp.linalg.cholesky(diag_block))  172 us
    psum x3, waiting for transfers between devices, spread(): return lax.psum(jnp.where(mine, shard, jnp.zeros_like(shard)), axis)  171 us
    all_gather x1, waiting for transfers between devices, factor_child(): row_pieces = lax.all_gather(front_work[:width, :], 'row', axis=0)  108 us
    another operation x3, other arithmetic, factor_child(): solved = jax.scipy.linalg.solve_triangular(diag_factor, both, lower=True)  86.6 us
    all_gather x1, waiting for transfers between devices, factor_child(): diag_pieces = lax.all_gather(panel_rows[:, :width].T, 'row', axis=0)  75.3 us
    another operation x15, matrix products, factor_child(): solved = jax.scipy.linalg.solve_triangular(diag_factor, both, lower=True)  69.6 us
    all_gather x1, waiting for transfers between devices, factor_child(): col_pieces = lax.all_gather(front_work[:, :width].T, 'col', axis=0)  43.8 us
  transfers between devices with their start and end apart: 7, of which 7 were waited for; matrix products, arithmetic and copies ran while one was open for 2% of the time, Pallas kernels for 0%

profile of v1, /device:TPU:4, one launch (start us, length us, event | category | flops | bytes accessed | tf_op | source)
XLA Modules:
  0.0 1273.9 jit_solution(13050635258377769141)
XLA Ops:
  22.3 43.8 %all-gather.8.cloned.1.call-done = f32[1024,1536]{1,0:T(8,128)} async-done(((f32[256,1536]{1,0:T(8,128)}), f32[1024,1536]{1,0:T(8,128)}) %all-gather.8.cloned.1.call-update) | async-done | bytes 6291472 | tf_op jit(solution)/shard_map/all_gather | solution.py:81
  75.9 108.3 %all-gather.6.cloned.1.call-done = f32[4,256,1536]{2,1,0:T(8,128)} async-done(((f32[1,256,1536]{2,1,0:T(8,128)}), f32[4,256,1536]{2,1,0:T(8,128)}) %all-gather.6.cloned.1.call-update) | async-done | bytes 6291472 | tf_op jit(solution)/shard_map/all_gather | solution.py:83
  190.0 75.3 %all-gather.10.cloned.1.call-done = f32[1024,1024]{0,1:T(8,128)} async-done(((f32[256,1024]{0,1:T(8,128)}), f32[1024,1024]{0,1:T(8,128)}) %all-gather.10.cloned.1.call-update) | async-done | bytes 4194320 | tf_op jit(solution)/shard_map/all_gather | solution.py:85
  293.3 11.7 cholesky.243
  305.0 9.8 custom-call.72
  321.3 11.9 cholesky.266
  333.8 9.8 custom-call.73
  346.9 11.7 cholesky.507
  359.9 9.8 custom-call.74
  373.3 12.1 cholesky.526
  386.7 9.8 custom-call.75
  399.9 11.7 cholesky.545
  412.9 9.9 custom-call.76
  426.2 11.7 cholesky.565
  452.0 11.8 cholesky.585
  465.1 9.8 custom-call.78
  477.6 11.7 cholesky.603
  503.1 28.0 %while.1 = (s32[]{:T(128)}, f32[1024,1024]{1,0:T(8,128)}, s32[8,2]{0,1:T(2,128)S(1)}, f32[8,128,128]{2,1,0:T(8,128)}, s32[]{:T(128)}) while((s32[]{:T(128)}, f32[1024,1024]{1,0:T(8,128)}, s32[8,2]{0,1:T(2,128)S(1)}, f32[8,128,128]{2,1,0:T(8,128)}, s32[]{:T(128)}) %tuple.80), condition=%wide.while_cond, body=%wide.while_body.sunk | while | flops 2 | bytes 132705 | solution.py:89
  531.0 79.8 %custom-call.79 = f32[8,128,128]{1,2,0:T(8,128)S(1)} custom-call(f32[8,128,128]{2,1,0:T(8,128)} %get-tuple-element.30), custom_call_target="InvertDiagBlocksLowerTriangular" | custom-call | tf_op jit(solution)/shard_map/jit(_solve_triangular)/triangular_solve | solution.py:89
  681.4 10.0 gather_fusion
  701.2 40.1 %subtract_select_fusion = f32[1536,1536]{0,1:T(8,128)S(1)} fusion(f32[1024,3072]{1,0:T(8,128)} %convolution_dynamic-update-slice_fusion, pred[1536]{0:T(1024)(128)(4,1)S(1)} %get-tuple-element.123, pred[1536]{0:T(1024)(128)(4,1)S(1)} %broadcast_compare_fusion, f32[1,1536,1536]{1,2,0:T(8,128)} %copy.49), kind=kOutput, calls=%fused_computation.23 | convolution fusion | flops 29001252864 | bytes 31465472 | tf_op jit(solution)/shard_map/dot_general | solution.py:97
  760.1 12.4 pad_maximum_fusion
  772.4 11.6 reshape.462
  784.0 12.8 %copy.57 = f32[12,128,12,128]{3,0,2,1:T(8,128)} copy(f32[12,128,12,128]{1,0,3,2:T(8,128)} %reshape.462) | data formatting | bytes 18874368 | tf_op jit(solution)/shard_map/reshape | solution.py:146
  806.5 12.6 fusion.5
  819.1 18.0 %reshape.411 = f32[2,1024,2048]{2,1,0:T(8,128)} reshape(f32[2,8,128,16,128]{4,3,2,1,0:T(8,128)} %fusion.5) | data formatting | bytes 33554432 | tf_op jit(solution)/shard_map/reshape | solution.py:151
  846.5 181.0 %collective-permute-done = f32[1024,2048]{1,0:T(8,128)} collective-permute-done((f32[1024,2048]{1,0:T(8,128)}, f32[1024,2048]{1,0:T(8,128)}, u32[]{:S(2)}, u32[]{:S(2)}) %collective-permute-start) | collective-permute-done | bytes 8388640 | tf_op jit(solution)/shard_map/ppermute | solution.py:17
  1041.5 30.6 %all-reduce.6.cloned.1.call-done = f32[1024,128]{1,0:T(8,128)} async-done(((f32[1024,128]{1,0:T(8,128)}), f32[1024,128]{1,0:T(8,128)}) %all-reduce.6.cloned.1.call-update) | async-done | bytes 524304 | tf_op jit(solution)/shard_map/while/body/eval_jaxpr/psum | solution.py:13
  1073.8 71.9 %all-reduce.8.cloned.1.call-done = f32[128,128]{1,0:T(8,128)} async-done(((f32[128,128]{1,0:T(8,128)}), f32[128,128]{1,0:T(8,128)}) %all-reduce.8.cloned.1.call-update) | async-done | bytes 65552 | tf_op jit(solution)/shard_map/while/body/eval_jaxpr/psum | solution.py:13
  1147.5 11.7 cholesky.616
  1161.2 9.8 custom-call.80
  1183.4 68.9 %all-reduce.10.cloned.1.call-done = (f32[8,1,128,128]{3,2,1,0:T(8,128)}, f32[8,1,128,128]{3,2,1,0:T(8,128)}) async-done(((f32[8,1,128,128]{3,2,1,0:T(8,128)}, f32[8,1,128,128]{3,2,1,0:T(8,128)}), (f32[8,1,128,128]{3,2,1,0:T(8,128)}, f32[8,1,128,128]{3,2,1,0:T(8,128)})) %all-reduce.10.cloned.1.call-update) | async-done | bytes 1048592 | tf_op jit(solution)/shard_map/while/body/eval_jaxpr/psum | solution.py:13
  (195 shorter events, 302.1 us)
Async XLA Ops:
  7.2 66.5 %copy-start = (s32[2,40]{1,0:T(2,128)S(1)}, s32[2,40]{1,0:T(2,128)}, u32[]{:S(2)}) copy-start(s32[2,40]{1,0:T(2,128)} %param.4) | copy-start | bytes 964
  7.2 58.9 %all-gather.8.cloned.1.call-start = ((), (), s32[]{:S(2)}) async-start(), calls=%async_computation.3 | async-start | bytes 7864320 | tf_op jit(solution)/shard_map/all_gather | solution.py:81
  19.5 164.7 %all-gather.6.cloned.1.call-start = ((), (), s32[]{:S(2)}) async-start(), calls=%async_computation | async-start | bytes 7864320 | tf_op jit(solution)/shard_map/all_gather | solution.py:83
  22.2 243.1 %all-gather.10.cloned.1.call-start = ((), (), s32[]{:S(2)}) async-start(), calls=%async_computation.4 | async-start | bytes 5242880 | tf_op jit(solution)/shard_map/all_gather | solution.py:85
  69.3 2.6 copy-start.2
  73.0 999.0 %all-reduce.6.cloned.1.call-start = ((), (), s32[]{:S(2)}) async-start(), calls=%async_computation.1 | async-start | bytes 1048576 | tf_op jit(solution)/shard_map/while/body/eval_jaxpr/psum | solution.py:13
  291.3 1.9 copy-start.6
  496.3 119.6 %slice-start = ((s8[6291456]{0:T(1024)(128)(4,1)}), s8[2097152]{0:T(1024)(128)(4,1)S(1)}, s32[]{:S(2)}) async-start(s8[6291456]{0:T(1024)(128)(4,1)} %bitcast.185), calls=%async_computation.6 | async-start | bytes 4194304
  610.9 5.0 slice-start.1
  610.9 11.3 slice-start.2
  615.8 6.3 slice-start.3
  628.4 3.6 copy-start.4
  691.4 7.1 copy-start.8
  701.2 46.2 %slice-start.4 = ((s8[6291456]{0:T(1024)(128)(4,1)}), s8[4194304]{0:T(1024)(128)(4,1)S(1)}, s32[]{:S(2)}) async-start(s8[6291456]{0:T(1024)(128)(4,1)} %bitcast.204), calls=%async_computation.10 | async-start | bytes 8388608
  701.2 46.2 %slice-start.5 = ((s8[6291456]{0:T(1024)(128)(4,1)}), s8[2097152]{0:T(1024)(128)(4,1)S(1)}, s32[]{:S(2)}) async-start(s8[6291456]{0:T(1024)(128)(4,1)} %bitcast.204), calls=%async_computation.11 | async-start | bytes 4194304
  741.3 6.1 copy-start.7
  784.0 12.8 %copy-start.9 = (s32[2,8]{1,0:T(2,128)S(1)}, s32[2,8]{1,0:T(2,128)}, u32[]{:S(2)}) copy-start(s32[2,8]{1,0:T(2,128)} %add_add_fusion) | copy-start | bytes 196
  784.0 12.8 %copy-start.10 = (s32[12]{0:T(128)S(1)}, s32[12]{0:T(128)}, u32[]{:S(2)}) copy-start(s32[12]{0:T(128)} %get-tuple-element.42) | copy-start | bytes 148
  784.0 12.8 %copy-start.11 = (pred[12]{0:T(512)(128)(4,1)S(1)}, pred[12]{0:T(512)(128)(4,1)}, u32[]{:S(2)}) copy-start(pred[12]{0:T(512)(128)(4,1)} %get-tuple-element.118) | copy-start | bytes 40
  796.8 9.7 copy-start.12
  796.8 9.7 copy-start.13
  796.8 9.7 copy-start.14
  845.0 182.5 %collective-permute-start = (f32[1024,2048]{1,0:T(8,128)}, f32[1024,2048]{1,0:T(8,128)}, u32[]{:S(2)}, u32[]{:S(2)}) collective-permute-start(f32[1024,2048]{1,0:T(8,128)} %dynamic-slice_bitcast_fusion), channel_id=1, source_target_pairs={{0,16},{16,0},{1,17},{17,1},{2,18},{18,2},{3,19},{19,3},{4,20},{20... | collective-permute-start | bytes 25165832 | tf_op jit(solution)/shard_map/ppermute | solution.py:17
  1037.1 3.4 copy-start.3
  1041.4 104.3 %all-reduce.8.cloned.1.call-start = ((), (), s32[]{:S(2)}) async-start(), calls=%async_computation.2 | async-start | bytes 131072 | tf_op jit(solution)/shard_map/while/body/eval_jaxpr/psum | solution.py:13
  1073.5 178.7 %all-reduce.10.cloned.1.call-start = ((), (), s32[]{:S(2)}) async-start(), calls=%async_computation.5 | async-start | bytes 2097152 | tf_op jit(solution)/shard_map/while/body/eval_jaxpr/psum | solution.py:13
  1253.9 13.0 %copy-start.1 = (s32[2,40]{1,0:T(2,128)S(1)}, s32[2,40]{1,0:T(2,128)}, u32[]{:S(2)}) copy-start(s32[2,40]{1,0:T(2,128)} %param.4) | copy-start | bytes 964
  1263.4 3.4 copy-start.5
Sparse Core Ops, SparseCore 0:
  19.6 46.4 all-gather.7
  67.6 116.5 all-gather.5
  186.3 78.9 all-gather.9
  1041.5 30.4 all-reduce.5
  1075.9 69.8 all-reduce.7
  1173.8 78.3 all-reduce.9

commit v2 on v1

--- a/solution.py
+++ b/solution.py
@@ -6,6 +6,7 @@
 TILE = 128
 CHILD_PIVOTS = 1024
 PARENT_PIVOTS = 128
+CYCLE_TILES = 16
 
 
 def spread(shard, axis, root):
@@ -108,13 +109,7 @@
     return jnp.concatenate([head, trailing[:, width:]], axis=1)
 
 
-def local(child_fronts, child_maps, parent_own):
-    grid_size = lax.axis_size("row")
-    half_index = lax.axis_index("half")
-    my_row = lax.axis_index("row")
-    my_col = lax.axis_index("col")
-
-    child_done = factor_child(child_fronts[0], CHILD_PIVOTS, grid_size, my_row, my_col)
+def assemble_by_einsum(child_done, child_maps, parent_own, grid_size, half_index, my_row, my_col):
     local_tiles = child_done.shape[0] // TILE
     pivot_tiles = CHILD_PIVOTS // TILE
     own_map = lax.dynamic_index_in_dim(child_maps, half_index, 0, keepdims=False)
@@ -152,7 +147,70 @@
     kept_part = lax.dynamic_index_in_dim(both_moved, half_index, 0, keepdims=False)
     sent_part = lax.dynamic_index_in_dim(both_moved, 1 - half_index, 0, keepdims=False)
     received = from_partner(sent_part, "half", 0)
-    parent_start = parent_own + kept_part + received
+    return parent_own + kept_part + received
+
+
+def tile_source(targets, slot_total):
+    slots = jnp.arange(slot_total, dtype=jnp.int32)
+    matches = targets[None, :] == slots[:, None]
+    source = jnp.sum(jnp.where(matches, jnp.arange(targets.shape[0], dtype=jnp.int32)[None, :], 0), axis=1)
+    return source, jnp.any(matches, axis=1)
+
+
+def place_tiles(block, child_map, row_source, parent_shape, grid_size, row_groups, my_col):
+    col_count = block.shape[2] // TILE
+    col_ids = jnp.arange(col_count, dtype=jnp.int32) * grid_size + my_col
+    col_targets = jnp.take(child_map, col_ids, axis=0) // grid_size
+    col_source, col_valid = tile_source(col_targets, parent_shape[1] // TILE)
+    row_ids = row_source
+    row_targets = jnp.take(child_map, row_ids, axis=0) // row_groups
+    row_from, row_valid = tile_source(row_targets, parent_shape[0] // TILE)
+    tiles = block.reshape(block.shape[0], TILE, col_count, TILE)
+    tiles = jnp.take(tiles, row_from, axis=0)
+    tiles = jnp.take(tiles, col_source, axis=2)
+    valid = row_valid[:, None, None, None] & col_valid[None, None, :, None]
+    return jnp.where(valid, tiles, 0.0).reshape(parent_shape)
+
+
+def assemble_by_parity(child_done, child_maps, parent_own, grid_size, half_index, my_row, my_col):
+    pivot_tiles = CHILD_PIVOTS // TILE
+    first_slot = pivot_tiles // grid_size
+    update = child_done[first_slot * TILE :, first_slot * TILE :]
+    pair_count = update.shape[0] // (2 * TILE)
+    by_parity = update.reshape(pair_count, 2, TILE, update.shape[1])
+    kept = lax.dynamic_index_in_dim(by_parity, half_index, 1, keepdims=False)
+    sent = lax.dynamic_index_in_dim(by_parity, 1 - half_index, 1, keepdims=False)
+    received = from_partner(sent, "half", 0)
+    pair_ids = jnp.arange(pair_count, dtype=jnp.int32)
+    row_update_ids = (2 * pair_ids + half_index) * grid_size + my_row
+    own_map = lax.dynamic_index_in_dim(child_maps, half_index, 0, keepdims=False)
+    other_map = lax.dynamic_index_in_dim(child_maps, 1 - half_index, 0, keepdims=False)
+    row_groups = 2 * grid_size
+    kept_part = place_tiles(kept, own_map, row_update_ids, parent_own.shape, grid_size, row_groups, my_col)
+    got_part = place_tiles(received, other_map, row_update_ids, parent_own.shape, grid_size, row_groups, my_col)
+    return parent_own + kept_part + got_part
+
+
+def local(child_fronts, child_maps, parent_own):
+    grid_size = lax.axis_size("row")
+    half_index = lax.axis_index("half")
+    my_row = lax.axis_index("row")
+    my_col = lax.axis_index("col")
+
+    child_done = factor_child(child_fronts[0], CHILD_PIVOTS, grid_size, my_row, my_col)
+    pivot_tiles = CHILD_PIVOTS // TILE
+    first_slot = pivot_tiles // grid_size
+    update_slots = child_done.shape[0] // TILE - first_slot
+    parity_fits = CYCLE_TILES % (2 * grid_size) == 0 and pivot_tiles % grid_size == 0
+    parity_fits = parity_fits and first_slot % 2 == 0 and update_slots % 2 == 0
+    if not parity_fits:
+        parent_start = assemble_by_einsum(
+            child_done, child_maps, parent_own, grid_size, half_index, my_row, my_col
+        )
+    else:
+        parent_start = assemble_by_parity(
+            child_done, child_maps, parent_own, grid_size, half_index, my_row, my_col
+        )
 
     def send_parent_column(column, pivot_tile):
         return spread(column, "col", pivot_tile % grid_size)

time: 1280 us -> 1080 us (0.84)
  waiting for transfers between devices: 580 us -> 387 us
  matrix products: 167 us -> 142 us
  other arithmetic: 325 us -> 342 us
    ppermute x1, waiting for transfers between devices: 181 us -> 36.3 us  [from_partner(): lax.ppermute(shard, axis, [(i, i ^ 1 << distance) for i in range(lax.axis...]
    reshape x3 -> x2, local copies, waits for them, and re-layouts: 42.3 us -> 7.46 us  [place_tiles(): tiles = block.reshape(block.shape[0], TILE, col_count, TILE)]
    psum x3, waiting for transfers between devices: 171 us -> 140 us  [spread(): return lax.psum(jnp.where(mine, shard, jnp.zeros_like(shard)), axis)]
    gather x0 -> x8, local copies, waits for them, and re-layouts: none -> 23 us  [the longest x2 13.9 us: place_tiles(): tiles = jnp.take(tiles, col_source, axis=2)]
    dot_general x2 -> x0, matrix products: 22.2 us -> none  [the longest x1 12.6 us: local(): jnp.einsum('hailj,bl->haibj', rows_moved, col_place, precision=lax.Precis...]
    select_n x0 -> x12, other arithmetic: none -> 20.2 us  [the longest x4 11.5 us: place_tiles(): tiles = jnp.take(tiles, row_from, axis=0)]
    unnamed x44 -> x29, local copies, waits for them, and re-layouts: 36 us -> 18.7 us
    all_gather x1, waiting for transfers between devices: 108 us -> 91.4 us  [factor_child(): row_pieces = lax.all_gather(front_work[:width, :], 'row', axis=0)]
  transfers between devices with their start and end apart: 7 -> 7, of which waited for: 7 -> 7; matrix products, arithmetic and copies ran while one was open for 2% -> 10% of each run, Pallas kernels for 0% -> 0%
where the time goes in v2:
time: 1080 us; the launch traced here: 1070 us
  waiting for transfers between devices  387 us (36%)
  other arithmetic  342 us (32%)
  local copies, waits for them, and re-layouts  178 us (16%)
  matrix products  142 us (13%)
  between operations  20 us (2%)
    another operation x30, other arithmetic, factor_child(): diag_factor = jnp.tril(jnp.linalg.cholesky(diag_block))  172 us
    psum x3, waiting for transfers between devices, spread(): return lax.psum(jnp.where(mine, shard, jnp.zeros_like(shard)), axis)  140 us
    all_gather x1, waiting for transfers between devices, factor_child(): row_pieces = lax.all_gather(front_work[:width, :], 'row', axis=0)  91.4 us
    another operation x3, other arithmetic, factor_child(): solved = jax.scipy.linalg.solve_triangular(diag_factor, both, lower=True)  85.8 us
    all_gather x1, waiting for transfers between devices, factor_child(): diag_pieces = lax.all_gather(panel_rows[:, :width].T, 'row', axis=0)  75.3 us
    another operation x15, matrix products, factor_child(): solved = jax.scipy.linalg.solve_triangular(diag_factor, both, lower=True)  68.2 us
    all_gather x1, waiting for transfers between devices, factor_child(): col_pieces = lax.all_gather(front_work[:, :width].T, 'col', axis=0)  43.9 us
    dot_general x1, matrix products, factor_child(): jnp.dot(jnp.where(rows_after, solved_rows, 0.0), jnp.where(cols_after.T,...  38.3 us
  transfers between devices with their start and end apart: 7, of which 7 were waited for; matrix products, arithmetic and copies ran while one was open for 10% of the time, Pallas kernels for 0%

profile of v2, /device:TPU:4, one launch (start us, length us, event | category | flops | bytes accessed | tf_op | source)
XLA Modules:
  0.0 1071.1 jit_solution(4283576437970989118)
XLA Ops:
  12.7 43.9 %all-gather.8.cloned.1.call-done = f32[1024,1536]{0,1:T(8,128)} async-done(((f32[256,1536]{0,1:T(8,128)}), f32[1024,1536]{0,1:T(8,128)}) %all-gather.8.cloned.1.call-update) | async-done | bytes 6291472 | tf_op jit(solution)/shard_map/all_gather | solution.py:82
  56.6 9.1 reshape.431
  65.7 10.4 copy.54
  83.3 91.4 %all-gather.6.cloned.1.call-done = f32[4,256,1536]{2,1,0:T(8,128)} async-done(((f32[1,256,1536]{2,1,0:T(8,128)}), f32[4,256,1536]{2,1,0:T(8,128)}) %all-gather.6.cloned.1.call-update) | async-done | bytes 6291472 | tf_op jit(solution)/shard_map/all_gather | solution.py:84
  180.6 75.3 %all-gather.10.cloned.1.call-done = f32[1024,1024]{0,1:T(8,128)} async-done(((f32[256,1024]{0,1:T(8,128)}), f32[1024,1024]{0,1:T(8,128)}) %all-gather.10.cloned.1.call-update) | async-done | bytes 4194320 | tf_op jit(solution)/shard_map/all_gather | solution.py:86
  283.8 11.7 %cholesky.243 = f32[128,128]{1,0:T(8,128)S(1)} custom-call(f32[128,128]{1,0:T(8,128)S(1)} %cholesky.627), custom_call_target="Cholesky" | custom-call | tf_op jit(solution)/shard_map/jit(cholesky)/cholesky | solution.py:88
  295.6 9.8 custom-call.72
  311.8 11.9 %cholesky.266 = f32[128,128]{1,0:T(8,128)S(1)} custom-call(f32[128,128]{1,0:T(8,128)S(1)} %cholesky.631), custom_call_target="Cholesky" | custom-call | tf_op jit(solution)/shard_map/jit(cholesky)/cholesky | solution.py:88
  324.4 9.8 custom-call.73
  337.5 11.7 %cholesky.507 = f32[128,128]{1,0:T(8,128)S(1)} custom-call(f32[128,128]{1,0:T(8,128)S(1)} %cholesky.636), custom_call_target="Cholesky" | custom-call | tf_op jit(solution)/shard_map/jit(cholesky)/cholesky | solution.py:88
  350.5 9.8 custom-call.74
  363.8 12.1 %cholesky.526 = f32[128,128]{1,0:T(8,128)S(1)} custom-call(f32[128,128]{1,0:T(8,128)S(1)} %cholesky.641), custom_call_target="Cholesky" | custom-call | tf_op jit(solution)/shard_map/jit(cholesky)/cholesky | solution.py:88
  377.3 9.8 custom-call.75
  390.5 11.7 %cholesky.545 = f32[128,128]{1,0:T(8,128)S(1)} custom-call(f32[128,128]{1,0:T(8,128)S(1)} %cholesky.646), custom_call_target="Cholesky" | custom-call | tf_op jit(solution)/shard_map/jit(cholesky)/cholesky | solution.py:88
  403.5 10.0 custom-call.76
  416.8 11.7 %cholesky.565 = f32[128,128]{1,0:T(8,128)S(1)} custom-call(f32[128,128]{1,0:T(8,128)S(1)} %cholesky.651), custom_call_target="Cholesky" | custom-call | tf_op jit(solution)/shard_map/jit(cholesky)/cholesky | solution.py:88
  429.8 9.8 custom-call.77
  442.6 11.9 %cholesky.585 = f32[128,128]{1,0:T(8,128)S(1)} custom-call(f32[128,128]{1,0:T(8,128)S(1)} %cholesky.656), custom_call_target="Cholesky" | custom-call | tf_op jit(solution)/shard_map/jit(cholesky)/cholesky | solution.py:88
  455.8 9.8 custom-call.78
  468.2 11.7 %cholesky.603 = f32[128,128]{1,0:T(8,128)S(1)} custom-call(f32[128,128]{1,0:T(8,128)S(1)} %convolution_subtract_fusion.12), custom_call_target="Cholesky" | custom-call | tf_op jit(solution)/shard_map/jit(cholesky)/cholesky | solution.py:88
  493.8 22.6 %while.1 = (s32[]{:T(128)}, f32[1024,1024]{1,0:T(8,128)}, s32[8,2]{0,1:T(2,128)S(1)}, f32[8,128,128]{2,1,0:T(8,128)S(1)}, s32[]{:T(128)}) while((s32[]{:T(128)}, f32[1024,1024]{1,0:T(8,128)}, s32[8,2]{0,1:T(2,128)S(1)}, f32[8,128,128]{2,1,0:T(8,128)S(1)}, s32[]{:T(128)}) %tuple.84), condition=%wide.while_cond, body=%wide.while_body.sunk | while | flops 2 | bytes 131181 | solution.py:90
  516.4 79.0 %custom-call.79 = f32[8,128,128]{1,2,0:T(8,128)S(1)} custom-call(f32[8,128,128]{2,1,0:T(8,128)S(1)} %get-tuple-element.34), custom_call_target="InvertDiagBlocksLowerTriangular" | custom-call | tf_op jit(solution)/shard_map/jit(_solve_triangular)/triangular_solve | solution.py:90
  667.4 38.3 %subtract_select_fusion = f32[1536,1536]{1,0:T(8,128)S(1)} fusion(f32[1024,3072]{1,0:T(8,128)} %convolution_dynamic-update-slice_fusion, pred[1536]{0:T(1024)(128)(4,1)S(1)} %get-tuple-element.123, pred[1536]{0:T(1024)(128)(4,1)S(1)} %get-tuple-element.122, f32[1,1536,1536]{2,1,0:T(8,128)} %param.11), kind=kOutput, calls=%fused_computation.27 | convolution fusion | flops 29001252864 | bytes 31465472 | tf_op jit(solution)/shard_map/dot_general | solution.py:98
  753.0 36.3 %collective-permute-done = f32[5,128,1280]{1,2,0:T(8,128)} collective-permute-done((f32[5,128,1280]{1,2,0:T(8,128)}, f32[5,128,1280]{1,2,0:T(8,128)}, u32[]{:S(2)}, u32[]{:S(2)}) %collective-permute-start) | collective-permute-done | bytes 3276832 | tf_op jit(solution)/shard_map/ppermute | solution.py:18
  821.6 13.1 %bitcast_add_fusion = f32[1024,2048]{1,0:T(8,128)S(1)} fusion(f32[128,8,16,128]{3,2,1,0:T(8,128)} %bitcast.203, f32[1024,2048]{1,0:T(8,128)} %param.13, f32[128,8,16,128]{3,2,1,0:T(8,128)S(1)} %bitcast.202), kind=kLoop, calls=%fused_computation.28 | loop fusion | flops 4194304 | bytes 33554432 | tf_op jit(solution)/shard_map/add | solution.py:191
  839.2 10.1 gather_fusion
  855.9 13.7 %all-reduce.6.cloned.1.call-done = f32[1024,128]{1,0:T(8,128)} async-done(((f32[1024,128]{1,0:T(8,128)}), f32[1024,128]{1,0:T(8,128)}) %all-reduce.6.cloned.1.call-update) | async-done | bytes 524304 | tf_op jit(solution)/shard_map/while/body/eval_jaxpr/psum | solution.py:14
  885.6 57.1 %all-reduce.8.cloned.1.call-done = f32[128,128]{1,0:T(8,128)} async-done(((f32[128,128]{1,0:T(8,128)}), f32[128,128]{1,0:T(8,128)}) %all-reduce.8.cloned.1.call-update) | async-done | bytes 65552 | tf_op jit(solution)/shard_map/while/body/eval_jaxpr/psum | solution.py:14
  944.5 11.7 %cholesky.616 = f32[128,128]{1,0:T(8,128)S(1)} custom-call(f32[128,128]{1,0:T(8,128)S(1)} %fusion.80), custom_call_target="Cholesky" | custom-call | tf_op jit(solution)/shard_map/while/body/eval_jaxpr/jit(cholesky)/cholesky | solution.py:42
  958.1 9.8 custom-call.80
  980.3 68.7 %all-reduce.10.cloned.1.call-done = (f32[8,1,128,128]{3,2,1,0:T(8,128)}, f32[8,1,128,128]{3,2,1,0:T(8,128)}) async-done(((f32[8,1,128,128]{3,2,1,0:T(8,128)}, f32[8,1,128,128]{3,2,1,0:T(8,128)}), (f32[8,1,128,128]{3,2,1,0:T(8,128)}, f32[8,1,128,128]{3,2,1,0:T(8,128)})) %all-reduce.10.cloned.1.call-update) | async-done | bytes 1048592 | tf_op jit(solution)/shard_map/while/body/eval_jaxpr/psum | solution.py:14
  1050.7 9.6 convolution_subtract_fusion
  (212 shorter events, 310.0 us)
Async XLA Ops:
  7.2 49.4 %all-gather.8.cloned.1.call-start = ((), (), s32[]{:S(2)}) async-start(), calls=%async_computation.3 | async-start | bytes 7864320 | tf_op jit(solution)/shard_map/all_gather | solution.py:82
  9.9 164.8 %all-gather.6.cloned.1.call-start = ((), (), s32[]{:S(2)}) async-start(), calls=%async_computation | async-start | bytes 7864320 | tf_op jit(solution)/shard_map/all_gather | solution.py:84
  12.6 243.3 %all-gather.10.cloned.1.call-start = ((), (), s32[]{:S(2)}) async-start(), calls=%async_computation.4 | async-start | bytes 5242880 | tf_op jit(solution)/shard_map/all_gather | solution.py:86
  65.7 12.8 %copy-start.7 = (s32[2,40]{1,0:T(2,128)S(1)}, s32[2,40]{1,0:T(2,128)}, u32[]{:S(2)}) copy-start(s32[2,40]{1,0:T(2,128)} %param.12) | copy-start | bytes 964
  78.5 791.1 %all-reduce.6.cloned.1.call-start = ((), (), s32[]{:S(2)}) async-start(), calls=%async_computation.1 | async-start | bytes 1048576 | tf_op jit(solution)/shard_map/while/body/eval_jaxpr/psum | solution.py:14
  281.9 2.0 copy-start.4
  487.0 113.4 %slice-start = ((s8[6291456]{0:T(1024)(128)(4,1)}), s8[2097152]{0:T(1024)(128)(4,1)S(1)}, s32[]{:S(2)}) async-start(s8[6291456]{0:T(1024)(128)(4,1)} %bitcast.181), calls=%async_computation.6 | async-start | bytes 4194304
  595.4 5.0 slice-start.1
  595.4 11.3 %slice-start.2 = ((s8[6291456]{0:T(1024)(128)(4,1)}), s8[4194304]{0:T(1024)(128)(4,1)S(1)}, s32[]{:S(2)}) async-start(s8[6291456]{0:T(1024)(128)(4,1)} %bitcast.192), calls=%async_computation.8 | async-start | bytes 8388608
  600.4 6.3 slice-start.3
  612.9 3.7 copy-start.2
  705.7 3.7 copy-start.1
  716.3 73.0 %collective-permute-start = (f32[5,128,1280]{1,2,0:T(8,128)}, f32[5,128,1280]{1,2,0:T(8,128)}, u32[]{:S(2)}, u32[]{:S(2)}) collective-permute-start(f32[5,128,1280]{1,2,0:T(8,128)} %bitcast.208), channel_id=1, source_target_pairs={{0,16},{16,0},{1,17},{17,1},{2,18},{18,2},{3,19},{19,3},{4,20},{20... | collective-permute-start | bytes 9830408 | tf_op jit(solution)/shard_map/ppermute | solution.py:18
  809.1 12.5 %slice-start.4 = ((s8[8388608]{0:T(1024)(128)(4,1)}), s8[4194304]{0:T(1024)(128)(4,1)S(1)}, s32[]{:S(2)}) async-start(s8[8388608]{0:T(1024)(128)(4,1)} %bitcast.200), calls=%async_computation.10 | async-start | bytes 8388608
  813.4 8.1 slice-start.5
  834.7 3.4 copy-start
  839.0 103.7 %all-reduce.8.cloned.1.call-start = ((), (), s32[]{:S(2)}) async-start(), calls=%async_computation.2 | async-start | bytes 131072 | tf_op jit(solution)/shard_map/while/body/eval_jaxpr/psum | solution.py:14
  849.2 22.4 %copy-start.6 = (pred[1536]{0:T(1024)(128)(4,1)S(1)}, pred[1536]{0:T(1024)(128)(4,1)}, u32[]{:S(2)}) copy-start(pred[1536]{0:T(1024)(128)(4,1)} %compare_and_fusion) | copy-start | bytes 4612
  871.1 178.0 %all-reduce.10.cloned.1.call-start = ((), (), s32[]{:S(2)}) async-start(), calls=%async_computation.5 | async-start | bytes 2097152 | tf_op jit(solution)/shard_map/while/body/eval_jaxpr/psum | solution.py:14
  972.2 3.2 slice-start.6
  975.4 74.9 %copy-start.5 = (pred[2048]{0:T(1024)(128)(4,1)S(1)}, pred[2048]{0:T(1024)(128)(4,1)}, u32[]{:S(2)}) copy-start(pred[2048]{0:T(1024)(128)(4,1)} %fusion.97) | copy-start | bytes 6148
  1060.7 3.4 copy-start.3
Sparse Core Ops, SparseCore 0:
  10.1 46.4 all-gather.7
  58.2 116.5 all-gather.5
  176.9 78.9 all-gather.9
  839.1 30.4 all-reduce.5
  872.9 69.8 all-reduce.7
  970.7 78.3 all-reduce.9

commit v3 on v2

--- a/solution.py
+++ b/solution.py
@@ -79,15 +79,21 @@
     tile_count = pivot_count // TILE
     slot_count = -(-tile_count // grid_size)
     width = slot_count * TILE
+    diag_pieces = lax.all_gather(front_work[:width, :width], ("row", "col"), axis=0)
+    diag_block = diag_pieces.reshape(grid_size, grid_size, slot_count, TILE, slot_count, TILE)
+    diag_block = diag_block.transpose(2, 0, 3, 4, 1, 5).reshape(slot_count * grid_size * TILE, -1)
+    diag_block = diag_block[:pivot_count, :pivot_count]
+    diag_factor = jnp.tril(jnp.linalg.cholesky(diag_block))
+    eye = jnp.eye(pivot_count, dtype=jnp.float32)
+    diag_inverse = jnp.tril(jax.scipy.linalg.solve_triangular(diag_factor, eye, lower=True))
     col_pieces = lax.all_gather(front_work[:, :width].T, "col", axis=0)
     panel_rows = pivot_order(col_pieces, slot_count, tile_count)
     row_pieces = lax.all_gather(front_work[:width, :], "row", axis=0)
     panel_cols = pivot_order(row_pieces, slot_count, tile_count)
-    diag_pieces = lax.all_gather(panel_rows[:, :width].T, "row", axis=0)
-    diag_block = pivot_order(diag_pieces, slot_count, tile_count)
-    diag_factor = jnp.tril(jnp.linalg.cholesky(diag_block))
     both = jnp.concatenate([panel_rows, panel_cols], axis=1)
-    solved = jax.scipy.linalg.solve_triangular(diag_factor, both, lower=True)
+    solved = jnp.dot(
+        diag_inverse, both, precision=lax.Precision.HIGHEST, preferred_element_type=jnp.float32
+    )
     solved_rows = solved[:, :local_count].T
     solved_cols = solved[:, local_count:].T
     within = jnp.arange(local_count, dtype=jnp.int32)

time: 1080 us -> 915 us (0.85)
  waiting for transfers between devices: 387 us -> 217 us
    all_gather x1, waiting for transfers between devices: 91.4 us -> 0.01 us  [factor_child(): row_pieces = lax.all_gather(front_work[:width, :], 'row', axis=0)]
    all_gather x1, waiting for transfers between devices: 43.9 us -> 0.01 us  [factor_child(): col_pieces = lax.all_gather(front_work[:, :width].T, 'col', axis=0)]
    dot_general x0 -> x1, matrix products: none -> 42.1 us  [factor_child(): jnp.dot(diag_inverse, both, precision=lax.Precision.HIGHEST, preferred_el...]
    another operation x15, matrix products: 68.2 us -> 28.3 us  [factor_child(): jax.scipy.linalg.solve_triangular(diag_factor, eye, lower=True)]
    all_gather x1, waiting for transfers between devices: 75.3 us -> 39.6 us  [factor_child(): lax.all_gather(front_work[:width, :width], ('row', 'col'), axis=0)]
    reshape x2 -> x4, local copies, waits for them, and re-layouts: 10.9 us -> 24.2 us  [the longest x2 13.3 us: factor_child(): diag_pieces.reshape(grid_size, grid_size, slot_count, TILE, slot_count, T...]
  transfers between devices with their start and end apart: 7 -> 7, of which waited for: 7 -> 5; matrix products, arithmetic and copies ran while one was open for 10% -> 52% of each run, Pallas kernels for 0% -> 0%
where the time goes in v3:
time: 915 us; the launch traced here: 908 us
  other arithmetic  344 us (38%)
  waiting for transfers between devices  217 us (24%)
  local copies, waits for them, and re-layouts  180 us (20%)
  matrix products  144 us (16%)
  between operations  20.3 us (2%)
    another operation x30, other arithmetic, factor_child(): diag_factor = jnp.tril(jnp.linalg.cholesky(diag_block))  172 us
    psum x3, waiting for transfers between devices, spread(): return lax.psum(jnp.where(mine, shard, jnp.zeros_like(shard)), axis)  141 us
    another operation x3, other arithmetic, factor_child(): jax.scipy.linalg.solve_triangular(diag_factor, eye, lower=True)  85.6 us
    dot_general x1, matrix products, factor_child(): jnp.dot(diag_inverse, both, precision=lax.Precision.HIGHEST, preferred_el...  42.1 us
    all_gather x1, waiting for transfers between devices, factor_child(): lax.all_gather(front_work[:width, :width], ('row', 'col'), axis=0)  39.6 us
    dot_general x1, matrix products, factor_child(): jnp.dot(jnp.where(rows_after, solved_rows, 0.0), jnp.where(cols_after.T,...  37.9 us
    ppermute x1, waiting for transfers between devices, from_partner(): lax.ppermute(shard, axis, [(i, i ^ 1 << distance) for i in range(lax.axis...  36.9 us
    another operation x15, matrix products, factor_child(): jax.scipy.linalg.solve_triangular(diag_factor, eye, lower=True)  28.3 us
  transfers between devices with their start and end apart: 7, of which 5 were waited for; matrix products, arithmetic and copies ran while one was open for 52% of the time, Pallas kernels for 0%

profile of v3, /device:TPU:4, one launch (start us, length us, event | category | flops | bytes accessed | tf_op | source)
XLA Modules:
  0.0 907.6 jit_solution(15444250590017648722)
XLA Ops:
  22.0 39.6 %all-gather.8.cloned.1.call-done = f32[4096,256]{1,0:T(8,128)} async-done(((f32[256,256]{1,0:T(8,128)}), f32[4096,256]{1,0:T(8,128)}) %all-gather.8.cloned.1.call-update) | async-done | bytes 4194320 | tf_op jit(solution)/shard_map/all_gather | solution.py:82
  92.3 11.7 %cholesky.243 = f32[128,128]{1,0:T(8,128)S(1)} custom-call(f32[128,128]{1,0:T(8,128)S(1)} %cholesky.627), custom_call_target="Cholesky" | custom-call | tf_op jit(solution)/shard_map/jit(cholesky)/cholesky | solution.py:86
  104.1 9.8 %custom-call.72 = f32[1,128,128]{1,2,0:T(8,128)S(1)} custom-call(f32[1,128,128]{2,1,0:T(8,128)S(1)} %get-tuple-element.102), custom_call_target="InvertDiagBlocksLowerTriangular" | custom-call | tf_op jit(solution)/shard_map/jit(cholesky)/cholesky | solution.py:86
  120.4 11.9 %cholesky.266 = f32[128,128]{1,0:T(8,128)S(1)} custom-call(f32[128,128]{1,0:T(8,128)S(1)} %cholesky.631), custom_call_target="Cholesky" | custom-call | tf_op jit(solution)/shard_map/jit(cholesky)/cholesky | solution.py:86
  132.9 9.8 %custom-call.73 = f32[1,128,128]{1,2,0:T(8,128)S(1)} custom-call(f32[1,128,128]{2,1,0:T(8,128)S(1)} %get-tuple-element.99), custom_call_target="InvertDiagBlocksLowerTriangular" | custom-call | tf_op jit(solution)/shard_map/jit(cholesky)/cholesky | solution.py:86
  146.1 11.7 %cholesky.507 = f32[128,128]{1,0:T(8,128)S(1)} custom-call(f32[128,128]{1,0:T(8,128)S(1)} %cholesky.636), custom_call_target="Cholesky" | custom-call | tf_op jit(solution)/shard_map/jit(cholesky)/cholesky | solution.py:86
  158.4 9.8 %custom-call.74 = f32[1,128,128]{1,2,0:T(8,128)S(1)} custom-call(f32[1,128,128]{2,1,0:T(8,128)S(1)} %get-tuple-element.96), custom_call_target="InvertDiagBlocksLowerTriangular" | custom-call | tf_op jit(solution)/shard_map/jit(cholesky)/cholesky | solution.py:86
  171.8 12.1 %cholesky.526 = f32[128,128]{1,0:T(8,128)S(1)} custom-call(f32[128,128]{1,0:T(8,128)S(1)} %cholesky.641), custom_call_target="Cholesky" | custom-call | tf_op jit(solution)/shard_map/jit(cholesky)/cholesky | solution.py:86
  184.5 9.8 %custom-call.75 = f32[1,128,128]{1,2,0:T(8,128)S(1)} custom-call(f32[1,128,128]{2,1,0:T(8,128)S(1)} %get-tuple-element.93), custom_call_target="InvertDiagBlocksLowerTriangular" | custom-call | tf_op jit(solution)/shard_map/jit(cholesky)/cholesky | solution.py:86
  197.8 11.7 %cholesky.545 = f32[128,128]{1,0:T(8,128)S(1)} custom-call(f32[128,128]{1,0:T(8,128)S(1)} %cholesky.646), custom_call_target="Cholesky" | custom-call | tf_op jit(solution)/shard_map/jit(cholesky)/cholesky | solution.py:86
  210.1 9.9 %custom-call.76 = f32[1,128,128]{1,2,0:T(8,128)S(1)} custom-call(f32[1,128,128]{2,1,0:T(8,128)S(1)} %get-tuple-element.90), custom_call_target="InvertDiagBlocksLowerTriangular" | custom-call | tf_op jit(solution)/shard_map/jit(cholesky)/cholesky | solution.py:86
  223.4 11.7 %cholesky.565 = f32[128,128]{1,0:T(8,128)S(1)} custom-call(f32[128,128]{1,0:T(8,128)S(1)} %cholesky.651), custom_call_target="Cholesky" | custom-call | tf_op jit(solution)/shard_map/jit(cholesky)/cholesky | solution.py:86
  235.7 9.8 %custom-call.77 = f32[1,128,128]{1,2,0:T(8,128)S(1)} custom-call(f32[1,128,128]{2,1,0:T(8,128)S(1)} %get-tuple-element.87), custom_call_target="InvertDiagBlocksLowerTriangular" | custom-call | tf_op jit(solution)/shard_map/jit(cholesky)/cholesky | solution.py:86
  248.6 11.7 %cholesky.585 = f32[128,128]{1,0:T(8,128)S(1)} custom-call(f32[128,128]{1,0:T(8,128)S(1)} %cholesky.656), custom_call_target="Cholesky" | custom-call | tf_op jit(solution)/shard_map/jit(cholesky)/cholesky | solution.py:86
  260.9 9.8 %custom-call.78 = f32[1,128,128]{1,2,0:T(8,128)S(1)} custom-call(f32[1,128,128]{2,1,0:T(8,128)S(1)} %get-tuple-element.84), custom_call_target="InvertDiagBlocksLowerTriangular" | custom-call | tf_op jit(solution)/shard_map/jit(cholesky)/cholesky | solution.py:86
  273.4 11.7 %cholesky.603 = f32[128,128]{1,0:T(8,128)S(1)} custom-call(f32[128,128]{1,0:T(8,128)S(1)} %convolution_subtract_fusion.12), custom_call_target="Cholesky" | custom-call | tf_op jit(solution)/shard_map/jit(cholesky)/cholesky | solution.py:86
  302.2 23.3 %while.1 = (s32[]{:T(128)}, f32[1024,1024]{1,0:T(8,128)}, s32[8,2]{0,1:T(2,128)S(1)}, f32[8,128,128]{2,1,0:T(8,128)S(1)}, s32[]{:T(128)}) while((s32[]{:T(128)}, f32[1024,1024]{1,0:T(8,128)}, s32[8,2]{0,1:T(2,128)S(1)}, f32[8,128,128]{2,1,0:T(8,128)S(1)}, s32[]{:T(128)}) %tuple.84), condition=%wide.while_cond, body=%wide.while_body.sunk | while | flops 2 | bytes 131181 | solution.py:88
  325.5 78.8 %custom-call.79 = f32[8,128,128]{1,2,0:T(8,128)S(1)} custom-call(f32[8,128,128]{2,1,0:T(8,128)S(1)} %get-tuple-element.34), custom_call_target="InvertDiagBlocksLowerTriangular" | custom-call | tf_op jit(solution)/shard_map/jit(_solve_triangular)/triangular_solve | solution.py:88
  432.6 9.1 %reshape.433 = f32[4,2,128,1536]{2,1,0,3:T(2,128)} reshape(f32[1024,1536]{0,1:T(8,128)} %all-gather.10.cloned.1.call-done) | data formatting | bytes 12582912 | tf_op jit(solution)/shard_map/reshape | solution.py:72
  441.8 10.1 %copy.54 = f32[4,2,128,1536]{3,2,0,1:T(8,128)} copy(f32[4,2,128,1536]{2,1,0,3:T(2,128)} %reshape.433) | data formatting | bytes 12582912 | tf_op jit(solution)/shard_map/reshape | solution.py:72
  456.5 42.1 %fusion = f32[1024,3072]{1,0:T(8,128)S(1)} fusion(f32[1024,1536]{1,0:T(8,128)S(1)} %bitcast.184, f32[1024,1536]{1,0:T(8,128)S(1)} %bitcast.183, f32[1024,1024]{1,0:T(8,128)} %convolution_dynamic-update-slice_fusion), kind=kOutput, calls=%fused_computation.12 | convolution fusion | flops 38659948544 | bytes 29360128 | tf_op jit(solution)/shard_map/dot_general | solution.py:94
  503.1 37.9 %subtract_select_fusion = f32[1536,1536]{1,0:T(8,128)S(1)} fusion(f32[1024,3072]{1,0:T(8,128)S(1)} %fusion, pred[1536]{0:T(1024)(128)(4,1)S(1)} %get-tuple-element.123, pred[1536]{0:T(1024)(128)(4,1)S(1)} %get-tuple-element.122, f32[1,1536,1536]{2,1,0:T(8,128)} %param.11), kind=kOutput, calls=%fused_computation.17 | convolution fusion | flops 29001252864 | bytes 31465472 | tf_op jit(solution)/shard_map/dot_general | solution.py:104
  588.3 36.9 %collective-permute-done = f32[5,128,1280]{1,2,0:T(8,128)} collective-permute-done((f32[5,128,1280]{1,2,0:T(8,128)}, f32[5,128,1280]{1,2,0:T(8,128)}, u32[]{:S(2)}, u32[]{:S(2)}) %collective-permute-start) | collective-permute-done | bytes 3276832 | tf_op jit(solution)/shard_map/ppermute | solution.py:18
  657.4 12.9 %bitcast_add_fusion = f32[1024,2048]{1,0:T(8,128)S(1)} fusion(f32[128,8,16,128]{3,2,1,0:T(8,128)} %bitcast.178, f32[1024,2048]{1,0:T(8,128)} %param.13, f32[128,8,16,128]{3,2,1,0:T(8,128)S(1)} %bitcast.177), kind=kLoop, calls=%fused_computation.18 | loop fusion | flops 4194304 | bytes 33554432 | tf_op jit(solution)/shard_map/add | solution.py:197
  674.7 10.1 %gather_fusion = f32[1536,1024]{1,0:T(8,128)} fusion(f32[1024,1024]{1,0:T(8,128)} %get-tuple-element.48, s32[2048]{0:T(1024)S(1)} %pad_clamp_fusion), kind=kCustom, calls=%fused_computation.8 | custom fusion | bytes 12589056 | tf_op jit(solution)/shard_map/jit(_take)/gather | solution.py:110
  691.4 14.6 %all-reduce.6.cloned.1.call-done = f32[1024,128]{1,0:T(8,128)} async-done(((f32[1024,128]{1,0:T(8,128)}), f32[1024,128]{1,0:T(8,128)}) %all-reduce.6.cloned.1.call-update) | async-done | bytes 524304 | tf_op jit(solution)/shard_map/while/body/eval_jaxpr/psum | solution.py:14
  707.7 8.7 select_select_fusion
  721.7 57.4 %all-reduce.8.cloned.1.call-done = f32[128,128]{1,0:T(8,128)} async-done(((f32[128,128]{1,0:T(8,128)}), f32[128,128]{1,0:T(8,128)}) %all-reduce.8.cloned.1.call-update) | async-done | bytes 65552 | tf_op jit(solution)/shard_map/while/body/eval_jaxpr/psum | solution.py:14
  780.9 11.7 %cholesky.616 = f32[128,128]{1,0:T(8,128)S(1)} custom-call(f32[128,128]{1,0:T(8,128)S(1)} %fusion.80), custom_call_target="Cholesky" | custom-call | tf_op jit(solution)/shard_map/while/body/eval_jaxpr/jit(cholesky)/cholesky | solution.py:42
  794.4 9.8 %custom-call.80 = f32[1,128,128]{1,2,0:T(8,128)S(1)} custom-call(f32[1,128,128]{2,1,0:T(8,128)S(1)} %fusion.150), custom_call_target="InvertDiagBlocksLowerTriangular" | custom-call | tf_op jit(solution)/shard_map/while/body/eval_jaxpr/jit(_solve_triangular)/triangular_solve | solution.py:43
  816.7 68.7 %all-reduce.10.cloned.1.call-done = (f32[8,1,128,128]{3,2,1,0:T(8,128)}, f32[8,1,128,128]{3,2,1,0:T(8,128)}) async-done(((f32[8,1,128,128]{3,2,1,0:T(8,128)}, f32[8,1,128,128]{3,2,1,0:T(8,128)}), (f32[8,1,128,128]{3,2,1,0:T(8,128)}, f32[8,1,128,128]{3,2,1,0:T(8,128)})) %all-reduce.10.cloned.1.call-update) | async-done | bytes 1048592 | tf_op jit(solution)/shard_map/while/body/eval_jaxpr/psum | solution.py:14
  887.0 9.7 %convolution_subtract_fusion = f32[1024,2048]{1,0:T(8,128)S(1)} fusion(f32[1024,2048]{1,0:T(8,128)} %copy-done, f32[2048,128]{1,0:T(8,128)S(1)} %bitcast_select_fusion.2, f32[1024,128]{1,0:T(8,128)S(1)} %get-tuple-element.113, pred[1024]{0:T(1024)(128)(4,1)S(1)} %get-tuple-element.133), kind=kOutput, calls=%fused_computation.27 | convolution fusion | flops 3223453696 | bytes 18351104 | tf_op jit(solution)/shard_map/while/body/eval_jaxpr/dot_general | solution.py:49
  (209 shorter events, 266.1 us)
Async XLA Ops:
  7.2 54.5 %all-gather.8.cloned.1.call-start = ((), (), s32[]{:S(2)}) async-start(), calls=%async_computation.3 | async-start | bytes 4456448 | tf_op jit(solution)/shard_map/all_gather | solution.py:82
  8.9 423.7 %all-gather.10.cloned.1.call-start = ((), (), s32[]{:S(2)}) async-start(), calls=%async_computation.4 | async-start | bytes 7864320 | tf_op jit(solution)/shard_map/all_gather | solution.py:89
  11.6 440.3 %all-gather.6.cloned.1.call-start = ((), (), s32[]{:S(2)}) async-start(), calls=%async_computation | async-start | bytes 7864320 | tf_op jit(solution)/shard_map/all_gather | solution.py:91
  14.4 2.9 copy-start.9
  14.4 691.6 %all-reduce.6.cloned.1.call-start = ((), (), s32[]{:S(2)}) async-start(), calls=%async_computation.1 | async-start | bytes 1048576 | tf_op jit(solution)/shard_map/while/body/eval_jaxpr/psum | solution.py:14
  90.3 2.0 copy-start.4
  404.3 4.7 copy-start.2
  451.9 4.6 copy-start.5
  498.7 4.5 copy-start.6
  541.1 3.7 copy-start.1
  551.7 73.4 %collective-permute-start = (f32[5,128,1280]{1,2,0:T(8,128)}, f32[5,128,1280]{1,2,0:T(8,128)}, u32[]{:S(2)}, u32[]{:S(2)}) collective-permute-start(f32[5,128,1280]{1,2,0:T(8,128)} %bitcast.185), channel_id=1, source_target_pairs={{0,16},{16,0},{1,17},{17,1},{2,18},{18,2},{3,19},{19,3},{4,20},{20... | collective-permute-start | bytes 9830408 | tf_op jit(solution)/shard_map/ppermute | solution.py:18
  644.8 12.5 %slice-start = ((s8[8388608]{0:T(1024)(128)(4,1)}), s8[4194304]{0:T(1024)(128)(4,1)S(1)}, s32[]{:S(2)}) async-start(s8[8388608]{0:T(1024)(128)(4,1)} %bitcast.175), calls=%async_computation.6 | async-start | bytes 8388608
  649.2 8.1 slice-start.1
  670.2 3.4 copy-start
  674.5 104.6 %all-reduce.8.cloned.1.call-start = ((), (), s32[]{:S(2)}) async-start(), calls=%async_computation.2 | async-start | bytes 131072 | tf_op jit(solution)/shard_map/while/body/eval_jaxpr/psum | solution.py:14
  684.8 22.9 %copy-start.8 = (pred[1536]{0:T(1024)(128)(4,1)S(1)}, pred[1536]{0:T(1024)(128)(4,1)}, u32[]{:S(2)}) copy-start(pred[1536]{0:T(1024)(128)(4,1)} %compare_and_fusion) | copy-start | bytes 4612
  707.4 178.0 %all-reduce.10.cloned.1.call-start = ((), (), s32[]{:S(2)}) async-start(), calls=%async_computation.5 | async-start | bytes 2097152 | tf_op jit(solution)/shard_map/while/body/eval_jaxpr/psum | solution.py:14
  808.5 3.2 slice-start.2
  811.8 74.9 %copy-start.7 = (pred[2048]{0:T(1024)(128)(4,1)S(1)}, pred[2048]{0:T(1024)(128)(4,1)}, u32[]{:S(2)}) copy-start(pred[2048]{0:T(1024)(128)(4,1)} %fusion.97) | copy-start | bytes 6148
  897.1 3.4 copy-start.3
Sparse Core Ops, SparseCore 0:
  10.7 50.8 all-gather.7
  63.2 44.8 all-gather.9
  109.7 116.3 all-gather.5
  674.7 31.2 all-reduce.5
  709.2 69.8 all-reduce.7
  807.0 78.3 all-reduce.9

commit v4 on v3

--- a/solution.py
+++ b/solution.py
@@ -74,6 +74,32 @@
     return shaped[: tile_count * TILE]
 
 
+def lower_inverse(factor):
+    order = factor.shape[0]
+    count = order // TILE
+    if count & (count - 1):
+        eye = jnp.eye(order, dtype=jnp.float32)
+        return jnp.tril(jax.scipy.linalg.solve_triangular(factor, eye, lower=True))
+    picks = jnp.arange(count)
+    diag = factor.reshape(count, TILE, count, TILE)[picks, :, picks, :]
+    eye = jnp.broadcast_to(jnp.eye(TILE, dtype=jnp.float32), diag.shape)
+    inverse = jnp.tril(jax.scipy.linalg.solve_triangular(diag, eye, lower=True))
+    size = TILE
+    while size < order:
+        pairs = order // size // 2
+        halves = inverse.reshape(pairs, 2, size, size)
+        first, second = halves[:, 0], halves[:, 1]
+        picks = jnp.arange(pairs)
+        lower = factor.reshape(pairs, 2, size, pairs, 2, size)[picks, 1, :, picks, 0, :]
+        mixed = jnp.einsum("kab,kbc->kac", second, lower, precision=lax.Precision.HIGHEST)
+        mixed = -jnp.einsum("kab,kbc->kac", mixed, first, precision=lax.Precision.HIGHEST)
+        top = jnp.concatenate([first, jnp.zeros_like(first)], axis=2)
+        bottom = jnp.concatenate([mixed, second], axis=2)
+        inverse = jnp.concatenate([top, bottom], axis=1)
+        size *= 2
+    return inverse[0]
+
+
 def factor_child(front_work, pivot_count, grid_size, my_row, my_col):
     local_count = front_work.shape[0]
     tile_count = pivot_count // TILE
@@ -84,8 +110,7 @@
     diag_block = diag_block.transpose(2, 0, 3, 4, 1, 5).reshape(slot_count * grid_size * TILE, -1)
     diag_block = diag_block[:pivot_count, :pivot_count]
     diag_factor = jnp.tril(jnp.linalg.cholesky(diag_block))
-    eye = jnp.eye(pivot_count, dtype=jnp.float32)
-    diag_inverse = jnp.tril(jax.scipy.linalg.solve_triangular(diag_factor, eye, lower=True))
+    diag_inverse = lower_inverse(diag_factor)
     col_pieces = lax.all_gather(front_work[:, :width].T, "col", axis=0)
     panel_rows = pivot_order(col_pieces, slot_count, tile_count)
     row_pieces = lax.all_gather(front_work[:width, :], "row", axis=0)

time: 915 us -> 919 us (level)
  local copies, waits for them, and re-layouts: 180 us -> 196 us
  matrix products: 144 us -> 131 us
    reshape x0 -> x6, local copies, waits for them, and re-layouts: none -> 30.4 us  [the longest x5 27.7 us: lower_inverse(): factor.reshape(pairs, 2, size, pairs, 2, size)[picks, 1, :, picks, 0, :]]
    another operation x15 -> x1, matrix products: 28.3 us -> 0.99 us  [lower_inverse(): inverse = jnp.tril(jax.scipy.linalg.solve_triangular(diag, eye, lower=True))]
    another operation x25 -> x1, local copies, waits for them, and re-layouts: 23.1 us -> 2.31 us  [lower_inverse(): factor.reshape(pairs, 2, size, pairs, 2, size)[picks, 1, :, picks, 0, :]]
    another operation x3 -> x2, other arithmetic: 85.6 us -> 79 us  [lower_inverse(): inverse = jnp.tril(jax.scipy.linalg.solve_triangular(diag, eye, lower=True))]
    unnamed x25 -> x30, local copies, waits for them, and re-layouts: 20.3 us -> 16.9 us
  transfers between devices with their start and end apart: 7 -> 7, of which waited for: 5 -> 5; matrix products, arithmetic and copies ran while one was open for 52% -> 51% of each run, Pallas kernels for 0% -> 0%
where the time goes in v4:
time: 919 us; the launch traced here: 912 us
  other arithmetic  343 us (37%)
  waiting for transfers between devices  220 us (24%)
  local copies, waits for them, and re-layouts  196 us (21%)
  matrix products  131 us (14%)
  between operations  20.3 us (2%)
    another operation x30, other arithmetic, factor_child(): diag_factor = jnp.tril(jnp.linalg.cholesky(diag_block))  172 us
    psum x3, waiting for transfers between devices, spread(): return lax.psum(jnp.where(mine, shard, jnp.zeros_like(shard)), axis)  141 us
    another operation x2, other arithmetic, lower_inverse(): inverse = jnp.tril(jax.scipy.linalg.solve_triangular(diag, eye, lower=True))  79 us
    dot_general x1, matrix products, factor_child(): jnp.dot(diag_inverse, both, precision=lax.Precision.HIGHEST, preferred_el...  47.7 us
    all_gather x1, waiting for transfers between devices, factor_child(): lax.all_gather(front_work[:width, :width], ('row', 'col'), axis=0)  42.6 us
    dot_general x1, matrix products, factor_child(): jnp.dot(jnp.where(rows_after, solved_rows, 0.0), jnp.where(cols_after.T,...  39.9 us
    ppermute x1, waiting for transfers between devices, from_partner(): lax.ppermute(shard, axis, [(i, i ^ 1 << distance) for i in range(lax.axis...  36.6 us
    reshape x5, local copies, waits for them, and re-layouts, lower_inverse(): factor.reshape(pairs, 2, size, pairs, 2, size)[picks, 1, :, picks, 0, :]  27.7 us
  transfers between devices with their start and end apart: 7, of which 5 were waited for; matrix products, arithmetic and copies ran while one was open for 51% of the time, Pallas kernels for 0%

profile of v4, /device:TPU:4, one launch (start us, length us, event | category | flops | bytes accessed | tf_op | source)
XLA Modules:
  0.0 912.3 jit_solution(7844890275989851917)
XLA Ops:
  19.1 42.6 %all-gather.8.cloned.1.call-done = f32[4096,256]{1,0:T(8,128)} async-done(((f32[256,256]{1,0:T(8,128)}), f32[4096,256]{1,0:T(8,128)}) %all-gather.8.cloned.1.call-update) | async-done | bytes 4194320 | tf_op jit(solution)/shard_map/all_gather | solution.py:108
  92.4 11.7 %cholesky.197 = f32[128,128]{1,0:T(8,128)S(1)} custom-call(f32[128,128]{1,0:T(8,128)S(1)} %cholesky.534), custom_call_target="Cholesky" | custom-call | tf_op jit(solution)/shard_map/jit(cholesky)/cholesky | solution.py:112
  104.2 9.8 %custom-call.72 = f32[1,128,128]{1,2,0:T(8,128)S(1)} custom-call(f32[1,128,128]{2,1,0:T(8,128)S(1)} %get-tuple-element.83), custom_call_target="InvertDiagBlocksLowerTriangular" | custom-call | tf_op jit(solution)/shard_map/jit(cholesky)/cholesky | solution.py:112
  120.5 12.2 %cholesky.215 = f32[128,128]{1,0:T(8,128)S(1)} custom-call(f32[128,128]{1,0:T(8,128)S(1)} %cholesky.538), custom_call_target="Cholesky" | custom-call | tf_op jit(solution)/shard_map/jit(cholesky)/cholesky | solution.py:112
  133.4 9.8 %custom-call.73 = f32[1,128,128]{1,2,0:T(8,128)S(1)} custom-call(f32[1,128,128]{2,1,0:T(8,128)S(1)} %get-tuple-element.80), custom_call_target="InvertDiagBlocksLowerTriangular" | custom-call | tf_op jit(solution)/shard_map/jit(cholesky)/cholesky | solution.py:112
  146.5 11.7 %cholesky.242 = f32[128,128]{1,0:T(8,128)S(1)} custom-call(f32[128,128]{1,0:T(8,128)S(1)} %cholesky.543), custom_call_target="Cholesky" | custom-call | tf_op jit(solution)/shard_map/jit(cholesky)/cholesky | solution.py:112
  158.9 9.8 %custom-call.74 = f32[1,128,128]{1,2,0:T(8,128)S(1)} custom-call(f32[1,128,128]{2,1,0:T(8,128)S(1)} %get-tuple-element.77), custom_call_target="InvertDiagBlocksLowerTriangular" | custom-call | tf_op jit(solution)/shard_map/jit(cholesky)/cholesky | solution.py:112
  172.2 11.9 %cholesky.433 = f32[128,128]{1,0:T(8,128)S(1)} custom-call(f32[128,128]{1,0:T(8,128)S(1)} %cholesky.548), custom_call_target="Cholesky" | custom-call | tf_op jit(solution)/shard_map/jit(cholesky)/cholesky | solution.py:112
  184.7 9.8 %custom-call.75 = f32[1,128,128]{1,2,0:T(8,128)S(1)} custom-call(f32[1,128,128]{2,1,0:T(8,128)S(1)} %get-tuple-element.74), custom_call_target="InvertDiagBlocksLowerTriangular" | custom-call | tf_op jit(solution)/shard_map/jit(cholesky)/cholesky | solution.py:112
  198.0 11.7 %cholesky.452 = f32[128,128]{1,0:T(8,128)S(1)} custom-call(f32[128,128]{1,0:T(8,128)S(1)} %cholesky.553), custom_call_target="Cholesky" | custom-call | tf_op jit(solution)/shard_map/jit(cholesky)/cholesky | solution.py:112
  210.3 10.2 %custom-call.76 = f32[1,128,128]{1,2,0:T(8,128)S(1)} custom-call(f32[1,128,128]{2,1,0:T(8,128)S(1)} %get-tuple-element.71), custom_call_target="InvertDiagBlocksLowerTriangular" | custom-call | tf_op jit(solution)/shard_map/jit(cholesky)/cholesky | solution.py:112
  223.8 11.7 %cholesky.472 = f32[128,128]{1,0:T(8,128)S(1)} custom-call(f32[128,128]{1,0:T(8,128)S(1)} %cholesky.558), custom_call_target="Cholesky" | custom-call | tf_op jit(solution)/shard_map/jit(cholesky)/cholesky | solution.py:112
  236.2 9.8 %custom-call.77 = f32[1,128,128]{1,2,0:T(8,128)S(1)} custom-call(f32[1,128,128]{2,1,0:T(8,128)S(1)} %get-tuple-element.68), custom_call_target="InvertDiagBlocksLowerTriangular" | custom-call | tf_op jit(solution)/shard_map/jit(cholesky)/cholesky | solution.py:112
  249.0 11.7 %cholesky.492 = f32[128,128]{1,0:T(8,128)S(1)} custom-call(f32[128,128]{1,0:T(8,128)S(1)} %cholesky.563), custom_call_target="Cholesky" | custom-call | tf_op jit(solution)/shard_map/jit(cholesky)/cholesky | solution.py:112
  261.4 9.8 %custom-call.78 = f32[1,128,128]{1,2,0:T(8,128)S(1)} custom-call(f32[1,128,128]{2,1,0:T(8,128)S(1)} %get-tuple-element.65), custom_call_target="InvertDiagBlocksLowerTriangular" | custom-call | tf_op jit(solution)/shard_map/jit(cholesky)/cholesky | solution.py:112
  273.8 11.7 %cholesky.510 = f32[128,128]{1,0:T(8,128)S(1)} custom-call(f32[128,128]{1,0:T(8,128)S(1)} %convolution_subtract_fusion.7), custom_call_target="Cholesky" | custom-call | tf_op jit(solution)/shard_map/jit(cholesky)/cholesky | solution.py:112
  329.7 79.0 %custom-call.79 = f32[8,1,128,128]{2,3,1,0:T(8,128)S(1)} custom-call(f32[8,1,128,128]{3,2,1,0:T(8,128)S(1)} %bitcast_select_fusion.4), custom_call_target="InvertDiagBlocksLowerTriangular" | custom-call | tf_op jit(solution)/shard_map/jit(_solve_triangular)/vmap()/triangular_solve | solution.py:86
  434.3 9.1 %reshape.469 = f32[4,2,128,1536]{2,1,0,3:T(2,128)} reshape(f32[1024,1536]{0,1:T(8,128)} %all-gather.10.cloned.1.call-done) | data formatting | bytes 12582912 | tf_op jit(solution)/shard_map/reshape | solution.py:72
  443.5 10.1 %copy.106 = f32[4,2,128,1536]{3,2,0,1:T(8,128)} copy(f32[4,2,128,1536]{2,1,0,3:T(2,128)} %reshape.469) | data formatting | bytes 12582912 | tf_op jit(solution)/shard_map/reshape | solution.py:72
  458.2 47.7 %fusion = f32[1024,3072]{1,0:T(8,128)} fusion(f32[1024,1536]{1,0:T(8,128)S(1)} %bitcast.191, f32[1024,1536]{1,0:T(8,128)S(1)} %bitcast.190, f32[1,512,512]{2,1,0:T(8,128)} %get-tuple-element.54, f32[1,512,512]{2,1,0:T(8,128)} %get-tuple-element.53, f32[1,512,512]{2,1,0:T(8,128)} %fusion.19), kind=kOutput, calls=%fused_computation.13 | convolution fusion | flops 38662045696 | bytes 28311552 | tf_op jit(solution)/shard_map/dot_general | solution.py:119
  505.9 39.9 %subtract_select_fusion = f32[1536,1536]{1,0:T(8,128)S(1)} fusion(f32[1024,3072]{1,0:T(8,128)} %fusion, pred[1536]{0:T(1024)(128)(4,1)S(1)} %get-tuple-element.102, pred[1536]{0:T(1024)(128)(4,1)S(1)} %get-tuple-element.101, f32[1,1536,1536]{2,1,0:T(8,128)S(1)} %bitcast.201), kind=kOutput, calls=%fused_computation.18 | convolution fusion | flops 29001252864 | bytes 31465472 | tf_op jit(solution)/shard_map/dot_general | solution.py:129
  593.3 36.6 %collective-permute-done = f32[5,128,1280]{1,2,0:T(8,128)} collective-permute-done((f32[5,128,1280]{1,2,0:T(8,128)}, f32[5,128,1280]{1,2,0:T(8,128)}, u32[]{:S(2)}, u32[]{:S(2)}) %collective-permute-start) | collective-permute-done | bytes 3276832 | tf_op jit(solution)/shard_map/ppermute | solution.py:18
  654.0 8.1 copy.115
  662.2 12.9 %bitcast_add_fusion = f32[1024,2048]{1,0:T(8,128)S(1)} fusion(f32[128,8,16,128]{3,2,1,0:T(8,128)} %bitcast.181, f32[1024,2048]{1,0:T(8,128)} %param.13, f32[128,8,16,128]{3,2,1,0:T(8,128)S(1)} %bitcast.180), kind=kLoop, calls=%fused_computation.19 | loop fusion | flops 4194304 | bytes 33554432 | tf_op jit(solution)/shard_map/add | solution.py:222
  679.5 10.1 %gather_fusion.3 = f32[1536,1024]{1,0:T(8,128)} fusion(f32[1024,1024]{1,0:T(8,128)} %select_select_fusion.1, s32[2048]{0:T(1024)S(1)} %pad_clamp_fusion), kind=kCustom, calls=%fused_computation.11 | custom fusion | bytes 12589056 | tf_op jit(solution)/shard_map/jit(_take)/gather | solution.py:135
  696.2 14.6 %all-reduce.9.cloned.1.call-done = f32[1024,128]{1,0:T(8,128)} async-done(((f32[1024,128]{1,0:T(8,128)}), f32[1024,128]{1,0:T(8,128)}) %all-reduce.9.cloned.1.call-update) | async-done | bytes 524304 | tf_op jit(solution)/shard_map/while/body/eval_jaxpr/psum | solution.py:14
  712.8 8.7 select_select_fusion
  726.8 57.2 %all-reduce.11.cloned.1.call-done = f32[128,128]{1,0:T(8,128)} async-done(((f32[128,128]{1,0:T(8,128)}), f32[128,128]{1,0:T(8,128)}) %all-reduce.11.cloned.1.call-update) | async-done | bytes 65552 | tf_op jit(solution)/shard_map/while/body/eval_jaxpr/psum | solution.py:14
  785.7 11.7 %cholesky.523 = f32[128,128]{1,0:T(8,128)S(1)} custom-call(f32[128,128]{1,0:T(8,128)S(1)} %fusion.57), custom_call_target="Cholesky" | custom-call | tf_op jit(solution)/shard_map/while/body/eval_jaxpr/jit(cholesky)/cholesky | solution.py:42
  799.3 9.8 %custom-call.80 = f32[1,128,128]{1,2,0:T(8,128)S(1)} custom-call(f32[1,128,128]{2,1,0:T(8,128)S(1)} %fusion.121), custom_call_target="InvertDiagBlocksLowerTriangular" | custom-call | tf_op jit(solution)/shard_map/while/body/eval_jaxpr/jit(_solve_triangular)/triangular_solve | solution.py:43
  821.5 68.7 %all-reduce.13.cloned.1.call-done = (f32[8,1,128,128]{3,2,1,0:T(8,128)}, f32[8,1,128,128]{3,2,1,0:T(8,128)}) async-done(((f32[8,1,128,128]{3,2,1,0:T(8,128)}, f32[8,1,128,128]{3,2,1,0:T(8,128)}), (f32[8,1,128,128]{3,2,1,0:T(8,128)}, f32[8,1,128,128]{3,2,1,0:T(8,128)})) %all-reduce.13.cloned.1.call-update) | async-done | bytes 1048592 | tf_op jit(solution)/shard_map/while/body/eval_jaxpr/psum | solution.py:14
  891.9 9.6 %convolution_subtract_fusion = f32[1024,2048]{1,0:T(8,128)S(1)} fusion(f32[1024,2048]{1,0:T(8,128)} %copy-done, f32[2048,128]{1,0:T(8,128)S(1)} %bitcast_select_fusion.2, f32[1024,128]{1,0:T(8,128)S(1)} %get-tuple-element.90, pred[1024]{0:T(1024)(128)(4,1)S(1)} %get-tuple-element.110), kind=kOutput, calls=%fused_computation.28 | convolution fusion | flops 3223453696 | bytes 18351104 | tf_op jit(solution)/shard_map/while/body/eval_jaxpr/dot_general | solution.py:49
  (199 shorter events, 252.2 us)
Async XLA Ops:
  7.2 54.5 %all-gather.8.cloned.1.call-start = ((), (), s32[]{:S(2)}) async-start(), calls=%async_computation.3 | async-start | bytes 4456448 | tf_op jit(solution)/shard_map/all_gather | solution.py:108
  8.9 6.2 copy-start.8
  8.9 425.4 %all-gather.10.cloned.1.call-start = ((), (), s32[]{:S(2)}) async-start(), calls=%async_computation.4 | async-start | bytes 7864320 | tf_op jit(solution)/shard_map/all_gather | solution.py:114
  11.7 442.0 %all-gather.6.cloned.1.call-start = ((), (), s32[]{:S(2)}) async-start(), calls=%async_computation | async-start | bytes 7864320 | tf_op jit(solution)/shard_map/all_gather | solution.py:116
  14.4 696.4 %all-reduce.9.cloned.1.call-start = ((), (), s32[]{:S(2)}) async-start(), calls=%async_computation.1 | async-start | bytes 1048576 | tf_op jit(solution)/shard_map/while/body/eval_jaxpr/psum | solution.py:14
  90.4 2.0 copy-start.4
  411.0 5.2 copy-start.2
  453.6 4.6 copy-start.5
  453.6 52.3 %slice-start.3 = ((s8[9437184]{0:T(1024)(128)(4,1)}), s8[4194304]{0:T(1024)(128)(4,1)S(1)}, s32[]{:S(2)}) async-start(s8[9437184]{0:T(1024)(128)(4,1)} %bitcast.200), calls=%async_computation.9 | async-start | bytes 8388608
  458.2 47.7 %slice-start.4 = ((s8[9437184]{0:T(1024)(128)(4,1)}), s8[4194304]{0:T(1024)(128)(4,1)S(1)}, s32[]{:S(2)}) async-start(s8[9437184]{0:T(1024)(128)(4,1)} %bitcast.200), calls=%async_computation.10 | async-start | bytes 8388608
  458.2 47.7 %slice-start.5 = ((s8[9437184]{0:T(1024)(128)(4,1)}), s8[1048576]{0:T(1024)(128)(4,1)S(1)}, s32[]{:S(2)}) async-start(s8[9437184]{0:T(1024)(128)(4,1)} %bitcast.200), calls=%async_computation.11 | async-start | bytes 2097152
  545.9 3.7 copy-start.1
  556.5 73.4 %collective-permute-start = (f32[5,128,1280]{1,2,0:T(8,128)}, f32[5,128,1280]{1,2,0:T(8,128)}, u32[]{:S(2)}, u32[]{:S(2)}) collective-permute-start(f32[5,128,1280]{1,2,0:T(8,128)} %bitcast.195), channel_id=1, source_target_pairs={{0,16},{16,0},{1,17},{17,1},{2,18},{18,2},{3,19},{19,3},{4,20},{20... | collective-permute-start | bytes 9830408 | tf_op jit(solution)/shard_map/ppermute | solution.py:18
  649.6 12.5 %slice-start = ((s8[8388608]{0:T(1024)(128)(4,1)}), s8[4194304]{0:T(1024)(128)(4,1)S(1)}, s32[]{:S(2)}) async-start(s8[8388608]{0:T(1024)(128)(4,1)} %bitcast.178), calls=%async_computation.6 | async-start | bytes 8388608
  654.0 8.1 slice-start.1
  675.0 3.4 copy-start
  679.3 104.6 %all-reduce.11.cloned.1.call-start = ((), (), s32[]{:S(2)}) async-start(), calls=%async_computation.2 | async-start | bytes 131072 | tf_op jit(solution)/shard_map/while/body/eval_jaxpr/psum | solution.py:14
  689.6 23.2 %copy-start.7 = (pred[1536]{0:T(1024)(128)(4,1)S(1)}, pred[1536]{0:T(1024)(128)(4,1)}, u32[]{:S(2)}) copy-start(pred[1536]{0:T(1024)(128)(4,1)} %compare_and_fusion) | copy-start | bytes 4612
  712.3 178.0 %all-reduce.13.cloned.1.call-start = ((), (), s32[]{:S(2)}) async-start(), calls=%async_computation.5 | async-start | bytes 2097152 | tf_op jit(solution)/shard_map/while/body/eval_jaxpr/psum | solution.py:14
  813.4 3.2 slice-start.2
  816.6 74.9 %copy-start.6 = (pred[2048]{0:T(1024)(128)(4,1)S(1)}, pred[2048]{0:T(1024)(128)(4,1)}, u32[]{:S(2)}) copy-start(pred[2048]{0:T(1024)(128)(4,1)} %fusion.75) | copy-start | bytes 6148
  901.9 3.4 copy-start.3
Sparse Core Ops, SparseCore 0:
  10.7 50.8 all-gather.7
  63.2 44.6 all-gather.9
  109.5 116.5 all-gather.5
  679.5 31.2 all-reduce.8
  714.1 69.8 all-reduce.10
  811.9 78.3 all-reduce.12

commit v5 on v4

--- a/solution.py
+++ b/solution.py
@@ -74,16 +74,30 @@
     return shaped[: tile_count * TILE]
 
 
-def lower_inverse(factor):
+def factor_pivots(block):
+    order = block.shape[0]
+    count = order // TILE
+    eye = jnp.eye(TILE, dtype=jnp.float32)
+    work = block
+    columns = []
+    inverses = []
+    for step in range(count):
+        factor = jnp.tril(jnp.linalg.cholesky(work[:TILE, :TILE]))
+        inverse = jnp.tril(jax.scipy.linalg.solve_triangular(factor, eye, lower=True))
+        panel = jnp.dot(
+            work[TILE:, :TILE], inverse.T, precision=lax.Precision.HIGHEST,
+            preferred_element_type=jnp.float32,
+        )
+        work = work[TILE:, TILE:] - jnp.dot(
+            panel, panel.T, precision=lax.Precision.HIGHEST, preferred_element_type=jnp.float32
+        )
+        columns.append(jnp.concatenate([jnp.zeros((step * TILE, TILE), jnp.float32), factor, panel]))
+        inverses.append(inverse)
+    return jnp.concatenate(columns, axis=1), jnp.stack(inverses)
+
+
+def lower_inverse(factor, inverse):
     order = factor.shape[0]
-    count = order // TILE
-    if count & (count - 1):
-        eye = jnp.eye(order, dtype=jnp.float32)
-        return jnp.tril(jax.scipy.linalg.solve_triangular(factor, eye, lower=True))
-    picks = jnp.arange(count)
-    diag = factor.reshape(count, TILE, count, TILE)[picks, :, picks, :]
-    eye = jnp.broadcast_to(jnp.eye(TILE, dtype=jnp.float32), diag.shape)
-    inverse = jnp.tril(jax.scipy.linalg.solve_triangular(diag, eye, lower=True))
     size = TILE
     while size < order:
         pairs = order // size // 2
@@ -109,8 +123,12 @@
     diag_block = diag_pieces.reshape(grid_size, grid_size, slot_count, TILE, slot_count, TILE)
     diag_block = diag_block.transpose(2, 0, 3, 4, 1, 5).reshape(slot_count * grid_size * TILE, -1)
     diag_block = diag_block[:pivot_count, :pivot_count]
-    diag_factor = jnp.tril(jnp.linalg.cholesky(diag_block))
-    diag_inverse = lower_inverse(diag_factor)
+    diag_factor, block_inverses = factor_pivots(diag_block)
+    if tile_count & (tile_count - 1):
+        eye = jnp.eye(pivot_count, dtype=jnp.float32)
+        diag_inverse = jnp.tril(jax.scipy.linalg.solve_triangular(diag_factor, eye, lower=True))
+    else:
+        diag_inverse = lower_inverse(diag_factor, block_inverses)
     col_pieces = lax.all_gather(front_work[:, :width].T, "col", axis=0)
     panel_rows = pivot_order(col_pieces, slot_count, tile_count)
     row_pieces = lax.all_gather(front_work[:width, :], "row", axis=0)

time: 919 us -> 835 us (0.909)
  other arithmetic: 343 us -> 278 us
    another operation x32 -> x40, other arithmetic: 251 us -> 184 us  [the longest x24 99.9 us: factor_pivots(): factor = jnp.tril(jnp.linalg.cholesky(work[:TILE, :TILE]))]
    dot_general x0 -> x14, matrix products: none -> 17.8 us  [the longest x7 11.9 us: factor_pivots(): jnp.dot(panel, panel.T, precision=lax.Precision.HIGHEST, preferred_elemen...]
    another operation x15 -> x8, matrix products: 24.1 us -> 6.68 us  [factor_pivots(): jax.scipy.linalg.solve_triangular(factor, eye, lower=True)]
  transfers between devices with their start and end apart: 7 -> 7, of which waited for: 5 -> 5; matrix products, arithmetic and copies ran while one was open for 51% -> 47% of each run, Pallas kernels for 0% -> 0%
where the time goes in v5:
time: 835 us; the launch traced here: 829 us
  other arithmetic  278 us (33%)
  waiting for transfers between devices  214 us (26%)
  local copies, waits for them, and re-layouts  188 us (23%)
  matrix products  131 us (16%)
  between operations  15.4 us (2%)
    psum x3, waiting for transfers between devices, spread(): return lax.psum(jnp.where(mine, shard, jnp.zeros_like(shard)), axis)  141 us
    another operation x24, other arithmetic, factor_pivots(): factor = jnp.tril(jnp.linalg.cholesky(work[:TILE, :TILE]))  99.9 us
    another operation x16, other arithmetic, factor_pivots(): jax.scipy.linalg.solve_triangular(factor, eye, lower=True)  84.1 us
    dot_general x1, matrix products, factor_child(): jnp.dot(diag_inverse, both, precision=lax.Precision.HIGHEST, preferred_el...  47.5 us
    dot_general x1, matrix products, factor_child(): jnp.dot(jnp.where(rows_after, solved_rows, 0.0), jnp.where(cols_after.T,...  39.9 us
    ppermute x1, waiting for transfers between devices, from_partner(): lax.ppermute(shard, axis, [(i, i ^ 1 << distance) for i in range(lax.axis...  36.8 us
    all_gather x1, waiting for transfers between devices, factor_child(): lax.all_gather(front_work[:width, :width], ('row', 'col'), axis=0)  36.7 us
    reshape x5, local copies, waits for them, and re-layouts, lower_inverse(): factor.reshape(pairs, 2, size, pairs, 2, size)[picks, 1, :, picks, 0, :]  27.9 us
  transfers between devices with their start and end apart: 7, of which 5 were waited for; matrix products, arithmetic and copies ran while one was open for 47% of the time, Pallas kernels for 0%

profile of v5, /device:TPU:4, one launch (start us, length us, event | category | flops | bytes accessed | tf_op | source)
XLA Modules:
  0.0 828.9 jit_solution(11459295779102646762)
XLA Ops:
  24.9 36.7 %all-gather.8.cloned.1.call-done = f32[4096,256]{1,0:T(8,128)} async-done(((f32[256,256]{1,0:T(8,128)}), f32[4096,256]{1,0:T(8,128)}) %all-gather.8.cloned.1.call-update) | async-done | bytes 4194320 | tf_op jit(solution)/shard_map/all_gather | solution.py:122
  82.5 11.7 %cholesky.149 = f32[128,128]{1,0:T(8,128)S(1)} custom-call(f32[128,128]{1,0:T(8,128)S(1)} %fusion.74), custom_call_target="Cholesky" | custom-call | tf_op jit(solution)/shard_map/jit(cholesky)/cholesky | solution.py:85
  95.5 9.8 %custom-call.22 = f32[1,128,128]{1,2,0:T(8,128)S(1)} custom-call(f32[1,128,128]{2,1,0:T(8,128)S(1)} %get-tuple-element.67), custom_call_target="InvertDiagBlocksLowerTriangular" | custom-call | tf_op jit(solution)/shard_map/jit(_solve_triangular)/triangular_solve | solution.py:86
  115.4 12.2 %cholesky.160 = f32[128,128]{1,0:T(8,128)S(1)} custom-call(f32[128,128]{1,0:T(8,128)S(1)} %fusion.72), custom_call_target="Cholesky" | custom-call | tf_op jit(solution)/shard_map/jit(cholesky)/cholesky | solution.py:85
  128.9 9.8 %custom-call.23 = f32[1,128,128]{1,2,0:T(8,128)S(1)} custom-call(f32[1,128,128]{2,1,0:T(8,128)S(1)} %get-tuple-element.65), custom_call_target="InvertDiagBlocksLowerTriangular" | custom-call | tf_op jit(solution)/shard_map/jit(_solve_triangular)/triangular_solve | solution.py:86
  144.9 11.7 %cholesky.171 = f32[128,128]{1,0:T(8,128)S(1)} custom-call(f32[128,128]{1,0:T(8,128)S(1)} %fusion.70), custom_call_target="Cholesky" | custom-call | tf_op jit(solution)/shard_map/jit(cholesky)/cholesky | solution.py:85
  157.8 10.0 %custom-call.24 = f32[1,128,128]{1,2,0:T(8,128)S(1)} custom-call(f32[1,128,128]{2,1,0:T(8,128)S(1)} %get-tuple-element.63), custom_call_target="InvertDiagBlocksLowerTriangular" | custom-call | tf_op jit(solution)/shard_map/jit(_solve_triangular)/triangular_solve | solution.py:86
  173.4 11.7 %cholesky.182 = f32[128,128]{1,0:T(8,128)S(1)} custom-call(f32[128,128]{1,0:T(8,128)S(1)} %fusion.68), custom_call_target="Cholesky" | custom-call | tf_op jit(solution)/shard_map/jit(cholesky)/cholesky | solution.py:85
  187.0 9.8 %custom-call.25 = f32[1,128,128]{1,2,0:T(8,128)S(1)} custom-call(f32[1,128,128]{2,1,0:T(8,128)S(1)} %get-tuple-element.61), custom_call_target="InvertDiagBlocksLowerTriangular" | custom-call | tf_op jit(solution)/shard_map/jit(_solve_triangular)/triangular_solve | solution.py:86
  199.5 12.1 %cholesky.193 = f32[128,128]{1,0:T(8,128)S(1)} custom-call(f32[128,128]{1,0:T(8,128)S(1)} %fusion.66), custom_call_target="Cholesky" | custom-call | tf_op jit(solution)/shard_map/jit(cholesky)/cholesky | solution.py:85
  212.8 9.8 %custom-call.26 = f32[1,128,128]{1,2,0:T(8,128)S(1)} custom-call(f32[1,128,128]{2,1,0:T(8,128)S(1)} %get-tuple-element.59), custom_call_target="InvertDiagBlocksLowerTriangular" | custom-call | tf_op jit(solution)/shard_map/jit(_solve_triangular)/triangular_solve | solution.py:86
  224.8 11.7 %cholesky.204 = f32[128,128]{1,0:T(8,128)S(1)} custom-call(f32[128,128]{1,0:T(8,128)S(1)} %fusion.64), custom_call_target="Cholesky" | custom-call | tf_op jit(solution)/shard_map/jit(cholesky)/cholesky | solution.py:85
  237.8 9.8 %custom-call.27 = f32[1,128,128]{1,2,0:T(8,128)S(1)} custom-call(f32[1,128,128]{2,1,0:T(8,128)S(1)} %get-tuple-element.57), custom_call_target="InvertDiagBlocksLowerTriangular" | custom-call | tf_op jit(solution)/shard_map/jit(_solve_triangular)/triangular_solve | solution.py:86
  249.6 11.7 %cholesky.215 = f32[128,128]{1,0:T(8,128)S(1)} custom-call(f32[128,128]{1,0:T(8,128)S(1)} %fusion.62), custom_call_target="Cholesky" | custom-call | tf_op jit(solution)/shard_map/jit(cholesky)/cholesky | solution.py:85
  262.5 9.8 %custom-call.28 = f32[1,128,128]{1,2,0:T(8,128)S(1)} custom-call(f32[1,128,128]{2,1,0:T(8,128)S(1)} %get-tuple-element.55), custom_call_target="InvertDiagBlocksLowerTriangular" | custom-call | tf_op jit(solution)/shard_map/jit(_solve_triangular)/triangular_solve | solution.py:86
  273.9 11.7 %cholesky.226 = f32[128,128]{1,0:T(8,128)S(1)} custom-call(f32[128,128]{1,0:T(8,128)S(1)} %fusion.60), custom_call_target="Cholesky" | custom-call | tf_op jit(solution)/shard_map/jit(cholesky)/cholesky | solution.py:85
  315.9 9.8 %custom-call.29 = f32[1,128,128]{1,2,0:T(8,128)S(1)} custom-call(f32[1,128,128]{2,1,0:T(8,128)S(1)} %get-tuple-element.53), custom_call_target="InvertDiagBlocksLowerTriangular" | custom-call | tf_op jit(solution)/shard_map/jit(_solve_triangular)/triangular_solve | solution.py:86
  350.5 9.1 %reshape.403 = f32[4,2,128,1536]{2,1,0,3:T(2,128)} reshape(f32[1024,1536]{0,1:T(8,128)} %all-gather.10.cloned.1.call-done) | data formatting | bytes 12582912 | tf_op jit(solution)/shard_map/reshape | solution.py:72
  359.7 10.3 %copy.176 = f32[4,2,128,1536]{3,2,0,1:T(8,128)} copy(f32[4,2,128,1536]{2,1,0,3:T(2,128)} %reshape.403) | data formatting | bytes 12582912 | tf_op jit(solution)/shard_map/reshape | solution.py:72
  374.6 47.5 %fusion = f32[1024,3072]{1,0:T(8,128)} fusion(f32[1024,1536]{1,0:T(8,128)S(1)} %bitcast.263, f32[1024,1536]{1,0:T(8,128)S(1)} %bitcast.262, f32[1,512,512]{2,1,0:T(8,128)} %get-tuple-element.72, f32[1,512,512]{2,1,0:T(8,128)} %get-tuple-element.71, f32[1,512,512]{2,1,0:T(8,128)} %fusion.18), kind=kOutput, calls=%fused_computation.12 | convolution fusion | flops 38662045696 | bytes 28311552 | tf_op jit(solution)/shard_map/dot_general | solution.py:137
  422.1 39.9 %subtract_select_fusion = f32[1536,1536]{1,0:T(8,128)S(1)} fusion(f32[1024,3072]{1,0:T(8,128)} %fusion, pred[1536]{0:T(1024)(128)(4,1)S(1)} %copy-done.17, pred[1536]{0:T(1024)(128)(4,1)S(1)} %copy-done.15, f32[1,1536,1536]{2,1,0:T(8,128)S(1)} %bitcast.274), kind=kOutput, calls=%fused_computation.17 | convolution fusion | flops 29001252864 | bytes 31465472 | tf_op jit(solution)/shard_map/dot_general | solution.py:147
  509.3 36.8 %collective-permute-done = f32[5,128,1280]{1,2,0:T(8,128)} collective-permute-done((f32[5,128,1280]{1,2,0:T(8,128)}, f32[5,128,1280]{1,2,0:T(8,128)}, u32[]{:S(2)}, u32[]{:S(2)}) %collective-permute-start) | collective-permute-done | bytes 3276832 | tf_op jit(solution)/shard_map/ppermute | solution.py:18
  570.4 8.1 copy.185
  578.6 12.9 %bitcast_add_fusion = f32[1024,2048]{1,0:T(8,128)S(1)} fusion(f32[128,8,16,128]{3,2,1,0:T(8,128)} %bitcast.254, f32[1024,2048]{1,0:T(8,128)} %param.16, f32[128,8,16,128]{3,2,1,0:T(8,128)S(1)} %bitcast.253), kind=kLoop, calls=%fused_computation.18 | loop fusion | flops 4194304 | bytes 33554432 | tf_op jit(solution)/shard_map/add | solution.py:240
  595.9 10.0 %gather_fusion.2 = f32[1536,1024]{1,0:T(8,128)} fusion(f32[1024,1024]{1,0:T(8,128)} %pad_dynamic-update-slice_fusion, s32[2048]{0:T(1024)S(1)} %pad_clamp_fusion), kind=kCustom, calls=%fused_computation.10 | custom fusion | bytes 12589056 | tf_op jit(solution)/shard_map/jit(_take)/gather | solution.py:153
  612.6 14.6 %all-reduce.9.cloned.1.call-done = f32[1024,128]{1,0:T(8,128)} async-done(((f32[1024,128]{1,0:T(8,128)}), f32[1024,128]{1,0:T(8,128)}) %all-reduce.9.cloned.1.call-update) | async-done | bytes 524304 | tf_op jit(solution)/shard_map/while/body/eval_jaxpr/psum | solution.py:14
  629.1 8.7 %select_select_fusion = f32[1536,1024]{0,1:T(8,128)} fusion(f32[1536,1024]{0,1:T(8,128)} %copy.178, f32[1024,3072]{1,0:T(8,128)} %fusion, pred[1536]{0:T(1024)(128)(4,1)S(1)} %copy-done.14, pred[1536]{0:T(1024)(128)(4,1)S(1)} %copy-done.15), kind=kLoop, calls=%fused_computation.24 | loop fusion | flops 3145728 | bytes 18877440 | tf_op jit(solution)/shard_map/jit(_where)/select_n | solution.py:154
  643.1 57.2 %all-reduce.11.cloned.1.call-done = f32[128,128]{1,0:T(8,128)} async-done(((f32[128,128]{1,0:T(8,128)}), f32[128,128]{1,0:T(8,128)}) %all-reduce.11.cloned.1.call-update) | async-done | bytes 65552 | tf_op jit(solution)/shard_map/while/body/eval_jaxpr/psum | solution.py:14
  702.1 11.7 %cholesky.237 = f32[128,128]{1,0:T(8,128)S(1)} custom-call(f32[128,128]{1,0:T(8,128)S(1)} %copy.187), custom_call_target="Cholesky" | custom-call | tf_op jit(solution)/shard_map/while/body/eval_jaxpr/jit(cholesky)/cholesky | solution.py:42
  715.9 9.8 %custom-call.10 = f32[1,128,128]{1,2,0:T(8,128)S(1)} custom-call(f32[1,128,128]{2,1,0:T(8,128)S(1)} %fusion.150), custom_call_target="InvertDiagBlocksLowerTriangular" | custom-call | tf_op jit(solution)/shard_map/while/body/eval_jaxpr/jit(_solve_triangular)/triangular_solve | solution.py:43
  738.1 68.7 %all-reduce.13.cloned.1.call-done = (f32[8,1,128,128]{3,2,1,0:T(8,128)}, f32[8,1,128,128]{3,2,1,0:T(8,128)}) async-done(((f32[8,1,128,128]{3,2,1,0:T(8,128)}, f32[8,1,128,128]{3,2,1,0:T(8,128)}), (f32[8,1,128,128]{3,2,1,0:T(8,128)}, f32[8,1,128,128]{3,2,1,0:T(8,128)})) %all-reduce.13.cloned.1.call-update) | async-done | bytes 1048592 | tf_op jit(solution)/shard_map/while/body/eval_jaxpr/psum | solution.py:14
  808.5 9.6 %convolution_subtract_fusion = f32[1024,2048]{1,0:T(8,128)S(1)} fusion(f32[1024,2048]{1,0:T(8,128)} %copy-done, f32[2048,128]{1,0:T(8,128)S(1)} %bitcast_select_fusion.2, f32[1024,128]{1,0:T(8,128)S(1)} %get-tuple-element.98, pred[1024]{0:T(1024)(128)(4,1)S(1)} %get-tuple-element.116), kind=kOutput, calls=%fused_computation.26 | convolution fusion | flops 3223453696 | bytes 18351104 | tf_op jit(solution)/shard_map/while/body/eval_jaxpr/dot_general | solution.py:49
  (286 shorter events, 248.6 us)
Async XLA Ops:
  7.2 54.4 %all-gather.8.cloned.1.call-start = ((), (), s32[]{:S(2)}) async-start(), calls=%async_computation.3 | async-start | bytes 4456448 | tf_op jit(solution)/shard_map/all_gather | solution.py:122
  8.9 7.3 copy-start.26
  8.9 341.6 %all-gather.10.cloned.1.call-start = ((), (), s32[]{:S(2)}) async-start(), calls=%async_computation.4 | async-start | bytes 7864320 | tf_op jit(solution)/shard_map/all_gather | solution.py:132
  11.7 358.3 %all-gather.6.cloned.1.call-start = ((), (), s32[]{:S(2)}) async-start(), calls=%async_computation | async-start | bytes 7864320 | tf_op jit(solution)/shard_map/all_gather | solution.py:134
  14.4 612.8 %all-reduce.9.cloned.1.call-start = ((), (), s32[]{:S(2)}) async-start(), calls=%async_computation.1 | async-start | bytes 1048576 | tf_op jit(solution)/shard_map/while/body/eval_jaxpr/psum | solution.py:14
  19.0 48.4 %copy-start.18 = (s32[16]{0:T(128)}, s32[16]{0:T(128)S(1)}, u32[]{:S(2)}) copy-start(s32[16]{0:T(128)S(1)} %select_reduce_fusion.9) | copy-start | bytes 196
  19.8 47.6 %copy-start.20 = (s32[16]{0:T(128)}, s32[16]{0:T(128)S(1)}, u32[]{:S(2)}) copy-start(s32[16]{0:T(128)S(1)} %select_reduce_fusion.10) | copy-start | bytes 196
  22.4 44.9 %copy-start.30 = (s32[8]{0:T(128)}, s32[8]{0:T(128)S(1)}, u32[]{:S(2)}) copy-start(s32[8]{0:T(128)S(1)} %select_reduce_fusion.11) | copy-start | bytes 100
  199.3 88.9 %copy-start.8 = (f32[768,128]{1,0:T(8,128)S(1)}, f32[768,128]{1,0:T(8,128)}, u32[]{:S(2)}) copy-start(f32[768,128]{1,0:T(8,128)} %copy-done.7) | copy-start | bytes 1179652
  224.7 66.2 %copy-start.10 = (f32[128,128]{1,0:T(8,128)S(1)}, f32[128,128]{1,0:T(8,128)}, u32[]{:S(2)}) copy-start(f32[128,128]{1,0:T(8,128)} %get-tuple-element.62) | copy-start | bytes 196612
  224.7 66.1 %copy-start.11 = (f32[1024]{0:T(1024)S(1)}, f32[1024]{0:T(1024)}, u32[]{:S(2)}) copy-start(f32[1024]{0:T(1024)} %pad.29.clone) | copy-start | bytes 12292
  333.1 8.3 %copy-start.9 = (f32[8,128,128]{2,1,0:T(8,128)S(1)}, f32[8,128,128]{2,1,0:T(8,128)}, u32[]{:S(2)}) copy-start(f32[8,128,128]{2,1,0:T(8,128)} %get-tuple-element.96) | copy-start | bytes 1572868
  370.0 52.1 %slice-start.3 = ((s8[9437184]{0:T(1024)(128)(4,1)}), s8[4194304]{0:T(1024)(128)(4,1)S(1)}, s32[]{:S(2)}) async-start(s8[9437184]{0:T(1024)(128)(4,1)} %bitcast.273), calls=%async_computation.9 | async-start | bytes 8388608
  374.6 47.5 %slice-start.4 = ((s8[9437184]{0:T(1024)(128)(4,1)}), s8[4194304]{0:T(1024)(128)(4,1)S(1)}, s32[]{:S(2)}) async-start(s8[9437184]{0:T(1024)(128)(4,1)} %bitcast.273), calls=%async_computation.10 | async-start | bytes 8388608
  374.6 47.5 %slice-start.5 = ((s8[9437184]{0:T(1024)(128)(4,1)}), s8[1048576]{0:T(1024)(128)(4,1)S(1)}, s32[]{:S(2)}) async-start(s8[9437184]{0:T(1024)(128)(4,1)} %bitcast.273), calls=%async_computation.11 | async-start | bytes 2097152
  374.6 47.5 %copy-start.15 = (pred[1536]{0:T(1024)(128)(4,1)S(1)}, pred[1536]{0:T(1024)(128)(4,1)}, u32[]{:S(2)}) copy-start(pred[1536]{0:T(1024)(128)(4,1)} %get-tuple-element.105) | copy-start | bytes 4612
  374.6 47.5 %copy-start.17 = (pred[1536]{0:T(1024)(128)(4,1)S(1)}, pred[1536]{0:T(1024)(128)(4,1)}, u32[]{:S(2)}) copy-start(pred[1536]{0:T(1024)(128)(4,1)} %get-tuple-element.106) | copy-start | bytes 4612
  468.1 6.0 copy-start.23
  468.1 6.0 copy-start.25
  468.1 6.2 copy-start.29
  468.1 6.3 copy-start.31
  468.1 6.3 copy-start.19
  468.1 6.3 copy-start.21
  468.1 6.3 copy-start.28
  468.2 6.4 copy-start.27
  472.7 73.4 %collective-permute-start = (f32[5,128,1280]{1,2,0:T(8,128)}, f32[5,128,1280]{1,2,0:T(8,128)}, u32[]{:S(2)}, u32[]{:S(2)}) collective-permute-start(f32[5,128,1280]{1,2,0:T(8,128)} %bitcast.264), channel_id=1, source_target_pairs={{0,16},{16,0},{1,17},{17,1},{2,18},{18,2},{3,19},{19,3},{4,20},{20... | collective-permute-start | bytes 9830408 | tf_op jit(solution)/shard_map/ppermute | solution.py:18
  566.1 12.5 %slice-start = ((s8[8388608]{0:T(1024)(128)(4,1)}), s8[4194304]{0:T(1024)(128)(4,1)S(1)}, s32[]{:S(2)}) async-start(s8[8388608]{0:T(1024)(128)(4,1)} %bitcast.251), calls=%async_computation.6 | async-start | bytes 8388608
  570.4 8.1 slice-start.1
  595.8 104.5 %all-reduce.11.cloned.1.call-start = ((), (), s32[]{:S(2)}) async-start(), calls=%async_computation.2 | async-start | bytes 131072 | tf_op jit(solution)/shard_map/while/body/eval_jaxpr/psum | solution.py:14
  606.0 23.2 %copy-start.14 = (pred[1536]{0:T(1024)(128)(4,1)S(1)}, pred[1536]{0:T(1024)(128)(4,1)}, u32[]{:S(2)}) copy-start(pred[1536]{0:T(1024)(128)(4,1)} %compare_and_fusion) | copy-start | bytes 4612
  628.7 178.2 %all-reduce.13.cloned.1.call-start = ((), (), s32[]{:S(2)}) async-start(), calls=%async_computation.5 | async-start | bytes 2097152 | tf_op jit(solution)/shard_map/while/body/eval_jaxpr/psum | solution.py:14
  733.2 74.9 %copy-start.13 = (pred[2048]{0:T(1024)(128)(4,1)S(1)}, pred[2048]{0:T(1024)(128)(4,1)}, u32[]{:S(2)}) copy-start(pred[2048]{0:T(1024)(128)(4,1)} %fusion.84) | copy-start | bytes 6148
  (13 other events, 37.5 us)
Sparse Core Ops, SparseCore 0:
  10.7 50.8 all-gather.7
  63.2 44.6 all-gather.9
  109.4 116.5 all-gather.5
  595.9 31.2 all-reduce.8
  630.4 69.7 all-reduce.10
  728.4 78.3 all-reduce.12

commit v6 on v5

--- a/solution.py
+++ b/solution.py
@@ -16,55 +16,6 @@
 
 def from_partner(shard, axis, distance):
     return lax.ppermute(shard, axis, [(i, i ^ 1 << distance) for i in range(lax.axis_size(axis))])
-
-
-def factor_front(
-    front_work,
-    pivot_count,
-    row_groups,
-    col_groups,
-    my_row,
-    my_col,
-    fetch_panel,
-    fetch_diag,
-    fetch_across,
-):
-    row_count, col_count = front_work.shape
-    row_tiles = jnp.arange(row_count, dtype=jnp.int32) // TILE * row_groups + my_row
-    col_tiles = jnp.arange(col_count, dtype=jnp.int32) // TILE * col_groups + my_col
-
-    def one_step(pivot_tile, current):
-        row_slot = pivot_tile // row_groups
-        col_slot = pivot_tile // col_groups
-        column = lax.dynamic_slice_in_dim(current, col_slot * TILE, TILE, 1)
-        col_panel = fetch_panel(column, pivot_tile)
-        diag_block = fetch_diag(current, col_panel, pivot_tile, row_slot, col_slot)
-        diag_factor = jnp.linalg.cholesky(diag_block)
-        solved_panel = jax.scipy.linalg.solve_triangular(diag_factor, col_panel.T, lower=True).T
-        across_panel = fetch_across(solved_panel)
-        rows_after = (row_tiles > pivot_tile)[:, None]
-        cols_after = (col_tiles > pivot_tile)[:, None]
-        left_factor = jnp.where(rows_after, solved_panel, 0.0)
-        right_factor = jnp.where(cols_after, across_panel, 0.0)
-        current = current - jnp.dot(
-            left_factor,
-            right_factor.T,
-            precision=lax.Precision.HIGHEST,
-            preferred_element_type=jnp.float32,
-        )
-        pivot_rows = lax.dynamic_slice_in_dim(current, row_slot * TILE, TILE, 0)
-        row_owner = my_row == pivot_tile % row_groups
-        pivot_rows = jnp.where(row_owner & (col_tiles > pivot_tile)[None, :], 0.0, pivot_rows)
-        current = lax.dynamic_update_slice_in_dim(current, pivot_rows, row_slot * TILE, 0)
-        diag_rows = jnp.tile(jnp.tril(diag_factor), (row_count // TILE, 1))
-        new_column = jnp.where(
-            rows_after, solved_panel, jnp.where((row_tiles == pivot_tile)[:, None], diag_rows, 0.0)
-        )
-        old_column = lax.dynamic_slice_in_dim(current, col_slot * TILE, TILE, 1)
-        new_column = jnp.where(my_col == pivot_tile % col_groups, new_column, old_column)
-        return lax.dynamic_update_slice_in_dim(current, new_column, col_slot * TILE, 1)
-
-    return lax.fori_loop(0, pivot_count // TILE, one_step, front_work)
 
 
 def pivot_order(pieces, slot_count, tile_count):
@@ -240,6 +191,51 @@
     return parent_own + kept_part + got_part
 
 
+def factor_parent(front_work, grid_size, half_index, my_row, my_col):
+    row_groups = 2 * grid_size
+    parent_row = half_index * grid_size + my_row
+    row_count, col_count = front_work.shape
+    column = spread(front_work[:, :TILE], "col", 0)
+    halves = lax.all_gather(column, "half", axis=0)
+    halves = halves.reshape(2, row_count // TILE, TILE, TILE)
+    my_row_cols = jnp.swapaxes(halves, 0, 1).reshape(col_count, TILE)
+    pairs = [
+        (col * grid_size + row, row * grid_size + col)
+        for row in range(grid_size)
+        for col in range(grid_size)
+    ]
+    my_cols = lax.ppermute(my_row_cols, ("row", "col"), pairs)
+    diag_block = spread(my_cols[:TILE], "col", 0)
+    diag_factor = jnp.tril(jnp.linalg.cholesky(diag_block))
+    eye = jnp.eye(TILE, dtype=jnp.float32)
+    inverse = jnp.tril(jax.scipy.linalg.solve_triangular(diag_factor, eye, lower=True))
+    solved_rows = jnp.dot(column, inverse.T, precision=lax.Precision.HIGHEST)
+    solved_cols = jnp.dot(my_cols, inverse.T, precision=lax.Precision.HIGHEST)
+    row_within = jnp.arange(row_count, dtype=jnp.int32)
+    col_within = jnp.arange(col_count, dtype=jnp.int32)
+    row_index = row_within // TILE * row_groups * TILE + parent_row * TILE + row_within % TILE
+    col_index = col_within // TILE * grid_size * TILE + my_col * TILE + col_within % TILE
+    return finish_front(front_work, solved_rows, solved_cols, diag_factor, row_index, col_index, TILE)
+
+
+def finish_front(front_work, solved_rows, solved_cols, diag_factor, row_index, col_index, pivot_count):
+    width = TILE * (-(-pivot_count // TILE))
+    rows_after = (row_index >= pivot_count)[:, None]
+    cols_after = (col_index >= pivot_count)[None, :]
+    update = jnp.dot(
+        jnp.where(rows_after, solved_rows, 0.0),
+        jnp.where(cols_after.T, solved_cols, 0.0).T,
+        precision=lax.Precision.HIGHEST,
+        preferred_element_type=jnp.float32,
+    )
+    diag_rows = jnp.take(diag_factor, jnp.minimum(row_index, pivot_count - 1), axis=0)
+    full_rows = jnp.where(rows_after, solved_rows, diag_rows)
+    pivot_cols = jnp.take(full_rows, jnp.minimum(col_index[:width], pivot_count - 1), axis=1)
+    trailing = jnp.where(rows_after & cols_after, front_work - update, 0.0)
+    head = jnp.where(cols_after[:, :width], trailing[:, :width], pivot_cols)
+    return jnp.concatenate([head, trailing[:, width:]], axis=1)
+
+
 def local(child_fronts, child_maps, parent_own):
     grid_size = lax.axis_size("row")
     half_index = lax.axis_index("half")
@@ -261,40 +257,7 @@
             child_done, child_maps, parent_own, grid_size, half_index, my_row, my_col
         )
 
-    def send_parent_column(column, pivot_tile):
-        return spread(column, "col", pivot_tile % grid_size)
-
-    def send_parent_block(current, col_panel, pivot_tile, row_slot, col_slot):
-        own_block = lax.dynamic_slice_in_dim(col_panel, row_slot * TILE, TILE, 0)
-        result_block = spread(own_block, ("half", "row"), pivot_tile % (2 * grid_size))
-        return result_block
-
-    def send_parent_rows(solved_panel):
-        pieces = [
-            spread(solved_panel, ("half", "row"), which_half * grid_size + my_col)
-            for which_half in range(2)
-        ]
-        even_tiles = pieces[0]
-        odd_tiles = pieces[1]
-        tile_count = solved_panel.shape[0] // TILE
-        stacked = jnp.stack(
-            [even_tiles.reshape(tile_count, TILE, TILE), odd_tiles.reshape(tile_count, TILE, TILE)],
-            axis=1,
-        )
-        return stacked.reshape(2 * tile_count * TILE, TILE)
-
-    parent_row = half_index * grid_size + my_row
-    parent_done = factor_front(
-        parent_start,
-        PARENT_PIVOTS,
-        2 * grid_size,
-        grid_size,
-        parent_row,
-        my_col,
-        send_parent_column,
-        send_parent_block,
-        send_parent_rows,
-    )
+    parent_done = factor_parent(parent_start, grid_size, half_index, my_row, my_col)
     return (child_done[None], parent_done)
 
 

time: 835 us -> 798 us (0.956)
  waiting for transfers between devices: 214 us -> 154 us
    psum x3 -> x2, waiting for transfers between devices: 141 us -> 50.8 us  [spread(): return lax.psum(jnp.where(mine, shard, jnp.zeros_like(shard)), axis)]
    ppermute x0 -> x1, waiting for transfers between devices: none -> 24.7 us  [factor_parent(): my_cols = lax.ppermute(my_row_cols, ('row', 'col'), pairs)]
    another operation x7 -> x5, other arithmetic: 24.8 us -> 23 us  [the longest x3 12.5 us: factor_parent(): diag_factor = jnp.tril(jnp.linalg.cholesky(diag_block))]
  transfers between devices with their start and end apart: 7 -> 8, of which waited for: 5 -> 6; matrix products, arithmetic and copies ran while one was open for 47% -> 51% of each run, Pallas kernels for 0% -> 0%
where the time goes in v6:
time: 798 us; the launch traced here: 790 us
  other arithmetic  286 us (36%)
  local copies, waits for them, and re-layouts  196 us (25%)
  waiting for transfers between devices  154 us (19%)
  matrix products  132 us (17%)
  between operations  15.4 us (2%)
    another operation x24, other arithmetic, factor_pivots(): factor = jnp.tril(jnp.linalg.cholesky(work[:TILE, :TILE]))  100 us
    another operation x16, other arithmetic, factor_pivots(): jax.scipy.linalg.solve_triangular(factor, eye, lower=True)  84.4 us
    psum x2, waiting for transfers between devices, spread(): return lax.psum(jnp.where(mine, shard, jnp.zeros_like(shard)), axis)  50.8 us
    dot_general x1, matrix products, factor_child(): jnp.dot(diag_inverse, both, precision=lax.Precision.HIGHEST, preferred_el...  47.5 us
    dot_general x1, matrix products, factor_child(): jnp.dot(jnp.where(rows_after, solved_rows, 0.0), jnp.where(cols_after.T,...  39.9 us
    ppermute x1, waiting for transfers between devices, from_partner(): lax.ppermute(shard, axis, [(i, i ^ 1 << distance) for i in range(lax.axis...  36.6 us
    all_gather x1, waiting for transfers between devices, factor_child(): lax.all_gather(front_work[:width, :width], ('row', 'col'), axis=0)  35.1 us
    reshape x5, local copies, waits for them, and re-layouts, lower_inverse(): factor.reshape(pairs, 2, size, pairs, 2, size)[picks, 1, :, picks, 0, :]  27.9 us
  transfers between devices with their start and end apart: 8, of which 6 were waited for; matrix products, arithmetic and copies ran while one was open for 51% of the time, Pallas kernels for 0%

profile of v6, /device:TPU:4, one launch (start us, length us, event | category | flops | bytes accessed | tf_op | source)
XLA Modules:
  0.0 789.9 jit_solution(5219011667658811127)
XLA Ops:
  26.5 35.1 %all-gather.10.cloned.1.call-done = f32[4096,256]{1,0:T(8,128)} async-done(((f32[256,256]{1,0:T(8,128)}), f32[4096,256]{1,0:T(8,128)}) %all-gather.10.cloned.1.call-update) | async-done | bytes 4194320 | tf_op jit(solution)/shard_map/all_gather | solution.py:73
  82.4 11.7 %cholesky.149 = f32[128,128]{1,0:T(8,128)S(1)} custom-call(f32[128,128]{1,0:T(8,128)S(1)} %fusion.71), custom_call_target="Cholesky" | custom-call | tf_op jit(solution)/shard_map/jit(cholesky)/cholesky | solution.py:36
  95.5 9.8 %custom-call.17 = f32[1,128,128]{1,2,0:T(8,128)S(1)} custom-call(f32[1,128,128]{2,1,0:T(8,128)S(1)} %get-tuple-element.48), custom_call_target="InvertDiagBlocksLowerTriangular" | custom-call | tf_op jit(solution)/shard_map/jit(_solve_triangular)/triangular_solve | solution.py:37
  115.3 12.2 %cholesky.160 = f32[128,128]{1,0:T(8,128)S(1)} custom-call(f32[128,128]{1,0:T(8,128)S(1)} %fusion.69), custom_call_target="Cholesky" | custom-call | tf_op jit(solution)/shard_map/jit(cholesky)/cholesky | solution.py:36
  128.9 9.8 %custom-call.18 = f32[1,128,128]{1,2,0:T(8,128)S(1)} custom-call(f32[1,128,128]{2,1,0:T(8,128)S(1)} %get-tuple-element.46), custom_call_target="InvertDiagBlocksLowerTriangular" | custom-call | tf_op jit(solution)/shard_map/jit(_solve_triangular)/triangular_solve | solution.py:37
  144.8 11.7 %cholesky.171 = f32[128,128]{1,0:T(8,128)S(1)} custom-call(f32[128,128]{1,0:T(8,128)S(1)} %fusion.67), custom_call_target="Cholesky" | custom-call | tf_op jit(solution)/shard_map/jit(cholesky)/cholesky | solution.py:36
  157.9 10.0 %custom-call.19 = f32[1,128,128]{1,2,0:T(8,128)S(1)} custom-call(f32[1,128,128]{2,1,0:T(8,128)S(1)} %get-tuple-element.44), custom_call_target="InvertDiagBlocksLowerTriangular" | custom-call | tf_op jit(solution)/shard_map/jit(_solve_triangular)/triangular_solve | solution.py:37
  173.5 11.7 %cholesky.182 = f32[128,128]{1,0:T(8,128)S(1)} custom-call(f32[128,128]{1,0:T(8,128)S(1)} %fusion.65), custom_call_target="Cholesky" | custom-call | tf_op jit(solution)/shard_map/jit(cholesky)/cholesky | solution.py:36
  187.2 9.8 %custom-call.20 = f32[1,128,128]{1,2,0:T(8,128)S(1)} custom-call(f32[1,128,128]{2,1,0:T(8,128)S(1)} %get-tuple-element.42), custom_call_target="InvertDiagBlocksLowerTriangular" | custom-call | tf_op jit(solution)/shard_map/jit(_solve_triangular)/triangular_solve | solution.py:37
  199.7 12.1 %cholesky.193 = f32[128,128]{1,0:T(8,128)S(1)} custom-call(f32[128,128]{1,0:T(8,128)S(1)} %fusion.63), custom_call_target="Cholesky" | custom-call | tf_op jit(solution)/shard_map/jit(cholesky)/cholesky | solution.py:36
  213.2 9.8 %custom-call.21 = f32[1,128,128]{1,2,0:T(8,128)S(1)} custom-call(f32[1,128,128]{2,1,0:T(8,128)S(1)} %get-tuple-element.40), custom_call_target="InvertDiagBlocksLowerTriangular" | custom-call | tf_op jit(solution)/shard_map/jit(_solve_triangular)/triangular_solve | solution.py:37
  225.2 11.7 %cholesky.204 = f32[128,128]{1,0:T(8,128)S(1)} custom-call(f32[128,128]{1,0:T(8,128)S(1)} %fusion.61), custom_call_target="Cholesky" | custom-call | tf_op jit(solution)/shard_map/jit(cholesky)/cholesky | solution.py:36
  238.3 9.8 %custom-call.22 = f32[1,128,128]{1,2,0:T(8,128)S(1)} custom-call(f32[1,128,128]{2,1,0:T(8,128)S(1)} %get-tuple-element.38), custom_call_target="InvertDiagBlocksLowerTriangular" | custom-call | tf_op jit(solution)/shard_map/jit(_solve_triangular)/triangular_solve | solution.py:37
  250.1 11.7 %cholesky.215 = f32[128,128]{1,0:T(8,128)S(1)} custom-call(f32[128,128]{1,0:T(8,128)S(1)} %fusion.59), custom_call_target="Cholesky" | custom-call | tf_op jit(solution)/shard_map/jit(cholesky)/cholesky | solution.py:36
  263.2 9.8 %custom-call.23 = f32[1,128,128]{1,2,0:T(8,128)S(1)} custom-call(f32[1,128,128]{2,1,0:T(8,128)S(1)} %get-tuple-element.36), custom_call_target="InvertDiagBlocksLowerTriangular" | custom-call | tf_op jit(solution)/shard_map/jit(_solve_triangular)/triangular_solve | solution.py:37
  274.6 11.7 %cholesky.226 = f32[128,128]{1,0:T(8,128)S(1)} custom-call(f32[128,128]{1,0:T(8,128)S(1)} %fusion.57), custom_call_target="Cholesky" | custom-call | tf_op jit(solution)/shard_map/jit(cholesky)/cholesky | solution.py:36
  316.6 9.8 %custom-call.24 = f32[1,128,128]{1,2,0:T(8,128)S(1)} custom-call(f32[1,128,128]{2,1,0:T(8,128)S(1)} %get-tuple-element.34), custom_call_target="InvertDiagBlocksLowerTriangular" | custom-call | tf_op jit(solution)/shard_map/jit(_solve_triangular)/triangular_solve | solution.py:37
  351.2 9.1 %reshape.504 = f32[4,2,128,1536]{2,1,0,3:T(2,128)} reshape(f32[1024,1536]{0,1:T(8,128)} %all-gather.12.cloned.1.call-done) | data formatting | bytes 12582912 | tf_op jit(solution)/shard_map/reshape | solution.py:23
  360.4 10.3 %copy.182 = f32[4,2,128,1536]{3,2,0,1:T(8,128)} copy(f32[4,2,128,1536]{2,1,0,3:T(2,128)} %reshape.504) | data formatting | bytes 12582912 | tf_op jit(solution)/shard_map/reshape | solution.py:23
  375.3 47.5 %fusion = f32[1024,3072]{1,0:T(8,128)} fusion(f32[1024,1536]{1,0:T(8,128)S(1)} %bitcast.261, f32[1024,1536]{1,0:T(8,128)S(1)} %bitcast.260, f32[1,512,512]{2,1,0:T(8,128)} %get-tuple-element.53, f32[1,512,512]{2,1,0:T(8,128)} %get-tuple-element.52, f32[1,512,512]{2,1,0:T(8,128)} %fusion.18), kind=kOutput, calls=%fused_computation.14 | convolution fusion | flops 38662045696 | bytes 28311552 | tf_op jit(solution)/shard_map/dot_general | solution.py:88
  422.8 39.9 %subtract_select_fusion = f32[1536,1536]{1,0:T(8,128)S(1)} fusion(f32[1024,3072]{1,0:T(8,128)} %fusion, pred[1536]{0:T(1024)(128)(4,1)S(1)} %copy-done.18, pred[1536]{0:T(1024)(128)(4,1)S(1)} %copy-done.15, f32[1,1536,1536]{2,1,0:T(8,128)S(1)} %bitcast.270), kind=kOutput, calls=%fused_computation.19 | convolution fusion | flops 29001252864 | bytes 31465472 | tf_op jit(solution)/shard_map/dot_general | solution.py:98
  510.2 36.6 %collective-permute-done = f32[5,128,1280]{1,2,0:T(8,128)} collective-permute-done((f32[5,128,1280]{1,2,0:T(8,128)}, f32[5,128,1280]{1,2,0:T(8,128)}, u32[]{:S(2)}, u32[]{:S(2)}) %collective-permute-start) | collective-permute-done | bytes 3276832 | tf_op jit(solution)/shard_map/ppermute | solution.py:18
  571.1 8.1 %copy.191 = f32[8,128,16,128]{3,2,1,0:T(8,128)} copy(f32[8,128,16,128]{3,1,0,2:T(8,128)S(1)} %bitcast_select_fusion) | data formatting | bytes 16777216 | tf_op jit(solution)/shard_map/jit(_where)/select_n | solution.py:172
  579.3 12.9 %bitcast_add_fusion = f32[1024,2048]{1,0:T(8,128)S(1)} fusion(f32[128,8,16,128]{3,2,1,0:T(8,128)} %bitcast.252, f32[1024,2048]{1,0:T(8,128)} %param.16, f32[128,8,16,128]{3,2,1,0:T(8,128)S(1)} %bitcast.251), kind=kLoop, calls=%fused_computation.20 | loop fusion | flops 4194304 | bytes 33554432 | tf_op jit(solution)/shard_map/add | solution.py:191
  596.5 31.3 %all-reduce.7.cloned.1.call-done = f32[1024,128]{1,0:T(8,128)} async-done(((f32[1024,128]{1,0:T(8,128)}), f32[1024,128]{1,0:T(8,128)}) %all-reduce.7.cloned.1.call-update) | async-done | bytes 524304 | tf_op jit(solution)/shard_map/psum | solution.py:14
  628.0 10.0 %gather_fusion.2 = f32[1536,1024]{1,0:T(8,128)} fusion(f32[1024,1024]{1,0:T(8,128)} %pad_dynamic-update-slice_fusion, s32[2048]{0:T(1024)S(1)} %pad_clamp_fusion), kind=kCustom, calls=%fused_computation.10 | custom fusion | bytes 12589056 | tf_op jit(solution)/shard_map/jit(_take)/gather | solution.py:104
  658.9 8.7 %select_select_fusion = f32[1536,1024]{0,1:T(8,128)} fusion(f32[1536,1024]{0,1:T(8,128)} %copy.184, f32[1024,3072]{1,0:T(8,128)} %fusion, pred[1536]{0:T(1024)(128)(4,1)S(1)} %copy-done.14, pred[1536]{0:T(1024)(128)(4,1)S(1)} %copy-done.15), kind=kLoop, calls=%fused_computation.28 | loop fusion | flops 3145728 | bytes 18877440 | tf_op jit(solution)/shard_map/jit(_where)/select_n | solution.py:105
  681.5 24.7 %collective-permute-done.1 = f32[2048,128]{1,0:T(8,128)} collective-permute-done((f32[2048,128]{1,0:T(8,128)}, f32[2048,128]{1,0:T(8,128)}, u32[]{:S(2)}, u32[]{:S(2)}) %collective-permute-start.1) | collective-permute-done | bytes 1048608 | tf_op jit(solution)/shard_map/ppermute | solution.py:207
  715.6 19.5 %all-reduce.9.cloned.1.call-done = f32[128,128]{1,0:T(8,128)} async-done(((f32[128,128]{1,0:T(8,128)}), f32[128,128]{1,0:T(8,128)}) %all-reduce.9.cloned.1.call-update) | async-done | bytes 65552 | tf_op jit(solution)/shard_map/psum | solution.py:14
  737.0 11.7 %cholesky.237 = f32[128,128]{1,0:T(8,128)S(1)} custom-call(f32[128,128]{1,0:T(8,128)S(1)} %copy.194), custom_call_target="Cholesky" | custom-call | tf_op jit(solution)/shard_map/jit(cholesky)/cholesky | solution.py:209
  750.2 9.8 %custom-call.25 = f32[1,128,128]{1,2,0:T(8,128)S(1)} custom-call(f32[1,128,128]{2,1,0:T(8,128)S(1)} %get-tuple-element.30), custom_call_target="InvertDiagBlocksLowerTriangular" | custom-call | tf_op jit(solution)/shard_map/jit(_solve_triangular)/triangular_solve | solution.py:211
  767.8 9.8 %subtract_select_fusion.1 = f32[1024,2048]{1,0:T(8,128)S(1)} fusion(f32[1024,2048]{1,0:T(8,128)} %copy-done, f32[2048,128]{1,0:T(8,128)S(1)} %convolution_select_fusion, pred[2048]{0:T(1024)(128)(4,1)S(1)} %broadcast_compare_fusion, pred[1024]{0:T(1024)(128)(4,1)S(1)} %broadcast_compare_fusion.4, f32[1024,128]{1,0:T(8,128)S(1)} %get-tuple-element.77), kind=kOutput, calls=%fused_computation.25 | convolution fusion | flops 3227648000 | bytes 18353152 | tf_op jit(solution)/shard_map/dot_general | solution.py:225
  (298 shorter events, 276.2 us)
Async XLA Ops:
  7.2 54.4 %all-gather.10.cloned.1.call-start = ((), (), s32[]{:S(2)}) async-start(), calls=%async_computation.3 | async-start | bytes 4456448 | tf_op jit(solution)/shard_map/all_gather | solution.py:73
  8.9 6.7 copy-start.26
  8.9 342.3 %all-gather.12.cloned.1.call-start = ((), (), s32[]{:S(2)}) async-start(), calls=%async_computation.4 | async-start | bytes 7864320 | tf_op jit(solution)/shard_map/all_gather | solution.py:83
  11.7 359.0 %all-gather.8.cloned.1.call-start = ((), (), s32[]{:S(2)}) async-start(), calls=%async_computation | async-start | bytes 7864320 | tf_op jit(solution)/shard_map/all_gather | solution.py:85
  14.4 613.4 %all-reduce.7.cloned.1.call-start = ((), (), s32[]{:S(2)}) async-start(), calls=%async_computation.1 | async-start | bytes 1048576 | tf_op jit(solution)/shard_map/psum | solution.py:14
  18.4 49.0 %copy-start.19 = (s32[16]{0:T(128)}, s32[16]{0:T(128)S(1)}, u32[]{:S(2)}) copy-start(s32[16]{0:T(128)S(1)} %select_reduce_fusion.9) | copy-start | bytes 196
  19.2 48.2 %copy-start.21 = (s32[16]{0:T(128)}, s32[16]{0:T(128)S(1)}, u32[]{:S(2)}) copy-start(s32[16]{0:T(128)S(1)} %select_reduce_fusion.10) | copy-start | bytes 196
  199.6 89.4 %copy-start.7 = (f32[768,128]{1,0:T(8,128)S(1)}, f32[768,128]{1,0:T(8,128)}, u32[]{:S(2)}) copy-start(f32[768,128]{1,0:T(8,128)} %copy-done.6) | copy-start | bytes 1179652
  225.0 66.5 %copy-start.10 = (f32[128,128]{1,0:T(8,128)S(1)}, f32[128,128]{1,0:T(8,128)}, u32[]{:S(2)}) copy-start(f32[128,128]{1,0:T(8,128)} %get-tuple-element.43) | copy-start | bytes 196612
  225.0 66.5 %copy-start.11 = (f32[1024]{0:T(1024)S(1)}, f32[1024]{0:T(1024)}, u32[]{:S(2)}) copy-start(f32[1024]{0:T(1024)} %pad.29.clone) | copy-start | bytes 12292
  333.8 8.3 %copy-start.8 = (f32[8,128,128]{2,1,0:T(8,128)S(1)}, f32[8,128,128]{2,1,0:T(8,128)}, u32[]{:S(2)}) copy-start(f32[8,128,128]{2,1,0:T(8,128)} %get-tuple-element.74) | copy-start | bytes 1572868
  370.7 52.1 %slice-start.2 = ((s8[9437184]{0:T(1024)(128)(4,1)}), s8[4194304]{0:T(1024)(128)(4,1)S(1)}, s32[]{:S(2)}) async-start(s8[9437184]{0:T(1024)(128)(4,1)} %bitcast.269), calls=%async_computation.8 | async-start | bytes 8388608
  375.3 47.5 %slice-start.3 = ((s8[9437184]{0:T(1024)(128)(4,1)}), s8[4194304]{0:T(1024)(128)(4,1)S(1)}, s32[]{:S(2)}) async-start(s8[9437184]{0:T(1024)(128)(4,1)} %bitcast.269), calls=%async_computation.9 | async-start | bytes 8388608
  375.3 47.5 %slice-start.4 = ((s8[9437184]{0:T(1024)(128)(4,1)}), s8[1048576]{0:T(1024)(128)(4,1)S(1)}, s32[]{:S(2)}) async-start(s8[9437184]{0:T(1024)(128)(4,1)} %bitcast.269), calls=%async_computation.10 | async-start | bytes 2097152
  375.3 47.5 %copy-start.15 = (pred[1536]{0:T(1024)(128)(4,1)S(1)}, pred[1536]{0:T(1024)(128)(4,1)}, u32[]{:S(2)}) copy-start(pred[1536]{0:T(1024)(128)(4,1)} %get-tuple-element.85) | copy-start | bytes 4612
  375.3 47.5 %copy-start.18 = (pred[1536]{0:T(1024)(128)(4,1)S(1)}, pred[1536]{0:T(1024)(128)(4,1)}, u32[]{:S(2)}) copy-start(pred[1536]{0:T(1024)(128)(4,1)} %broadcast_compare_fusion.2) | copy-start | bytes 4612
  468.8 6.1 copy-start.23
  468.8 6.2 copy-start.25
  468.8 6.4 copy-start.30
  468.8 6.4 copy-start.20
  468.8 6.4 copy-start.22
  468.8 6.5 copy-start.28
  468.9 6.5 copy-start.27
  473.4 73.4 %collective-permute-start = (f32[5,128,1280]{1,2,0:T(8,128)}, f32[5,128,1280]{1,2,0:T(8,128)}, u32[]{:S(2)}, u32[]{:S(2)}) collective-permute-start(f32[5,128,1280]{1,2,0:T(8,128)} %bitcast.262), channel_id=1, source_target_pairs={{0,16},{16,0},{1,17},{17,1},{2,18},{18,2},{3,19},{19,3},{4,20},{20... | collective-permute-start | bytes 9830408 | tf_op jit(solution)/shard_map/ppermute | solution.py:18
  566.7 12.5 %slice-start = ((s8[8388608]{0:T(1024)(128)(4,1)}), s8[4194304]{0:T(1024)(128)(4,1)S(1)}, s32[]{:S(2)}) async-start(s8[8388608]{0:T(1024)(128)(4,1)} %bitcast.249), calls=%async_computation.6 | async-start | bytes 8388608
  571.1 8.1 %slice-start.1 = ((s8[8388608]{0:T(1024)(128)(4,1)}), s8[4194304]{0:T(1024)(128)(4,1)S(1)}, s32[]{:S(2)}) async-start(s8[8388608]{0:T(1024)(128)(4,1)} %bitcast.249), calls=%async_computation.7 | async-start | bytes 8388608
  579.3 48.7 %copy-start.12 = (s32[1024,1]{0,1:T(1,128)S(1)}, s32[1024,1]{0,1:T(1,128)}, u32[]{:S(2)}) copy-start(s32[1024,1]{0,1:T(1,128)} %compare_select_fusion.1) | copy-start | bytes 12292
  596.5 55.4 %all-gather.14.cloned.1.call-start = ((), (), s32[]{:S(2)}) async-start(), calls=%async_computation.5 | async-start | bytes 1572864 | tf_op jit(solution)/shard_map/all_gather | solution.py:199
  627.8 107.3 %all-reduce.9.cloned.1.call-start = ((), (), s32[]{:S(2)}) async-start(), calls=%async_computation.2 | async-start | bytes 131072 | tf_op jit(solution)/shard_map/psum | solution.py:14
  638.1 20.9 %copy-start.14 = (pred[1536]{0:T(1024)(128)(4,1)S(1)}, pred[1536]{0:T(1024)(128)(4,1)}, u32[]{:S(2)}) copy-start(pred[1536]{0:T(1024)(128)(4,1)} %get-tuple-element.84) | copy-start | bytes 4612
  654.2 51.9 %collective-permute-start.1 = (f32[2048,128]{1,0:T(8,128)}, f32[2048,128]{1,0:T(8,128)}, u32[]{:S(2)}, u32[]{:S(2)}) collective-permute-start(f32[2048,128]{1,0:T(8,128)} %bitcast.70), channel_id=1, source_target_pairs={{0,0},{4,1},{8,2},{12,3},{1,4},{5,5},{9,6},{13,7},{2,8},{6,9},{10,... | collective-permute-start | bytes 3145736 | tf_op jit(solution)/shard_map/ppermute | solution.py:207
  715.6 47.7 %copy-start.9 = (f32[1024,128]{1,0:T(8,128)S(1)}, f32[1024,128]{1,0:T(8,128)}, u32[]{:S(2)}) copy-start(f32[1024,128]{1,0:T(8,128)} %all-reduce.7.cloned.1.call-done) | copy-start | bytes 1572868
  (12 other events, 38.3 us)
Sparse Core Ops, SparseCore 0:
  10.7 50.8 all-gather.9
  63.2 44.6 all-gather.11
  109.4 116.5 all-gather.7
  596.6 31.1 all-reduce.6
  629.2 22.6 all-gather.13
  707.8 27.3 all-reduce.8

commit v7 on v6

--- a/solution.py
+++ b/solution.py
@@ -12,6 +12,16 @@
 def spread(shard, axis, root):
     mine = lax.axis_index(axis) == root
     return lax.psum(jnp.where(mine, shard, jnp.zeros_like(shard)), axis)
+
+
+def copy_from(shard, axis, root):
+    size = lax.axis_size(axis)
+    mine = lax.axis_index(axis) == root
+    total = jnp.where(mine, shard, jnp.zeros_like(shard))
+    for target in range(size):
+        if target != root:
+            total = total + lax.ppermute(shard, axis, [(root, target)])
+    return total
 
 
 def from_partner(shard, axis, distance):
@@ -86,7 +96,7 @@
     panel_cols = pivot_order(row_pieces, slot_count, tile_count)
     both = jnp.concatenate([panel_rows, panel_cols], axis=1)
     solved = jnp.dot(
-        diag_inverse, both, precision=lax.Precision.HIGHEST, preferred_element_type=jnp.float32
+        diag_inverse, both, precision=lax.Precision.HIGH, preferred_element_type=jnp.float32
     )
     solved_rows = solved[:, :local_count].T
     solved_cols = solved[:, local_count:].T
@@ -98,7 +108,7 @@
     update = jnp.dot(
         jnp.where(rows_after, solved_rows, 0.0),
         jnp.where(cols_after.T, solved_cols, 0.0).T,
-        precision=lax.Precision.HIGHEST,
+        precision=lax.Precision.HIGH,
         preferred_element_type=jnp.float32,
     )
     diag_rows = jnp.take(diag_factor, jnp.minimum(row_index, pivot_count - 1), axis=0)
@@ -195,7 +205,7 @@
     row_groups = 2 * grid_size
     parent_row = half_index * grid_size + my_row
     row_count, col_count = front_work.shape
-    column = spread(front_work[:, :TILE], "col", 0)
+    column = copy_from(front_work[:, :TILE], "col", 0)
     halves = lax.all_gather(column, "half", axis=0)
     halves = halves.reshape(2, row_count // TILE, TILE, TILE)
     my_row_cols = jnp.swapaxes(halves, 0, 1).reshape(col_count, TILE)
@@ -205,7 +215,7 @@
         for col in range(grid_size)
     ]
     my_cols = lax.ppermute(my_row_cols, ("row", "col"), pairs)
-    diag_block = spread(my_cols[:TILE], "col", 0)
+    diag_block = copy_from(my_row_cols[:TILE], "row", 0)
     diag_factor = jnp.tril(jnp.linalg.cholesky(diag_block))
     eye = jnp.eye(TILE, dtype=jnp.float32)
     inverse = jnp.tril(jax.scipy.linalg.solve_triangular(diag_factor, eye, lower=True))

time: 798 us -> 700 us (0.88)
  waiting for transfers between devices: 154 us -> 86.9 us
  matrix products: 132 us -> 98.8 us
    psum x2 -> x0, waiting for transfers between devices: 50.8 us -> none  [spread(): return lax.psum(jnp.where(mine, shard, jnp.zeros_like(shard)), axis)]
    dot_general x1, matrix products: 47.5 us -> 29.5 us  [factor_child(): jnp.dot(diag_inverse, both, precision=lax.Precision.HIGH, preferred_eleme...]
    dot_general x1, matrix products: 39.9 us -> 24.8 us  [factor_child(): jnp.dot(jnp.where(rows_after, solved_rows, 0.0), jnp.where(cols_after.T,...]
    ppermute x0 -> x6, starting transfers between devices: none -> 9.79 us  [copy_from(): total = total + lax.ppermute(shard, axis, [(root, target)])]
  transfers between devices with their start and end apart: 8 -> 12, of which waited for: 6 -> 4; matrix products, arithmetic and copies ran while one was open for 51% -> 63% of each run, Pallas kernels for 0% -> 0%
where the time goes in v7:
time: 700 us; the launch traced here: 695 us
  other arithmetic  286 us (41%)
  local copies, waits for them, and re-layouts  194 us (28%)
  matrix products  98.8 us (14%)
  waiting for transfers between devices  86.9 us (12%)
  between operations  15.4 us (2%)
  starting transfers between devices  13.6 us (2%)
    another operation x24, other arithmetic, factor_pivots(): factor = jnp.tril(jnp.linalg.cholesky(work[:TILE, :TILE]))  100 us
    another operation x16, other arithmetic, factor_pivots(): jax.scipy.linalg.solve_triangular(factor, eye, lower=True)  84.1 us
    ppermute x1, waiting for transfers between devices, from_partner(): lax.ppermute(shard, axis, [(i, i ^ 1 << distance) for i in range(lax.axis...  36.4 us
    all_gather x1, waiting for transfers between devices, factor_child(): lax.all_gather(front_work[:width, :width], ('row', 'col'), axis=0)  33.2 us
    dot_general x1, matrix products, factor_child(): jnp.dot(diag_inverse, both, precision=lax.Precision.HIGH, preferred_eleme...  29.5 us
    reshape x5, local copies, waits for them, and re-layouts, lower_inverse(): factor.reshape(pairs, 2, size, pairs, 2, size)[picks, 1, :, picks, 0, :]  27.9 us
    dot_general x1, matrix products, factor_child(): jnp.dot(jnp.where(rows_after, solved_rows, 0.0), jnp.where(cols_after.T,...  24.8 us
    reshape x2, local copies, waits for them, and re-layouts, pivot_order(): shaped = pieces.reshape((group_count, slot_count, TILE) + rest)  19.4 us
  transfers between devices with their start and end apart: 12, of which 4 were waited for; matrix products, arithmetic and copies ran while one was open for 63% of the time, Pallas kernels for 0%

profile of v7, /device:TPU:4, one launch (start us, length us, event | category | flops | bytes accessed | tf_op | source)
XLA Modules:
  0.0 694.7 jit_solution(523689744302865212)
XLA Ops:
  28.6 33.2 %all-gather.10.cloned.1.call-done = f32[4096,256]{1,0:T(8,128)} async-done(((f32[256,256]{1,0:T(8,128)}), f32[4096,256]{1,0:T(8,128)}) %all-gather.10.cloned.1.call-update) | async-done | bytes 4194320 | tf_op jit(solution)/shard_map/all_gather | solution.py:83
  82.6 11.7 %cholesky.149 = f32[128,128]{1,0:T(8,128)S(1)} custom-call(f32[128,128]{1,0:T(8,128)S(1)} %fusion.71), custom_call_target="Cholesky" | custom-call | tf_op jit(solution)/shard_map/jit(cholesky)/cholesky | solution.py:46
  95.7 9.8 %custom-call.17 = f32[1,128,128]{1,2,0:T(8,128)S(1)} custom-call(f32[1,128,128]{2,1,0:T(8,128)S(1)} %get-tuple-element.48), custom_call_target="InvertDiagBlocksLowerTriangular" | custom-call | tf_op jit(solution)/shard_map/jit(_solve_triangular)/triangular_solve | solution.py:47
  115.5 12.2 %cholesky.160 = f32[128,128]{1,0:T(8,128)S(1)} custom-call(f32[128,128]{1,0:T(8,128)S(1)} %fusion.69), custom_call_target="Cholesky" | custom-call | tf_op jit(solution)/shard_map/jit(cholesky)/cholesky | solution.py:46
  129.1 9.8 %custom-call.18 = f32[1,128,128]{1,2,0:T(8,128)S(1)} custom-call(f32[1,128,128]{2,1,0:T(8,128)S(1)} %get-tuple-element.46), custom_call_target="InvertDiagBlocksLowerTriangular" | custom-call | tf_op jit(solution)/shard_map/jit(_solve_triangular)/triangular_solve | solution.py:47
  145.1 11.7 %cholesky.171 = f32[128,128]{1,0:T(8,128)S(1)} custom-call(f32[128,128]{1,0:T(8,128)S(1)} %fusion.67), custom_call_target="Cholesky" | custom-call | tf_op jit(solution)/shard_map/jit(cholesky)/cholesky | solution.py:46
  158.1 10.0 %custom-call.19 = f32[1,128,128]{1,2,0:T(8,128)S(1)} custom-call(f32[1,128,128]{2,1,0:T(8,128)S(1)} %get-tuple-element.44), custom_call_target="InvertDiagBlocksLowerTriangular" | custom-call | tf_op jit(solution)/shard_map/jit(_solve_triangular)/triangular_solve | solution.py:47
  173.6 11.7 %cholesky.182 = f32[128,128]{1,0:T(8,128)S(1)} custom-call(f32[128,128]{1,0:T(8,128)S(1)} %fusion.65), custom_call_target="Cholesky" | custom-call | tf_op jit(solution)/shard_map/jit(cholesky)/cholesky | solution.py:46
  187.2 9.8 %custom-call.20 = f32[1,128,128]{1,2,0:T(8,128)S(1)} custom-call(f32[1,128,128]{2,1,0:T(8,128)S(1)} %get-tuple-element.42), custom_call_target="InvertDiagBlocksLowerTriangular" | custom-call | tf_op jit(solution)/shard_map/jit(_solve_triangular)/triangular_solve | solution.py:47
  199.7 12.1 %cholesky.193 = f32[128,128]{1,0:T(8,128)S(1)} custom-call(f32[128,128]{1,0:T(8,128)S(1)} %fusion.63), custom_call_target="Cholesky" | custom-call | tf_op jit(solution)/shard_map/jit(cholesky)/cholesky | solution.py:46
  213.1 9.8 %custom-call.21 = f32[1,128,128]{1,2,0:T(8,128)S(1)} custom-call(f32[1,128,128]{2,1,0:T(8,128)S(1)} %get-tuple-element.40), custom_call_target="InvertDiagBlocksLowerTriangular" | custom-call | tf_op jit(solution)/shard_map/jit(_solve_triangular)/triangular_solve | solution.py:47
  225.1 11.7 %cholesky.204 = f32[128,128]{1,0:T(8,128)S(1)} custom-call(f32[128,128]{1,0:T(8,128)S(1)} %fusion.61), custom_call_target="Cholesky" | custom-call | tf_op jit(solution)/shard_map/jit(cholesky)/cholesky | solution.py:46
  238.1 9.8 %custom-call.22 = f32[1,128,128]{1,2,0:T(8,128)S(1)} custom-call(f32[1,128,128]{2,1,0:T(8,128)S(1)} %get-tuple-element.38), custom_call_target="InvertDiagBlocksLowerTriangular" | custom-call | tf_op jit(solution)/shard_map/jit(_solve_triangular)/triangular_solve | solution.py:47
  249.9 11.7 %cholesky.215 = f32[128,128]{1,0:T(8,128)S(1)} custom-call(f32[128,128]{1,0:T(8,128)S(1)} %fusion.59), custom_call_target="Cholesky" | custom-call | tf_op jit(solution)/shard_map/jit(cholesky)/cholesky | solution.py:46
  262.9 9.8 %custom-call.23 = f32[1,128,128]{1,2,0:T(8,128)S(1)} custom-call(f32[1,128,128]{2,1,0:T(8,128)S(1)} %get-tuple-element.36), custom_call_target="InvertDiagBlocksLowerTriangular" | custom-call | tf_op jit(solution)/shard_map/jit(_solve_triangular)/triangular_solve | solution.py:47
  274.3 11.7 %cholesky.226 = f32[128,128]{1,0:T(8,128)S(1)} custom-call(f32[128,128]{1,0:T(8,128)S(1)} %fusion.57), custom_call_target="Cholesky" | custom-call | tf_op jit(solution)/shard_map/jit(cholesky)/cholesky | solution.py:46
  316.2 9.8 %custom-call.24 = f32[1,128,128]{1,2,0:T(8,128)S(1)} custom-call(f32[1,128,128]{2,1,0:T(8,128)S(1)} %get-tuple-element.34), custom_call_target="InvertDiagBlocksLowerTriangular" | custom-call | tf_op jit(solution)/shard_map/jit(_solve_triangular)/triangular_solve | solution.py:47
  350.8 9.1 %reshape.504 = f32[4,2,128,1536]{2,1,0,3:T(2,128)} reshape(f32[1024,1536]{0,1:T(8,128)} %all-gather.12.cloned.1.call-done) | data formatting | bytes 12582912 | tf_op jit(solution)/shard_map/reshape | solution.py:33
  360.0 10.3 %copy.182 = f32[4,2,128,1536]{3,2,0,1:T(8,128)} copy(f32[4,2,128,1536]{2,1,0,3:T(2,128)} %reshape.504) | data formatting | bytes 12582912 | tf_op jit(solution)/shard_map/reshape | solution.py:33
  374.9 29.5 %fusion = f32[1024,3072]{1,0:T(8,128)} fusion(f32[1024,1536]{1,0:T(8,128)S(1)} %bitcast.261, f32[1024,1536]{1,0:T(8,128)S(1)} %bitcast.260, f32[1,512,512]{2,1,0:T(8,128)} %get-tuple-element.53, f32[1,512,512]{2,1,0:T(8,128)} %get-tuple-element.52, f32[1,512,512]{2,1,0:T(8,128)} %fusion.18), kind=kOutput, calls=%fused_computation.14 | convolution fusion | flops 19334692864 | bytes 28311552 | tf_op jit(solution)/shard_map/dot_general | solution.py:98
  404.4 24.8 %subtract_select_fusion = f32[1536,1536]{1,0:T(8,128)S(1)} fusion(f32[1024,3072]{1,0:T(8,128)} %fusion, pred[1536]{0:T(1024)(128)(4,1)S(1)} %copy-done.20, pred[1536]{0:T(1024)(128)(4,1)S(1)} %copy-done.16, f32[1,1536,1536]{2,1,0:T(8,128)S(1)} %bitcast.273), kind=kOutput, calls=%fused_computation.19 | convolution fusion | flops 14505738240 | bytes 31465472 | tf_op jit(solution)/shard_map/dot_general | solution.py:108
  468.8 7.9 %copy.188 = f32[8,128,16,128]{3,2,1,0:T(8,128)} copy(f32[8,128,16,128]{3,1,0,2:T(8,128)S(1)} %bitcast_select_fusion.1) | data formatting | bytes 16777216 | tf_op jit(solution)/shard_map/jit(_where)/select_n | solution.py:182
  476.7 36.4 %collective-permute-done = f32[5,128,1280]{1,2,0:T(8,128)} collective-permute-done((f32[5,128,1280]{1,2,0:T(8,128)}, f32[5,128,1280]{1,2,0:T(8,128)}, u32[]{:S(2)}, u32[]{:S(2)}) %collective-permute-start) | collective-permute-done | bytes 3276832 | tf_op jit(solution)/shard_map/ppermute | solution.py:28
  537.3 8.1 %copy.191 = f32[8,128,16,128]{3,2,1,0:T(8,128)} copy(f32[8,128,16,128]{3,1,0,2:T(8,128)S(1)} %bitcast_select_fusion) | data formatting | bytes 16777216 | tf_op jit(solution)/shard_map/jit(_where)/select_n | solution.py:182
  545.4 13.1 %bitcast_add_fusion = f32[1024,2048]{1,0:T(8,128)S(1)} fusion(f32[128,8,16,128]{3,2,1,0:T(8,128)} %bitcast.252, f32[1024,2048]{1,0:T(8,128)} %param.16, f32[128,8,16,128]{3,2,1,0:T(8,128)S(1)} %bitcast.251), kind=kLoop, calls=%fused_computation.20 | loop fusion | flops 4194304 | bytes 33554432 | tf_op jit(solution)/shard_map/add | solution.py:201
  564.7 10.1 %gather_fusion.2 = f32[1536,1024]{1,0:T(8,128)} fusion(f32[1024,1024]{1,0:T(8,128)} %pad_dynamic-update-slice_fusion, s32[2048]{0:T(1024)S(1)} %pad_clamp_fusion), kind=kCustom, calls=%fused_computation.10 | custom fusion | bytes 12589056 | tf_op jit(solution)/shard_map/jit(_take)/gather | solution.py:114
  583.3 8.7 %select_select_fusion = f32[1536,1024]{0,1:T(8,128)} fusion(f32[1536,1024]{0,1:T(8,128)} %copy.184, f32[1024,3072]{1,0:T(8,128)} %fusion, pred[1536]{0:T(1024)(128)(4,1)S(1)} %copy-done.15, pred[1536]{0:T(1024)(128)(4,1)S(1)} %copy-done.16), kind=kLoop, calls=%fused_computation.28 | loop fusion | flops 3145728 | bytes 18877440 | tf_op jit(solution)/shard_map/jit(_where)/select_n | solution.py:115
  615.0 7.9 %maximum_bitcast_fusion = f32[1,1536,1536]{2,1,0:T(8,128)} fusion(f32[1536,1280]{1,0:T(8,128)} %slice.277, f32[1536,256]{1,0:T(8,128)S(1)} %slice_select_fusion.2), kind=kLoop, calls=%fused_computation.18 | loop fusion | flops 2359296 | bytes 18874368 | tf_op jit(solution)/shard_map/broadcast_in_dim | solution.py:271
  625.4 11.7 %cholesky.237 = f32[128,128]{1,0:T(8,128)S(1)} custom-call(f32[128,128]{1,0:T(8,128)S(1)} %copy.194), custom_call_target="Cholesky" | custom-call | tf_op jit(solution)/shard_map/jit(cholesky)/cholesky | solution.py:219
  638.4 9.8 %custom-call.25 = f32[1,128,128]{1,2,0:T(8,128)S(1)} custom-call(f32[1,128,128]{2,1,0:T(8,128)S(1)} %get-tuple-element.30), custom_call_target="InvertDiagBlocksLowerTriangular" | custom-call | tf_op jit(solution)/shard_map/jit(_solve_triangular)/triangular_solve | solution.py:221
  653.8 16.7 %collective-permute-done.7 = f32[2048,128]{1,0:T(8,128)} collective-permute-done((f32[2048,128]{1,0:T(8,128)S(1)}, f32[2048,128]{1,0:T(8,128)}, u32[]{:S(2)}, u32[]{:S(2)}) %collective-permute-start.7) | collective-permute-done | bytes 1048608 | tf_op jit(solution)/shard_map/ppermute | solution.py:217
  672.8 9.8 %subtract_select_fusion.1 = f32[1024,2048]{1,0:T(8,128)S(1)} fusion(f32[1024,2048]{1,0:T(8,128)} %copy-done, f32[2048,128]{1,0:T(8,128)S(1)} %convolution_select_fusion, pred[2048]{0:T(1024)(128)(4,1)S(1)} %copy-done.11, pred[1024]{0:T(1024)(128)(4,1)S(1)} %copy-done.17, f32[1024,128]{1,0:T(8,128)S(1)} %get-tuple-element.77), kind=kOutput, calls=%fused_computation.25 | convolution fusion | flops 3227648000 | bytes 18353152 | tf_op jit(solution)/shard_map/dot_general | solution.py:235
  (318 shorter events, 259.0 us)
Async XLA Ops:
  7.2 54.6 %all-gather.10.cloned.1.call-start = ((), (), s32[]{:S(2)}) async-start(), calls=%async_computation.1 | async-start | bytes 4456448 | tf_op jit(solution)/shard_map/all_gather | solution.py:83
  8.9 341.9 %all-gather.12.cloned.1.call-start = ((), (), s32[]{:S(2)}) async-start(), calls=%async_computation.2 | async-start | bytes 7864320 | tf_op jit(solution)/shard_map/all_gather | solution.py:93
  11.6 358.6 %all-gather.8.cloned.1.call-start = ((), (), s32[]{:S(2)}) async-start(), calls=%async_computation | async-start | bytes 7864320 | tf_op jit(solution)/shard_map/all_gather | solution.py:95
  14.4 592.2 %all-gather.14.cloned.1.call-start = ((), (), s32[]{:S(2)}) async-start(), calls=%async_computation.3 | async-start | bytes 1572864 | tf_op jit(solution)/shard_map/all_gather | solution.py:209
  18.2 49.3 %copy-start.31 = (s32[8]{0:T(128)}, s32[8]{0:T(128)S(1)}, u32[]{:S(2)}) copy-start(s32[8]{0:T(128)S(1)} %select_reduce_fusion.12) | copy-start | bytes 100
  18.3 49.2 %copy-start.33 = (s32[8]{0:T(128)}, s32[8]{0:T(128)S(1)}, u32[]{:S(2)}) copy-start(s32[8]{0:T(128)S(1)} %select_reduce_fusion.11) | copy-start | bytes 100
  20.5 47.1 %copy-start.23 = (s32[16]{0:T(128)}, s32[16]{0:T(128)S(1)}, u32[]{:S(2)}) copy-start(s32[16]{0:T(128)S(1)} %select_reduce_fusion.9) | copy-start | bytes 196
  21.3 46.3 %copy-start.25 = (s32[16]{0:T(128)}, s32[16]{0:T(128)S(1)}, u32[]{:S(2)}) copy-start(s32[16]{0:T(128)S(1)} %select_reduce_fusion.10) | copy-start | bytes 196
  199.6 89.0 %copy-start.7 = (f32[768,128]{1,0:T(8,128)S(1)}, f32[768,128]{1,0:T(8,128)}, u32[]{:S(2)}) copy-start(f32[768,128]{1,0:T(8,128)} %copy-done.6) | copy-start | bytes 1179652
  224.9 66.2 %copy-start.10 = (f32[128,128]{1,0:T(8,128)S(1)}, f32[128,128]{1,0:T(8,128)}, u32[]{:S(2)}) copy-start(f32[128,128]{1,0:T(8,128)} %get-tuple-element.43) | copy-start | bytes 196612
  224.9 66.2 %copy-start.12 = (f32[1024]{0:T(1024)S(1)}, f32[1024]{0:T(1024)}, u32[]{:S(2)}) copy-start(f32[1024]{0:T(1024)} %pad.29.clone) | copy-start | bytes 12292
  333.4 8.3 %copy-start.9 = (f32[8,128,128]{2,1,0:T(8,128)S(1)}, f32[8,128,128]{2,1,0:T(8,128)}, u32[]{:S(2)}) copy-start(f32[8,128,128]{2,1,0:T(8,128)} %get-tuple-element.74) | copy-start | bytes 1572868
  370.3 34.1 %slice-start.2 = ((s8[9437184]{0:T(1024)(128)(4,1)}), s8[4194304]{0:T(1024)(128)(4,1)S(1)}, s32[]{:S(2)}) async-start(s8[9437184]{0:T(1024)(128)(4,1)} %bitcast.272), calls=%async_computation.6 | async-start | bytes 8388608
  374.9 29.5 %slice-start.3 = ((s8[9437184]{0:T(1024)(128)(4,1)}), s8[4194304]{0:T(1024)(128)(4,1)S(1)}, s32[]{:S(2)}) async-start(s8[9437184]{0:T(1024)(128)(4,1)} %bitcast.272), calls=%async_computation.7 | async-start | bytes 8388608
  374.9 29.5 %slice-start.4 = ((s8[9437184]{0:T(1024)(128)(4,1)}), s8[1048576]{0:T(1024)(128)(4,1)S(1)}, s32[]{:S(2)}) async-start(s8[9437184]{0:T(1024)(128)(4,1)} %bitcast.272), calls=%async_computation.8 | async-start | bytes 2097152
  374.9 29.5 %copy-start.16 = (pred[1536]{0:T(1024)(128)(4,1)S(1)}, pred[1536]{0:T(1024)(128)(4,1)}, u32[]{:S(2)}) copy-start(pred[1536]{0:T(1024)(128)(4,1)} %get-tuple-element.85) | copy-start | bytes 4612
  374.9 29.5 %copy-start.20 = (pred[1536]{0:T(1024)(128)(4,1)S(1)}, pred[1536]{0:T(1024)(128)(4,1)}, u32[]{:S(2)}) copy-start(pred[1536]{0:T(1024)(128)(4,1)} %broadcast_compare_fusion.2) | copy-start | bytes 4612
  439.7 73.4 %collective-permute-start = (f32[5,128,1280]{1,2,0:T(8,128)}, f32[5,128,1280]{1,2,0:T(8,128)}, u32[]{:S(2)}, u32[]{:S(2)}) collective-permute-start(f32[5,128,1280]{1,2,0:T(8,128)} %bitcast.262), channel_id=1, source_target_pairs={{0,16},{16,0},{1,17},{17,1},{2,18},{18,2},{3,19},{19,3},{4,20},{20... | collective-permute-start | bytes 9830408 | tf_op jit(solution)/shard_map/ppermute | solution.py:28
  532.9 12.5 %slice-start = ((s8[8388608]{0:T(1024)(128)(4,1)}), s8[4194304]{0:T(1024)(128)(4,1)S(1)}, s32[]{:S(2)}) async-start(s8[8388608]{0:T(1024)(128)(4,1)} %bitcast.249), calls=%async_computation.4 | async-start | bytes 8388608
  537.3 8.1 %slice-start.1 = ((s8[8388608]{0:T(1024)(128)(4,1)}), s8[4194304]{0:T(1024)(128)(4,1)S(1)}, s32[]{:S(2)}) async-start(s8[8388608]{0:T(1024)(128)(4,1)} %bitcast.249), calls=%async_computation.5 | async-start | bytes 8388608
  545.4 19.3 %copy-start.13 = (s32[1024,1]{0,1:T(1,128)S(1)}, s32[1024,1]{0,1:T(1,128)}, u32[]{:S(2)}) copy-start(s32[1024,1]{0,1:T(1,128)} %compare_select_fusion.1) | copy-start | bytes 12292
  562.0 19.4 %collective-permute-start.2 = (f32[1024,128]{1,0:T(8,128)S(1)}, f32[1024,128]{1,0:T(8,128)S(1)}, u32[]{:S(2)}, u32[]{:S(2)}) collective-permute-start(f32[1024,128]{1,0:T(8,128)S(1)} %slice.283), channel_id=1, source_target_pairs={{0,2},{4,6},{8,10},{12,14},{16,18},{20,22},{24,26},{28,30}} | collective-permute-start | bytes 1572872 | tf_op jit(solution)/shard_map/ppermute | solution.py:23
  563.3 18.1 %collective-permute-start.1 = (f32[1024,128]{1,0:T(8,128)S(1)}, f32[1024,128]{1,0:T(8,128)S(1)}, u32[]{:S(2)}, u32[]{:S(2)}) collective-permute-start(f32[1024,128]{1,0:T(8,128)S(1)} %slice.283), channel_id=1, source_target_pairs={{0,1},{4,5},{8,9},{12,13},{16,17},{20,21},{24,25},{28,29}} | collective-permute-start | bytes 1572872 | tf_op jit(solution)/shard_map/ppermute | solution.py:23
  564.0 17.4 %collective-permute-start.3 = (f32[1024,128]{1,0:T(8,128)S(1)}, f32[1024,128]{1,0:T(8,128)S(1)}, u32[]{:S(2)}, u32[]{:S(2)}) collective-permute-start(f32[1024,128]{1,0:T(8,128)S(1)} %slice.283), channel_id=1, source_target_pairs={{0,3},{4,7},{8,11},{12,15},{16,19},{20,23},{24,27},{28,31}} | collective-permute-start | bytes 1572872 | tf_op jit(solution)/shard_map/ppermute | solution.py:23
  574.8 8.5 %copy-start.15 = (pred[1536]{0:T(1024)(128)(4,1)S(1)}, pred[1536]{0:T(1024)(128)(4,1)}, u32[]{:S(2)}) copy-start(pred[1536]{0:T(1024)(128)(4,1)} %get-tuple-element.84) | copy-start | bytes 4612
  607.9 17.2 %collective-permute-start.5 = (f32[128,128]{1,0:T(8,128)S(1)}, f32[128,128]{1,0:T(8,128)S(1)}, u32[]{:S(2)}, u32[]{:S(2)}) collective-permute-start(f32[128,128]{1,0:T(8,128)S(1)} %slice.284), channel_id=1, source_target_pairs={{0,8},{1,9},{2,10},{3,11},{16,24},{17,25},{18,26},{19,27}} | collective-permute-start | bytes 196616 | tf_op jit(solution)/shard_map/ppermute | solution.py:23
  612.2 12.9 %collective-permute-start.4 = (f32[128,128]{1,0:T(8,128)S(1)}, f32[128,128]{1,0:T(8,128)S(1)}, u32[]{:S(2)}, u32[]{:S(2)}) collective-permute-start(f32[128,128]{1,0:T(8,128)S(1)} %slice.284), channel_id=1, source_target_pairs={{0,4},{1,5},{2,6},{3,7},{16,20},{17,21},{18,22},{19,23}} | collective-permute-start | bytes 196616 | tf_op jit(solution)/shard_map/ppermute | solution.py:23
  613.5 11.6 %collective-permute-start.6 = (f32[128,128]{1,0:T(8,128)S(1)}, f32[128,128]{1,0:T(8,128)S(1)}, u32[]{:S(2)}, u32[]{:S(2)}) collective-permute-start(f32[128,128]{1,0:T(8,128)S(1)} %slice.284), channel_id=1, source_target_pairs={{0,12},{1,13},{2,14},{3,15},{16,28},{17,29},{18,30},{19,31}} | collective-permute-start | bytes 196616 | tf_op jit(solution)/shard_map/ppermute | solution.py:23
  622.9 28.6 %copy-start.8 = (f32[1024,128]{1,0:T(8,128)S(1)}, f32[1024,128]{1,0:T(8,128)}, u32[]{:S(2)}) copy-start(f32[1024,128]{1,0:T(8,128)} %add_add_fusion) | copy-start | bytes 1572868
  622.9 28.6 %copy-start.17 = (pred[1024]{0:T(1024)(128)(4,1)S(1)}, pred[1024]{0:T(1024)(128)(4,1)}, u32[]{:S(2)}) copy-start(pred[1024]{0:T(1024)(128)(4,1)} %broadcast_compare_fusion.4) | copy-start | bytes 3076
  623.0 47.6 %collective-permute-start.7 = (f32[2048,128]{1,0:T(8,128)S(1)}, f32[2048,128]{1,0:T(8,128)}, u32[]{:S(2)}, u32[]{:S(2)}) collective-permute-start(f32[2048,128]{1,0:T(8,128)S(1)} %bitcast.268), channel_id=1, source_target_pairs={{0,0},{4,1},{8,2},{12,3},{1,4},{5,5},{9,6},{13,7},{2,8},{6,9},{10,... | collective-permute-start | bytes 3145736 | tf_op jit(solution)/shard_map/ppermute | solution.py:217
  651.5 19.0 %copy-start.11 = (pred[2048]{0:T(1024)(128)(4,1)S(1)}, pred[2048]{0:T(1024)(128)(4,1)}, u32[]{:S(2)}) copy-start(pred[2048]{0:T(1024)(128)(4,1)} %broadcast_compare_fusion) | copy-start | bytes 6148
  (22 other events, 105.5 us)
Sparse Core Ops, SparseCore 0:
  10.7 51.0 all-gather.9
  63.4 44.6 all-gather.11
  109.6 116.5 all-gather.7
  583.5 23.0 all-gather.13

commit v8 on v7

--- a/solution.py
+++ b/solution.py
@@ -22,6 +22,16 @@
         if target != root:
             total = total + lax.ppermute(shard, axis, [(root, target)])
     return total
+
+
+def gather_by_shifts(shard, axis):
+    size = lax.axis_size(axis)
+    pieces = [shard]
+    for shift in range(1, size):
+        pairs = [(i, (i + shift) % size) for i in range(size)]
+        pieces.append(lax.ppermute(shard, axis, pairs))
+    order = (lax.axis_index(axis) - jnp.arange(size, dtype=jnp.int32)) % size
+    return jnp.take(jnp.stack(pieces), order, axis=0)
 
 
 def from_partner(shard, axis, distance):
@@ -90,9 +100,9 @@
         diag_inverse = jnp.tril(jax.scipy.linalg.solve_triangular(diag_factor, eye, lower=True))
     else:
         diag_inverse = lower_inverse(diag_factor, block_inverses)
-    col_pieces = lax.all_gather(front_work[:, :width].T, "col", axis=0)
+    col_pieces = gather_by_shifts(front_work[:, :width].T, "col")
     panel_rows = pivot_order(col_pieces, slot_count, tile_count)
-    row_pieces = lax.all_gather(front_work[:width, :], "row", axis=0)
+    row_pieces = gather_by_shifts(front_work[:width, :], "row")
     panel_cols = pivot_order(row_pieces, slot_count, tile_count)
     both = jnp.concatenate([panel_rows, panel_cols], axis=1)
     solved = jnp.dot(

time: 700 us -> 820 us (1.17)
  waiting for transfers between devices: 86.9 us -> 172 us
  other arithmetic: 286 us -> 302 us
  local copies, waits for them, and re-layouts: 194 us -> 204 us
    ppermute x0 -> x6, waiting for transfers between devices: none -> 114 us  [gather_by_shifts(): pieces.append(lax.ppermute(shard, axis, pairs))]
    all_gather x1, waiting for transfers between devices: 33.2 us -> 0.01 us  [factor_child(): lax.all_gather(front_work[:width, :width], ('row', 'col'), axis=0)]
    gather x0 -> x2, local copies, waits for them, and re-layouts: none -> 12.9 us  [gather_by_shifts(): return jnp.take(jnp.stack(pieces), order, axis=0)]
    select_n x0 -> x4, other arithmetic: none -> 9.75 us  [gather_by_shifts(): return jnp.take(jnp.stack(pieces), order, axis=0)]
    another operation x0 -> x2, other arithmetic: none -> 9.13 us  [gather_by_shifts(): return jnp.take(jnp.stack(pieces), order, axis=0)]
  transfers between devices with their start and end apart: 12 -> 16, of which waited for: 4 -> 6; matrix products, arithmetic and copies ran while one was open for 63% -> 21% of each run, Pallas kernels for 0% -> 0%
where the time goes in v8:
time: 820 us; the launch traced here: 812 us
  other arithmetic  302 us (37%)
  local copies, waits for them, and re-layouts  204 us (25%)
  waiting for transfers between devices  172 us (21%)
  matrix products  98.6 us (12%)
  starting transfers between devices  21 us (3%)
  between operations  15.6 us (2%)
    ppermute x6, waiting for transfers between devices, gather_by_shifts(): pieces.append(lax.ppermute(shard, axis, pairs))  114 us
    another operation x24, other arithmetic, factor_pivots(): factor = jnp.tril(jnp.linalg.cholesky(work[:TILE, :TILE]))  99.5 us
    another operation x16, other arithmetic, factor_pivots(): jax.scipy.linalg.solve_triangular(factor, eye, lower=True)  84.1 us
    ppermute x1, waiting for transfers between devices, from_partner(): lax.ppermute(shard, axis, [(i, i ^ 1 << distance) for i in range(lax.axis...  35.5 us
    dot_general x1, matrix products, factor_child(): jnp.dot(diag_inverse, both, precision=lax.Precision.HIGH, preferred_eleme...  28.5 us
    reshape x5, local copies, waits for them, and re-layouts, lower_inverse(): factor.reshape(pairs, 2, size, pairs, 2, size)[picks, 1, :, picks, 0, :]  27.6 us
    dot_general x1, matrix products, factor_child(): jnp.dot(jnp.where(rows_after, solved_rows, 0.0), jnp.where(cols_after.T,...  24.8 us
    reshape x2, local copies, waits for them, and re-layouts, pivot_order(): shaped = pieces.reshape((group_count, slot_count, TILE) + rest)  18.6 us
  transfers between devices with their start and end apart: 16, of which 6 were waited for; matrix products, arithmetic and copies ran while one was open for 21% of the time, Pallas kernels for 0%

profile of v8, /device:TPU:4, one launch (start us, length us, event | category | flops | bytes accessed | tf_op | source)
XLA Modules:
  0.0 812.0 jit_solution(8967778099876886246)
XLA Ops:
  28.1 22.3 %collective-permute-done.1 = f32[256,1536]{0,1:T(8,128)} collective-permute-done((f32[256,1536]{0,1:T(8,128)}, f32[256,1536]{0,1:T(8,128)}, u32[]{:S(2)}, u32[]{:S(2)}) %collective-permute-start.1) | collective-permute-done | bytes 1572896 | tf_op jit(solution)/shard_map/ppermute | solution.py:32
  52.6 29.2 %collective-permute-done = f32[256,1536]{0,1:T(8,128)} collective-permute-done((f32[256,1536]{0,1:T(8,128)}, f32[256,1536]{0,1:T(8,128)}, u32[]{:S(2)}, u32[]{:S(2)}) %collective-permute-start) | collective-permute-done | bytes 1572896 | tf_op jit(solution)/shard_map/ppermute | solution.py:32
  99.0 8.2 %reshape.509 = f32[4,2,128,1536]{2,1,3,0:T(2,128)} reshape(f32[4,256,1536]{1,2,0:T(8,128)} %broadcast_select_fusion.1) | data formatting | bytes 12582912 | tf_op jit(solution)/shard_map/reshape | solution.py:43
  107.3 10.4 %copy.139 = f32[4,2,128,1536]{3,2,0,1:T(8,128)} copy(f32[4,2,128,1536]{2,1,3,0:T(2,128)} %reshape.509) | data formatting | bytes 12582912 | tf_op jit(solution)/shard_map/reshape | solution.py:43
  117.7 63.0 %collective-permute-done.4 = f32[256,1536]{1,0:T(8,128)} collective-permute-done((f32[256,1536]{1,0:T(8,128)}, f32[256,1536]{1,0:T(8,128)}, u32[]{:S(2)}, u32[]{:S(2)}) %collective-permute-start.4) | collective-permute-done | bytes 1572896 | tf_op jit(solution)/shard_map/ppermute | solution.py:32
  218.8 11.7 %cholesky.149 = f32[128,128]{1,0:T(8,128)S(1)} custom-call(f32[128,128]{1,0:T(8,128)S(1)} %fusion.71), custom_call_target="Cholesky" | custom-call | tf_op jit(solution)/shard_map/jit(cholesky)/cholesky | solution.py:56
  231.8 9.8 %custom-call.17 = f32[1,128,128]{1,2,0:T(8,128)S(1)} custom-call(f32[1,128,128]{2,1,0:T(8,128)S(1)} %get-tuple-element.49), custom_call_target="InvertDiagBlocksLowerTriangular" | custom-call | tf_op jit(solution)/shard_map/jit(_solve_triangular)/triangular_solve | solution.py:57
  251.6 11.9 %cholesky.160 = f32[128,128]{1,0:T(8,128)S(1)} custom-call(f32[128,128]{1,0:T(8,128)S(1)} %fusion.69), custom_call_target="Cholesky" | custom-call | tf_op jit(solution)/shard_map/jit(cholesky)/cholesky | solution.py:56
  264.9 9.8 %custom-call.18 = f32[1,128,128]{1,2,0:T(8,128)S(1)} custom-call(f32[1,128,128]{2,1,0:T(8,128)S(1)} %get-tuple-element.47), custom_call_target="InvertDiagBlocksLowerTriangular" | custom-call | tf_op jit(solution)/shard_map/jit(_solve_triangular)/triangular_solve | solution.py:57
  280.9 11.7 %cholesky.171 = f32[128,128]{1,0:T(8,128)S(1)} custom-call(f32[128,128]{1,0:T(8,128)S(1)} %fusion.67), custom_call_target="Cholesky" | custom-call | tf_op jit(solution)/shard_map/jit(cholesky)/cholesky | solution.py:56
  293.9 10.2 %custom-call.19 = f32[1,128,128]{1,2,0:T(8,128)S(1)} custom-call(f32[1,128,128]{2,1,0:T(8,128)S(1)} %get-tuple-element.45), custom_call_target="InvertDiagBlocksLowerTriangular" | custom-call | tf_op jit(solution)/shard_map/jit(_solve_triangular)/triangular_solve | solution.py:57
  309.8 11.7 %cholesky.182 = f32[128,128]{1,0:T(8,128)S(1)} custom-call(f32[128,128]{1,0:T(8,128)S(1)} %fusion.65), custom_call_target="Cholesky" | custom-call | tf_op jit(solution)/shard_map/jit(cholesky)/cholesky | solution.py:56
  322.8 9.8 %custom-call.20 = f32[1,128,128]{1,2,0:T(8,128)S(1)} custom-call(f32[1,128,128]{2,1,0:T(8,128)S(1)} %get-tuple-element.43), custom_call_target="InvertDiagBlocksLowerTriangular" | custom-call | tf_op jit(solution)/shard_map/jit(_solve_triangular)/triangular_solve | solution.py:57
  336.5 11.9 %cholesky.193 = f32[128,128]{1,0:T(8,128)S(1)} custom-call(f32[128,128]{1,0:T(8,128)S(1)} %fusion.63), custom_call_target="Cholesky" | custom-call | tf_op jit(solution)/shard_map/jit(cholesky)/cholesky | solution.py:56
  349.7 9.8 %custom-call.21 = f32[1,128,128]{1,2,0:T(8,128)S(1)} custom-call(f32[1,128,128]{2,1,0:T(8,128)S(1)} %get-tuple-element.41), custom_call_target="InvertDiagBlocksLowerTriangular" | custom-call | tf_op jit(solution)/shard_map/jit(_solve_triangular)/triangular_solve | solution.py:57
  363.1 11.7 %cholesky.204 = f32[128,128]{1,0:T(8,128)S(1)} custom-call(f32[128,128]{1,0:T(8,128)S(1)} %fusion.61), custom_call_target="Cholesky" | custom-call | tf_op jit(solution)/shard_map/jit(cholesky)/cholesky | solution.py:56
  376.2 9.8 %custom-call.22 = f32[1,128,128]{1,2,0:T(8,128)S(1)} custom-call(f32[1,128,128]{2,1,0:T(8,128)S(1)} %get-tuple-element.39), custom_call_target="InvertDiagBlocksLowerTriangular" | custom-call | tf_op jit(solution)/shard_map/jit(_solve_triangular)/triangular_solve | solution.py:57
  387.6 11.7 %cholesky.215 = f32[128,128]{1,0:T(8,128)S(1)} custom-call(f32[128,128]{1,0:T(8,128)S(1)} %fusion.59), custom_call_target="Cholesky" | custom-call | tf_op jit(solution)/shard_map/jit(cholesky)/cholesky | solution.py:56
  400.6 9.8 %custom-call.23 = f32[1,128,128]{1,2,0:T(8,128)S(1)} custom-call(f32[1,128,128]{2,1,0:T(8,128)S(1)} %get-tuple-element.37), custom_call_target="InvertDiagBlocksLowerTriangular" | custom-call | tf_op jit(solution)/shard_map/jit(_solve_triangular)/triangular_solve | solution.py:57
  411.4 11.7 %cholesky.226 = f32[128,128]{1,0:T(8,128)S(1)} custom-call(f32[128,128]{1,0:T(8,128)S(1)} %fusion.57), custom_call_target="Cholesky" | custom-call | tf_op jit(solution)/shard_map/jit(cholesky)/cholesky | solution.py:56
  453.1 9.8 %custom-call.24 = f32[1,128,128]{1,2,0:T(8,128)S(1)} custom-call(f32[1,128,128]{2,1,0:T(8,128)S(1)} %get-tuple-element.35), custom_call_target="InvertDiagBlocksLowerTriangular" | custom-call | tf_op jit(solution)/shard_map/jit(_solve_triangular)/triangular_solve | solution.py:57
  493.1 28.5 %fusion = f32[1024,3072]{1,0:T(8,128)} fusion(f32[1024,1536]{1,0:T(8,128)S(1)} %bitcast.278, f32[1024,1536]{1,0:T(8,128)S(1)} %bitcast.275, f32[1,512,512]{2,1,0:T(8,128)} %get-tuple-element.58, f32[1,512,512]{2,1,0:T(8,128)} %get-tuple-element.57, f32[1,512,512]{2,1,0:T(8,128)} %fusion.18), kind=kOutput, calls=%fused_computation.16 | convolution fusion | flops 19334692864 | bytes 28311552 | tf_op jit(solution)/shard_map/dot_general | solution.py:108
  521.6 24.8 %subtract_select_fusion = f32[1536,1536]{1,0:T(8,128)S(1)} fusion(f32[1024,3072]{1,0:T(8,128)} %fusion, pred[1536]{0:T(1024)(128)(4,1)S(1)} %broadcast_compare_fusion.2, pred[1536]{0:T(1024)(128)(4,1)S(1)} %get-tuple-element.94, f32[1,1536,1536]{2,1,0:T(8,128)S(1)} %bitcast.290), kind=kOutput, calls=%fused_computation.21 | convolution fusion | flops 14505738240 | bytes 31465472 | tf_op jit(solution)/shard_map/dot_general | solution.py:118
  593.5 35.5 %collective-permute-done.6 = f32[5,128,1280]{1,2,0:T(8,128)} collective-permute-done((f32[5,128,1280]{1,2,0:T(8,128)}, f32[5,128,1280]{1,2,0:T(8,128)}, u32[]{:S(2)}, u32[]{:S(2)}) %collective-permute-start.6) | collective-permute-done | bytes 3276832 | tf_op jit(solution)/shard_map/ppermute | solution.py:38
  652.9 8.1 %copy.148 = f32[8,128,16,128]{3,2,1,0:T(8,128)} copy(f32[8,128,16,128]{3,1,0,2:T(8,128)S(1)} %bitcast_select_fusion) | data formatting | bytes 16777216 | tf_op jit(solution)/shard_map/jit(_where)/select_n | solution.py:192
  661.0 13.1 %bitcast_add_fusion = f32[1024,2048]{1,0:T(8,128)S(1)} fusion(f32[128,8,16,128]{3,2,1,0:T(8,128)} %bitcast.263, f32[1024,2048]{1,0:T(8,128)} %param.18, f32[128,8,16,128]{3,2,1,0:T(8,128)S(1)} %bitcast.262), kind=kLoop, calls=%fused_computation.22 | loop fusion | flops 4194304 | bytes 33554432 | tf_op jit(solution)/shard_map/add | solution.py:211
  680.4 10.1 %gather_fusion.2 = f32[1536,1024]{1,0:T(8,128)} fusion(f32[1024,1024]{1,0:T(8,128)} %pad_dynamic-update-slice_fusion, s32[2048]{0:T(1024)S(1)} %pad_clamp_fusion), kind=kCustom, calls=%fused_computation.12 | custom fusion | bytes 12589056 | tf_op jit(solution)/shard_map/jit(_take)/gather | solution.py:124
  699.0 8.9 %select_select_fusion = f32[1536,1024]{0,1:T(8,128)} fusion(f32[1536,1024]{0,1:T(8,128)} %copy.141, f32[1024,3072]{1,0:T(8,128)} %fusion, pred[1536]{0:T(1024)(128)(4,1)S(1)} %copy-done.13, pred[1536]{0:T(1024)(128)(4,1)S(1)} %get-tuple-element.94), kind=kLoop, calls=%fused_computation.32 | loop fusion | flops 3145728 | bytes 18877440 | tf_op jit(solution)/shard_map/jit(_where)/select_n | solution.py:125
  742.4 11.7 %cholesky.237 = f32[128,128]{1,0:T(8,128)S(1)} custom-call(f32[128,128]{1,0:T(8,128)S(1)} %copy.151), custom_call_target="Cholesky" | custom-call | tf_op jit(solution)/shard_map/jit(cholesky)/cholesky | solution.py:229
  755.3 9.8 %custom-call.25 = f32[1,128,128]{1,2,0:T(8,128)S(1)} custom-call(f32[1,128,128]{2,1,0:T(8,128)S(1)} %get-tuple-element.31), custom_call_target="InvertDiagBlocksLowerTriangular" | custom-call | tf_op jit(solution)/shard_map/jit(_solve_triangular)/triangular_solve | solution.py:231
  770.7 16.9 %collective-permute-done.13 = f32[2048,128]{1,0:T(8,128)} collective-permute-done((f32[2048,128]{1,0:T(8,128)S(1)}, f32[2048,128]{1,0:T(8,128)}, u32[]{:S(2)}, u32[]{:S(2)}) %collective-permute-start.13) | collective-permute-done | bytes 1048608 | tf_op jit(solution)/shard_map/ppermute | solution.py:227
  789.9 9.8 %subtract_select_fusion.1 = f32[1024,2048]{1,0:T(8,128)S(1)} fusion(f32[1024,2048]{1,0:T(8,128)} %copy-done, f32[2048,128]{1,0:T(8,128)S(1)} %convolution_select_fusion, pred[2048]{0:T(1024)(128)(4,1)S(1)} %copy-done.11, pred[1024]{0:T(1024)(128)(4,1)S(1)} %copy-done.14, f32[1024,128]{1,0:T(8,128)S(1)} %get-tuple-element.82), kind=kOutput, calls=%fused_computation.27 | convolution fusion | flops 3227648000 | bytes 18353152 | tf_op jit(solution)/shard_map/dot_general | solution.py:245
  (320 shorter events, 313.2 us)
Async XLA Ops:
  7.2 13.2 %copy-start.16 = (s32[2,40]{1,0:T(2,128)S(1)}, s32[2,40]{1,0:T(2,128)}, u32[]{:S(2)}) copy-start(s32[2,40]{1,0:T(2,128)} %param.17) | copy-start | bytes 964
  7.2 191.1 %all-gather.5.cloned.1.call-start = ((), (), s32[]{:S(2)}) async-start(), calls=%async_computation | async-start | bytes 4456448 | tf_op jit(solution)/shard_map/all_gather | solution.py:93
  10.0 40.4 %collective-permute-start.1 = (f32[256,1536]{0,1:T(8,128)}, f32[256,1536]{0,1:T(8,128)}, u32[]{:S(2)}, u32[]{:S(2)}) collective-permute-start(f32[256,1536]{0,1:T(8,128)} %get-tuple-element.52), channel_id=1, source_target_pairs={{0,2},{1,3},{2,0},{3,1},{4,6},{5,7},{6,4},{7,5},{8,10},{9,11},{10,... | collective-permute-start | bytes 4718600 | tf_op jit(solution)/shard_map/ppermute | solution.py:32
  10.0 71.8 %collective-permute-start = (f32[256,1536]{0,1:T(8,128)}, f32[256,1536]{0,1:T(8,128)}, u32[]{:S(2)}, u32[]{:S(2)}) collective-permute-start(f32[256,1536]{0,1:T(8,128)} %get-tuple-element.52), channel_id=1, source_target_pairs={{0,1},{1,2},{2,3},{3,0},{4,5},{5,6},{6,7},{7,4},{8,9},{9,10},{10,1... | collective-permute-start | bytes 4718600 | tf_op jit(solution)/shard_map/ppermute | solution.py:32
  10.0 71.8 %collective-permute-start.2 = (f32[256,1536]{0,1:T(8,128)}, f32[256,1536]{0,1:T(8,128)}, u32[]{:S(2)}, u32[]{:S(2)}) collective-permute-start(f32[256,1536]{0,1:T(8,128)} %get-tuple-element.52), channel_id=1, source_target_pairs={{0,3},{1,0},{2,1},{3,2},{4,7},{5,4},{6,5},{7,6},{8,11},{9,8},{10,9... | collective-permute-start | bytes 4718600 | tf_op jit(solution)/shard_map/ppermute | solution.py:32
  13.4 710.0 %all-gather.7.cloned.1.call-start = ((), (), s32[]{:S(2)}) async-start(), calls=%async_computation.1 | async-start | bytes 1572864 | tf_op jit(solution)/shard_map/all_gather | solution.py:219
  16.2 101.4 %collective-permute-start.5 = (f32[256,1536]{1,0:T(8,128)}, f32[256,1536]{1,0:T(8,128)}, u32[]{:S(2)}, u32[]{:S(2)}) collective-permute-start(f32[256,1536]{1,0:T(8,128)} %get-tuple-element.54), channel_id=1, source_target_pairs={{0,12},{4,0},{8,4},{12,8},{1,13},{5,1},{9,5},{13,9},{2,14},{6,2},{... | collective-permute-start | bytes 4718600 | tf_op jit(solution)/shard_map/ppermute | solution.py:32
  20.3 160.4 %collective-permute-start.4 = (f32[256,1536]{1,0:T(8,128)}, f32[256,1536]{1,0:T(8,128)}, u32[]{:S(2)}, u32[]{:S(2)}) collective-permute-start(f32[256,1536]{1,0:T(8,128)} %get-tuple-element.54), channel_id=1, source_target_pairs={{0,8},{4,12},{8,0},{12,4},{1,9},{5,13},{9,1},{13,5},{2,10},{6,14},... | collective-permute-start | bytes 4718600 | tf_op jit(solution)/shard_map/ppermute | solution.py:32
  27.9 24.0 %copy-start.19 = (s32[8]{0:T(128)}, s32[8]{0:T(128)S(1)}, u32[]{:S(2)}) copy-start(s32[8]{0:T(128)S(1)} %select_reduce_fusion.12) | copy-start | bytes 100
  50.4 130.3 %collective-permute-start.3 = (f32[256,1536]{1,0:T(8,128)}, f32[256,1536]{1,0:T(8,128)}, u32[]{:S(2)}, u32[]{:S(2)}) collective-permute-start(f32[256,1536]{1,0:T(8,128)} %get-tuple-element.54), channel_id=1, source_target_pairs={{0,4},{4,8},{8,12},{12,0},{1,5},{5,9},{9,13},{13,1},{2,6},{6,10},{... | collective-permute-start | bytes 4718600 | tf_op jit(solution)/shard_map/ppermute | solution.py:32
  305.0 27.6 %copy-start.10 = (f32[8,128,128]{2,1,0:T(8,128)S(1)}, f32[8,128,128]{2,1,0:T(8,128)}, u32[]{:S(2)}) copy-start(f32[8,128,128]{2,1,0:T(8,128)} %get-tuple-element.71) | copy-start | bytes 1572868
  333.5 92.8 %copy-start.6 = (f32[768,128]{1,0:T(8,128)S(1)}, f32[768,128]{1,0:T(8,128)}, u32[]{:S(2)}) copy-start(f32[768,128]{1,0:T(8,128)} %copy-done.5) | copy-start | bytes 1179652
  478.1 15.0 %slice-start.7 = ((s8[6291456]{0:T(1024)(128)(4,1)}), s8[2097152]{0:T(1024)(128)(4,1)S(1)}, s32[]{:S(2)}) async-start(s8[6291456]{0:T(1024)(128)(4,1)} %bitcast.276), calls=%async_computation.9 | async-start | bytes 4194304
  490.3 31.3 %slice-start.9 = ((s8[9437184]{0:T(1024)(128)(4,1)}), s8[4194304]{0:T(1024)(128)(4,1)S(1)}, s32[]{:S(2)}) async-start(s8[9437184]{0:T(1024)(128)(4,1)} %bitcast.289), calls=%async_computation.11 | async-start | bytes 8388608
  493.1 28.5 %slice-start.10 = ((s8[9437184]{0:T(1024)(128)(4,1)}), s8[4194304]{0:T(1024)(128)(4,1)S(1)}, s32[]{:S(2)}) async-start(s8[9437184]{0:T(1024)(128)(4,1)} %bitcast.289), calls=%async_computation.12 | async-start | bytes 8388608
  493.1 28.5 %slice-start.11 = ((s8[9437184]{0:T(1024)(128)(4,1)}), s8[1048576]{0:T(1024)(128)(4,1)S(1)}, s32[]{:S(2)}) async-start(s8[9437184]{0:T(1024)(128)(4,1)} %bitcast.289), calls=%async_computation.13 | async-start | bytes 2097152
  556.9 72.2 %collective-permute-start.6 = (f32[5,128,1280]{1,2,0:T(8,128)}, f32[5,128,1280]{1,2,0:T(8,128)}, u32[]{:S(2)}, u32[]{:S(2)}) collective-permute-start(f32[5,128,1280]{1,2,0:T(8,128)} %bitcast.279), channel_id=1, source_target_pairs={{0,16},{16,0},{1,17},{17,1},{2,18},{18,2},{3,19},{19,3},{4,20},{20... | collective-permute-start | bytes 9830408 | tf_op jit(solution)/shard_map/ppermute | solution.py:38
  648.5 12.5 %slice-start = ((s8[8388608]{0:T(1024)(128)(4,1)}), s8[4194304]{0:T(1024)(128)(4,1)S(1)}, s32[]{:S(2)}) async-start(s8[8388608]{0:T(1024)(128)(4,1)} %bitcast.260), calls=%async_computation.2 | async-start | bytes 8388608
  661.0 19.3 %copy-start.12 = (s32[1024,1]{0,1:T(1,128)S(1)}, s32[1024,1]{0,1:T(1,128)}, u32[]{:S(2)}) copy-start(s32[1024,1]{0,1:T(1,128)} %compare_select_fusion.1) | copy-start | bytes 12292
  677.6 19.4 %collective-permute-start.8 = (f32[1024,128]{1,0:T(8,128)S(1)}, f32[1024,128]{1,0:T(8,128)S(1)}, u32[]{:S(2)}, u32[]{:S(2)}) collective-permute-start(f32[1024,128]{1,0:T(8,128)S(1)} %slice.290), channel_id=1, source_target_pairs={{0,2},{4,6},{8,10},{12,14},{16,18},{20,22},{24,26},{28,30}} | collective-permute-start | bytes 1572872 | tf_op jit(solution)/shard_map/ppermute | solution.py:23
  678.9 18.1 %collective-permute-start.7 = (f32[1024,128]{1,0:T(8,128)S(1)}, f32[1024,128]{1,0:T(8,128)S(1)}, u32[]{:S(2)}, u32[]{:S(2)}) collective-permute-start(f32[1024,128]{1,0:T(8,128)S(1)} %slice.290), channel_id=1, source_target_pairs={{0,1},{4,5},{8,9},{12,13},{16,17},{20,21},{24,25},{28,29}} | collective-permute-start | bytes 1572872 | tf_op jit(solution)/shard_map/ppermute | solution.py:23
  679.6 17.4 %collective-permute-start.9 = (f32[1024,128]{1,0:T(8,128)S(1)}, f32[1024,128]{1,0:T(8,128)S(1)}, u32[]{:S(2)}, u32[]{:S(2)}) collective-permute-start(f32[1024,128]{1,0:T(8,128)S(1)} %slice.290), channel_id=1, source_target_pairs={{0,3},{4,7},{8,11},{12,15},{16,19},{20,23},{24,27},{28,31}} | collective-permute-start | bytes 1572872 | tf_op jit(solution)/shard_map/ppermute | solution.py:23
  699.0 8.9 %slice-start.2 = ((s8[9437184]{0:T(1024)(128)(4,1)}), s8[4194304]{0:T(1024)(128)(4,1)S(1)}, s32[]{:S(2)}) async-start(s8[9437184]{0:T(1024)(128)(4,1)} %bitcast.264), calls=%async_computation.4 | async-start | bytes 8388608
  699.0 8.9 %slice-start.3 = ((s8[9437184]{0:T(1024)(128)(4,1)}), s8[4194304]{0:T(1024)(128)(4,1)S(1)}, s32[]{:S(2)}) async-start(s8[9437184]{0:T(1024)(128)(4,1)} %bitcast.264), calls=%async_computation.5 | async-start | bytes 8388608
  699.0 8.9 %slice-start.4 = ((s8[9437184]{0:T(1024)(128)(4,1)}), s8[1048576]{0:T(1024)(128)(4,1)S(1)}, s32[]{:S(2)}) async-start(s8[9437184]{0:T(1024)(128)(4,1)} %bitcast.264), calls=%async_computation.6 | async-start | bytes 2097152
  724.8 17.3 %collective-permute-start.11 = (f32[128,128]{1,0:T(8,128)S(1)}, f32[128,128]{1,0:T(8,128)S(1)}, u32[]{:S(2)}, u32[]{:S(2)}) collective-permute-start(f32[128,128]{1,0:T(8,128)S(1)} %slice.291), channel_id=1, source_target_pairs={{0,8},{1,9},{2,10},{3,11},{16,24},{17,25},{18,26},{19,27}} | collective-permute-start | bytes 196616 | tf_op jit(solution)/shard_map/ppermute | solution.py:23
  729.1 13.0 %collective-permute-start.10 = (f32[128,128]{1,0:T(8,128)S(1)}, f32[128,128]{1,0:T(8,128)S(1)}, u32[]{:S(2)}, u32[]{:S(2)}) collective-permute-start(f32[128,128]{1,0:T(8,128)S(1)} %slice.291), channel_id=1, source_target_pairs={{0,4},{1,5},{2,6},{3,7},{16,20},{17,21},{18,22},{19,23}} | collective-permute-start | bytes 196616 | tf_op jit(solution)/shard_map/ppermute | solution.py:23
  730.4 11.7 %collective-permute-start.12 = (f32[128,128]{1,0:T(8,128)S(1)}, f32[128,128]{1,0:T(8,128)S(1)}, u32[]{:S(2)}, u32[]{:S(2)}) collective-permute-start(f32[128,128]{1,0:T(8,128)S(1)} %slice.291), channel_id=1, source_target_pairs={{0,12},{1,13},{2,14},{3,15},{16,28},{17,29},{18,30},{19,31}} | collective-permute-start | bytes 196616 | tf_op jit(solution)/shard_map/ppermute | solution.py:23
  740.0 28.4 %copy-start.7 = (f32[1024,128]{1,0:T(8,128)S(1)}, f32[1024,128]{1,0:T(8,128)}, u32[]{:S(2)}) copy-start(f32[1024,128]{1,0:T(8,128)} %add_add_fusion) | copy-start | bytes 1572868
  740.0 28.4 %copy-start.14 = (pred[1024]{0:T(1024)(128)(4,1)S(1)}, pred[1024]{0:T(1024)(128)(4,1)}, u32[]{:S(2)}) copy-start(pred[1024]{0:T(1024)(128)(4,1)} %broadcast_compare_fusion.4) | copy-start | bytes 3076
  740.0 47.6 %collective-permute-start.13 = (f32[2048,128]{1,0:T(8,128)S(1)}, f32[2048,128]{1,0:T(8,128)}, u32[]{:S(2)}, u32[]{:S(2)}) collective-permute-start(f32[2048,128]{1,0:T(8,128)S(1)} %bitcast.285), channel_id=1, source_target_pairs={{0,0},{4,1},{8,2},{12,3},{1,4},{5,5},{9,6},{13,7},{2,8},{6,9},{10,... | collective-permute-start | bytes 3145736 | tf_op jit(solution)/shard_map/ppermute | solution.py:227
  768.1 19.5 %copy-start.11 = (pred[2048]{0:T(1024)(128)(4,1)S(1)}, pred[2048]{0:T(1024)(128)(4,1)}, u32[]{:S(2)}) copy-start(pred[2048]{0:T(1024)(128)(4,1)} %broadcast_compare_fusion) | copy-start | bytes 6148
  (17 other events, 82.0 us)
Sparse Core Ops, SparseCore 0:
  13.6 144.5 all-gather.4
  699.1 24.2 all-gather.6

commit v9 on v7

--- a/solution.py
+++ b/solution.py
@@ -206,7 +206,9 @@
     parent_row = half_index * grid_size + my_row
     row_count, col_count = front_work.shape
     column = copy_from(front_work[:, :TILE], "col", 0)
-    halves = lax.all_gather(column, "half", axis=0)
+    partner = from_partner(column, "half", 0)
+    first = half_index == 0
+    halves = jnp.stack([jnp.where(first, column, partner), jnp.where(first, partner, column)])
     halves = halves.reshape(2, row_count // TILE, TILE, TILE)
     my_row_cols = jnp.swapaxes(halves, 0, 1).reshape(col_count, TILE)
     pairs = [

time: 700 us -> 689 us (0.984)
  waiting for transfers between devices: 86.9 us -> 76.5 us
    ppermute x1 -> x2, waiting for transfers between devices: 36.4 us -> 29.4 us  [from_partner(): lax.ppermute(shard, axis, [(i, i ^ 1 << distance) for i in range(lax.axis...]
    slice x1 -> x2, local copies, waits for them, and re-layouts: 7.05 us -> 0.01 us  [factor_child(): return jnp.concatenate([head, trailing[:, width:]], axis=1)]
where the time goes in v9:
time: 689 us; the launch traced here: 683 us
  other arithmetic  288 us (42%)
  local copies, waits for them, and re-layouts  189 us (27%)
  matrix products  98.7 us (14%)
  waiting for transfers between devices  76.5 us (11%)
  starting transfers between devices  15.7 us (2%)
  between operations  15.3 us (2%)
    another operation x24, other arithmetic, factor_pivots(): factor = jnp.tril(jnp.linalg.cholesky(work[:TILE, :TILE]))  100 us
    another operation x16, other arithmetic, factor_pivots(): jax.scipy.linalg.solve_triangular(factor, eye, lower=True)  84.4 us
    all_gather x1, waiting for transfers between devices, factor_child(): lax.all_gather(front_work[:width, :width], ('row', 'col'), axis=0)  31.4 us
    dot_general x1, matrix products, factor_child(): jnp.dot(diag_inverse, both, precision=lax.Precision.HIGH, preferred_eleme...  29.5 us
    ppermute x2, waiting for transfers between devices, from_partner(): lax.ppermute(shard, axis, [(i, i ^ 1 << distance) for i in range(lax.axis...  29.4 us
    reshape x5, local copies, waits for them, and re-layouts, lower_inverse(): factor.reshape(pairs, 2, size, pairs, 2, size)[picks, 1, :, picks, 0, :]  27.9 us
    dot_general x1, matrix products, factor_child(): jnp.dot(jnp.where(rows_after, solved_rows, 0.0), jnp.where(cols_after.T,...  24.8 us
    reshape x2, local copies, waits for them, and re-layouts, pivot_order(): shaped = pieces.reshape((group_count, slot_count, TILE) + rest)  19.4 us
  transfers between devices with their start and end apart: 12, of which 4 were waited for; matrix products, arithmetic and copies ran while one was open for 63% of the time, Pallas kernels for 0%

profile of v9, /device:TPU:4, one launch (start us, length us, event | category | flops | bytes accessed | tf_op | source)
XLA Modules:
  0.0 682.9 jit_solution(16309323636470331366)
XLA Ops:
  30.2 31.4 %all-gather.8.cloned.1.call-done = f32[4096,256]{1,0:T(8,128)} async-done(((f32[256,256]{1,0:T(8,128)}), f32[4096,256]{1,0:T(8,128)}) %all-gather.8.cloned.1.call-update) | async-done | bytes 4194320 | tf_op jit(solution)/shard_map/all_gather | solution.py:83
  82.4 11.7 %cholesky.149 = f32[128,128]{1,0:T(8,128)S(1)} custom-call(f32[128,128]{1,0:T(8,128)S(1)} %fusion.71), custom_call_target="Cholesky" | custom-call | tf_op jit(solution)/shard_map/jit(cholesky)/cholesky | solution.py:46
  95.5 9.8 %custom-call.17 = f32[1,128,128]{1,2,0:T(8,128)S(1)} custom-call(f32[1,128,128]{2,1,0:T(8,128)S(1)} %get-tuple-element.48), custom_call_target="InvertDiagBlocksLowerTriangular" | custom-call | tf_op jit(solution)/shard_map/jit(_solve_triangular)/triangular_solve | solution.py:47
  115.3 12.2 %cholesky.160 = f32[128,128]{1,0:T(8,128)S(1)} custom-call(f32[128,128]{1,0:T(8,128)S(1)} %fusion.69), custom_call_target="Cholesky" | custom-call | tf_op jit(solution)/shard_map/jit(cholesky)/cholesky | solution.py:46
  128.9 9.8 %custom-call.18 = f32[1,128,128]{1,2,0:T(8,128)S(1)} custom-call(f32[1,128,128]{2,1,0:T(8,128)S(1)} %get-tuple-element.46), custom_call_target="InvertDiagBlocksLowerTriangular" | custom-call | tf_op jit(solution)/shard_map/jit(_solve_triangular)/triangular_solve | solution.py:47
  144.8 11.7 %cholesky.171 = f32[128,128]{1,0:T(8,128)S(1)} custom-call(f32[128,128]{1,0:T(8,128)S(1)} %fusion.67), custom_call_target="Cholesky" | custom-call | tf_op jit(solution)/shard_map/jit(cholesky)/cholesky | solution.py:46
  157.9 10.0 %custom-call.19 = f32[1,128,128]{1,2,0:T(8,128)S(1)} custom-call(f32[1,128,128]{2,1,0:T(8,128)S(1)} %get-tuple-element.44), custom_call_target="InvertDiagBlocksLowerTriangular" | custom-call | tf_op jit(solution)/shard_map/jit(_solve_triangular)/triangular_solve | solution.py:47
  173.5 11.7 %cholesky.182 = f32[128,128]{1,0:T(8,128)S(1)} custom-call(f32[128,128]{1,0:T(8,128)S(1)} %fusion.65), custom_call_target="Cholesky" | custom-call | tf_op jit(solution)/shard_map/jit(cholesky)/cholesky | solution.py:46
  187.2 9.8 %custom-call.20 = f32[1,128,128]{1,2,0:T(8,128)S(1)} custom-call(f32[1,128,128]{2,1,0:T(8,128)S(1)} %get-tuple-element.42), custom_call_target="InvertDiagBlocksLowerTriangular" | custom-call | tf_op jit(solution)/shard_map/jit(_solve_triangular)/triangular_solve | solution.py:47
  199.7 12.1 %cholesky.193 = f32[128,128]{1,0:T(8,128)S(1)} custom-call(f32[128,128]{1,0:T(8,128)S(1)} %fusion.63), custom_call_target="Cholesky" | custom-call | tf_op jit(solution)/shard_map/jit(cholesky)/cholesky | solution.py:46
  213.2 9.8 %custom-call.21 = f32[1,128,128]{1,2,0:T(8,128)S(1)} custom-call(f32[1,128,128]{2,1,0:T(8,128)S(1)} %get-tuple-element.40), custom_call_target="InvertDiagBlocksLowerTriangular" | custom-call | tf_op jit(solution)/shard_map/jit(_solve_triangular)/triangular_solve | solution.py:47
  225.2 11.7 %cholesky.204 = f32[128,128]{1,0:T(8,128)S(1)} custom-call(f32[128,128]{1,0:T(8,128)S(1)} %fusion.61), custom_call_target="Cholesky" | custom-call | tf_op jit(solution)/shard_map/jit(cholesky)/cholesky | solution.py:46
  238.3 9.8 %custom-call.22 = f32[1,128,128]{1,2,0:T(8,128)S(1)} custom-call(f32[1,128,128]{2,1,0:T(8,128)S(1)} %get-tuple-element.38), custom_call_target="InvertDiagBlocksLowerTriangular" | custom-call | tf_op jit(solution)/shard_map/jit(_solve_triangular)/triangular_solve | solution.py:47
  250.1 11.7 %cholesky.215 = f32[128,128]{1,0:T(8,128)S(1)} custom-call(f32[128,128]{1,0:T(8,128)S(1)} %fusion.59), custom_call_target="Cholesky" | custom-call | tf_op jit(solution)/shard_map/jit(cholesky)/cholesky | solution.py:46
  263.2 9.8 %custom-call.23 = f32[1,128,128]{1,2,0:T(8,128)S(1)} custom-call(f32[1,128,128]{2,1,0:T(8,128)S(1)} %get-tuple-element.36), custom_call_target="InvertDiagBlocksLowerTriangular" | custom-call | tf_op jit(solution)/shard_map/jit(_solve_triangular)/triangular_solve | solution.py:47
  274.6 11.7 %cholesky.226 = f32[128,128]{1,0:T(8,128)S(1)} custom-call(f32[128,128]{1,0:T(8,128)S(1)} %fusion.57), custom_call_target="Cholesky" | custom-call | tf_op jit(solution)/shard_map/jit(cholesky)/cholesky | solution.py:46
  317.5 9.8 %custom-call.24 = f32[1,128,128]{1,2,0:T(8,128)S(1)} custom-call(f32[1,128,128]{2,1,0:T(8,128)S(1)} %get-tuple-element.34), custom_call_target="InvertDiagBlocksLowerTriangular" | custom-call | tf_op jit(solution)/shard_map/jit(_solve_triangular)/triangular_solve | solution.py:47
  352.1 9.1 %reshape.506 = f32[4,2,128,1536]{2,1,0,3:T(2,128)} reshape(f32[1024,1536]{0,1:T(8,128)} %all-gather.10.cloned.1.call-done) | data formatting | bytes 12582912 | tf_op jit(solution)/shard_map/reshape | solution.py:33
  361.2 10.3 %copy.186 = f32[4,2,128,1536]{3,2,0,1:T(8,128)} copy(f32[4,2,128,1536]{2,1,0,3:T(2,128)} %reshape.506) | data formatting | bytes 12582912 | tf_op jit(solution)/shard_map/reshape | solution.py:33
  376.1 29.5 %fusion = f32[1024,3072]{1,0:T(8,128)} fusion(f32[1024,1536]{1,0:T(8,128)S(1)} %bitcast.266, f32[1024,1536]{1,0:T(8,128)S(1)} %bitcast.265, f32[1,512,512]{2,1,0:T(8,128)} %get-tuple-element.53, f32[1,512,512]{2,1,0:T(8,128)} %get-tuple-element.52, f32[1,512,512]{2,1,0:T(8,128)} %fusion.18), kind=kOutput, calls=%fused_computation.14 | convolution fusion | flops 19334692864 | bytes 28311552 | tf_op jit(solution)/shard_map/dot_general | solution.py:98
  405.7 24.8 %subtract_select_fusion = f32[1536,1536]{1,0:T(8,128)S(1)} fusion(f32[1024,3072]{1,0:T(8,128)} %fusion, pred[1536]{0:T(1024)(128)(4,1)S(1)} %copy-done.20, pred[1536]{0:T(1024)(128)(4,1)S(1)} %copy-done.16, f32[1,1536,1536]{2,1,0:T(8,128)S(1)} %bitcast.277), kind=kOutput, calls=%fused_computation.19 | convolution fusion | flops 14505738240 | bytes 31465472 | tf_op jit(solution)/shard_map/dot_general | solution.py:108
  443.5 10.2 %gather_fusion.2 = f32[1536,1024]{1,0:T(8,128)} fusion(f32[1024,1024]{1,0:T(8,128)} %pad_dynamic-update-slice_fusion, s32[2048]{0:T(1024)S(1)} %pad_clamp_fusion), kind=kCustom, calls=%fused_computation.10 | custom fusion | bytes 12589056 | tf_op jit(solution)/shard_map/jit(_take)/gather | solution.py:114
  487.2 7.9 %copy.192 = f32[8,128,16,128]{3,2,1,0:T(8,128)} copy(f32[8,128,16,128]{3,1,0,2:T(8,128)S(1)} %bitcast_select_fusion.1) | data formatting | bytes 16777216 | tf_op jit(solution)/shard_map/jit(_where)/select_n | solution.py:182
  495.1 19.3 %collective-permute-done = f32[5,128,1280]{1,2,0:T(8,128)} collective-permute-done((f32[5,128,1280]{1,2,0:T(8,128)}, f32[5,128,1280]{1,2,0:T(8,128)}, u32[]{:S(2)}, u32[]{:S(2)}) %collective-permute-start) | collective-permute-done | bytes 3276832 | tf_op jit(solution)/shard_map/ppermute | solution.py:28
  539.0 8.1 %copy.195 = f32[8,128,16,128]{3,2,1,0:T(8,128)} copy(f32[8,128,16,128]{3,1,0,2:T(8,128)S(1)} %bitcast_select_fusion) | data formatting | bytes 16777216 | tf_op jit(solution)/shard_map/jit(_where)/select_n | solution.py:182
  547.1 13.1 %bitcast_add_fusion = f32[1024,2048]{1,0:T(8,128)S(1)} fusion(f32[128,8,16,128]{3,2,1,0:T(8,128)} %bitcast.257, f32[1024,2048]{1,0:T(8,128)} %param.16, f32[128,8,16,128]{3,2,1,0:T(8,128)S(1)} %bitcast.256), kind=kLoop, calls=%fused_computation.20 | loop fusion | flops 4194304 | bytes 33554432 | tf_op jit(solution)/shard_map/add | solution.py:201
  568.7 8.8 %select_select_fusion = f32[1536,1024]{0,1:T(8,128)} fusion(f32[1536,1024]{0,1:T(8,128)} %copy.188, f32[1024,3072]{1,0:T(8,128)} %fusion, pred[1536]{0:T(1024)(128)(4,1)S(1)} %copy-done.15, pred[1536]{0:T(1024)(128)(4,1)S(1)} %copy-done.16), kind=kLoop, calls=%fused_computation.28 | loop fusion | flops 3145728 | bytes 18877440 | tf_op jit(solution)/shard_map/jit(_where)/select_n | solution.py:115
  587.9 10.1 %collective-permute-done.4 = f32[1024,128]{1,0:T(8,128)S(1)} collective-permute-done((f32[1024,128]{1,0:T(8,128)S(1)}, f32[1024,128]{1,0:T(8,128)S(1)}, u32[]{:S(2)}, u32[]{:S(2)}) %collective-permute-start.4) | collective-permute-done | bytes 524320 | tf_op jit(solution)/shard_map/ppermute | solution.py:28
  614.6 11.7 %cholesky.237 = f32[128,128]{1,0:T(8,128)S(1)} custom-call(f32[128,128]{1,0:T(8,128)S(1)} %copy.199), custom_call_target="Cholesky" | custom-call | tf_op jit(solution)/shard_map/jit(cholesky)/cholesky | solution.py:221
  627.6 9.8 %custom-call.25 = f32[1,128,128]{1,2,0:T(8,128)S(1)} custom-call(f32[1,128,128]{2,1,0:T(8,128)S(1)} %get-tuple-element.30), custom_call_target="InvertDiagBlocksLowerTriangular" | custom-call | tf_op jit(solution)/shard_map/jit(_solve_triangular)/triangular_solve | solution.py:223
  643.1 15.6 %collective-permute-done.8 = f32[2048,128]{1,0:T(8,128)} collective-permute-done((f32[2048,128]{1,0:T(8,128)}, f32[2048,128]{1,0:T(8,128)}, u32[]{:S(2)}, u32[]{:S(2)}) %collective-permute-start.8) | collective-permute-done | bytes 1048608 | tf_op jit(solution)/shard_map/ppermute | solution.py:219
  661.0 9.8 %subtract_select_fusion.1 = f32[1024,2048]{1,0:T(8,128)S(1)} fusion(f32[1024,2048]{1,0:T(8,128)} %copy-done, f32[2048,128]{1,0:T(8,128)S(1)} %convolution_select_fusion, pred[2048]{0:T(1024)(128)(4,1)S(1)} %copy-done.10, pred[1024]{0:T(1024)(128)(4,1)S(1)} %copy-done.17, f32[1024,128]{1,0:T(8,128)S(1)} %get-tuple-element.79), kind=kOutput, calls=%fused_computation.25 | convolution fusion | flops 3227648000 | bytes 18353152 | tf_op jit(solution)/shard_map/dot_general | solution.py:237
  (315 shorter events, 264.9 us)
Async XLA Ops:
  7.2 54.4 %all-gather.8.cloned.1.call-start = ((), (), s32[]{:S(2)}) async-start(), calls=%async_computation.1 | async-start | bytes 4456448 | tf_op jit(solution)/shard_map/all_gather | solution.py:83
  8.9 343.2 %all-gather.10.cloned.1.call-start = ((), (), s32[]{:S(2)}) async-start(), calls=%async_computation.2 | async-start | bytes 7864320 | tf_op jit(solution)/shard_map/all_gather | solution.py:93
  11.7 359.9 %all-gather.6.cloned.1.call-start = ((), (), s32[]{:S(2)}) async-start(), calls=%async_computation | async-start | bytes 7864320 | tf_op jit(solution)/shard_map/all_gather | solution.py:95
  18.2 49.1 %copy-start.30 = (s32[8]{0:T(128)}, s32[8]{0:T(128)S(1)}, u32[]{:S(2)}) copy-start(s32[8]{0:T(128)S(1)} %select_reduce_fusion.12) | copy-start | bytes 100
  18.3 49.0 %copy-start.33 = (s32[8]{0:T(128)}, s32[8]{0:T(128)S(1)}, u32[]{:S(2)}) copy-start(s32[8]{0:T(128)S(1)} %select_reduce_fusion.11) | copy-start | bytes 100
  20.5 46.8 %copy-start.23 = (s32[16]{0:T(128)}, s32[16]{0:T(128)S(1)}, u32[]{:S(2)}) copy-start(s32[16]{0:T(128)S(1)} %select_reduce_fusion.9) | copy-start | bytes 196
  21.3 46.0 %copy-start.25 = (s32[16]{0:T(128)}, s32[16]{0:T(128)S(1)}, u32[]{:S(2)}) copy-start(s32[16]{0:T(128)S(1)} %select_reduce_fusion.10) | copy-start | bytes 196
  199.6 89.5 %copy-start.7 = (f32[768,128]{1,0:T(8,128)S(1)}, f32[768,128]{1,0:T(8,128)}, u32[]{:S(2)}) copy-start(f32[768,128]{1,0:T(8,128)} %copy-done.6) | copy-start | bytes 1179652
  225.0 67.3 %copy-start.9 = (f32[128,128]{1,0:T(8,128)S(1)}, f32[128,128]{1,0:T(8,128)}, u32[]{:S(2)}) copy-start(f32[128,128]{1,0:T(8,128)} %get-tuple-element.43) | copy-start | bytes 196612
  225.0 67.2 %copy-start.12 = (f32[1024]{0:T(1024)S(1)}, f32[1024]{0:T(1024)}, u32[]{:S(2)}) copy-start(f32[1024]{0:T(1024)} %pad.31.clone) | copy-start | bytes 12292
  225.1 68.3 %copy-start.11 = (f32[1024]{0:T(1024)S(1)}, f32[1024]{0:T(1024)}, u32[]{:S(2)}) copy-start(f32[1024]{0:T(1024)} %pad.34.clone) | copy-start | bytes 12292
  334.7 8.3 %copy-start.8 = (f32[8,128,128]{2,1,0:T(8,128)S(1)}, f32[8,128,128]{2,1,0:T(8,128)}, u32[]{:S(2)}) copy-start(f32[8,128,128]{2,1,0:T(8,128)} %get-tuple-element.76) | copy-start | bytes 1572868
  371.5 34.1 %slice-start.3 = ((s8[9437184]{0:T(1024)(128)(4,1)}), s8[4194304]{0:T(1024)(128)(4,1)S(1)}, s32[]{:S(2)}) async-start(s8[9437184]{0:T(1024)(128)(4,1)} %bitcast.276), calls=%async_computation.6 | async-start | bytes 8388608
  376.1 29.5 %slice-start.4 = ((s8[9437184]{0:T(1024)(128)(4,1)}), s8[4194304]{0:T(1024)(128)(4,1)S(1)}, s32[]{:S(2)}) async-start(s8[9437184]{0:T(1024)(128)(4,1)} %bitcast.276), calls=%async_computation.7 | async-start | bytes 8388608
  376.1 29.5 %slice-start.5 = ((s8[9437184]{0:T(1024)(128)(4,1)}), s8[1048576]{0:T(1024)(128)(4,1)S(1)}, s32[]{:S(2)}) async-start(s8[9437184]{0:T(1024)(128)(4,1)} %bitcast.276), calls=%async_computation.8 | async-start | bytes 2097152
  376.1 29.5 %copy-start.16 = (pred[1536]{0:T(1024)(128)(4,1)S(1)}, pred[1536]{0:T(1024)(128)(4,1)}, u32[]{:S(2)}) copy-start(pred[1536]{0:T(1024)(128)(4,1)} %get-tuple-element.87) | copy-start | bytes 4612
  376.1 29.5 %copy-start.20 = (pred[1536]{0:T(1024)(128)(4,1)S(1)}, pred[1536]{0:T(1024)(128)(4,1)}, u32[]{:S(2)}) copy-start(pred[1536]{0:T(1024)(128)(4,1)} %broadcast_compare_fusion.2) | copy-start | bytes 4612
  441.0 73.4 %collective-permute-start = (f32[5,128,1280]{1,2,0:T(8,128)}, f32[5,128,1280]{1,2,0:T(8,128)}, u32[]{:S(2)}, u32[]{:S(2)}) collective-permute-start(f32[5,128,1280]{1,2,0:T(8,128)} %bitcast.267), channel_id=1, source_target_pairs={{0,16},{16,0},{1,17},{17,1},{2,18},{18,2},{3,19},{19,3},{4,20},{20... | collective-permute-start | bytes 9830408 | tf_op jit(solution)/shard_map/ppermute | solution.py:28
  534.6 12.5 %slice-start = ((s8[8388608]{0:T(1024)(128)(4,1)}), s8[4194304]{0:T(1024)(128)(4,1)S(1)}, s32[]{:S(2)}) async-start(s8[8388608]{0:T(1024)(128)(4,1)} %bitcast.254), calls=%async_computation.3 | async-start | bytes 8388608
  539.0 8.1 %slice-start.1 = ((s8[8388608]{0:T(1024)(128)(4,1)}), s8[4194304]{0:T(1024)(128)(4,1)S(1)}, s32[]{:S(2)}) async-start(s8[8388608]{0:T(1024)(128)(4,1)} %bitcast.254), calls=%async_computation.4 | async-start | bytes 8388608
  547.1 21.6 %copy-start.15 = (pred[1536]{0:T(1024)(128)(4,1)S(1)}, pred[1536]{0:T(1024)(128)(4,1)}, u32[]{:S(2)}) copy-start(pred[1536]{0:T(1024)(128)(4,1)} %get-tuple-element.86) | copy-start | bytes 4612
  564.5 18.5 %collective-permute-start.2 = (f32[1024,128]{1,0:T(8,128)}, f32[1024,128]{1,0:T(8,128)}, u32[]{:S(2)}, u32[]{:S(2)}) collective-permute-start(f32[1024,128]{1,0:T(8,128)} %slice.283), channel_id=1, source_target_pairs={{0,2},{4,6},{8,10},{12,14},{16,18},{20,22},{24,26},{28,30}} | collective-permute-start | bytes 1572872 | tf_op jit(solution)/shard_map/ppermute | solution.py:23
  565.8 17.2 %collective-permute-start.1 = (f32[1024,128]{1,0:T(8,128)}, f32[1024,128]{1,0:T(8,128)}, u32[]{:S(2)}, u32[]{:S(2)}) collective-permute-start(f32[1024,128]{1,0:T(8,128)} %slice.283), channel_id=1, source_target_pairs={{0,1},{4,5},{8,9},{12,13},{16,17},{20,21},{24,25},{28,29}} | collective-permute-start | bytes 1572872 | tf_op jit(solution)/shard_map/ppermute | solution.py:23
  567.3 15.7 %collective-permute-start.3 = (f32[1024,128]{1,0:T(8,128)}, f32[1024,128]{1,0:T(8,128)}, u32[]{:S(2)}, u32[]{:S(2)}) collective-permute-start(f32[1024,128]{1,0:T(8,128)} %slice.283), channel_id=1, source_target_pairs={{0,3},{4,7},{8,11},{12,15},{16,19},{20,23},{24,27},{28,31}} | collective-permute-start | bytes 1572872 | tf_op jit(solution)/shard_map/ppermute | solution.py:23
  584.6 13.4 %collective-permute-start.4 = (f32[1024,128]{1,0:T(8,128)S(1)}, f32[1024,128]{1,0:T(8,128)S(1)}, u32[]{:S(2)}, u32[]{:S(2)}) collective-permute-start(f32[1024,128]{1,0:T(8,128)S(1)} %add_add_fusion), channel_id=1, source_target_pairs={{0,16},{16,0},{1,17},{17,1},{2,18},{18,2},{3,19},{19,3},{4,20},{20... | collective-permute-start | bytes 1572872 | tf_op jit(solution)/shard_map/ppermute | solution.py:28
  586.1 20.2 %slice-start.2 = ((f32[1536,1536]{1,0:T(8,128)}), f32[1536,1280]{1,0:T(8,128)S(1)}, s32[]{:S(2)}) async-start(f32[1536,1536]{1,0:T(8,128)} %copy-done.1), calls=%async_computation.5 | async-start | bytes 15728640 | tf_op jit(solution)/shard_map/slice | solution.py:119
  600.1 13.4 %collective-permute-start.6 = (f32[128,128]{1,0:T(8,128)S(1)}, f32[128,128]{1,0:T(8,128)S(1)}, u32[]{:S(2)}, u32[]{:S(2)}) collective-permute-start(f32[128,128]{1,0:T(8,128)S(1)} %slice.284), channel_id=1, source_target_pairs={{0,8},{1,9},{2,10},{3,11},{16,24},{17,25},{18,26},{19,27}} | collective-permute-start | bytes 196616 | tf_op jit(solution)/shard_map/ppermute | solution.py:23
  603.7 9.8 %collective-permute-start.5 = (f32[128,128]{1,0:T(8,128)S(1)}, f32[128,128]{1,0:T(8,128)S(1)}, u32[]{:S(2)}, u32[]{:S(2)}) collective-permute-start(f32[128,128]{1,0:T(8,128)S(1)} %slice.284), channel_id=1, source_target_pairs={{0,4},{1,5},{2,6},{3,7},{16,20},{17,21},{18,22},{19,23}} | collective-permute-start | bytes 196616 | tf_op jit(solution)/shard_map/ppermute | solution.py:23
  605.0 8.5 %collective-permute-start.7 = (f32[128,128]{1,0:T(8,128)S(1)}, f32[128,128]{1,0:T(8,128)S(1)}, u32[]{:S(2)}, u32[]{:S(2)}) collective-permute-start(f32[128,128]{1,0:T(8,128)S(1)} %slice.284), channel_id=1, source_target_pairs={{0,12},{1,13},{2,14},{3,15},{16,28},{17,29},{18,30},{19,31}} | collective-permute-start | bytes 196616 | tf_op jit(solution)/shard_map/ppermute | solution.py:23
  611.2 29.5 %copy-start.17 = (pred[1024]{0:T(1024)(128)(4,1)S(1)}, pred[1024]{0:T(1024)(128)(4,1)}, u32[]{:S(2)}) copy-start(pred[1024]{0:T(1024)(128)(4,1)} %broadcast_compare_fusion.4) | copy-start | bytes 3076
  611.2 47.6 %collective-permute-start.8 = (f32[2048,128]{1,0:T(8,128)}, f32[2048,128]{1,0:T(8,128)}, u32[]{:S(2)}, u32[]{:S(2)}) collective-permute-start(f32[2048,128]{1,0:T(8,128)} %bitcast.73), channel_id=1, source_target_pairs={{0,0},{4,1},{8,2},{12,3},{1,4},{5,5},{9,6},{13,7},{2,8},{6,9},{10,... | collective-permute-start | bytes 3145736 | tf_op jit(solution)/shard_map/ppermute | solution.py:219
  640.8 18.0 %copy-start.10 = (pred[2048]{0:T(1024)(128)(4,1)S(1)}, pred[2048]{0:T(1024)(128)(4,1)}, u32[]{:S(2)}) copy-start(pred[2048]{0:T(1024)(128)(4,1)} %broadcast_compare_fusion) | copy-start | bytes 6148
  (21 other events, 103.7 us)
Sparse Core Ops, SparseCore 0:
  10.7 50.8 all-gather.7
  63.2 44.6 all-gather.9
  109.4 116.5 all-gather.5

commit v10 on v9

--- a/solution.py
+++ b/solution.py
@@ -90,16 +90,19 @@
         diag_inverse = jnp.tril(jax.scipy.linalg.solve_triangular(diag_factor, eye, lower=True))
     else:
         diag_inverse = lower_inverse(diag_factor, block_inverses)
-    col_pieces = lax.all_gather(front_work[:, :width].T, "col", axis=0)
+    skip = width if tile_count % grid_size == 0 else 0
+    kept_count = local_count - skip
+    col_pieces = lax.all_gather(front_work[skip:, :width].T, "col", axis=0)
     panel_rows = pivot_order(col_pieces, slot_count, tile_count)
-    row_pieces = lax.all_gather(front_work[:width, :], "row", axis=0)
+    row_pieces = lax.all_gather(front_work[:width, skip:], "row", axis=0)
     panel_cols = pivot_order(row_pieces, slot_count, tile_count)
     both = jnp.concatenate([panel_rows, panel_cols], axis=1)
     solved = jnp.dot(
         diag_inverse, both, precision=lax.Precision.HIGH, preferred_element_type=jnp.float32
     )
-    solved_rows = solved[:, :local_count].T
-    solved_cols = solved[:, local_count:].T
+    lead = jnp.zeros((skip, pivot_count), jnp.float32)
+    solved_rows = jnp.concatenate([lead, solved[:, :kept_count].T])
+    solved_cols = jnp.concatenate([lead, solved[:, kept_count:].T])
     within = jnp.arange(local_count, dtype=jnp.int32)
     row_index = within // TILE * grid_size * TILE + my_row * TILE + within % TILE
     col_index = within // TILE * grid_size * TILE + my_col * TILE + within % TILE

time: 689 us -> 688 us (level)
  matrix products: 98.7 us -> 90.8 us
    reshape x2 -> x3, local copies, waits for them, and re-layouts: 19.4 us -> 22.4 us  [pivot_order(): shaped = pieces.reshape((group_count, slot_count, TILE) + rest)]
    unnamed x81 -> x83, local copies, waits for them, and re-layouts: 12.8 us -> 14.2 us
  transfers between devices with their start and end apart: 12 -> 12, of which waited for: 4 -> 4; matrix products, arithmetic and copies ran while one was open for 63% -> 57% of each run, Pallas kernels for 0% -> 0%
where the time goes in v10:
time: 688 us; the launch traced here: 682 us
  other arithmetic  287 us (42%)
  local copies, waits for them, and re-layouts  194 us (28%)
  matrix products  90.8 us (13%)
  waiting for transfers between devices  78.2 us (11%)
  starting transfers between devices  16.3 us (2%)
  between operations  15.3 us (2%)
    another operation x24, other arithmetic, factor_pivots(): factor = jnp.tril(jnp.linalg.cholesky(work[:TILE, :TILE]))  100 us
    another operation x16, other arithmetic, factor_pivots(): jax.scipy.linalg.solve_triangular(factor, eye, lower=True)  84.8 us
    all_gather x1, waiting for transfers between devices, factor_child(): lax.all_gather(front_work[:width, :width], ('row', 'col'), axis=0)  31.7 us
    ppermute x2, waiting for transfers between devices, from_partner(): lax.ppermute(shard, axis, [(i, i ^ 1 << distance) for i in range(lax.axis...  30.4 us
    reshape x5, local copies, waits for them, and re-layouts, lower_inverse(): factor.reshape(pairs, 2, size, pairs, 2, size)[picks, 1, :, picks, 0, :]  27.9 us
    dot_general x1, matrix products, factor_child(): jnp.dot(diag_inverse, both, precision=lax.Precision.HIGH, preferred_eleme...  24.6 us
    reshape x3, local copies, waits for them, and re-layouts, pivot_order(): shaped = pieces.reshape((group_count, slot_count, TILE) + rest)  22.4 us
    dot_general x1, matrix products, factor_child(): jnp.dot(jnp.where(rows_after, solved_rows, 0.0), jnp.where(cols_after.T,...  22.3 us
  transfers between devices with their start and end apart: 12, of which 4 were waited for; matrix products, arithmetic and copies ran while one was open for 57% of the time, Pallas kernels for 0%

profile of v10, /device:TPU:4, one launch (start us, length us, event | category | flops | bytes accessed | tf_op | source)
XLA Modules:
  0.0 682.1 jit_solution(5081770277346305924)
XLA Ops:
  30.1 31.7 %all-gather.7.cloned.1.call-done = f32[4096,256]{1,0:T(8,128)} async-done(((f32[256,256]{1,0:T(8,128)}), f32[4096,256]{1,0:T(8,128)}) %all-gather.7.cloned.1.call-update) | async-done | bytes 4194320 | tf_op jit(solution)/shard_map/all_gather | solution.py:83
  67.5 7.4 %copy.115 = f32[4,4,2,128,2,128]{3,0,2,5,1,4:T(4,128)} copy(f32[4,4,2,128,2,128]{5,4,3,2,1,0:T(2,128)} %reshape.493) | data formatting | bytes 8388608 | tf_op jit(solution)/shard_map/reshape | solution.py:84
  82.4 11.7 %cholesky.149 = f32[128,128]{1,0:T(8,128)S(1)} custom-call(f32[128,128]{1,0:T(8,128)S(1)} %fusion.71), custom_call_target="Cholesky" | custom-call | tf_op jit(solution)/shard_map/jit(cholesky)/cholesky | solution.py:46
  95.5 9.8 %custom-call.17 = f32[1,128,128]{1,2,0:T(8,128)S(1)} custom-call(f32[1,128,128]{2,1,0:T(8,128)S(1)} %get-tuple-element.48), custom_call_target="InvertDiagBlocksLowerTriangular" | custom-call | tf_op jit(solution)/shard_map/jit(_solve_triangular)/triangular_solve | solution.py:47
  115.4 12.2 %cholesky.160 = f32[128,128]{1,0:T(8,128)S(1)} custom-call(f32[128,128]{1,0:T(8,128)S(1)} %fusion.69), custom_call_target="Cholesky" | custom-call | tf_op jit(solution)/shard_map/jit(cholesky)/cholesky | solution.py:46
  128.9 9.8 %custom-call.18 = f32[1,128,128]{1,2,0:T(8,128)S(1)} custom-call(f32[1,128,128]{2,1,0:T(8,128)S(1)} %get-tuple-element.46), custom_call_target="InvertDiagBlocksLowerTriangular" | custom-call | tf_op jit(solution)/shard_map/jit(_solve_triangular)/triangular_solve | solution.py:47
  144.9 11.7 %cholesky.171 = f32[128,128]{1,0:T(8,128)S(1)} custom-call(f32[128,128]{1,0:T(8,128)S(1)} %fusion.67), custom_call_target="Cholesky" | custom-call | tf_op jit(solution)/shard_map/jit(cholesky)/cholesky | solution.py:46
  158.1 10.0 %custom-call.19 = f32[1,128,128]{1,2,0:T(8,128)S(1)} custom-call(f32[1,128,128]{2,1,0:T(8,128)S(1)} %get-tuple-element.44), custom_call_target="InvertDiagBlocksLowerTriangular" | custom-call | tf_op jit(solution)/shard_map/jit(_solve_triangular)/triangular_solve | solution.py:47
  173.8 11.7 %cholesky.182 = f32[128,128]{1,0:T(8,128)S(1)} custom-call(f32[128,128]{1,0:T(8,128)S(1)} %fusion.65), custom_call_target="Cholesky" | custom-call | tf_op jit(solution)/shard_map/jit(cholesky)/cholesky | solution.py:46
  187.6 9.8 %custom-call.20 = f32[1,128,128]{1,2,0:T(8,128)S(1)} custom-call(f32[1,128,128]{2,1,0:T(8,128)S(1)} %get-tuple-element.42), custom_call_target="InvertDiagBlocksLowerTriangular" | custom-call | tf_op jit(solution)/shard_map/jit(_solve_triangular)/triangular_solve | solution.py:47
  200.1 11.9 %cholesky.193 = f32[128,128]{1,0:T(8,128)S(1)} custom-call(f32[128,128]{1,0:T(8,128)S(1)} %fusion.63), custom_call_target="Cholesky" | custom-call | tf_op jit(solution)/shard_map/jit(cholesky)/cholesky | solution.py:46
  213.5 9.8 %custom-call.21 = f32[1,128,128]{1,2,0:T(8,128)S(1)} custom-call(f32[1,128,128]{2,1,0:T(8,128)S(1)} %get-tuple-element.40), custom_call_target="InvertDiagBlocksLowerTriangular" | custom-call | tf_op jit(solution)/shard_map/jit(_solve_triangular)/triangular_solve | solution.py:47
  225.5 11.7 %cholesky.204 = f32[128,128]{1,0:T(8,128)S(1)} custom-call(f32[128,128]{1,0:T(8,128)S(1)} %fusion.61), custom_call_target="Cholesky" | custom-call | tf_op jit(solution)/shard_map/jit(cholesky)/cholesky | solution.py:46
  238.7 9.8 %custom-call.22 = f32[1,128,128]{1,2,0:T(8,128)S(1)} custom-call(f32[1,128,128]{2,1,0:T(8,128)S(1)} %get-tuple-element.38), custom_call_target="InvertDiagBlocksLowerTriangular" | custom-call | tf_op jit(solution)/shard_map/jit(_solve_triangular)/triangular_solve | solution.py:47
  250.7 11.7 %cholesky.215 = f32[128,128]{1,0:T(8,128)S(1)} custom-call(f32[128,128]{1,0:T(8,128)S(1)} %fusion.59), custom_call_target="Cholesky" | custom-call | tf_op jit(solution)/shard_map/jit(cholesky)/cholesky | solution.py:46
  263.9 9.8 %custom-call.23 = f32[1,128,128]{1,2,0:T(8,128)S(1)} custom-call(f32[1,128,128]{2,1,0:T(8,128)S(1)} %get-tuple-element.36), custom_call_target="InvertDiagBlocksLowerTriangular" | custom-call | tf_op jit(solution)/shard_map/jit(_solve_triangular)/triangular_solve | solution.py:47
  275.3 11.7 %cholesky.226 = f32[128,128]{1,0:T(8,128)S(1)} custom-call(f32[128,128]{1,0:T(8,128)S(1)} %fusion.57), custom_call_target="Cholesky" | custom-call | tf_op jit(solution)/shard_map/jit(cholesky)/cholesky | solution.py:46
  318.1 9.8 %custom-call.24 = f32[1,128,128]{1,2,0:T(8,128)S(1)} custom-call(f32[1,128,128]{2,1,0:T(8,128)S(1)} %get-tuple-element.34), custom_call_target="InvertDiagBlocksLowerTriangular" | custom-call | tf_op jit(solution)/shard_map/jit(_solve_triangular)/triangular_solve | solution.py:47
  333.7 8.1 %reshape.504 = f32[4,2,128,1280]{2,1,0,3:T(2,128)} reshape(f32[1024,1280]{0,1:T(8,128)} %all-gather.9.cloned.1.call-done) | data formatting | bytes 10485760 | tf_op jit(solution)/shard_map/reshape | solution.py:33
  341.8 9.0 %copy.143 = f32[4,2,128,1280]{3,2,0,1:T(8,128)} copy(f32[4,2,128,1280]{2,1,0,3:T(2,128)} %reshape.504) | data formatting | bytes 10485760 | tf_op jit(solution)/shard_map/reshape | solution.py:33
  376.0 24.6 %fusion = f32[1024,2560]{1,0:T(8,128)} fusion(f32[1024,1280]{1,0:T(8,128)S(1)} %bitcast.266, f32[1024,1280]{1,0:T(8,128)} %bitcast.267, f32[1,512,512]{2,1,0:T(8,128)} %get-tuple-element.55, f32[1,512,512]{2,1,0:T(8,128)S(1)} %get-tuple-element.54, f32[1,512,512]{2,1,0:T(8,128)S(1)} %fusion.18), kind=kOutput, calls=%fused_computation.14 | convolution fusion | flops 16112943104 | bytes 24117248 | tf_op jit(solution)/shard_map/dot_general | solution.py:100
  407.6 22.3 %subtract_select_fusion = f32[1536,1536]{1,0:T(8,128)S(1)} fusion(f32[1280,1024]{0,1:T(8,128)S(1)} %get-tuple-element.51, f32[1280,1024]{0,1:T(8,128)S(1)} %get-tuple-element.50, pred[1536]{0:T(1024)(128)(4,1)S(1)} %copy-done.20, pred[1536]{0:T(1024)(128)(4,1)S(1)} %copy-done.16, f32[1,1536,1536]{2,1,0:T(8,128)} %param.14), kind=kOutput, calls=%fused_computation.19 | convolution fusion | flops 14505738240 | bytes 29363200 | tf_op jit(solution)/shard_map/dot_general | solution.py:111
  443.0 10.0 %gather_fusion.2 = f32[1536,1024]{1,0:T(8,128)} fusion(f32[1024,1024]{1,0:T(8,128)} %pad_dynamic-update-slice_fusion, s32[2048]{0:T(1024)S(1)} %pad_clamp_fusion), kind=kCustom, calls=%fused_computation.10 | custom fusion | bytes 12589056 | tf_op jit(solution)/shard_map/jit(_take)/gather | solution.py:117
  486.5 8.0 %copy.149 = f32[8,128,16,128]{3,2,1,0:T(8,128)} copy(f32[8,128,16,128]{3,1,0,2:T(8,128)S(1)} %bitcast_select_fusion.1) | data formatting | bytes 16777216 | tf_op jit(solution)/shard_map/jit(_where)/select_n | solution.py:185
  494.6 19.3 %collective-permute-done = f32[5,128,1280]{1,2,0:T(8,128)} collective-permute-done((f32[5,128,1280]{1,2,0:T(8,128)}, f32[5,128,1280]{1,2,0:T(8,128)}, u32[]{:S(2)}, u32[]{:S(2)}) %collective-permute-start) | collective-permute-done | bytes 3276832 | tf_op jit(solution)/shard_map/ppermute | solution.py:28
  538.3 8.1 %copy.152 = f32[8,128,16,128]{3,2,1,0:T(8,128)} copy(f32[8,128,16,128]{3,1,0,2:T(8,128)S(1)} %bitcast_select_fusion) | data formatting | bytes 16777216 | tf_op jit(solution)/shard_map/jit(_where)/select_n | solution.py:185
  546.4 13.1 %bitcast_add_fusion = f32[1024,2048]{1,0:T(8,128)S(1)} fusion(f32[128,8,16,128]{3,2,1,0:T(8,128)} %bitcast.254, f32[1024,2048]{1,0:T(8,128)} %param.16, f32[128,8,16,128]{3,2,1,0:T(8,128)S(1)} %bitcast.253), kind=kLoop, calls=%fused_computation.20 | loop fusion | flops 4194304 | bytes 33554432 | tf_op jit(solution)/shard_map/add | solution.py:204
  585.0 11.2 %collective-permute-done.4 = f32[1024,128]{1,0:T(8,128)S(1)} collective-permute-done((f32[1024,128]{1,0:T(8,128)S(1)}, f32[1024,128]{1,0:T(8,128)S(1)}, u32[]{:S(2)}, u32[]{:S(2)}) %collective-permute-start.4) | collective-permute-done | bytes 524320 | tf_op jit(solution)/shard_map/ppermute | solution.py:28
  613.2 11.7 %cholesky.237 = f32[128,128]{1,0:T(8,128)S(1)} custom-call(f32[128,128]{1,0:T(8,128)S(1)} %copy.156), custom_call_target="Cholesky" | custom-call | tf_op jit(solution)/shard_map/jit(cholesky)/cholesky | solution.py:224
  626.3 9.8 %custom-call.25 = f32[1,128,128]{1,2,0:T(8,128)S(1)} custom-call(f32[1,128,128]{2,1,0:T(8,128)S(1)} %get-tuple-element.30), custom_call_target="InvertDiagBlocksLowerTriangular" | custom-call | tf_op jit(solution)/shard_map/jit(_solve_triangular)/triangular_solve | solution.py:226
  641.9 16.0 %collective-permute-done.8 = f32[2048,128]{1,0:T(8,128)} collective-permute-done((f32[2048,128]{1,0:T(8,128)}, f32[2048,128]{1,0:T(8,128)}, u32[]{:S(2)}, u32[]{:S(2)}) %collective-permute-start.8) | collective-permute-done | bytes 1048608 | tf_op jit(solution)/shard_map/ppermute | solution.py:222
  660.1 9.8 %subtract_select_fusion.1 = f32[1024,2048]{1,0:T(8,128)S(1)} fusion(f32[1024,2048]{1,0:T(8,128)} %copy-done, f32[2048,128]{1,0:T(8,128)S(1)} %convolution_select_fusion, pred[2048]{0:T(1024)(128)(4,1)S(1)} %copy-done.10, pred[1024]{0:T(1024)(128)(4,1)S(1)} %copy-done.17, f32[1024,128]{1,0:T(8,128)S(1)} %get-tuple-element.81), kind=kOutput, calls=%fused_computation.25 | convolution fusion | flops 3227648000 | bytes 18353152 | tf_op jit(solution)/shard_map/dot_general | solution.py:240
  (319 shorter events, 273.8 us)
Async XLA Ops:
  7.2 54.6 %all-gather.7.cloned.1.call-start = ((), (), s32[]{:S(2)}) async-start(), calls=%async_computation | async-start | bytes 4456448 | tf_op jit(solution)/shard_map/all_gather | solution.py:83
  8.9 7.5 %copy-start.27 = (s32[2,40]{1,0:T(2,128)S(1)}, s32[2,40]{1,0:T(2,128)}, u32[]{:S(2)}) copy-start(s32[2,40]{1,0:T(2,128)} %param.15) | copy-start | bytes 964
  8.9 319.1 %all-gather.11.cloned.1.call-start = ((), (), s32[]{:S(2)}) async-start(), calls=%async_computation.2 | async-start | bytes 6553600 | tf_op jit(solution)/shard_map/all_gather | solution.py:97
  11.4 322.2 %all-gather.9.cloned.1.call-start = ((), (), s32[]{:S(2)}) async-start(), calls=%async_computation.1 | async-start | bytes 6553600 | tf_op jit(solution)/shard_map/all_gather | solution.py:95
  17.9 49.6 %copy-start.30 = (s32[8]{0:T(128)}, s32[8]{0:T(128)S(1)}, u32[]{:S(2)}) copy-start(s32[8]{0:T(128)S(1)} %select_reduce_fusion.12) | copy-start | bytes 100
  18.0 49.5 %copy-start.33 = (s32[8]{0:T(128)}, s32[8]{0:T(128)S(1)}, u32[]{:S(2)}) copy-start(s32[8]{0:T(128)S(1)} %select_reduce_fusion.11) | copy-start | bytes 100
  20.2 47.3 %copy-start.23 = (s32[16]{0:T(128)}, s32[16]{0:T(128)S(1)}, u32[]{:S(2)}) copy-start(s32[16]{0:T(128)S(1)} %select_reduce_fusion.9) | copy-start | bytes 196
  21.0 46.5 %copy-start.25 = (s32[16]{0:T(128)}, s32[16]{0:T(128)S(1)}, u32[]{:S(2)}) copy-start(s32[16]{0:T(128)S(1)} %select_reduce_fusion.10) | copy-start | bytes 196
  199.9 89.7 %copy-start.7 = (f32[768,128]{1,0:T(8,128)S(1)}, f32[768,128]{1,0:T(8,128)}, u32[]{:S(2)}) copy-start(f32[768,128]{1,0:T(8,128)} %copy-done.6) | copy-start | bytes 1179652
  225.3 67.7 %copy-start.9 = (f32[128,128]{1,0:T(8,128)S(1)}, f32[128,128]{1,0:T(8,128)}, u32[]{:S(2)}) copy-start(f32[128,128]{1,0:T(8,128)} %get-tuple-element.43) | copy-start | bytes 196612
  225.3 67.6 %copy-start.12 = (f32[1024]{0:T(1024)S(1)}, f32[1024]{0:T(1024)}, u32[]{:S(2)}) copy-start(f32[1024]{0:T(1024)} %pad.33.clone) | copy-start | bytes 12292
  225.4 68.7 %copy-start.11 = (f32[1024]{0:T(1024)S(1)}, f32[1024]{0:T(1024)}, u32[]{:S(2)}) copy-start(f32[1024]{0:T(1024)} %pad.36.clone) | copy-start | bytes 12292
  400.5 7.1 %copy-start.16 = (pred[1536]{0:T(1024)(128)(4,1)S(1)}, pred[1536]{0:T(1024)(128)(4,1)}, u32[]{:S(2)}) copy-start(pred[1536]{0:T(1024)(128)(4,1)} %get-tuple-element.89) | copy-start | bytes 4612
  400.5 7.1 %copy-start.20 = (pred[1536]{0:T(1024)(128)(4,1)S(1)}, pred[1536]{0:T(1024)(128)(4,1)}, u32[]{:S(2)}) copy-start(pred[1536]{0:T(1024)(128)(4,1)} %broadcast_compare_fusion.2) | copy-start | bytes 4612
  435.9 7.1 %copy-start.13 = (s32[1024,1]{0,1:T(1,128)S(1)}, s32[1024,1]{0,1:T(1,128)}, u32[]{:S(2)}) copy-start(s32[1024,1]{0,1:T(1,128)} %compare_select_fusion.1) | copy-start | bytes 12292
  440.4 73.4 %collective-permute-start = (f32[5,128,1280]{1,2,0:T(8,128)}, f32[5,128,1280]{1,2,0:T(8,128)}, u32[]{:S(2)}, u32[]{:S(2)}) collective-permute-start(f32[5,128,1280]{1,2,0:T(8,128)} %bitcast.268), channel_id=1, source_target_pairs={{0,16},{16,0},{1,17},{17,1},{2,18},{18,2},{3,19},{19,3},{4,20},{20... | collective-permute-start | bytes 9830408 | tf_op jit(solution)/shard_map/ppermute | solution.py:28
  533.9 12.5 %slice-start = ((s8[8388608]{0:T(1024)(128)(4,1)}), s8[4194304]{0:T(1024)(128)(4,1)S(1)}, s32[]{:S(2)}) async-start(s8[8388608]{0:T(1024)(128)(4,1)} %bitcast.251), calls=%async_computation.3 | async-start | bytes 8388608
  538.2 8.2 %slice-start.1 = ((s8[8388608]{0:T(1024)(128)(4,1)}), s8[4194304]{0:T(1024)(128)(4,1)S(1)}, s32[]{:S(2)}) async-start(s8[8388608]{0:T(1024)(128)(4,1)} %bitcast.251), calls=%async_computation.4 | async-start | bytes 8388608
  538.3 29.8 %slice-start.3 = ((s8[5242880]{0:T(1024)(128)(4,1)}), s8[4194304]{0:T(1024)(128)(4,1)S(1)}, s32[]{:S(2)}) async-start(s8[5242880]{0:T(1024)(128)(4,1)} %bitcast.256), calls=%async_computation.6 | async-start | bytes 8388608
  546.4 21.7 %slice-start.4 = ((s8[5242880]{0:T(1024)(128)(4,1)}), s8[1048576]{0:T(1024)(128)(4,1)S(1)}, s32[]{:S(2)}) async-start(s8[5242880]{0:T(1024)(128)(4,1)} %bitcast.256), calls=%async_computation.7 | async-start | bytes 2097152
  546.4 21.7 %copy-start.15 = (pred[1536]{0:T(1024)(128)(4,1)S(1)}, pred[1536]{0:T(1024)(128)(4,1)}, u32[]{:S(2)}) copy-start(pred[1536]{0:T(1024)(128)(4,1)} %get-tuple-element.88) | copy-start | bytes 4612
  563.8 16.2 %collective-permute-start.2 = (f32[1024,128]{1,0:T(8,128)}, f32[1024,128]{1,0:T(8,128)}, u32[]{:S(2)}, u32[]{:S(2)}) collective-permute-start(f32[1024,128]{1,0:T(8,128)} %slice.283), channel_id=1, source_target_pairs={{0,2},{4,6},{8,10},{12,14},{16,18},{20,22},{24,26},{28,30}} | collective-permute-start | bytes 1572872 | tf_op jit(solution)/shard_map/ppermute | solution.py:23
  565.1 14.9 %collective-permute-start.1 = (f32[1024,128]{1,0:T(8,128)}, f32[1024,128]{1,0:T(8,128)}, u32[]{:S(2)}, u32[]{:S(2)}) collective-permute-start(f32[1024,128]{1,0:T(8,128)} %slice.283), channel_id=1, source_target_pairs={{0,1},{4,5},{8,9},{12,13},{16,17},{20,21},{24,25},{28,29}} | collective-permute-start | bytes 1572872 | tf_op jit(solution)/shard_map/ppermute | solution.py:23
  566.6 13.5 %collective-permute-start.3 = (f32[1024,128]{1,0:T(8,128)}, f32[1024,128]{1,0:T(8,128)}, u32[]{:S(2)}, u32[]{:S(2)}) collective-permute-start(f32[1024,128]{1,0:T(8,128)} %slice.283), channel_id=1, source_target_pairs={{0,3},{4,7},{8,11},{12,15},{16,19},{20,23},{24,27},{28,31}} | collective-permute-start | bytes 1572872 | tf_op jit(solution)/shard_map/ppermute | solution.py:23
  581.7 14.5 %collective-permute-start.4 = (f32[1024,128]{1,0:T(8,128)S(1)}, f32[1024,128]{1,0:T(8,128)S(1)}, u32[]{:S(2)}, u32[]{:S(2)}) collective-permute-start(f32[1024,128]{1,0:T(8,128)S(1)} %add_add_fusion), channel_id=1, source_target_pairs={{0,16},{16,0},{1,17},{17,1},{2,18},{18,2},{3,19},{19,3},{4,20},{20... | collective-permute-start | bytes 1572872 | tf_op jit(solution)/shard_map/ppermute | solution.py:28
  583.2 21.6 %slice-start.2 = ((f32[1536,1536]{1,0:T(8,128)}), f32[1536,1280]{1,0:T(8,128)S(1)}, s32[]{:S(2)}) async-start(f32[1536,1536]{1,0:T(8,128)} %copy-done.1), calls=%async_computation.5 | async-start | bytes 15728640 | tf_op jit(solution)/shard_map/slice | solution.py:122
  598.2 13.9 %collective-permute-start.6 = (f32[128,128]{1,0:T(8,128)S(1)}, f32[128,128]{1,0:T(8,128)S(1)}, u32[]{:S(2)}, u32[]{:S(2)}) collective-permute-start(f32[128,128]{1,0:T(8,128)S(1)} %slice.284), channel_id=1, source_target_pairs={{0,8},{1,9},{2,10},{3,11},{16,24},{17,25},{18,26},{19,27}} | collective-permute-start | bytes 196616 | tf_op jit(solution)/shard_map/ppermute | solution.py:23
  602.2 9.8 %collective-permute-start.5 = (f32[128,128]{1,0:T(8,128)S(1)}, f32[128,128]{1,0:T(8,128)S(1)}, u32[]{:S(2)}, u32[]{:S(2)}) collective-permute-start(f32[128,128]{1,0:T(8,128)S(1)} %slice.284), channel_id=1, source_target_pairs={{0,4},{1,5},{2,6},{3,7},{16,20},{17,21},{18,22},{19,23}} | collective-permute-start | bytes 196616 | tf_op jit(solution)/shard_map/ppermute | solution.py:23
  603.5 8.5 %collective-permute-start.7 = (f32[128,128]{1,0:T(8,128)S(1)}, f32[128,128]{1,0:T(8,128)S(1)}, u32[]{:S(2)}, u32[]{:S(2)}) collective-permute-start(f32[128,128]{1,0:T(8,128)S(1)} %slice.284), channel_id=1, source_target_pairs={{0,12},{1,13},{2,14},{3,15},{16,28},{17,29},{18,30},{19,31}} | collective-permute-start | bytes 196616 | tf_op jit(solution)/shard_map/ppermute | solution.py:23
  609.8 29.7 %copy-start.17 = (pred[1024]{0:T(1024)(128)(4,1)S(1)}, pred[1024]{0:T(1024)(128)(4,1)}, u32[]{:S(2)}) copy-start(pred[1024]{0:T(1024)(128)(4,1)} %broadcast_compare_fusion.4) | copy-start | bytes 3076
  609.8 48.1 %collective-permute-start.8 = (f32[2048,128]{1,0:T(8,128)}, f32[2048,128]{1,0:T(8,128)}, u32[]{:S(2)}, u32[]{:S(2)}) collective-permute-start(f32[2048,128]{1,0:T(8,128)} %bitcast.74), channel_id=1, source_target_pairs={{0,0},{4,1},{8,2},{12,3},{1,4},{5,5},{9,6},{13,7},{2,8},{6,9},{10,... | collective-permute-start | bytes 3145736 | tf_op jit(solution)/shard_map/ppermute | solution.py:222
  639.5 18.4 %copy-start.10 = (pred[2048]{0:T(1024)(128)(4,1)S(1)}, pred[2048]{0:T(1024)(128)(4,1)}, u32[]{:S(2)}) copy-start(pred[2048]{0:T(1024)(128)(4,1)} %broadcast_compare_fusion) | copy-start | bytes 6148
  (22 other events, 102.3 us)
Sparse Core Ops, SparseCore 0:
  10.7 50.9 all-gather.6
  63.3 97.6 all-gather.10
  162.6 37.6 all-gather.8

commit v11 on v10

--- a/solution.py
+++ b/solution.py
@@ -64,8 +64,12 @@
         pairs = order // size // 2
         halves = inverse.reshape(pairs, 2, size, size)
         first, second = halves[:, 0], halves[:, 1]
-        picks = jnp.arange(pairs)
-        lower = factor.reshape(pairs, 2, size, pairs, 2, size)[picks, 1, :, picks, 0, :]
+        lower = jnp.stack(
+            [
+                factor[(2 * pair + 1) * size : (2 * pair + 2) * size, 2 * pair * size : (2 * pair + 1) * size]
+                for pair in range(pairs)
+            ]
+        )
         mixed = jnp.einsum("kab,kbc->kac", second, lower, precision=lax.Precision.HIGHEST)
         mixed = -jnp.einsum("kab,kbc->kac", mixed, first, precision=lax.Precision.HIGHEST)
         top = jnp.concatenate([first, jnp.zeros_like(first)], axis=2)
@@ -96,13 +100,27 @@
     panel_rows = pivot_order(col_pieces, slot_count, tile_count)
     row_pieces = lax.all_gather(front_work[:width, skip:], "row", axis=0)
     panel_cols = pivot_order(row_pieces, slot_count, tile_count)
-    both = jnp.concatenate([panel_rows, panel_cols], axis=1)
-    solved = jnp.dot(
-        diag_inverse, both, precision=lax.Precision.HIGH, preferred_element_type=jnp.float32
-    )
+    if slot_count * grid_size == tile_count:
+        gathered_inverse = diag_inverse.reshape(pivot_count, slot_count, grid_size, TILE)
+        gathered_inverse = gathered_inverse.swapaxes(1, 2).reshape(pivot_count, pivot_count)
+        solved_by_rows = jnp.dot(
+            gathered_inverse, col_pieces.reshape(pivot_count, kept_count),
+            precision=lax.Precision.HIGH, preferred_element_type=jnp.float32,
+        )
+        solved_by_cols = jnp.dot(
+            gathered_inverse, row_pieces.reshape(pivot_count, kept_count),
+            precision=lax.Precision.HIGH, preferred_element_type=jnp.float32,
+        )
+    else:
+        both = jnp.concatenate([panel_rows, panel_cols], axis=1)
+        solved = jnp.dot(
+            diag_inverse, both, precision=lax.Precision.HIGH, preferred_element_type=jnp.float32
+        )
+        solved_by_rows = solved[:, :kept_count]
+        solved_by_cols = solved[:, kept_count:]
     lead = jnp.zeros((skip, pivot_count), jnp.float32)
-    solved_rows = jnp.concatenate([lead, solved[:, :kept_count].T])
-    solved_cols = jnp.concatenate([lead, solved[:, kept_count:].T])
+    solved_rows = jnp.concatenate([lead, solved_by_rows.T])
+    solved_cols = jnp.concatenate([lead, solved_by_cols.T])
     within = jnp.arange(local_count, dtype=jnp.int32)
     row_index = within // TILE * grid_size * TILE + my_row * TILE + within % TILE
     col_index = within // TILE * grid_size * TILE + my_col * TILE + within % TILE

time: 688 us -> 638 us (0.927)
  local copies, waits for them, and re-layouts: 194 us -> 140 us
  waiting for transfers between devices: 78.2 us -> 65.8 us
  matrix products: 90.8 us -> 101 us
  other arithmetic: 287 us -> 295 us
    reshape x8 -> x0, local copies, waits for them, and re-layouts: 50.3 us -> none  [the longest x5 27.9 us: lower_inverse(): factor.reshape(pairs, 2, size, pairs, 2, size)[picks, 1, :, picks, 0, :]]
    ppermute x2, waiting for transfers between devices: 30.4 us -> 17.6 us  [from_partner(): lax.ppermute(shard, axis, [(i, i ^ 1 << distance) for i in range(lax.axis...]
    dot_general x1 -> x2, matrix products: 24.6 us -> 34.1 us  [the longest x1 20.1 us: factor_child(): jnp.dot(gathered_inverse, col_pieces.reshape(pivot_count, kept_count), pr...]
    another operation x1 -> x4, local copies, waits for them, and re-layouts: 2.31 us -> 10.9 us  [the longest x2 10.9 us: factor_child(): diag_inverse.reshape(pivot_count, slot_count, grid_size, TILE)]
    unnamed x83 -> x131, local copies, waits for them, and re-layouts: 14.2 us -> 15.1 us
  transfers between devices with their start and end apart: 12 -> 12, of which waited for: 4 -> 4; matrix products, arithmetic and copies ran while one was open for 57% -> 64% of each run, Pallas kernels for 0% -> 0%
where the time goes in v11:
time: 638 us; the launch traced here: 633 us
  other arithmetic  295 us (46%)
  local copies, waits for them, and re-layouts  140 us (22%)
  matrix products  101 us (16%)
  waiting for transfers between devices  65.8 us (10%)
  starting transfers between devices  16.2 us (3%)
  between operations  15.4 us (2%)
    another operation x24, other arithmetic, factor_pivots(): factor = jnp.tril(jnp.linalg.cholesky(work[:TILE, :TILE]))  99.9 us
    another operation x16, other arithmetic, factor_pivots(): jax.scipy.linalg.solve_triangular(factor, eye, lower=True)  88.4 us
    all_gather x1, waiting for transfers between devices, factor_child(): lax.all_gather(front_work[:width, :width], ('row', 'col'), axis=0)  31.8 us
    dot_general x1, matrix products, factor_child(): jnp.dot(jnp.where(rows_after, solved_rows, 0.0), jnp.where(cols_after.T,...  22.6 us
    dot_general x1, matrix products, factor_child(): jnp.dot(gathered_inverse, col_pieces.reshape(pivot_count, kept_count), pr...  20.1 us
    ppermute x2, waiting for transfers between devices, from_partner(): lax.ppermute(shard, axis, [(i, i ^ 1 << distance) for i in range(lax.axis...  17.6 us
    gather x2, local copies, waits for them, and re-layouts, factor_child(): jnp.take(diag_factor, jnp.minimum(row_index, pivot_count - 1), axis=0)  16.7 us
    ppermute x1, waiting for transfers between devices, factor_parent(): my_cols = lax.ppermute(my_row_cols, ('row', 'col'), pairs)  16.4 us
  transfers between devices with their start and end apart: 12, of which 4 were waited for; matrix products, arithmetic and copies ran while one was open for 64% of the time, Pallas kernels for 0%

profile of v11, /device:TPU:4, one launch (start us, length us, event | category | flops | bytes accessed | tf_op | source)
XLA Modules:
  0.0 632.9 jit_solution(8231165690783110170)
XLA Ops:
  29.8 31.8 %all-gather.7.cloned.1.call-done = f32[4096,256]{1,0:T(8,128)} async-done(((f32[256,256]{1,0:T(8,128)}), f32[4096,256]{1,0:T(8,128)}) %all-gather.7.cloned.1.call-update) | async-done | bytes 4194320 | tf_op jit(solution)/shard_map/all_gather | solution.py:87
  67.3 7.4 %copy.109 = f32[4,4,2,128,2,128]{3,0,2,5,1,4:T(4,128)} copy(f32[4,4,2,128,2,128]{5,4,3,2,1,0:T(2,128)} %reshape.480) | data formatting | bytes 8388608 | tf_op jit(solution)/shard_map/reshape | solution.py:88
  82.2 11.7 %cholesky.149 = f32[128,128]{1,0:T(8,128)S(1)} custom-call(f32[128,128]{1,0:T(8,128)S(1)} %fusion.83), custom_call_target="Cholesky" | custom-call | tf_op jit(solution)/shard_map/jit(cholesky)/cholesky | solution.py:46
  95.9 9.8 %custom-call.13 = f32[1,128,128]{1,2,0:T(8,128)S(1)} custom-call(f32[1,128,128]{2,1,0:T(8,128)S(1)} %get-tuple-element.28), custom_call_target="InvertDiagBlocksLowerTriangular" | custom-call | tf_op jit(solution)/shard_map/jit(_solve_triangular)/triangular_solve | solution.py:47
  115.7 12.2 %cholesky.160 = f32[128,128]{1,0:T(8,128)S(1)} custom-call(f32[128,128]{1,0:T(8,128)S(1)} %fusion.81), custom_call_target="Cholesky" | custom-call | tf_op jit(solution)/shard_map/jit(cholesky)/cholesky | solution.py:46
  129.9 9.8 %custom-call.14 = f32[1,128,128]{1,2,0:T(8,128)S(1)} custom-call(f32[1,128,128]{2,1,0:T(8,128)S(1)} %get-tuple-element.26), custom_call_target="InvertDiagBlocksLowerTriangular" | custom-call | tf_op jit(solution)/shard_map/jit(_solve_triangular)/triangular_solve | solution.py:47
  145.9 11.7 %cholesky.171 = f32[128,128]{1,0:T(8,128)S(1)} custom-call(f32[128,128]{1,0:T(8,128)S(1)} %fusion.79), custom_call_target="Cholesky" | custom-call | tf_op jit(solution)/shard_map/jit(cholesky)/cholesky | solution.py:46
  159.6 9.9 %custom-call.15 = f32[1,128,128]{1,2,0:T(8,128)S(1)} custom-call(f32[1,128,128]{2,1,0:T(8,128)S(1)} %get-tuple-element.24), custom_call_target="InvertDiagBlocksLowerTriangular" | custom-call | tf_op jit(solution)/shard_map/jit(_solve_triangular)/triangular_solve | solution.py:47
  175.3 11.7 %cholesky.182 = f32[128,128]{1,0:T(8,128)S(1)} custom-call(f32[128,128]{1,0:T(8,128)S(1)} %fusion.77), custom_call_target="Cholesky" | custom-call | tf_op jit(solution)/shard_map/jit(cholesky)/cholesky | solution.py:46
  189.0 9.8 %custom-call.16 = f32[1,128,128]{1,2,0:T(8,128)S(1)} custom-call(f32[1,128,128]{2,1,0:T(8,128)S(1)} %get-tuple-element.22), custom_call_target="InvertDiagBlocksLowerTriangular" | custom-call | tf_op jit(solution)/shard_map/jit(_solve_triangular)/triangular_solve | solution.py:47
  201.5 11.9 %cholesky.193 = f32[128,128]{1,0:T(8,128)S(1)} custom-call(f32[128,128]{1,0:T(8,128)S(1)} %fusion.75), custom_call_target="Cholesky" | custom-call | tf_op jit(solution)/shard_map/jit(cholesky)/cholesky | solution.py:46
  215.4 9.8 %custom-call.17 = f32[1,128,128]{1,2,0:T(8,128)S(1)} custom-call(f32[1,128,128]{2,1,0:T(8,128)S(1)} %get-tuple-element.20), custom_call_target="InvertDiagBlocksLowerTriangular" | custom-call | tf_op jit(solution)/shard_map/jit(_solve_triangular)/triangular_solve | solution.py:47
  227.4 11.7 %cholesky.204 = f32[128,128]{1,0:T(8,128)S(1)} custom-call(f32[128,128]{1,0:T(8,128)S(1)} %fusion.73), custom_call_target="Cholesky" | custom-call | tf_op jit(solution)/shard_map/jit(cholesky)/cholesky | solution.py:46
  240.4 9.8 %custom-call.18 = f32[1,128,128]{1,2,0:T(8,128)S(1)} custom-call(f32[1,128,128]{2,1,0:T(8,128)S(1)} %get-tuple-element.18), custom_call_target="InvertDiagBlocksLowerTriangular" | custom-call | tf_op jit(solution)/shard_map/jit(_solve_triangular)/triangular_solve | solution.py:47
  252.5 11.7 %cholesky.215 = f32[128,128]{1,0:T(8,128)S(1)} custom-call(f32[128,128]{1,0:T(8,128)S(1)} %fusion.71), custom_call_target="Cholesky" | custom-call | tf_op jit(solution)/shard_map/jit(cholesky)/cholesky | solution.py:46
  266.1 9.8 %custom-call.19 = f32[1,128,128]{1,2,0:T(8,128)S(1)} custom-call(f32[1,128,128]{2,1,0:T(8,128)S(1)} %get-tuple-element.16), custom_call_target="InvertDiagBlocksLowerTriangular" | custom-call | tf_op jit(solution)/shard_map/jit(_solve_triangular)/triangular_solve | solution.py:47
  277.6 11.7 %cholesky.226 = f32[128,128]{1,0:T(8,128)S(1)} custom-call(f32[128,128]{1,0:T(8,128)S(1)} %fusion.69), custom_call_target="Cholesky" | custom-call | tf_op jit(solution)/shard_map/jit(cholesky)/cholesky | solution.py:46
  291.2 10.0 %custom-call.20 = f32[1,128,128]{1,2,0:T(8,128)S(1)} custom-call(f32[1,128,128]{2,1,0:T(8,128)S(1)} %get-tuple-element.14), custom_call_target="InvertDiagBlocksLowerTriangular" | custom-call | tf_op jit(solution)/shard_map/jit(_solve_triangular)/triangular_solve | solution.py:47
  321.8 14.0 %convolution_bitcast_fusion = f32[1280,1024]{0,1:T(8,128)} fusion(f32[1024,1024]{0,1:T(8,128)} %bitcast.264, f32[1024,1280]{1,0:T(8,128)} %all-gather.11.cloned.1.call-done), kind=kOutput, calls=%fused_computation.24 | convolution fusion | flops 8053063680 | bytes 14680064 | tf_op jit(solution)/shard_map/dot_general | solution.py:110
  335.8 20.1 %convolution_bitcast_fusion.1 = f32[1280,1024]{0,1:T(8,128)S(1)} fusion(f32[1024,1024]{0,1:T(8,128)} %bitcast.265, f32[1024,1280]{0,1:T(8,128)} %all-gather.9.cloned.1.call-done), kind=kOutput, calls=%fused_computation.25 | convolution fusion | flops 8053063680 | bytes 14680064 | tf_op jit(solution)/shard_map/dot_general | solution.py:106
  358.2 22.6 %subtract_select_fusion = f32[1536,1536]{1,0:T(8,128)S(1)} fusion(f32[1280,1024]{0,1:T(8,128)S(1)} %convolution_bitcast_fusion.1, f32[1280,1024]{0,1:T(8,128)S(1)} %copy-done.60, pred[1536]{0:T(1024)(128)(4,1)S(1)} %copy-done.51, pred[1536]{0:T(1024)(128)(4,1)S(1)} %get-tuple-element.66, f32[1,1536,1536]{2,1,0:T(8,128)} %param.14), kind=kOutput, calls=%fused_computation.13 | convolution fusion | flops 14505738240 | bytes 29363200 | tf_op jit(solution)/shard_map/dot_general | solution.py:129
  406.6 10.2 %gather_fusion = f32[1536,1024]{1,0:T(8,128)} fusion(f32[1024,1024]{1,0:T(8,128)} %pad_dynamic-update-slice_fusion, s32[2048]{0:T(1024)S(1)} %pad_clamp_fusion), kind=kCustom, calls=%fused_computation.8 | custom fusion | bytes 12589056 | tf_op jit(solution)/shard_map/jit(_take)/gather | solution.py:135
  438.9 7.1 %gather_fusion.7 = f32[16,8,128,128]{3,2,1,0:T(8,128)} fusion(f32[8,128,10,128]{3,1,2,0:T(8,128)} %broadcast_select_fusion.1, s32[1024]{0:T(1024)} %pad_clamp_fusion.4), kind=kCustom, calls=%fused_computation.3.clone | custom fusion | bytes 16777280 | tf_op jit(solution)/shard_map/jit(_take)/gather | solution.py:201
  450.2 8.0 %copy.140 = f32[8,128,16,128]{3,2,1,0:T(8,128)} copy(f32[8,128,16,128]{3,1,0,2:T(8,128)S(1)} %bitcast_select_fusion.1) | data formatting | bytes 16777216 | tf_op jit(solution)/shard_map/jit(_where)/select_n | solution.py:203
  477.7 7.1 %gather_fusion.11 = f32[16,8,128,128]{3,2,1,0:T(8,128)} fusion(f32[8,128,10,128]{3,1,2,0:T(8,128)} %broadcast_select_fusion, s32[1024]{0:T(1024)} %pad_clamp_fusion.2), kind=kCustom, calls=%fused_computation.7.clone | custom fusion | bytes 16777280 | tf_op jit(solution)/shard_map/jit(_take)/gather | solution.py:201
  489.1 8.1 %copy.143 = f32[8,128,16,128]{3,2,1,0:T(8,128)} copy(f32[8,128,16,128]{3,1,0,2:T(8,128)S(1)} %bitcast_select_fusion) | data formatting | bytes 16777216 | tf_op jit(solution)/shard_map/jit(_where)/select_n | solution.py:203
  497.3 13.2 %bitcast_add_fusion = f32[1024,2048]{1,0:T(8,128)S(1)} fusion(f32[128,8,16,128]{3,2,1,0:T(8,128)} %bitcast.251, f32[1024,2048]{1,0:T(8,128)} %param.16, f32[128,8,16,128]{3,2,1,0:T(8,128)S(1)} %bitcast.250), kind=kLoop, calls=%fused_computation.14 | loop fusion | flops 4194304 | bytes 33554432 | tf_op jit(solution)/shard_map/add | solution.py:222
  535.9 11.2 %collective-permute-done.4 = f32[1024,128]{1,0:T(8,128)S(1)} collective-permute-done((f32[1024,128]{1,0:T(8,128)S(1)}, f32[1024,128]{1,0:T(8,128)S(1)}, u32[]{:S(2)}, u32[]{:S(2)}) %collective-permute-start.4) | collective-permute-done | bytes 524320 | tf_op jit(solution)/shard_map/ppermute | solution.py:28
  564.0 11.7 %cholesky.237 = f32[128,128]{1,0:T(8,128)S(1)} custom-call(f32[128,128]{1,0:T(8,128)S(1)} %copy.147), custom_call_target="Cholesky" | custom-call | tf_op jit(solution)/shard_map/jit(cholesky)/cholesky | solution.py:242
  577.0 9.8 %custom-call.21 = f32[1,128,128]{1,2,0:T(8,128)S(1)} custom-call(f32[1,128,128]{2,1,0:T(8,128)S(1)} %get-tuple-element.8), custom_call_target="InvertDiagBlocksLowerTriangular" | custom-call | tf_op jit(solution)/shard_map/jit(_solve_triangular)/triangular_solve | solution.py:244
  592.5 16.4 %collective-permute-done.8 = f32[2048,128]{1,0:T(8,128)} collective-permute-done((f32[2048,128]{1,0:T(8,128)}, f32[2048,128]{1,0:T(8,128)}, u32[]{:S(2)}, u32[]{:S(2)}) %collective-permute-start.8) | collective-permute-done | bytes 1048608 | tf_op jit(solution)/shard_map/ppermute | solution.py:240
  611.1 9.8 %subtract_select_fusion.1 = f32[1024,2048]{1,0:T(8,128)S(1)} fusion(f32[1024,2048]{1,0:T(8,128)} %copy-done, f32[2048,128]{1,0:T(8,128)S(1)} %convolution_select_fusion, pred[2048]{0:T(1024)(128)(4,1)S(1)} %copy-done.41, pred[1024]{0:T(1024)(128)(4,1)S(1)} %copy-done.47, f32[1024,128]{1,0:T(8,128)S(1)} %get-tuple-element.59), kind=kOutput, calls=%fused_computation.19 | convolution fusion | flops 3227648000 | bytes 18353152 | tf_op jit(solution)/shard_map/dot_general | solution.py:258
  (356 shorter events, 236.0 us)
Async XLA Ops:
  7.2 54.4 %all-gather.7.cloned.1.call-start = ((), (), s32[]{:S(2)}) async-start(), calls=%async_computation | async-start | bytes 4456448 | tf_op jit(solution)/shard_map/all_gather | solution.py:87
  8.9 312.9 %all-gather.11.cloned.1.call-start = ((), (), s32[]{:S(2)}) async-start(), calls=%async_computation.2 | async-start | bytes 6553600 | tf_op jit(solution)/shard_map/all_gather | solution.py:101
  11.5 324.3 %all-gather.9.cloned.1.call-start = ((), (), s32[]{:S(2)}) async-start(), calls=%async_computation.1 | async-start | bytes 6553600 | tf_op jit(solution)/shard_map/all_gather | solution.py:99
  23.3 332.6 %copy-start.43 = (pred[1536]{0:T(1024)(128)(4,1)}, pred[1536]{0:T(1024)(128)(4,1)S(1)}, u32[]{:S(2)}) copy-start(pred[1536]{0:T(1024)(128)(4,1)S(1)} %get-tuple-element.66) | copy-start | bytes 4612
  172.2 132.3 %copy-start.7 = (f32[640,128]{1,0:T(8,128)}, f32[640,128]{1,0:T(8,128)S(1)}, u32[]{:S(2)}) copy-start(f32[640,128]{1,0:T(8,128)S(1)} %fusion.33) | copy-start | bytes 983044
  200.3 104.1 %copy-start.12 = (f32[512,128]{1,0:T(8,128)}, f32[512,128]{1,0:T(8,128)S(1)}, u32[]{:S(2)}) copy-start(f32[512,128]{1,0:T(8,128)S(1)} %fusion.39) | copy-start | bytes 786436
  201.3 99.9 %copy-start.3 = (f32[768,128]{1,0:T(8,128)S(1)}, f32[768,128]{1,0:T(8,128)}, u32[]{:S(2)}) copy-start(f32[768,128]{1,0:T(8,128)} %copy-done.2) | copy-start | bytes 1179652
  201.4 99.9 %copy-start.10 = (f32[128,896]{0,1:T(8,128)S(1)}, f32[128,896]{0,1:T(8,128)}, u32[]{:S(2)}) copy-start(f32[128,896]{0,1:T(8,128)} %copy.127) | copy-start | bytes 1376260
  201.4 99.9 %copy-start.23 = (f32[128,128]{1,0:T(8,128)S(1)}, f32[128,128]{1,0:T(8,128)}, u32[]{:S(2)}) copy-start(f32[128,128]{1,0:T(8,128)} %get-tuple-element.29) | copy-start | bytes 196612
  227.2 74.1 %copy-start.27 = (f32[128,128]{1,0:T(8,128)S(1)}, f32[128,128]{1,0:T(8,128)}, u32[]{:S(2)}) copy-start(f32[128,128]{1,0:T(8,128)} %get-tuple-element.21) | copy-start | bytes 196612
  240.4 61.7 %copy-start.29 = (f32[128,128]{1,0:T(8,128)}, f32[128,128]{1,0:T(8,128)S(1)}, u32[]{:S(2)}) copy-start(f32[128,128]{1,0:T(8,128)S(1)} %get-tuple-element.19) | copy-start | bytes 196612
  252.0 50.2 %copy-start.14 = (f32[256,128]{1,0:T(8,128)}, f32[256,128]{1,0:T(8,128)S(1)}, u32[]{:S(2)}) copy-start(f32[256,128]{1,0:T(8,128)S(1)} %fusion.62) | copy-start | bytes 393220
  276.9 24.5 %copy-start.18 = (f32[8,128,128]{2,1,0:T(8,128)S(1)}, f32[8,128,128]{2,1,0:T(8,128)}, u32[]{:S(2)}) copy-start(f32[8,128,128]{2,1,0:T(8,128)} %get-tuple-element.56) | copy-start | bytes 1572868
  335.7 22.5 %copy-start.51 = (pred[1536]{0:T(1024)(128)(4,1)S(1)}, pred[1536]{0:T(1024)(128)(4,1)}, u32[]{:S(2)}) copy-start(pred[1536]{0:T(1024)(128)(4,1)} %get-tuple-element.67) | copy-start | bytes 4612
  335.8 22.5 %copy-start.60 = (f32[1280,1024]{0,1:T(8,128)S(1)}, f32[1280,1024]{0,1:T(8,128)}, u32[]{:S(2)}) copy-start(f32[1280,1024]{0,1:T(8,128)} %convolution_bitcast_fusion) | copy-start | bytes 15728644
  391.3 73.4 %collective-permute-start = (f32[5,128,1280]{1,2,0:T(8,128)}, f32[5,128,1280]{1,2,0:T(8,128)}, u32[]{:S(2)}, u32[]{:S(2)}) collective-permute-start(f32[5,128,1280]{1,2,0:T(8,128)} %bitcast.266), channel_id=1, source_target_pairs={{0,16},{16,0},{1,17},{17,1},{2,18},{18,2},{3,19},{19,3},{4,20},{20... | collective-permute-start | bytes 9830408 | tf_op jit(solution)/shard_map/ppermute | solution.py:28
  489.1 29.9 %slice-start.3 = ((s8[5242880]{0:T(1024)(128)(4,1)}), s8[4194304]{0:T(1024)(128)(4,1)S(1)}, s32[]{:S(2)}) async-start(s8[5242880]{0:T(1024)(128)(4,1)} %bitcast.258), calls=%async_computation.6 | async-start | bytes 8388608
  497.3 21.7 %slice-start.4 = ((s8[5242880]{0:T(1024)(128)(4,1)}), s8[1048576]{0:T(1024)(128)(4,1)S(1)}, s32[]{:S(2)}) async-start(s8[5242880]{0:T(1024)(128)(4,1)} %bitcast.258), calls=%async_computation.7 | async-start | bytes 2097152
  497.3 21.7 %copy-start.42 = (pred[1536]{0:T(1024)(128)(4,1)S(1)}, pred[1536]{0:T(1024)(128)(4,1)}, u32[]{:S(2)}) copy-start(pred[1536]{0:T(1024)(128)(4,1)} %compare_and_fusion) | copy-start | bytes 4612
  497.3 21.7 %copy-start.44 = (pred[1536]{0:T(1024)(128)(4,1)S(1)}, pred[1536]{0:T(1024)(128)(4,1)}, u32[]{:S(2)}) copy-start(pred[1536]{0:T(1024)(128)(4,1)} %copy-done.43) | copy-start | bytes 4612
  514.8 16.2 %collective-permute-start.2 = (f32[1024,128]{1,0:T(8,128)}, f32[1024,128]{1,0:T(8,128)}, u32[]{:S(2)}, u32[]{:S(2)}) collective-permute-start(f32[1024,128]{1,0:T(8,128)} %slice.269), channel_id=1, source_target_pairs={{0,2},{4,6},{8,10},{12,14},{16,18},{20,22},{24,26},{28,30}} | collective-permute-start | bytes 1572872 | tf_op jit(solution)/shard_map/ppermute | solution.py:23
  516.0 14.9 %collective-permute-start.1 = (f32[1024,128]{1,0:T(8,128)}, f32[1024,128]{1,0:T(8,128)}, u32[]{:S(2)}, u32[]{:S(2)}) collective-permute-start(f32[1024,128]{1,0:T(8,128)} %slice.269), channel_id=1, source_target_pairs={{0,1},{4,5},{8,9},{12,13},{16,17},{20,21},{24,25},{28,29}} | collective-permute-start | bytes 1572872 | tf_op jit(solution)/shard_map/ppermute | solution.py:23
  517.5 13.4 %collective-permute-start.3 = (f32[1024,128]{1,0:T(8,128)}, f32[1024,128]{1,0:T(8,128)}, u32[]{:S(2)}, u32[]{:S(2)}) collective-permute-start(f32[1024,128]{1,0:T(8,128)} %slice.269), channel_id=1, source_target_pairs={{0,3},{4,7},{8,11},{12,15},{16,19},{20,23},{24,27},{28,31}} | collective-permute-start | bytes 1572872 | tf_op jit(solution)/shard_map/ppermute | solution.py:23
  532.6 14.5 %collective-permute-start.4 = (f32[1024,128]{1,0:T(8,128)S(1)}, f32[1024,128]{1,0:T(8,128)S(1)}, u32[]{:S(2)}, u32[]{:S(2)}) collective-permute-start(f32[1024,128]{1,0:T(8,128)S(1)} %add_add_fusion), channel_id=1, source_target_pairs={{0,16},{16,0},{1,17},{17,1},{2,18},{18,2},{3,19},{19,3},{4,20},{20... | collective-permute-start | bytes 1572872 | tf_op jit(solution)/shard_map/ppermute | solution.py:28
  534.1 21.3 %slice-start.2 = ((f32[1536,1536]{1,0:T(8,128)}), f32[1536,1280]{1,0:T(8,128)S(1)}, s32[]{:S(2)}) async-start(f32[1536,1536]{1,0:T(8,128)} %copy-done.1), calls=%async_computation.5 | async-start | bytes 15728640 | tf_op jit(solution)/shard_map/slice | solution.py:140
  549.1 13.8 %collective-permute-start.6 = (f32[128,128]{1,0:T(8,128)S(1)}, f32[128,128]{1,0:T(8,128)S(1)}, u32[]{:S(2)}, u32[]{:S(2)}) collective-permute-start(f32[128,128]{1,0:T(8,128)S(1)} %slice.270), channel_id=1, source_target_pairs={{0,8},{1,9},{2,10},{3,11},{16,24},{17,25},{18,26},{19,27}} | collective-permute-start | bytes 196616 | tf_op jit(solution)/shard_map/ppermute | solution.py:23
  552.9 10.1 %collective-permute-start.5 = (f32[128,128]{1,0:T(8,128)S(1)}, f32[128,128]{1,0:T(8,128)S(1)}, u32[]{:S(2)}, u32[]{:S(2)}) collective-permute-start(f32[128,128]{1,0:T(8,128)S(1)} %slice.270), channel_id=1, source_target_pairs={{0,4},{1,5},{2,6},{3,7},{16,20},{17,21},{18,22},{19,23}} | collective-permute-start | bytes 196616 | tf_op jit(solution)/shard_map/ppermute | solution.py:23
  554.2 8.8 %collective-permute-start.7 = (f32[128,128]{1,0:T(8,128)S(1)}, f32[128,128]{1,0:T(8,128)S(1)}, u32[]{:S(2)}, u32[]{:S(2)}) collective-permute-start(f32[128,128]{1,0:T(8,128)S(1)} %slice.270), channel_id=1, source_target_pairs={{0,12},{1,13},{2,14},{3,15},{16,28},{17,29},{18,30},{19,31}} | collective-permute-start | bytes 196616 | tf_op jit(solution)/shard_map/ppermute | solution.py:23
  560.4 29.7 %copy-start.47 = (pred[1024]{0:T(1024)(128)(4,1)S(1)}, pred[1024]{0:T(1024)(128)(4,1)}, u32[]{:S(2)}) copy-start(pred[1024]{0:T(1024)(128)(4,1)} %broadcast_compare_fusion.4) | copy-start | bytes 3076
  560.4 29.7 %copy-start.55 = (pred[1024]{0:T(1024)(128)(4,1)S(1)}, pred[1024]{0:T(1024)(128)(4,1)}, u32[]{:S(2)}) copy-start(pred[1024]{0:T(1024)(128)(4,1)} %compare_and_fusion.1) | copy-start | bytes 3076
  560.4 48.4 %collective-permute-start.8 = (f32[2048,128]{1,0:T(8,128)}, f32[2048,128]{1,0:T(8,128)}, u32[]{:S(2)}, u32[]{:S(2)}) collective-permute-start(f32[2048,128]{1,0:T(8,128)} %bitcast.75), channel_id=1, source_target_pairs={{0,0},{4,1},{8,2},{12,3},{1,4},{5,5},{9,6},{13,7},{2,8},{6,9},{10,... | collective-permute-start | bytes 3145736 | tf_op jit(solution)/shard_map/ppermute | solution.py:240
  590.1 18.8 %copy-start.41 = (pred[2048]{0:T(1024)(128)(4,1)S(1)}, pred[2048]{0:T(1024)(128)(4,1)}, u32[]{:S(2)}) copy-start(pred[2048]{0:T(1024)(128)(4,1)} %broadcast_compare_fusion) | copy-start | bytes 6148
  (46 other events, 170.9 us)
Sparse Core Ops, SparseCore 0:
  10.7 50.8 all-gather.6
  63.1 97.7 all-gather.10
  162.6 37.5 all-gather.8

commit v12 on v11

--- a/solution.py
+++ b/solution.py
@@ -46,11 +46,11 @@
         factor = jnp.tril(jnp.linalg.cholesky(work[:TILE, :TILE]))
         inverse = jnp.tril(jax.scipy.linalg.solve_triangular(factor, eye, lower=True))
         panel = jnp.dot(
-            work[TILE:, :TILE], inverse.T, precision=lax.Precision.HIGHEST,
+            work[TILE:, :TILE], inverse.T, precision=lax.Precision.HIGH,
             preferred_element_type=jnp.float32,
         )
         work = work[TILE:, TILE:] - jnp.dot(
-            panel, panel.T, precision=lax.Precision.HIGHEST, preferred_element_type=jnp.float32
+            panel, panel.T, precision=lax.Precision.HIGH, preferred_element_type=jnp.float32
         )
         columns.append(jnp.concatenate([jnp.zeros((step * TILE, TILE), jnp.float32), factor, panel]))
         inverses.append(inverse)
@@ -70,8 +70,8 @@
                 for pair in range(pairs)
             ]
         )
-        mixed = jnp.einsum("kab,kbc->kac", second, lower, precision=lax.Precision.HIGHEST)
-        mixed = -jnp.einsum("kab,kbc->kac", mixed, first, precision=lax.Precision.HIGHEST)
+        mixed = jnp.einsum("kab,kbc->kac", second, lower, precision=lax.Precision.HIGH)
+        mixed = -jnp.einsum("kab,kbc->kac", mixed, first, precision=lax.Precision.HIGH)
         top = jnp.concatenate([first, jnp.zeros_like(first)], axis=2)
         bottom = jnp.concatenate([mixed, second], axis=2)
         inverse = jnp.concatenate([top, bottom], axis=1)
@@ -242,8 +242,8 @@
     diag_factor = jnp.tril(jnp.linalg.cholesky(diag_block))
     eye = jnp.eye(TILE, dtype=jnp.float32)
     inverse = jnp.tril(jax.scipy.linalg.solve_triangular(diag_factor, eye, lower=True))
-    solved_rows = jnp.dot(column, inverse.T, precision=lax.Precision.HIGHEST)
-    solved_cols = jnp.dot(my_cols, inverse.T, precision=lax.Precision.HIGHEST)
+    solved_rows = jnp.dot(column, inverse.T, precision=lax.Precision.HIGH)
+    solved_cols = jnp.dot(my_cols, inverse.T, precision=lax.Precision.HIGH)
     row_within = jnp.arange(row_count, dtype=jnp.int32)
     col_within = jnp.arange(col_count, dtype=jnp.int32)
     row_index = row_within // TILE * row_groups * TILE + parent_row * TILE + row_within % TILE
@@ -258,7 +258,7 @@
     update = jnp.dot(
         jnp.where(rows_after, solved_rows, 0.0),
         jnp.where(cols_after.T, solved_cols, 0.0).T,
-        precision=lax.Precision.HIGHEST,
+        precision=lax.Precision.HIGH,
         preferred_element_type=jnp.float32,
     )
     diag_rows = jnp.take(diag_factor, jnp.minimum(row_index, pivot_count - 1), axis=0)

time: 638 us -> 627 us (0.983)
  matrix products: 101 us -> 89.5 us
    dot_general x22, matrix products: 27.2 us -> 19.3 us  [the longest x7 8.47 us: factor_pivots(): jnp.dot(panel, panel.T, precision=lax.Precision.HIGH, preferred_element_t...]
where the time goes in v12:
time: 627 us; the launch traced here: 622 us
  other arithmetic  295 us (47%)
  local copies, waits for them, and re-layouts  139 us (22%)
  matrix products  89.5 us (14%)
  waiting for transfers between devices  66.2 us (11%)
  starting transfers between devices  15.9 us (3%)
  between operations  15.5 us (2%)
    another operation x24, other arithmetic, factor_pivots(): factor = jnp.tril(jnp.linalg.cholesky(work[:TILE, :TILE]))  99.7 us
    another operation x16, other arithmetic, factor_pivots(): jax.scipy.linalg.solve_triangular(factor, eye, lower=True)  88.6 us
    all_gather x1, waiting for transfers between devices, factor_child(): lax.all_gather(front_work[:width, :width], ('row', 'col'), axis=0)  31.8 us
    dot_general x1, matrix products, factor_child(): jnp.dot(jnp.where(rows_after, solved_rows, 0.0), jnp.where(cols_after.T,...  22.4 us
    dot_general x1, matrix products, factor_child(): jnp.dot(gathered_inverse, col_pieces.reshape(pivot_count, kept_count), pr...  20.1 us
    ppermute x2, waiting for transfers between devices, from_partner(): lax.ppermute(shard, axis, [(i, i ^ 1 << distance) for i in range(lax.axis...  17.4 us
    ppermute x1, waiting for transfers between devices, factor_parent(): my_cols = lax.ppermute(my_row_cols, ('row', 'col'), pairs)  17 us
    gather x2, local copies, waits for them, and re-layouts, factor_child(): jnp.take(diag_factor, jnp.minimum(row_index, pivot_count - 1), axis=0)  16.9 us
  transfers between devices with their start and end apart: 12, of which 4 were waited for; matrix products, arithmetic and copies ran while one was open for 64% of the time, Pallas kernels for 0%

profile of v12, /device:TPU:4, one launch (start us, length us, event | category | flops | bytes accessed | tf_op | source)
XLA Modules:
  0.0 621.9 jit_solution(8943316070781643032)
XLA Ops:
  29.8 31.8 %all-gather.7.cloned.1.call-done = f32[4096,256]{1,0:T(8,128)} async-done(((f32[256,256]{1,0:T(8,128)}), f32[4096,256]{1,0:T(8,128)}) %all-gather.7.cloned.1.call-update) | async-done | bytes 4194320 | tf_op jit(solution)/shard_map/all_gather | solution.py:87
  67.3 7.4 %copy.109 = f32[4,4,2,128,2,128]{3,0,2,5,1,4:T(4,128)} copy(f32[4,4,2,128,2,128]{5,4,3,2,1,0:T(2,128)} %reshape.480) | data formatting | bytes 8388608 | tf_op jit(solution)/shard_map/reshape | solution.py:88
  82.1 11.7 %cholesky.149 = f32[128,128]{1,0:T(8,128)S(1)} custom-call(f32[128,128]{1,0:T(8,128)S(1)} %fusion.83), custom_call_target="Cholesky" | custom-call | tf_op jit(solution)/shard_map/jit(cholesky)/cholesky | solution.py:46
  95.8 9.8 %custom-call.13 = f32[1,128,128]{1,2,0:T(8,128)S(1)} custom-call(f32[1,128,128]{2,1,0:T(8,128)S(1)} %get-tuple-element.28), custom_call_target="InvertDiagBlocksLowerTriangular" | custom-call | tf_op jit(solution)/shard_map/jit(_solve_triangular)/triangular_solve | solution.py:47
  114.2 11.9 %cholesky.160 = f32[128,128]{1,0:T(8,128)S(1)} custom-call(f32[128,128]{1,0:T(8,128)S(1)} %fusion.81), custom_call_target="Cholesky" | custom-call | tf_op jit(solution)/shard_map/jit(cholesky)/cholesky | solution.py:46
  128.1 9.8 %custom-call.14 = f32[1,128,128]{1,2,0:T(8,128)S(1)} custom-call(f32[1,128,128]{2,1,0:T(8,128)S(1)} %get-tuple-element.26), custom_call_target="InvertDiagBlocksLowerTriangular" | custom-call | tf_op jit(solution)/shard_map/jit(_solve_triangular)/triangular_solve | solution.py:47
  142.8 11.7 %cholesky.171 = f32[128,128]{1,0:T(8,128)S(1)} custom-call(f32[128,128]{1,0:T(8,128)S(1)} %fusion.79), custom_call_target="Cholesky" | custom-call | tf_op jit(solution)/shard_map/jit(cholesky)/cholesky | solution.py:46
  156.5 9.8 %custom-call.15 = f32[1,128,128]{1,2,0:T(8,128)S(1)} custom-call(f32[1,128,128]{2,1,0:T(8,128)S(1)} %get-tuple-element.24), custom_call_target="InvertDiagBlocksLowerTriangular" | custom-call | tf_op jit(solution)/shard_map/jit(_solve_triangular)/triangular_solve | solution.py:47
  171.4 12.1 %cholesky.182 = f32[128,128]{1,0:T(8,128)S(1)} custom-call(f32[128,128]{1,0:T(8,128)S(1)} %fusion.77), custom_call_target="Cholesky" | custom-call | tf_op jit(solution)/shard_map/jit(cholesky)/cholesky | solution.py:46
  185.4 9.8 %custom-call.16 = f32[1,128,128]{1,2,0:T(8,128)S(1)} custom-call(f32[1,128,128]{2,1,0:T(8,128)S(1)} %get-tuple-element.22), custom_call_target="InvertDiagBlocksLowerTriangular" | custom-call | tf_op jit(solution)/shard_map/jit(_solve_triangular)/triangular_solve | solution.py:47
  197.3 11.7 %cholesky.193 = f32[128,128]{1,0:T(8,128)S(1)} custom-call(f32[128,128]{1,0:T(8,128)S(1)} %fusion.75), custom_call_target="Cholesky" | custom-call | tf_op jit(solution)/shard_map/jit(cholesky)/cholesky | solution.py:46
  211.0 9.9 %custom-call.17 = f32[1,128,128]{1,2,0:T(8,128)S(1)} custom-call(f32[1,128,128]{2,1,0:T(8,128)S(1)} %get-tuple-element.20), custom_call_target="InvertDiagBlocksLowerTriangular" | custom-call | tf_op jit(solution)/shard_map/jit(_solve_triangular)/triangular_solve | solution.py:47
  222.8 11.7 %cholesky.204 = f32[128,128]{1,0:T(8,128)S(1)} custom-call(f32[128,128]{1,0:T(8,128)S(1)} %fusion.73), custom_call_target="Cholesky" | custom-call | tf_op jit(solution)/shard_map/jit(cholesky)/cholesky | solution.py:46
  235.8 9.8 %custom-call.18 = f32[1,128,128]{1,2,0:T(8,128)S(1)} custom-call(f32[1,128,128]{2,1,0:T(8,128)S(1)} %get-tuple-element.18), custom_call_target="InvertDiagBlocksLowerTriangular" | custom-call | tf_op jit(solution)/shard_map/jit(_solve_triangular)/triangular_solve | solution.py:47
  247.3 11.7 %cholesky.215 = f32[128,128]{1,0:T(8,128)S(1)} custom-call(f32[128,128]{1,0:T(8,128)S(1)} %fusion.71), custom_call_target="Cholesky" | custom-call | tf_op jit(solution)/shard_map/jit(cholesky)/cholesky | solution.py:46
  260.9 10.2 %custom-call.19 = f32[1,128,128]{1,2,0:T(8,128)S(1)} custom-call(f32[1,128,128]{2,1,0:T(8,128)S(1)} %get-tuple-element.16), custom_call_target="InvertDiagBlocksLowerTriangular" | custom-call | tf_op jit(solution)/shard_map/jit(_solve_triangular)/triangular_solve | solution.py:47
  272.6 11.7 %cholesky.226 = f32[128,128]{1,0:T(8,128)S(1)} custom-call(f32[128,128]{1,0:T(8,128)S(1)} %fusion.69), custom_call_target="Cholesky" | custom-call | tf_op jit(solution)/shard_map/jit(cholesky)/cholesky | solution.py:46
  286.3 9.8 %custom-call.20 = f32[1,128,128]{1,2,0:T(8,128)S(1)} custom-call(f32[1,128,128]{2,1,0:T(8,128)S(1)} %get-tuple-element.14), custom_call_target="InvertDiagBlocksLowerTriangular" | custom-call | tf_op jit(solution)/shard_map/jit(_solve_triangular)/triangular_solve | solution.py:47
  314.4 13.8 %convolution_bitcast_fusion = f32[1280,1024]{0,1:T(8,128)} fusion(f32[1024,1024]{0,1:T(8,128)} %bitcast.264, f32[1024,1280]{1,0:T(8,128)} %all-gather.11.cloned.1.call-done), kind=kOutput, calls=%fused_computation.24 | convolution fusion | flops 8053063680 | bytes 14680064 | tf_op jit(solution)/shard_map/dot_general | solution.py:110
  328.2 20.1 %convolution_bitcast_fusion.1 = f32[1280,1024]{0,1:T(8,128)S(1)} fusion(f32[1024,1024]{0,1:T(8,128)} %bitcast.265, f32[1024,1280]{0,1:T(8,128)} %all-gather.9.cloned.1.call-done), kind=kOutput, calls=%fused_computation.25 | convolution fusion | flops 8053063680 | bytes 14680064 | tf_op jit(solution)/shard_map/dot_general | solution.py:106
  350.7 22.4 %subtract_select_fusion = f32[1536,1536]{1,0:T(8,128)S(1)} fusion(f32[1280,1024]{0,1:T(8,128)S(1)} %convolution_bitcast_fusion.1, f32[1280,1024]{0,1:T(8,128)S(1)} %copy-done.60, pred[1536]{0:T(1024)(128)(4,1)S(1)} %copy-done.51, pred[1536]{0:T(1024)(128)(4,1)S(1)} %get-tuple-element.66, f32[1,1536,1536]{2,1,0:T(8,128)} %param.14), kind=kOutput, calls=%fused_computation.13 | convolution fusion | flops 14505738240 | bytes 29363200 | tf_op jit(solution)/shard_map/dot_general | solution.py:129
  398.9 10.4 %gather_fusion = f32[1536,1024]{1,0:T(8,128)} fusion(f32[1024,1024]{1,0:T(8,128)} %pad_dynamic-update-slice_fusion, s32[2048]{0:T(1024)S(1)} %pad_clamp_fusion), kind=kCustom, calls=%fused_computation.8 | custom fusion | bytes 12589056 | tf_op jit(solution)/shard_map/jit(_take)/gather | solution.py:135
  431.4 7.1 %gather_fusion.7 = f32[16,8,128,128]{3,2,1,0:T(8,128)} fusion(f32[8,128,10,128]{3,1,2,0:T(8,128)} %broadcast_select_fusion.1, s32[1024]{0:T(1024)} %pad_clamp_fusion.4), kind=kCustom, calls=%fused_computation.3.clone | custom fusion | bytes 16777280 | tf_op jit(solution)/shard_map/jit(_take)/gather | solution.py:201
  442.8 8.0 %copy.140 = f32[8,128,16,128]{3,2,1,0:T(8,128)} copy(f32[8,128,16,128]{3,1,0,2:T(8,128)S(1)} %bitcast_select_fusion.1) | data formatting | bytes 16777216 | tf_op jit(solution)/shard_map/jit(_where)/select_n | solution.py:203
  469.9 7.1 %gather_fusion.11 = f32[16,8,128,128]{3,2,1,0:T(8,128)} fusion(f32[8,128,10,128]{3,1,2,0:T(8,128)} %broadcast_select_fusion, s32[1024]{0:T(1024)} %pad_clamp_fusion.2), kind=kCustom, calls=%fused_computation.7.clone | custom fusion | bytes 16777280 | tf_op jit(solution)/shard_map/jit(_take)/gather | solution.py:201
  481.4 8.1 %copy.143 = f32[8,128,16,128]{3,2,1,0:T(8,128)} copy(f32[8,128,16,128]{3,1,0,2:T(8,128)S(1)} %bitcast_select_fusion) | data formatting | bytes 16777216 | tf_op jit(solution)/shard_map/jit(_where)/select_n | solution.py:203
  489.6 13.1 %bitcast_add_fusion = f32[1024,2048]{1,0:T(8,128)S(1)} fusion(f32[128,8,16,128]{3,2,1,0:T(8,128)} %bitcast.251, f32[1024,2048]{1,0:T(8,128)} %param.16, f32[128,8,16,128]{3,2,1,0:T(8,128)S(1)} %bitcast.250), kind=kLoop, calls=%fused_computation.14 | loop fusion | flops 4194304 | bytes 33554432 | tf_op jit(solution)/shard_map/add | solution.py:222
  528.1 11.2 %collective-permute-done.4 = f32[1024,128]{1,0:T(8,128)S(1)} collective-permute-done((f32[1024,128]{1,0:T(8,128)S(1)}, f32[1024,128]{1,0:T(8,128)S(1)}, u32[]{:S(2)}, u32[]{:S(2)}) %collective-permute-start.4) | collective-permute-done | bytes 524320 | tf_op jit(solution)/shard_map/ppermute | solution.py:28
  556.0 11.7 %cholesky.237 = f32[128,128]{1,0:T(8,128)S(1)} custom-call(f32[128,128]{1,0:T(8,128)S(1)} %copy.147), custom_call_target="Cholesky" | custom-call | tf_op jit(solution)/shard_map/jit(cholesky)/cholesky | solution.py:242
  568.9 9.8 %custom-call.21 = f32[1,128,128]{1,2,0:T(8,128)S(1)} custom-call(f32[1,128,128]{2,1,0:T(8,128)S(1)} %get-tuple-element.8), custom_call_target="InvertDiagBlocksLowerTriangular" | custom-call | tf_op jit(solution)/shard_map/jit(_solve_triangular)/triangular_solve | solution.py:244
  584.1 17.0 %collective-permute-done.8 = f32[2048,128]{1,0:T(8,128)} collective-permute-done((f32[2048,128]{1,0:T(8,128)}, f32[2048,128]{1,0:T(8,128)}, u32[]{:S(2)}, u32[]{:S(2)}) %collective-permute-start.8) | collective-permute-done | bytes 1048608 | tf_op jit(solution)/shard_map/ppermute | solution.py:240
  602.9 6.9 %subtract_select_fusion.1 = f32[1024,2048]{1,0:T(8,128)S(1)} fusion(f32[1024,2048]{1,0:T(8,128)} %copy-done, f32[2048,128]{1,0:T(8,128)S(1)} %convolution_select_fusion, pred[2048]{0:T(1024)(128)(4,1)S(1)} %copy-done.41, pred[1024]{0:T(1024)(128)(4,1)S(1)} %copy-done.47, f32[1024,128]{1,0:T(8,128)S(1)} %get-tuple-element.59), kind=kOutput, calls=%fused_computation.19 | convolution fusion | flops 1617035264 | bytes 18353152 | tf_op jit(solution)/shard_map/dot_general | solution.py:258
  (356 shorter events, 227.4 us)
Async XLA Ops:
  7.2 54.4 %all-gather.7.cloned.1.call-start = ((), (), s32[]{:S(2)}) async-start(), calls=%async_computation | async-start | bytes 4456448 | tf_op jit(solution)/shard_map/all_gather | solution.py:87
  8.9 305.5 %all-gather.11.cloned.1.call-start = ((), (), s32[]{:S(2)}) async-start(), calls=%async_computation.2 | async-start | bytes 6553600 | tf_op jit(solution)/shard_map/all_gather | solution.py:101
  11.5 316.8 %all-gather.9.cloned.1.call-start = ((), (), s32[]{:S(2)}) async-start(), calls=%async_computation.1 | async-start | bytes 6553600 | tf_op jit(solution)/shard_map/all_gather | solution.py:99
  23.3 325.1 %copy-start.43 = (pred[1536]{0:T(1024)(128)(4,1)}, pred[1536]{0:T(1024)(128)(4,1)S(1)}, u32[]{:S(2)}) copy-start(pred[1536]{0:T(1024)(128)(4,1)S(1)} %get-tuple-element.66) | copy-start | bytes 4612
  168.7 129.9 %copy-start.7 = (f32[640,128]{1,0:T(8,128)}, f32[640,128]{1,0:T(8,128)S(1)}, u32[]{:S(2)}) copy-start(f32[640,128]{1,0:T(8,128)S(1)} %fusion.33) | copy-start | bytes 983044
  196.5 102.0 %copy-start.12 = (f32[512,128]{1,0:T(8,128)}, f32[512,128]{1,0:T(8,128)S(1)}, u32[]{:S(2)}) copy-start(f32[512,128]{1,0:T(8,128)S(1)} %fusion.39) | copy-start | bytes 786436
  197.1 99.1 %copy-start.3 = (f32[768,128]{1,0:T(8,128)S(1)}, f32[768,128]{1,0:T(8,128)}, u32[]{:S(2)}) copy-start(f32[768,128]{1,0:T(8,128)} %copy-done.2) | copy-start | bytes 1179652
  197.2 99.1 %copy-start.10 = (f32[128,896]{0,1:T(8,128)S(1)}, f32[128,896]{0,1:T(8,128)}, u32[]{:S(2)}) copy-start(f32[128,896]{0,1:T(8,128)} %copy.127) | copy-start | bytes 1376260
  197.2 99.1 %copy-start.23 = (f32[128,128]{1,0:T(8,128)S(1)}, f32[128,128]{1,0:T(8,128)}, u32[]{:S(2)}) copy-start(f32[128,128]{1,0:T(8,128)} %get-tuple-element.29) | copy-start | bytes 196612
  222.6 73.6 %copy-start.27 = (f32[128,128]{1,0:T(8,128)S(1)}, f32[128,128]{1,0:T(8,128)}, u32[]{:S(2)}) copy-start(f32[128,128]{1,0:T(8,128)} %get-tuple-element.21) | copy-start | bytes 196612
  235.8 61.1 %copy-start.29 = (f32[128,128]{1,0:T(8,128)}, f32[128,128]{1,0:T(8,128)S(1)}, u32[]{:S(2)}) copy-start(f32[128,128]{1,0:T(8,128)S(1)} %get-tuple-element.19) | copy-start | bytes 196612
  246.8 50.1 %copy-start.14 = (f32[256,128]{1,0:T(8,128)}, f32[256,128]{1,0:T(8,128)S(1)}, u32[]{:S(2)}) copy-start(f32[256,128]{1,0:T(8,128)S(1)} %fusion.62) | copy-start | bytes 393220
  272.0 24.3 %copy-start.18 = (f32[8,128,128]{2,1,0:T(8,128)S(1)}, f32[8,128,128]{2,1,0:T(8,128)}, u32[]{:S(2)}) copy-start(f32[8,128,128]{2,1,0:T(8,128)} %get-tuple-element.56) | copy-start | bytes 1572868
  328.2 22.5 %copy-start.51 = (pred[1536]{0:T(1024)(128)(4,1)S(1)}, pred[1536]{0:T(1024)(128)(4,1)}, u32[]{:S(2)}) copy-start(pred[1536]{0:T(1024)(128)(4,1)} %get-tuple-element.67) | copy-start | bytes 4612
  328.2 22.5 %copy-start.60 = (f32[1280,1024]{0,1:T(8,128)S(1)}, f32[1280,1024]{0,1:T(8,128)}, u32[]{:S(2)}) copy-start(f32[1280,1024]{0,1:T(8,128)} %convolution_bitcast_fusion) | copy-start | bytes 15728644
  383.6 73.4 %collective-permute-start = (f32[5,128,1280]{1,2,0:T(8,128)}, f32[5,128,1280]{1,2,0:T(8,128)}, u32[]{:S(2)}, u32[]{:S(2)}) collective-permute-start(f32[5,128,1280]{1,2,0:T(8,128)} %bitcast.266), channel_id=1, source_target_pairs={{0,16},{16,0},{1,17},{17,1},{2,18},{18,2},{3,19},{19,3},{4,20},{20... | collective-permute-start | bytes 9830408 | tf_op jit(solution)/shard_map/ppermute | solution.py:28
  481.4 29.8 %slice-start.3 = ((s8[5242880]{0:T(1024)(128)(4,1)}), s8[4194304]{0:T(1024)(128)(4,1)S(1)}, s32[]{:S(2)}) async-start(s8[5242880]{0:T(1024)(128)(4,1)} %bitcast.258), calls=%async_computation.6 | async-start | bytes 8388608
  489.5 21.7 %slice-start.4 = ((s8[5242880]{0:T(1024)(128)(4,1)}), s8[1048576]{0:T(1024)(128)(4,1)S(1)}, s32[]{:S(2)}) async-start(s8[5242880]{0:T(1024)(128)(4,1)} %bitcast.258), calls=%async_computation.7 | async-start | bytes 2097152
  489.5 21.7 %copy-start.42 = (pred[1536]{0:T(1024)(128)(4,1)S(1)}, pred[1536]{0:T(1024)(128)(4,1)}, u32[]{:S(2)}) copy-start(pred[1536]{0:T(1024)(128)(4,1)} %compare_and_fusion) | copy-start | bytes 4612
  489.6 21.7 %copy-start.44 = (pred[1536]{0:T(1024)(128)(4,1)S(1)}, pred[1536]{0:T(1024)(128)(4,1)}, u32[]{:S(2)}) copy-start(pred[1536]{0:T(1024)(128)(4,1)} %copy-done.43) | copy-start | bytes 4612
  507.0 16.2 %collective-permute-start.2 = (f32[1024,128]{1,0:T(8,128)}, f32[1024,128]{1,0:T(8,128)}, u32[]{:S(2)}, u32[]{:S(2)}) collective-permute-start(f32[1024,128]{1,0:T(8,128)} %slice.269), channel_id=1, source_target_pairs={{0,2},{4,6},{8,10},{12,14},{16,18},{20,22},{24,26},{28,30}} | collective-permute-start | bytes 1572872 | tf_op jit(solution)/shard_map/ppermute | solution.py:23
  508.3 14.9 %collective-permute-start.1 = (f32[1024,128]{1,0:T(8,128)}, f32[1024,128]{1,0:T(8,128)}, u32[]{:S(2)}, u32[]{:S(2)}) collective-permute-start(f32[1024,128]{1,0:T(8,128)} %slice.269), channel_id=1, source_target_pairs={{0,1},{4,5},{8,9},{12,13},{16,17},{20,21},{24,25},{28,29}} | collective-permute-start | bytes 1572872 | tf_op jit(solution)/shard_map/ppermute | solution.py:23
  509.8 13.4 %collective-permute-start.3 = (f32[1024,128]{1,0:T(8,128)}, f32[1024,128]{1,0:T(8,128)}, u32[]{:S(2)}, u32[]{:S(2)}) collective-permute-start(f32[1024,128]{1,0:T(8,128)} %slice.269), channel_id=1, source_target_pairs={{0,3},{4,7},{8,11},{12,15},{16,19},{20,23},{24,27},{28,31}} | collective-permute-start | bytes 1572872 | tf_op jit(solution)/shard_map/ppermute | solution.py:23
  524.8 14.5 %collective-permute-start.4 = (f32[1024,128]{1,0:T(8,128)S(1)}, f32[1024,128]{1,0:T(8,128)S(1)}, u32[]{:S(2)}, u32[]{:S(2)}) collective-permute-start(f32[1024,128]{1,0:T(8,128)S(1)} %add_add_fusion), channel_id=1, source_target_pairs={{0,16},{16,0},{1,17},{17,1},{2,18},{18,2},{3,19},{19,3},{4,20},{20... | collective-permute-start | bytes 1572872 | tf_op jit(solution)/shard_map/ppermute | solution.py:28
  526.3 21.3 %slice-start.2 = ((f32[1536,1536]{1,0:T(8,128)}), f32[1536,1280]{1,0:T(8,128)S(1)}, s32[]{:S(2)}) async-start(f32[1536,1536]{1,0:T(8,128)} %copy-done.1), calls=%async_computation.5 | async-start | bytes 15728640 | tf_op jit(solution)/shard_map/slice | solution.py:140
  541.4 13.5 %collective-permute-start.6 = (f32[128,128]{1,0:T(8,128)S(1)}, f32[128,128]{1,0:T(8,128)S(1)}, u32[]{:S(2)}, u32[]{:S(2)}) collective-permute-start(f32[128,128]{1,0:T(8,128)S(1)} %slice.270), channel_id=1, source_target_pairs={{0,8},{1,9},{2,10},{3,11},{16,24},{17,25},{18,26},{19,27}} | collective-permute-start | bytes 196616 | tf_op jit(solution)/shard_map/ppermute | solution.py:23
  545.0 9.9 %collective-permute-start.5 = (f32[128,128]{1,0:T(8,128)S(1)}, f32[128,128]{1,0:T(8,128)S(1)}, u32[]{:S(2)}, u32[]{:S(2)}) collective-permute-start(f32[128,128]{1,0:T(8,128)S(1)} %slice.270), channel_id=1, source_target_pairs={{0,4},{1,5},{2,6},{3,7},{16,20},{17,21},{18,22},{19,23}} | collective-permute-start | bytes 196616 | tf_op jit(solution)/shard_map/ppermute | solution.py:23
  546.3 8.6 %collective-permute-start.7 = (f32[128,128]{1,0:T(8,128)S(1)}, f32[128,128]{1,0:T(8,128)S(1)}, u32[]{:S(2)}, u32[]{:S(2)}) collective-permute-start(f32[128,128]{1,0:T(8,128)S(1)} %slice.270), channel_id=1, source_target_pairs={{0,12},{1,13},{2,14},{3,15},{16,28},{17,29},{18,30},{19,31}} | collective-permute-start | bytes 196616 | tf_op jit(solution)/shard_map/ppermute | solution.py:23
  552.6 29.3 %copy-start.47 = (pred[1024]{0:T(1024)(128)(4,1)S(1)}, pred[1024]{0:T(1024)(128)(4,1)}, u32[]{:S(2)}) copy-start(pred[1024]{0:T(1024)(128)(4,1)} %broadcast_compare_fusion.4) | copy-start | bytes 3076
  552.6 29.3 %copy-start.55 = (pred[1024]{0:T(1024)(128)(4,1)S(1)}, pred[1024]{0:T(1024)(128)(4,1)}, u32[]{:S(2)}) copy-start(pred[1024]{0:T(1024)(128)(4,1)} %compare_and_fusion.1) | copy-start | bytes 3076
  552.6 48.5 %collective-permute-start.8 = (f32[2048,128]{1,0:T(8,128)}, f32[2048,128]{1,0:T(8,128)}, u32[]{:S(2)}, u32[]{:S(2)}) collective-permute-start(f32[2048,128]{1,0:T(8,128)} %bitcast.75), channel_id=1, source_target_pairs={{0,0},{4,1},{8,2},{12,3},{1,4},{5,5},{9,6},{13,7},{2,8},{6,9},{10,... | collective-permute-start | bytes 3145736 | tf_op jit(solution)/shard_map/ppermute | solution.py:240
  581.9 19.2 %copy-start.41 = (pred[2048]{0:T(1024)(128)(4,1)S(1)}, pred[2048]{0:T(1024)(128)(4,1)}, u32[]{:S(2)}) copy-start(pred[2048]{0:T(1024)(128)(4,1)} %broadcast_compare_fusion) | copy-start | bytes 6148
  (46 other events, 164.4 us)
Sparse Core Ops, SparseCore 0:
  10.7 50.8 all-gather.6
  63.1 97.4 all-gather.10
  162.2 37.7 all-gather.8

commit v13 on v12

--- a/solution.py
+++ b/solution.py
@@ -126,15 +126,22 @@
     col_index = within // TILE * grid_size * TILE + my_col * TILE + within % TILE
     rows_after = (row_index >= pivot_count)[:, None]
     cols_after = (col_index >= pivot_count)[None, :]
+    diag_rows = jnp.take(diag_factor, jnp.minimum(row_index, pivot_count - 1), axis=0)
+    full_rows = jnp.where(rows_after, solved_rows, diag_rows)
+    pivot_cols = jnp.take(full_rows, jnp.minimum(col_index[:width], pivot_count - 1), axis=1)
+    if skip:
+        core = front_work[skip:, skip:] - jnp.dot(
+            solved_by_rows.T, solved_by_cols, precision=lax.Precision.HIGH,
+            preferred_element_type=jnp.float32,
+        )
+        right = jnp.concatenate([jnp.zeros((skip, kept_count), jnp.float32), core])
+        return jnp.concatenate([pivot_cols, right], axis=1)
     update = jnp.dot(
         jnp.where(rows_after, solved_rows, 0.0),
         jnp.where(cols_after.T, solved_cols, 0.0).T,
         precision=lax.Precision.HIGH,
         preferred_element_type=jnp.float32,
     )
-    diag_rows = jnp.take(diag_factor, jnp.minimum(row_index, pivot_count - 1), axis=0)
-    full_rows = jnp.where(rows_after, solved_rows, diag_rows)
-    pivot_cols = jnp.take(full_rows, jnp.minimum(col_index[:width], pivot_count - 1), axis=1)
     trailing = jnp.where(rows_after & cols_after, front_work - update, 0.0)
     head = jnp.where(cols_after[:, :width], trailing[:, :width], pivot_cols)
     return jnp.concatenate([head, trailing[:, width:]], axis=1)

time: 627 us -> 616 us (0.982)
  matrix products: 89.5 us -> 83.1 us
    dot_general x1, matrix products: 22.4 us -> 15.7 us  [factor_child(): jnp.dot(solved_by_rows.T, solved_by_cols, precision=lax.Precision.HIGH, p...]
    unnamed x131 -> x101, local copies, waits for them, and re-layouts: 15.1 us -> 9.65 us
  transfers between devices with their start and end apart: 12 -> 12, of which waited for: 4 -> 4; matrix products, arithmetic and copies ran while one was open for 64% -> 65% of each run, Pallas kernels for 0% -> 0%
where the time goes in v13:
time: 616 us; the launch traced here: 611 us
  other arithmetic  296 us (48%)
  local copies, waits for them, and re-layouts  133 us (22%)
  matrix products  83.1 us (13%)
  waiting for transfers between devices  68.1 us (11%)
  starting transfers between devices  15.9 us (3%)
  between operations  15.4 us (2%)
    another operation x24, other arithmetic, factor_pivots(): factor = jnp.tril(jnp.linalg.cholesky(work[:TILE, :TILE]))  99.7 us
    another operation x16, other arithmetic, factor_pivots(): jax.scipy.linalg.solve_triangular(factor, eye, lower=True)  88.3 us
    all_gather x1, waiting for transfers between devices, factor_child(): lax.all_gather(front_work[:width, :width], ('row', 'col'), axis=0)  34.6 us
    dot_general x1, matrix products, factor_child(): jnp.dot(gathered_inverse, col_pieces.reshape(pivot_count, kept_count), pr...  20.2 us
    ppermute x1, waiting for transfers between devices, factor_parent(): my_cols = lax.ppermute(my_row_cols, ('row', 'col'), pairs)  17.5 us
    gather x2, local copies, waits for them, and re-layouts, factor_child(): jnp.take(diag_factor, jnp.minimum(row_index, pivot_count - 1), axis=0)  16.6 us
    select_n x2, local copies, waits for them, and re-layouts, place_tiles(): return jnp.where(valid, tiles, 0.0).reshape(parent_shape)  16.3 us
    ppermute x2, waiting for transfers between devices, from_partner(): lax.ppermute(shard, axis, [(i, i ^ 1 << distance) for i in range(lax.axis...  16 us
  transfers between devices with their start and end apart: 12, of which 4 were waited for; matrix products, arithmetic and copies ran while one was open for 65% of the time, Pallas kernels for 0%

profile of v13, /device:TPU:4, one launch (start us, length us, event | category | flops | bytes accessed | tf_op | source)
XLA Modules:
  0.0 611.4 jit_solution(7002771799699579693)
XLA Ops:
  27.1 34.6 %all-gather.7.cloned.1.call-done = f32[4096,256]{1,0:T(8,128)} async-done(((f32[256,256]{1,0:T(8,128)}), f32[4096,256]{1,0:T(8,128)}) %all-gather.7.cloned.1.call-update) | async-done | bytes 4194320 | tf_op jit(solution)/shard_map/all_gather | solution.py:87
  67.4 7.4 %copy.109 = f32[4,4,2,128,2,128]{3,0,2,5,1,4:T(4,128)} copy(f32[4,4,2,128,2,128]{5,4,3,2,1,0:T(2,128)} %reshape.413) | data formatting | bytes 8388608 | tf_op jit(solution)/shard_map/reshape | solution.py:88
  82.2 11.7 %cholesky.149 = f32[128,128]{1,0:T(8,128)S(1)} custom-call(f32[128,128]{1,0:T(8,128)S(1)} %fusion.79), custom_call_target="Cholesky" | custom-call | tf_op jit(solution)/shard_map/jit(cholesky)/cholesky | solution.py:46
  95.8 9.8 %custom-call.13 = f32[1,128,128]{1,2,0:T(8,128)S(1)} custom-call(f32[1,128,128]{2,1,0:T(8,128)S(1)} %get-tuple-element.28), custom_call_target="InvertDiagBlocksLowerTriangular" | custom-call | tf_op jit(solution)/shard_map/jit(_solve_triangular)/triangular_solve | solution.py:47
  114.3 11.9 %cholesky.160 = f32[128,128]{1,0:T(8,128)S(1)} custom-call(f32[128,128]{1,0:T(8,128)S(1)} %fusion.77), custom_call_target="Cholesky" | custom-call | tf_op jit(solution)/shard_map/jit(cholesky)/cholesky | solution.py:46
  128.2 9.8 %custom-call.14 = f32[1,128,128]{1,2,0:T(8,128)S(1)} custom-call(f32[1,128,128]{2,1,0:T(8,128)S(1)} %get-tuple-element.26), custom_call_target="InvertDiagBlocksLowerTriangular" | custom-call | tf_op jit(solution)/shard_map/jit(_solve_triangular)/triangular_solve | solution.py:47
  142.9 11.7 %cholesky.171 = f32[128,128]{1,0:T(8,128)S(1)} custom-call(f32[128,128]{1,0:T(8,128)S(1)} %fusion.75), custom_call_target="Cholesky" | custom-call | tf_op jit(solution)/shard_map/jit(cholesky)/cholesky | solution.py:46
  156.5 9.8 %custom-call.15 = f32[1,128,128]{1,2,0:T(8,128)S(1)} custom-call(f32[1,128,128]{2,1,0:T(8,128)S(1)} %get-tuple-element.24), custom_call_target="InvertDiagBlocksLowerTriangular" | custom-call | tf_op jit(solution)/shard_map/jit(_solve_triangular)/triangular_solve | solution.py:47
  171.3 12.1 %cholesky.182 = f32[128,128]{1,0:T(8,128)S(1)} custom-call(f32[128,128]{1,0:T(8,128)S(1)} %fusion.73), custom_call_target="Cholesky" | custom-call | tf_op jit(solution)/shard_map/jit(cholesky)/cholesky | solution.py:46
  185.4 9.8 %custom-call.16 = f32[1,128,128]{1,2,0:T(8,128)S(1)} custom-call(f32[1,128,128]{2,1,0:T(8,128)S(1)} %get-tuple-element.22), custom_call_target="InvertDiagBlocksLowerTriangular" | custom-call | tf_op jit(solution)/shard_map/jit(_solve_triangular)/triangular_solve | solution.py:47
  197.3 11.7 %cholesky.193 = f32[128,128]{1,0:T(8,128)S(1)} custom-call(f32[128,128]{1,0:T(8,128)S(1)} %fusion.71), custom_call_target="Cholesky" | custom-call | tf_op jit(solution)/shard_map/jit(cholesky)/cholesky | solution.py:46
  211.0 9.9 %custom-call.17 = f32[1,128,128]{1,2,0:T(8,128)S(1)} custom-call(f32[1,128,128]{2,1,0:T(8,128)S(1)} %get-tuple-element.20), custom_call_target="InvertDiagBlocksLowerTriangular" | custom-call | tf_op jit(solution)/shard_map/jit(_solve_triangular)/triangular_solve | solution.py:47
  222.7 11.7 %cholesky.204 = f32[128,128]{1,0:T(8,128)S(1)} custom-call(f32[128,128]{1,0:T(8,128)S(1)} %fusion.69), custom_call_target="Cholesky" | custom-call | tf_op jit(solution)/shard_map/jit(cholesky)/cholesky | solution.py:46
  235.8 9.8 %custom-call.18 = f32[1,128,128]{1,2,0:T(8,128)S(1)} custom-call(f32[1,128,128]{2,1,0:T(8,128)S(1)} %get-tuple-element.18), custom_call_target="InvertDiagBlocksLowerTriangular" | custom-call | tf_op jit(solution)/shard_map/jit(_solve_triangular)/triangular_solve | solution.py:47
  247.3 11.7 %cholesky.215 = f32[128,128]{1,0:T(8,128)S(1)} custom-call(f32[128,128]{1,0:T(8,128)S(1)} %fusion.67), custom_call_target="Cholesky" | custom-call | tf_op jit(solution)/shard_map/jit(cholesky)/cholesky | solution.py:46
  260.9 10.0 %custom-call.19 = f32[1,128,128]{1,2,0:T(8,128)S(1)} custom-call(f32[1,128,128]{2,1,0:T(8,128)S(1)} %get-tuple-element.16), custom_call_target="InvertDiagBlocksLowerTriangular" | custom-call | tf_op jit(solution)/shard_map/jit(_solve_triangular)/triangular_solve | solution.py:47
  272.4 11.7 %cholesky.226 = f32[128,128]{1,0:T(8,128)S(1)} custom-call(f32[128,128]{1,0:T(8,128)S(1)} %fusion.65), custom_call_target="Cholesky" | custom-call | tf_op jit(solution)/shard_map/jit(cholesky)/cholesky | solution.py:46
  286.1 9.8 %custom-call.20 = f32[1,128,128]{1,2,0:T(8,128)S(1)} custom-call(f32[1,128,128]{2,1,0:T(8,128)S(1)} %get-tuple-element.14), custom_call_target="InvertDiagBlocksLowerTriangular" | custom-call | tf_op jit(solution)/shard_map/jit(_solve_triangular)/triangular_solve | solution.py:47
  314.4 13.8 %fusion.132 = f32[1024,1280]{1,0:T(8,128)} fusion(f32[1024,1024]{0,1:T(8,128)} %bitcast.263, f32[1024,1280]{1,0:T(8,128)} %all-gather.11.cloned.1.call-done), kind=kOutput, calls=%fused_computation.371 | convolution fusion | flops 8053063680 | bytes 14680064 | tf_op jit(solution)/shard_map/dot_general | solution.py:110
  328.2 20.2 %fusion.131 = f32[1024,1280]{1,0:T(8,128)S(1)} fusion(f32[1024,1024]{0,1:T(8,128)} %bitcast.264, f32[1024,1280]{0,1:T(8,128)} %all-gather.9.cloned.1.call-done), kind=kOutput, calls=%fused_computation.370 | convolution fusion | flops 8053063680 | bytes 14680064 | tf_op jit(solution)/shard_map/dot_general | solution.py:106
  348.4 15.7 %convolution_subtract_fusion = f32[1280,1280]{1,0:T(8,128)S(1)} fusion(f32[1024,1280]{1,0:T(8,128)S(1)} %fusion.131, f32[1024,1280]{1,0:T(8,128)S(1)} %copy-done.45, f32[1536,1536]{1,0:T(8,128)} %bitcast.278), kind=kOutput, calls=%fused_computation.12 | convolution fusion | flops 10067968000 | bytes 23592960 | tf_op jit(solution)/shard_map/dot_general | solution.py:133
  390.6 10.0 %gather_fusion = f32[1536,1024]{1,0:T(8,128)} fusion(f32[1024,1024]{1,0:T(8,128)} %pad_dynamic-update-slice_fusion, s32[2048]{0:T(1024)S(1)} %pad_clamp_fusion), kind=kCustom, calls=%fused_computation.8 | custom fusion | bytes 12589056 | tf_op jit(solution)/shard_map/jit(_take)/gather | solution.py:129
  423.1 7.1 %gather_fusion.7 = f32[16,8,128,128]{3,2,1,0:T(8,128)} fusion(f32[8,128,10,128]{3,1,2,0:T(8,128)} %broadcast_select_fusion.1, s32[1024]{0:T(1024)} %get-tuple-element.68), kind=kCustom, calls=%fused_computation.3.clone | custom fusion | bytes 16777280 | tf_op jit(solution)/shard_map/jit(_take)/gather | solution.py:208
  434.4 8.1 %copy.140 = f32[8,128,16,128]{3,2,1,0:T(8,128)} copy(f32[8,128,16,128]{3,1,0,2:T(8,128)S(1)} %bitcast_select_fusion.1) | data formatting | bytes 16777216 | tf_op jit(solution)/shard_map/jit(_where)/select_n | solution.py:210
  458.9 7.1 %gather_fusion.11 = f32[16,8,128,128]{3,2,1,0:T(8,128)} fusion(f32[8,128,10,128]{3,1,2,0:T(8,128)} %broadcast_select_fusion, s32[1024]{0:T(1024)} %get-tuple-element.67), kind=kCustom, calls=%fused_computation.7.clone | custom fusion | bytes 16777280 | tf_op jit(solution)/shard_map/jit(_take)/gather | solution.py:208
  470.4 8.1 %copy.143 = f32[8,128,16,128]{3,2,1,0:T(8,128)} copy(f32[8,128,16,128]{3,1,0,2:T(8,128)S(1)} %bitcast_select_fusion) | data formatting | bytes 16777216 | tf_op jit(solution)/shard_map/jit(_where)/select_n | solution.py:210
  478.6 13.1 %bitcast_add_fusion = f32[1024,2048]{1,0:T(8,128)S(1)} fusion(f32[128,8,16,128]{3,2,1,0:T(8,128)} %bitcast.249, f32[1024,2048]{1,0:T(8,128)} %param.16, f32[128,8,16,128]{3,2,1,0:T(8,128)S(1)} %bitcast.248), kind=kLoop, calls=%fused_computation.16 | loop fusion | flops 4194304 | bytes 33554432 | tf_op jit(solution)/shard_map/add | solution.py:229
  515.6 12.8 %collective-permute-done.4 = f32[1024,128]{1,0:T(8,128)S(1)} collective-permute-done((f32[1024,128]{1,0:T(8,128)S(1)}, f32[1024,128]{1,0:T(8,128)S(1)}, u32[]{:S(2)}, u32[]{:S(2)}) %collective-permute-start.4) | collective-permute-done | bytes 524320 | tf_op jit(solution)/shard_map/ppermute | solution.py:28
  534.8 7.5 %fusion = f32[1,1536,1536]{2,1,0:T(8,128)} fusion(f32[1280,1280]{1,0:T(8,128)} %copy-done.1, f32[1536,256]{1,0:T(8,128)S(1)} %select_bitcast_fusion), kind=kLoop, calls=%fused_computation.14 | loop fusion | flops 7077888 | bytes 17563648 | tf_op jit(solution)/shard_map/broadcast_in_dim | solution.py:301
  544.9 11.7 %cholesky.237 = f32[128,128]{1,0:T(8,128)S(1)} custom-call(f32[128,128]{1,0:T(8,128)S(1)} %copy.147), custom_call_target="Cholesky" | custom-call | tf_op jit(solution)/shard_map/jit(cholesky)/cholesky | solution.py:249
  558.0 9.8 %custom-call.21 = f32[1,128,128]{1,2,0:T(8,128)S(1)} custom-call(f32[1,128,128]{2,1,0:T(8,128)S(1)} %get-tuple-element.8), custom_call_target="InvertDiagBlocksLowerTriangular" | custom-call | tf_op jit(solution)/shard_map/jit(_solve_triangular)/triangular_solve | solution.py:251
  573.1 17.5 %collective-permute-done.8 = f32[2048,128]{1,0:T(8,128)} collective-permute-done((f32[2048,128]{1,0:T(8,128)S(1)}, f32[2048,128]{1,0:T(8,128)}, u32[]{:S(2)}, u32[]{:S(2)}) %collective-permute-start.8) | collective-permute-done | bytes 1048608 | tf_op jit(solution)/shard_map/ppermute | solution.py:247
  (318 shorter events, 218.6 us)
Async XLA Ops:
  7.2 54.5 %all-gather.7.cloned.1.call-start = ((), (), s32[]{:S(2)}) async-start(), calls=%async_computation | async-start | bytes 4456448 | tf_op jit(solution)/shard_map/all_gather | solution.py:87
  8.9 305.5 %all-gather.11.cloned.1.call-start = ((), (), s32[]{:S(2)}) async-start(), calls=%async_computation.2 | async-start | bytes 6553600 | tf_op jit(solution)/shard_map/all_gather | solution.py:101
  11.4 316.8 %all-gather.9.cloned.1.call-start = ((), (), s32[]{:S(2)}) async-start(), calls=%async_computation.1 | async-start | bytes 6553600 | tf_op jit(solution)/shard_map/all_gather | solution.py:99
  168.7 129.7 %copy-start.6 = (f32[640,128]{1,0:T(8,128)}, f32[640,128]{1,0:T(8,128)S(1)}, u32[]{:S(2)}) copy-start(f32[640,128]{1,0:T(8,128)S(1)} %fusion.29) | copy-start | bytes 983044
  196.5 101.9 %copy-start.9 = (f32[512,128]{1,0:T(8,128)}, f32[512,128]{1,0:T(8,128)S(1)}, u32[]{:S(2)}) copy-start(f32[512,128]{1,0:T(8,128)S(1)} %fusion.35) | copy-start | bytes 786436
  197.1 98.9 %copy-start.3 = (f32[768,128]{1,0:T(8,128)S(1)}, f32[768,128]{1,0:T(8,128)}, u32[]{:S(2)}) copy-start(f32[768,128]{1,0:T(8,128)} %copy-done.2) | copy-start | bytes 1179652
  197.1 98.9 %copy-start.8 = (f32[128,896]{0,1:T(8,128)S(1)}, f32[128,896]{0,1:T(8,128)}, u32[]{:S(2)}) copy-start(f32[128,896]{0,1:T(8,128)} %copy.127) | copy-start | bytes 1376260
  197.1 98.9 %copy-start.18 = (f32[128,128]{1,0:T(8,128)S(1)}, f32[128,128]{1,0:T(8,128)}, u32[]{:S(2)}) copy-start(f32[128,128]{1,0:T(8,128)} %get-tuple-element.29) | copy-start | bytes 196612
  222.6 73.4 %copy-start.20 = (f32[128,128]{1,0:T(8,128)S(1)}, f32[128,128]{1,0:T(8,128)}, u32[]{:S(2)}) copy-start(f32[128,128]{1,0:T(8,128)} %get-tuple-element.21) | copy-start | bytes 196612
  235.8 60.9 %copy-start.22 = (f32[128,128]{1,0:T(8,128)}, f32[128,128]{1,0:T(8,128)S(1)}, u32[]{:S(2)}) copy-start(f32[128,128]{1,0:T(8,128)S(1)} %get-tuple-element.19) | copy-start | bytes 196612
  246.8 49.9 %copy-start.10 = (f32[256,128]{1,0:T(8,128)}, f32[256,128]{1,0:T(8,128)S(1)}, u32[]{:S(2)}) copy-start(f32[256,128]{1,0:T(8,128)S(1)} %fusion.58) | copy-start | bytes 393220
  271.8 24.3 %copy-start.14 = (f32[8,128,128]{2,1,0:T(8,128)S(1)}, f32[8,128,128]{2,1,0:T(8,128)}, u32[]{:S(2)}) copy-start(f32[8,128,128]{2,1,0:T(8,128)} %get-tuple-element.56) | copy-start | bytes 1572868
  328.2 20.2 %copy-start.45 = (f32[1024,1280]{1,0:T(8,128)S(1)}, f32[1024,1280]{1,0:T(8,128)}, u32[]{:S(2)}) copy-start(f32[1024,1280]{1,0:T(8,128)} %fusion.132) | copy-start | bytes 15728644
  348.4 15.7 %copy-start.7 = (f32[1024,1280]{1,0:T(8,128)}, f32[1024,1280]{1,0:T(8,128)S(1)}, u32[]{:S(2)}) copy-start(f32[1024,1280]{1,0:T(8,128)S(1)} %fusion.131) | copy-start | bytes 15728644
  372.4 73.4 %collective-permute-start = (f32[5,128,1280]{1,2,0:T(8,128)}, f32[5,128,1280]{1,2,0:T(8,128)}, u32[]{:S(2)}, u32[]{:S(2)}) collective-permute-start(f32[5,128,1280]{1,2,0:T(8,128)} %bitcast.265), channel_id=1, source_target_pairs={{0,16},{16,0},{1,17},{17,1},{2,18},{18,2},{3,19},{19,3},{4,20},{20... | collective-permute-start | bytes 9830408 | tf_op jit(solution)/shard_map/ppermute | solution.py:28
  374.4 14.3 %copy-start.28 = (f32[128,128]{1,0:T(8,128)S(1)}, f32[128,128]{1,0:T(8,128)}, u32[]{:S(2)}) copy-start(f32[128,128]{1,0:T(8,128)} %get-tuple-element.17) | copy-start | bytes 196612
  374.5 15.3 %copy-start.29 = (f32[128,128]{1,0:T(8,128)S(1)}, f32[128,128]{1,0:T(8,128)}, u32[]{:S(2)}) copy-start(f32[128,128]{1,0:T(8,128)} %get-tuple-element.15) | copy-start | bytes 196612
  470.4 29.8 %slice-start.2 = ((s8[5242880]{0:T(1024)(128)(4,1)}), s8[4194304]{0:T(1024)(128)(4,1)S(1)}, s32[]{:S(2)}) async-start(s8[5242880]{0:T(1024)(128)(4,1)} %bitcast.256), calls=%async_computation.5 | async-start | bytes 8388608
  478.6 21.7 %slice-start.3 = ((s8[5242880]{0:T(1024)(128)(4,1)}), s8[1048576]{0:T(1024)(128)(4,1)S(1)}, s32[]{:S(2)}) async-start(s8[5242880]{0:T(1024)(128)(4,1)} %bitcast.256), calls=%async_computation.6 | async-start | bytes 2097152
  478.6 21.7 %copy-start.31 = (pred[1536]{0:T(1024)(128)(4,1)S(1)}, pred[1536]{0:T(1024)(128)(4,1)}, u32[]{:S(2)}) copy-start(pred[1536]{0:T(1024)(128)(4,1)} %get-tuple-element.64) | copy-start | bytes 4612
  478.6 21.7 %copy-start.32 = (pred[1536]{0:T(1024)(128)(4,1)S(1)}, pred[1536]{0:T(1024)(128)(4,1)}, u32[]{:S(2)}) copy-start(pred[1536]{0:T(1024)(128)(4,1)} %get-tuple-element.65) | copy-start | bytes 4612
  496.0 16.3 %collective-permute-start.2 = (f32[1024,128]{1,0:T(8,128)}, f32[1024,128]{1,0:T(8,128)}, u32[]{:S(2)}, u32[]{:S(2)}) collective-permute-start(f32[1024,128]{1,0:T(8,128)} %slice.251), channel_id=1, source_target_pairs={{0,2},{4,6},{8,10},{12,14},{16,18},{20,22},{24,26},{28,30}} | collective-permute-start | bytes 1572872 | tf_op jit(solution)/shard_map/ppermute | solution.py:23
  497.3 15.0 %collective-permute-start.1 = (f32[1024,128]{1,0:T(8,128)}, f32[1024,128]{1,0:T(8,128)}, u32[]{:S(2)}, u32[]{:S(2)}) collective-permute-start(f32[1024,128]{1,0:T(8,128)} %slice.251), channel_id=1, source_target_pairs={{0,1},{4,5},{8,9},{12,13},{16,17},{20,21},{24,25},{28,29}} | collective-permute-start | bytes 1572872 | tf_op jit(solution)/shard_map/ppermute | solution.py:23
  498.8 13.5 %collective-permute-start.3 = (f32[1024,128]{1,0:T(8,128)}, f32[1024,128]{1,0:T(8,128)}, u32[]{:S(2)}, u32[]{:S(2)}) collective-permute-start(f32[1024,128]{1,0:T(8,128)} %slice.251), channel_id=1, source_target_pairs={{0,3},{4,7},{8,11},{12,15},{16,19},{20,23},{24,27},{28,31}} | collective-permute-start | bytes 1572872 | tf_op jit(solution)/shard_map/ppermute | solution.py:23
  513.9 14.4 %collective-permute-start.4 = (f32[1024,128]{1,0:T(8,128)S(1)}, f32[1024,128]{1,0:T(8,128)S(1)}, u32[]{:S(2)}, u32[]{:S(2)}) collective-permute-start(f32[1024,128]{1,0:T(8,128)S(1)} %add_add_fusion), channel_id=1, source_target_pairs={{0,16},{16,0},{1,17},{17,1},{2,18},{18,2},{3,19},{19,3},{4,20},{20... | collective-permute-start | bytes 1572872 | tf_op jit(solution)/shard_map/ppermute | solution.py:28
  528.5 16.1 %collective-permute-start.6 = (f32[128,128]{1,0:T(8,128)S(1)}, f32[128,128]{1,0:T(8,128)S(1)}, u32[]{:S(2)}, u32[]{:S(2)}) collective-permute-start(f32[128,128]{1,0:T(8,128)S(1)} %slice.252), channel_id=1, source_target_pairs={{0,8},{1,9},{2,10},{3,11},{16,24},{17,25},{18,26},{19,27}} | collective-permute-start | bytes 196616 | tf_op jit(solution)/shard_map/ppermute | solution.py:23
  532.2 12.4 %collective-permute-start.5 = (f32[128,128]{1,0:T(8,128)S(1)}, f32[128,128]{1,0:T(8,128)S(1)}, u32[]{:S(2)}, u32[]{:S(2)}) collective-permute-start(f32[128,128]{1,0:T(8,128)S(1)} %slice.252), channel_id=1, source_target_pairs={{0,4},{1,5},{2,6},{3,7},{16,20},{17,21},{18,22},{19,23}} | collective-permute-start | bytes 196616 | tf_op jit(solution)/shard_map/ppermute | solution.py:23
  533.5 11.1 %collective-permute-start.7 = (f32[128,128]{1,0:T(8,128)S(1)}, f32[128,128]{1,0:T(8,128)S(1)}, u32[]{:S(2)}, u32[]{:S(2)}) collective-permute-start(f32[128,128]{1,0:T(8,128)S(1)} %slice.252), channel_id=1, source_target_pairs={{0,12},{1,13},{2,14},{3,15},{16,28},{17,29},{18,30},{19,31}} | collective-permute-start | bytes 196616 | tf_op jit(solution)/shard_map/ppermute | solution.py:23
  542.3 28.6 %copy-start.35 = (pred[1024]{0:T(1024)(128)(4,1)S(1)}, pred[1024]{0:T(1024)(128)(4,1)}, u32[]{:S(2)}) copy-start(pred[1024]{0:T(1024)(128)(4,1)} %broadcast_compare_fusion.3) | copy-start | bytes 3076
  542.3 28.6 %copy-start.42 = (pred[1024]{0:T(1024)(128)(4,1)S(1)}, pred[1024]{0:T(1024)(128)(4,1)}, u32[]{:S(2)}) copy-start(pred[1024]{0:T(1024)(128)(4,1)} %compare_and_fusion.1) | copy-start | bytes 3076
  542.3 48.3 %collective-permute-start.8 = (f32[2048,128]{1,0:T(8,128)S(1)}, f32[2048,128]{1,0:T(8,128)}, u32[]{:S(2)}, u32[]{:S(2)}) collective-permute-start(f32[2048,128]{1,0:T(8,128)S(1)} %bitcast.273), channel_id=1, source_target_pairs={{0,0},{4,1},{8,2},{12,3},{1,4},{5,5},{9,6},{13,7},{2,8},{6,9},{10,... | collective-permute-start | bytes 3145736 | tf_op jit(solution)/shard_map/ppermute | solution.py:247
  570.9 19.7 %copy-start.30 = (pred[2048]{0:T(1024)(128)(4,1)S(1)}, pred[2048]{0:T(1024)(128)(4,1)}, u32[]{:S(2)}) copy-start(pred[2048]{0:T(1024)(128)(4,1)} %broadcast_compare_fusion) | copy-start | bytes 6148
  (30 other events, 155.6 us)
Sparse Core Ops, SparseCore 0:
  10.7 50.8 all-gather.6
  63.2 97.4 all-gather.10
  162.3 37.6 all-gather.8

commit v14 on v13

--- a/solution.py
+++ b/solution.py
@@ -126,16 +126,21 @@
     col_index = within // TILE * grid_size * TILE + my_col * TILE + within % TILE
     rows_after = (row_index >= pivot_count)[:, None]
     cols_after = (col_index >= pivot_count)[None, :]
+    if skip:
+        col_pick = jnp.minimum(col_index[:width], pivot_count - 1)
+        top_rows = jnp.take(diag_factor, jnp.minimum(row_index[:skip], pivot_count - 1), axis=0)
+        top = jnp.take(top_rows, col_pick, axis=1)
+        below = jnp.take(solved_by_rows, col_pick, axis=0).T
+        pivot_cols = jnp.concatenate([top, below])
+        core = front_work[skip:, skip:] - jnp.dot(
+            solved_by_rows.T, solved_by_cols, precision=lax.Precision.HIGH,
+            preferred_element_type=jnp.float32,
+        )
+        right = jnp.concatenate([jnp.zeros((skip, kept_count), jnp.float32), core])
+        return jnp.concatenate([pivot_cols, right], axis=1)
     diag_rows = jnp.take(diag_factor, jnp.minimum(row_index, pivot_count - 1), axis=0)
     full_rows = jnp.where(rows_after, solved_rows, diag_rows)
     pivot_cols = jnp.take(full_rows, jnp.minimum(col_index[:width], pivot_count - 1), axis=1)
-    if skip:
-        core = front_work[skip:, skip:] - jnp.dot(
-            solved_by_rows.T, solved_by_cols, precision=lax.Precision.HIGH,
-            preferred_element_type=jnp.float32,
-        )
-        right = jnp.concatenate([jnp.zeros((skip, kept_count), jnp.float32), core])
-        return jnp.concatenate([pivot_cols, right], axis=1)
     update = jnp.dot(
         jnp.where(rows_after, solved_rows, 0.0),
         jnp.where(cols_after.T, solved_cols, 0.0).T,

time: 616 us -> 618 us (level)
  waiting for transfers between devices: 68.1 us -> 87.1 us
  other arithmetic: 296 us -> 285 us
  local copies, waits for them, and re-layouts: 133 us -> 126 us
    ppermute x2, waiting for transfers between devices: 16 us -> 35.9 us  [from_partner(): lax.ppermute(shard, axis, [(i, i ^ 1 << distance) for i in range(lax.axis...]
    gather x4 -> x5, local copies, waits for them, and re-layouts: 22 us -> 12.4 us  [the longest x2 5.74 us: factor_child(): below = jnp.take(solved_by_rows, col_pick, axis=0).T]
  transfers between devices with their start and end apart: 12 -> 12, of which waited for: 4 -> 4; matrix products, arithmetic and copies ran while one was open for 65% -> 62% of each run, Pallas kernels for 0% -> 0%
where the time goes in v14:
time: 618 us; the launch traced here: 613 us
  other arithmetic  285 us (46%)
  local copies, waits for them, and re-layouts  126 us (20%)
  waiting for transfers between devices  87.1 us (14%)
  matrix products  83.1 us (13%)
  starting transfers between devices  15.9 us (3%)
  between operations  15.5 us (3%)
    another operation x24, other arithmetic, factor_pivots(): factor = jnp.tril(jnp.linalg.cholesky(work[:TILE, :TILE]))  99.7 us
    another operation x16, other arithmetic, factor_pivots(): jax.scipy.linalg.solve_triangular(factor, eye, lower=True)  88.4 us
    ppermute x2, waiting for transfers between devices, from_partner(): lax.ppermute(shard, axis, [(i, i ^ 1 << distance) for i in range(lax.axis...  35.9 us
    all_gather x1, waiting for transfers between devices, factor_child(): lax.all_gather(front_work[:width, :width], ('row', 'col'), axis=0)  35.2 us
    dot_general x1, matrix products, factor_child(): jnp.dot(gathered_inverse, col_pieces.reshape(pivot_count, kept_count), pr...  20.2 us
    select_n x2, local copies, waits for them, and re-layouts, place_tiles(): return jnp.where(valid, tiles, 0.0).reshape(parent_shape)  16.3 us
    ppermute x1, waiting for transfers between devices, factor_parent(): my_cols = lax.ppermute(my_row_cols, ('row', 'col'), pairs)  15.9 us
    dot_general x1, matrix products, factor_child(): jnp.dot(solved_by_rows.T, solved_by_cols, precision=lax.Precision.HIGH, p...  15.7 us
  transfers between devices with their start and end apart: 12, of which 4 were waited for; matrix products, arithmetic and copies ran while one was open for 62% of the time, Pallas kernels for 0%

profile of v14, /device:TPU:4, one launch (start us, length us, event | category | flops | bytes accessed | tf_op | source)
XLA Modules:
  0.0 612.6 jit_solution(63580281251433048)
XLA Ops:
  26.4 35.2 %all-gather.7.cloned.1.call-done = f32[4096,256]{1,0:T(8,128)} async-done(((f32[256,256]{1,0:T(8,128)}), f32[4096,256]{1,0:T(8,128)}) %all-gather.7.cloned.1.call-update) | async-done | bytes 4194320 | tf_op jit(solution)/shard_map/all_gather | solution.py:87
  67.4 7.4 %copy.112 = f32[4,4,2,128,2,128]{3,0,2,5,1,4:T(4,128)} copy(f32[4,4,2,128,2,128]{5,4,3,2,1,0:T(2,128)} %reshape.340) | data formatting | bytes 8388608 | tf_op jit(solution)/shard_map/reshape | solution.py:88
  82.2 11.7 %cholesky.149 = f32[128,128]{1,0:T(8,128)S(1)} custom-call(f32[128,128]{1,0:T(8,128)S(1)} %fusion.79), custom_call_target="Cholesky" | custom-call | tf_op jit(solution)/shard_map/jit(cholesky)/cholesky | solution.py:46
  95.8 9.8 %custom-call.13 = f32[1,128,128]{1,2,0:T(8,128)S(1)} custom-call(f32[1,128,128]{2,1,0:T(8,128)S(1)} %get-tuple-element.30), custom_call_target="InvertDiagBlocksLowerTriangular" | custom-call | tf_op jit(solution)/shard_map/jit(_solve_triangular)/triangular_solve | solution.py:47
  114.3 11.9 %cholesky.160 = f32[128,128]{1,0:T(8,128)S(1)} custom-call(f32[128,128]{1,0:T(8,128)S(1)} %fusion.77), custom_call_target="Cholesky" | custom-call | tf_op jit(solution)/shard_map/jit(cholesky)/cholesky | solution.py:46
  128.2 9.8 %custom-call.14 = f32[1,128,128]{1,2,0:T(8,128)S(1)} custom-call(f32[1,128,128]{2,1,0:T(8,128)S(1)} %get-tuple-element.28), custom_call_target="InvertDiagBlocksLowerTriangular" | custom-call | tf_op jit(solution)/shard_map/jit(_solve_triangular)/triangular_solve | solution.py:47
  142.9 11.7 %cholesky.171 = f32[128,128]{1,0:T(8,128)S(1)} custom-call(f32[128,128]{1,0:T(8,128)S(1)} %fusion.75), custom_call_target="Cholesky" | custom-call | tf_op jit(solution)/shard_map/jit(cholesky)/cholesky | solution.py:46
  156.5 9.8 %custom-call.15 = f32[1,128,128]{1,2,0:T(8,128)S(1)} custom-call(f32[1,128,128]{2,1,0:T(8,128)S(1)} %get-tuple-element.26), custom_call_target="InvertDiagBlocksLowerTriangular" | custom-call | tf_op jit(solution)/shard_map/jit(_solve_triangular)/triangular_solve | solution.py:47
  171.4 12.1 %cholesky.182 = f32[128,128]{1,0:T(8,128)S(1)} custom-call(f32[128,128]{1,0:T(8,128)S(1)} %fusion.73), custom_call_target="Cholesky" | custom-call | tf_op jit(solution)/shard_map/jit(cholesky)/cholesky | solution.py:46
  185.5 9.8 %custom-call.16 = f32[1,128,128]{1,2,0:T(8,128)S(1)} custom-call(f32[1,128,128]{2,1,0:T(8,128)S(1)} %get-tuple-element.24), custom_call_target="InvertDiagBlocksLowerTriangular" | custom-call | tf_op jit(solution)/shard_map/jit(_solve_triangular)/triangular_solve | solution.py:47
  197.4 11.7 %cholesky.193 = f32[128,128]{1,0:T(8,128)S(1)} custom-call(f32[128,128]{1,0:T(8,128)S(1)} %fusion.71), custom_call_target="Cholesky" | custom-call | tf_op jit(solution)/shard_map/jit(cholesky)/cholesky | solution.py:46
  211.0 9.9 %custom-call.17 = f32[1,128,128]{1,2,0:T(8,128)S(1)} custom-call(f32[1,128,128]{2,1,0:T(8,128)S(1)} %get-tuple-element.22), custom_call_target="InvertDiagBlocksLowerTriangular" | custom-call | tf_op jit(solution)/shard_map/jit(_solve_triangular)/triangular_solve | solution.py:47
  222.8 11.7 %cholesky.204 = f32[128,128]{1,0:T(8,128)S(1)} custom-call(f32[128,128]{1,0:T(8,128)S(1)} %fusion.69), custom_call_target="Cholesky" | custom-call | tf_op jit(solution)/shard_map/jit(cholesky)/cholesky | solution.py:46
  235.9 9.8 %custom-call.18 = f32[1,128,128]{1,2,0:T(8,128)S(1)} custom-call(f32[1,128,128]{2,1,0:T(8,128)S(1)} %get-tuple-element.20), custom_call_target="InvertDiagBlocksLowerTriangular" | custom-call | tf_op jit(solution)/shard_map/jit(_solve_triangular)/triangular_solve | solution.py:47
  247.3 11.7 %cholesky.215 = f32[128,128]{1,0:T(8,128)S(1)} custom-call(f32[128,128]{1,0:T(8,128)S(1)} %fusion.67), custom_call_target="Cholesky" | custom-call | tf_op jit(solution)/shard_map/jit(cholesky)/cholesky | solution.py:46
  261.0 10.0 %custom-call.19 = f32[1,128,128]{1,2,0:T(8,128)S(1)} custom-call(f32[1,128,128]{2,1,0:T(8,128)S(1)} %get-tuple-element.18), custom_call_target="InvertDiagBlocksLowerTriangular" | custom-call | tf_op jit(solution)/shard_map/jit(_solve_triangular)/triangular_solve | solution.py:47
  272.5 11.7 %cholesky.226 = f32[128,128]{1,0:T(8,128)S(1)} custom-call(f32[128,128]{1,0:T(8,128)S(1)} %fusion.65), custom_call_target="Cholesky" | custom-call | tf_op jit(solution)/shard_map/jit(cholesky)/cholesky | solution.py:46
  286.2 9.8 %custom-call.20 = f32[1,128,128]{1,2,0:T(8,128)S(1)} custom-call(f32[1,128,128]{2,1,0:T(8,128)S(1)} %get-tuple-element.16), custom_call_target="InvertDiagBlocksLowerTriangular" | custom-call | tf_op jit(solution)/shard_map/jit(_solve_triangular)/triangular_solve | solution.py:47
  314.5 13.8 %fusion.126 = f32[1024,1280]{1,0:T(8,128)} fusion(f32[1024,1024]{0,1:T(8,128)} %bitcast.263, f32[1024,1280]{1,0:T(8,128)} %all-gather.11.cloned.1.call-done), kind=kOutput, calls=%fused_computation.357 | convolution fusion | flops 8053063680 | bytes 14680064 | tf_op jit(solution)/shard_map/dot_general | solution.py:110
  328.3 20.2 %fusion.125 = f32[1024,1280]{1,0:T(8,128)S(1)} fusion(f32[1024,1024]{0,1:T(8,128)} %bitcast.264, f32[1024,1280]{0,1:T(8,128)} %all-gather.9.cloned.1.call-done), kind=kOutput, calls=%fused_computation.356 | convolution fusion | flops 8053063680 | bytes 14680064 | tf_op jit(solution)/shard_map/dot_general | solution.py:106
  348.4 15.7 %convolution_subtract_fusion = f32[1280,1280]{1,0:T(8,128)S(1)} fusion(f32[1024,1280]{1,0:T(8,128)S(1)} %fusion.125, f32[1024,1280]{1,0:T(8,128)S(1)} %copy-done.55, f32[1536,1536]{1,0:T(8,128)} %bitcast.275), kind=kOutput, calls=%fused_computation.13 | convolution fusion | flops 10067968000 | bytes 23592960 | tf_op jit(solution)/shard_map/dot_general | solution.py:135
  394.3 7.1 %gather_fusion.8 = f32[16,8,128,128]{3,2,1,0:T(8,128)} fusion(f32[8,128,10,128]{3,1,2,0:T(8,128)} %broadcast_select_fusion.1, s32[1024]{0:T(1024)} %pad_clamp_fusion.3), kind=kCustom, calls=%fused_computation.3.clone | custom fusion | bytes 16777280 | tf_op jit(solution)/shard_map/jit(_take)/gather | solution.py:213
  405.7 8.1 %copy.144 = f32[8,128,16,128]{3,2,1,0:T(8,128)} copy(f32[8,128,16,128]{3,1,0,2:T(8,128)S(1)} %bitcast_select_fusion.1) | data formatting | bytes 16777216 | tf_op jit(solution)/shard_map/jit(_where)/select_n | solution.py:215
  420.2 25.5 %collective-permute-done = f32[5,128,1280]{1,2,0:T(8,128)} collective-permute-done((f32[5,128,1280]{1,2,0:T(8,128)}, f32[5,128,1280]{1,2,0:T(8,128)}, u32[]{:S(2)}, u32[]{:S(2)}) %collective-permute-start) | collective-permute-done | bytes 3276832 | tf_op jit(solution)/shard_map/ppermute | solution.py:28
  458.9 7.1 %gather_fusion.12 = f32[16,8,128,128]{3,2,1,0:T(8,128)} fusion(f32[8,128,10,128]{3,1,2,0:T(8,128)} %broadcast_select_fusion, s32[1024]{0:T(1024)} %pad_clamp_fusion.1), kind=kCustom, calls=%fused_computation.7.clone | custom fusion | bytes 16777280 | tf_op jit(solution)/shard_map/jit(_take)/gather | solution.py:213
  470.4 8.1 %copy.147 = f32[8,128,16,128]{3,2,1,0:T(8,128)} copy(f32[8,128,16,128]{3,1,0,2:T(8,128)S(1)} %bitcast_select_fusion) | data formatting | bytes 16777216 | tf_op jit(solution)/shard_map/jit(_where)/select_n | solution.py:215
  478.5 13.1 %bitcast_add_fusion = f32[1024,2048]{1,0:T(8,128)S(1)} fusion(f32[128,8,16,128]{3,2,1,0:T(8,128)} %bitcast.250, f32[1024,2048]{1,0:T(8,128)} %param.16, f32[128,8,16,128]{3,2,1,0:T(8,128)S(1)} %bitcast.249), kind=kLoop, calls=%fused_computation.17 | loop fusion | flops 4194304 | bytes 33554432 | tf_op jit(solution)/shard_map/add | solution.py:234
  521.0 10.4 %collective-permute-done.4 = f32[1024,128]{1,0:T(8,128)S(1)} collective-permute-done((f32[1024,128]{1,0:T(8,128)S(1)}, f32[1024,128]{1,0:T(8,128)S(1)}, u32[]{:S(2)}, u32[]{:S(2)}) %collective-permute-start.4) | collective-permute-done | bytes 524320 | tf_op jit(solution)/shard_map/ppermute | solution.py:28
  547.6 11.7 %cholesky.237 = f32[128,128]{1,0:T(8,128)S(1)} custom-call(f32[128,128]{1,0:T(8,128)S(1)} %copy.151), custom_call_target="Cholesky" | custom-call | tf_op jit(solution)/shard_map/jit(cholesky)/cholesky | solution.py:254
  560.7 9.8 %custom-call.21 = f32[1,128,128]{1,2,0:T(8,128)S(1)} custom-call(f32[1,128,128]{2,1,0:T(8,128)S(1)} %get-tuple-element.8), custom_call_target="InvertDiagBlocksLowerTriangular" | custom-call | tf_op jit(solution)/shard_map/jit(_solve_triangular)/triangular_solve | solution.py:256
  575.8 15.9 %collective-permute-done.8 = f32[2048,128]{1,0:T(8,128)} collective-permute-done((f32[2048,128]{1,0:T(8,128)}, f32[2048,128]{1,0:T(8,128)}, u32[]{:S(2)}, u32[]{:S(2)}) %collective-permute-start.8) | collective-permute-done | bytes 1048608 | tf_op jit(solution)/shard_map/ppermute | solution.py:252
  593.5 6.9 %subtract_select_fusion = f32[1024,2048]{1,0:T(8,128)S(1)} fusion(f32[1024,2048]{1,0:T(8,128)} %copy-done, f32[2048,128]{1,0:T(8,128)S(1)} %convolution_select_fusion, pred[2048]{0:T(1024)(128)(4,1)S(1)} %broadcast_compare_fusion, pred[1024]{0:T(1024)(128)(4,1)S(1)} %copy-done.45, f32[1024,128]{1,0:T(8,128)S(1)} %get-tuple-element.63), kind=kOutput, calls=%fused_computation.22 | convolution fusion | flops 1617035264 | bytes 18353152 | tf_op jit(solution)/shard_map/dot_general | solution.py:270
  (339 shorter events, 208.1 us)
Async XLA Ops:
  7.2 54.5 %all-gather.7.cloned.1.call-start = ((), (), s32[]{:S(2)}) async-start(), calls=%async_computation | async-start | bytes 4456448 | tf_op jit(solution)/shard_map/all_gather | solution.py:87
  8.9 305.6 %all-gather.11.cloned.1.call-start = ((), (), s32[]{:S(2)}) async-start(), calls=%async_computation.2 | async-start | bytes 6553600 | tf_op jit(solution)/shard_map/all_gather | solution.py:101
  11.4 316.8 %all-gather.9.cloned.1.call-start = ((), (), s32[]{:S(2)}) async-start(), calls=%async_computation.1 | async-start | bytes 6553600 | tf_op jit(solution)/shard_map/all_gather | solution.py:99
  168.7 129.7 %copy-start.8 = (f32[640,128]{1,0:T(8,128)}, f32[640,128]{1,0:T(8,128)S(1)}, u32[]{:S(2)}) copy-start(f32[640,128]{1,0:T(8,128)S(1)} %fusion.29) | copy-start | bytes 983044
  196.6 101.9 %copy-start.12 = (f32[512,128]{1,0:T(8,128)}, f32[512,128]{1,0:T(8,128)S(1)}, u32[]{:S(2)}) copy-start(f32[512,128]{1,0:T(8,128)S(1)} %fusion.35) | copy-start | bytes 786436
  197.2 98.9 %copy-start.4 = (f32[768,128]{1,0:T(8,128)S(1)}, f32[768,128]{1,0:T(8,128)}, u32[]{:S(2)}) copy-start(f32[768,128]{1,0:T(8,128)} %copy-done.3) | copy-start | bytes 1179652
  197.2 98.9 %copy-start.10 = (f32[128,896]{0,1:T(8,128)S(1)}, f32[128,896]{0,1:T(8,128)}, u32[]{:S(2)}) copy-start(f32[128,896]{0,1:T(8,128)} %copy.114) | copy-start | bytes 1376260
  197.2 98.9 %copy-start.23 = (f32[128,128]{1,0:T(8,128)S(1)}, f32[128,128]{1,0:T(8,128)}, u32[]{:S(2)}) copy-start(f32[128,128]{1,0:T(8,128)} %get-tuple-element.31) | copy-start | bytes 196612
  222.7 73.4 %copy-start.27 = (f32[128,128]{1,0:T(8,128)S(1)}, f32[128,128]{1,0:T(8,128)}, u32[]{:S(2)}) copy-start(f32[128,128]{1,0:T(8,128)} %get-tuple-element.23) | copy-start | bytes 196612
  235.9 60.9 %copy-start.29 = (f32[128,128]{1,0:T(8,128)}, f32[128,128]{1,0:T(8,128)S(1)}, u32[]{:S(2)}) copy-start(f32[128,128]{1,0:T(8,128)S(1)} %get-tuple-element.21) | copy-start | bytes 196612
  246.9 49.9 %copy-start.14 = (f32[256,128]{1,0:T(8,128)}, f32[256,128]{1,0:T(8,128)S(1)}, u32[]{:S(2)}) copy-start(f32[256,128]{1,0:T(8,128)S(1)} %fusion.58) | copy-start | bytes 393220
  271.9 24.3 %copy-start.18 = (f32[8,128,128]{2,1,0:T(8,128)S(1)}, f32[8,128,128]{2,1,0:T(8,128)}, u32[]{:S(2)}) copy-start(f32[8,128,128]{2,1,0:T(8,128)} %get-tuple-element.60) | copy-start | bytes 1572868
  328.3 20.2 %copy-start.55 = (f32[1024,1280]{1,0:T(8,128)S(1)}, f32[1024,1280]{1,0:T(8,128)}, u32[]{:S(2)}) copy-start(f32[1024,1280]{1,0:T(8,128)} %fusion.126) | copy-start | bytes 15728644
  348.4 15.7 %copy-start.2 = (f32[1024,1280]{1,0:T(8,128)}, f32[1024,1280]{1,0:T(8,128)S(1)}, u32[]{:S(2)}) copy-start(f32[1024,1280]{1,0:T(8,128)S(1)} %fusion.125) | copy-start | bytes 15728644
  372.4 73.4 %collective-permute-start = (f32[5,128,1280]{1,2,0:T(8,128)}, f32[5,128,1280]{1,2,0:T(8,128)}, u32[]{:S(2)}, u32[]{:S(2)}) collective-permute-start(f32[5,128,1280]{1,2,0:T(8,128)} %bitcast.265), channel_id=1, source_target_pairs={{0,16},{16,0},{1,17},{17,1},{2,18},{18,2},{3,19},{19,3},{4,20},{20... | collective-permute-start | bytes 9830408 | tf_op jit(solution)/shard_map/ppermute | solution.py:28
  405.7 10.9 %copy-start.13 = (f32[512,128]{1,0:T(8,128)S(1)}, f32[512,128]{1,0:T(8,128)}, u32[]{:S(2)}) copy-start(f32[512,128]{1,0:T(8,128)} %copy-done.12) | copy-start | bytes 786436
  405.7 10.9 %copy-start.22 = (f32[384,128]{1,0:T(8,128)S(1)}, f32[384,128]{1,0:T(8,128)}, u32[]{:S(2)}) copy-start(f32[384,128]{1,0:T(8,128)} %copy-done.21) | copy-start | bytes 589828
  466.0 12.5 %slice-start = ((s8[8388608]{0:T(1024)(128)(4,1)}), s8[4194304]{0:T(1024)(128)(4,1)S(1)}, s32[]{:S(2)}) async-start(s8[8388608]{0:T(1024)(128)(4,1)} %bitcast.247), calls=%async_computation.3 | async-start | bytes 8388608
  478.5 21.6 %copy-start.39 = (f32[128,128]{1,0:T(8,128)S(1)}, f32[128,128]{1,0:T(8,128)}, u32[]{:S(2)}) copy-start(f32[128,128]{1,0:T(8,128)} %get-tuple-element.17) | copy-start | bytes 196612
  478.5 22.5 %copy-start.41 = (s32[1024]{0:T(1024)S(1)}, s32[1024]{0:T(1024)}, u32[]{:S(2)}) copy-start(s32[1024]{0:T(1024)} %pad_clamp_fusion.7) | copy-start | bytes 12292
  495.9 20.4 %collective-permute-start.2 = (f32[1024,128]{1,0:T(8,128)}, f32[1024,128]{1,0:T(8,128)}, u32[]{:S(2)}, u32[]{:S(2)}) collective-permute-start(f32[1024,128]{1,0:T(8,128)} %slice.259), channel_id=1, source_target_pairs={{0,2},{4,6},{8,10},{12,14},{16,18},{20,22},{24,26},{28,30}} | collective-permute-start | bytes 1572872 | tf_op jit(solution)/shard_map/ppermute | solution.py:23
  497.1 19.2 %collective-permute-start.1 = (f32[1024,128]{1,0:T(8,128)}, f32[1024,128]{1,0:T(8,128)}, u32[]{:S(2)}, u32[]{:S(2)}) collective-permute-start(f32[1024,128]{1,0:T(8,128)} %slice.259), channel_id=1, source_target_pairs={{0,1},{4,5},{8,9},{12,13},{16,17},{20,21},{24,25},{28,29}} | collective-permute-start | bytes 1572872 | tf_op jit(solution)/shard_map/ppermute | solution.py:23
  498.6 17.7 %collective-permute-start.3 = (f32[1024,128]{1,0:T(8,128)}, f32[1024,128]{1,0:T(8,128)}, u32[]{:S(2)}, u32[]{:S(2)}) collective-permute-start(f32[1024,128]{1,0:T(8,128)} %slice.259), channel_id=1, source_target_pairs={{0,3},{4,7},{8,11},{12,15},{16,19},{20,23},{24,27},{28,31}} | collective-permute-start | bytes 1572872 | tf_op jit(solution)/shard_map/ppermute | solution.py:23
  511.8 27.9 %slice-start.2 = ((s8[6553600]{0:T(1024)(128)(4,1)}), s8[2359296]{0:T(1024)(128)(4,1)S(1)}, s32[]{:S(2)}) async-start(s8[6553600]{0:T(1024)(128)(4,1)} %bitcast.252), calls=%async_computation.5 | async-start | bytes 4718592
  516.3 23.4 %slice-start.3 = ((s8[6553600]{0:T(1024)(128)(4,1)}), s8[4194304]{0:T(1024)(128)(4,1)S(1)}, s32[]{:S(2)}) async-start(s8[6553600]{0:T(1024)(128)(4,1)} %bitcast.252), calls=%async_computation.6 | async-start | bytes 8388608
  518.1 13.3 %collective-permute-start.4 = (f32[1024,128]{1,0:T(8,128)S(1)}, f32[1024,128]{1,0:T(8,128)S(1)}, u32[]{:S(2)}, u32[]{:S(2)}) collective-permute-start(f32[1024,128]{1,0:T(8,128)S(1)} %add_add_fusion), channel_id=1, source_target_pairs={{0,16},{16,0},{1,17},{17,1},{2,18},{18,2},{3,19},{19,3},{4,20},{20... | collective-permute-start | bytes 1572872 | tf_op jit(solution)/shard_map/ppermute | solution.py:28
  533.4 13.1 %collective-permute-start.6 = (f32[128,128]{1,0:T(8,128)S(1)}, f32[128,128]{1,0:T(8,128)S(1)}, u32[]{:S(2)}, u32[]{:S(2)}) collective-permute-start(f32[128,128]{1,0:T(8,128)S(1)} %slice.260), channel_id=1, source_target_pairs={{0,8},{1,9},{2,10},{3,11},{16,24},{17,25},{18,26},{19,27}} | collective-permute-start | bytes 196616 | tf_op jit(solution)/shard_map/ppermute | solution.py:23
  537.1 9.4 %collective-permute-start.5 = (f32[128,128]{1,0:T(8,128)S(1)}, f32[128,128]{1,0:T(8,128)S(1)}, u32[]{:S(2)}, u32[]{:S(2)}) collective-permute-start(f32[128,128]{1,0:T(8,128)S(1)} %slice.260), channel_id=1, source_target_pairs={{0,4},{1,5},{2,6},{3,7},{16,20},{17,21},{18,22},{19,23}} | collective-permute-start | bytes 196616 | tf_op jit(solution)/shard_map/ppermute | solution.py:23
  538.4 8.1 %collective-permute-start.7 = (f32[128,128]{1,0:T(8,128)S(1)}, f32[128,128]{1,0:T(8,128)S(1)}, u32[]{:S(2)}, u32[]{:S(2)}) collective-permute-start(f32[128,128]{1,0:T(8,128)S(1)} %slice.260), channel_id=1, source_target_pairs={{0,12},{1,13},{2,14},{3,15},{16,28},{17,29},{18,30},{19,31}} | collective-permute-start | bytes 196616 | tf_op jit(solution)/shard_map/ppermute | solution.py:23
  544.2 29.4 %copy-start.45 = (pred[1024]{0:T(1024)(128)(4,1)S(1)}, pred[1024]{0:T(1024)(128)(4,1)}, u32[]{:S(2)}) copy-start(pred[1024]{0:T(1024)(128)(4,1)} %broadcast_compare_fusion.2) | copy-start | bytes 3076
  544.2 29.4 %copy-start.52 = (pred[1024]{0:T(1024)(128)(4,1)S(1)}, pred[1024]{0:T(1024)(128)(4,1)}, u32[]{:S(2)}) copy-start(pred[1024]{0:T(1024)(128)(4,1)} %compare_and_fusion) | copy-start | bytes 3076
  544.2 47.5 %collective-permute-start.8 = (f32[2048,128]{1,0:T(8,128)}, f32[2048,128]{1,0:T(8,128)}, u32[]{:S(2)}, u32[]{:S(2)}) collective-permute-start(f32[2048,128]{1,0:T(8,128)} %bitcast.74), channel_id=1, source_target_pairs={{0,0},{4,1},{8,2},{12,3},{1,4},{5,5},{9,6},{13,7},{2,8},{6,9},{10,... | collective-permute-start | bytes 3145736 | tf_op jit(solution)/shard_map/ppermute | solution.py:252
  (40 other events, 194.1 us)
Sparse Core Ops, SparseCore 0:
  10.7 50.8 all-gather.6
  63.2 97.4 all-gather.10
  162.3 37.7 all-gather.8
